TPU v7x, 32 devices: a whole 2x2x4 slice. The times are simulated.
32 devices in a mesh: gx: 4 (over z), gy: 4 (over y, x), gz: 2 (over core).
Axes of the slice: x: 2, y: 2, z: 4, core: 2. Of those that a mesh axis runs over, the one named last changes fastest.
Arguments:
- residual: float32 [128, 139264], P(None, ('gx', 'gy', 'gz')), may hold values from -6 to 6
- diag_inverse: bfloat16 [640, 256, 256], P(('gx', 'gy', 'gz'))
- coupling: bfloat16 [608, 256, 256], P(('gx', 'gy', 'gz')), may hold values from -0.09375 to 0.09375
- parent: int32 [640], P(('gx', 'gy', 'gz')), may hold values from 0 to 18, as said below
- send_rows: int32 [192, 128], P(('gx', 'gy', 'gz')), may hold values from 0 to 4351
- counts: int32 [32], P(('gx', 'gy', 'gz')), may hold values from 10 to 40, as said below
- deflation: float32 [40, 139264], P(None, ('gx', 'gy', 'gz')), may hold values from -0.09375 to 0.09375
- coarse_inverse: float32 [1280, 1280], P(('gx', 'gy', 'gz')), as said below
Outputs:
- preconditioned: float32 [128, 139264], P(None, ('gx', 'gy', 'gz'))
Inputs may be any that keep to these rules, and one draw needn't show every extreme that they name: The parent of supernode b >= 1 is one of b - 4 to b - 1 of the same subdomain (0 at the least), the last supernode's parent is the one before it, and the entry of supernode 0 is 0. `counts`: every draw has a subdomain with 40 and one with 10 vectors. coarse_inverse is symmetric.
All inputs are finite; a program needn't handle non-finite values.
Results may differ from a plain program's by a relative error of at most 0.005.
Values may be sent and summed in bfloat16 or wider, within the bound.
No kernel may reach another device: no remote copies, remote signals or barrier semaphores. Data moves between devices by JAX's collectives and lax.ppermute only.
A program may use at most 128 MiB of HBM per device.

v0:
```python
import jax
import jax.numpy as jnp
from jax import lax
from jax.sharding import PartitionSpec as P


def with_halo(block, sides, width):
    for axis, dim in sides:
        count = lax.axis_size(axis)
        forward = [(i, i + 1) for i in range(count - 1)]
        backward = [(target, source) for source, target in forward]
        low = lax.ppermute(
            lax.slice_in_dim(block, block.shape[dim] - width, None, axis=dim), axis, forward
        )
        high = lax.ppermute(lax.slice_in_dim(block, 0, width, axis=dim), axis, backward)
        block = jnp.concatenate([low, block, high], axis=dim)
    return block


def solve_local(extended, diag_inverse, coupling, parent):
    nrhs_here, width_ext = extended.shape
    blocks_n, block_w, _ = diag_inverse.shape
    blocks = extended.reshape(nrhs_here, blocks_n, block_w).transpose(1, 0, 2)
    first = jnp.einsum(
        "rs,ts->rt",
        blocks[0].astype(jnp.bfloat16),
        diag_inverse[0],
        preferred_element_type=jnp.float32,
    ).astype(jnp.bfloat16)
    store = jnp.zeros((blocks_n, nrhs_here, block_w), jnp.bfloat16).at[0].set(first)
    places = lax.iota(jnp.int32, blocks_n)

    def forward(store, item):
        block, inverse_blk, couple, link, place = item
        prior = lax.dynamic_index_in_dim(store, link, 0, keepdims=False)
        lower = (
            block - jnp.einsum("rs,ts->rt", prior, couple, preferred_element_type=jnp.float32)
        ).astype(jnp.bfloat16)
        value = jnp.einsum(
            "rs,ts->rt", lower, inverse_blk, preferred_element_type=jnp.float32
        ).astype(jnp.bfloat16)
        return (lax.dynamic_update_index_in_dim(store, value, place, 0), None)

    store, _ = lax.scan(
        forward, store, (blocks[1:], diag_inverse[1:], coupling, parent[1:], places[1:])
    )

    def backward(carry, item):
        value, inverse_blk, link, place = item
        upper = (
            value.astype(jnp.float32) - lax.dynamic_index_in_dim(carry, place, 0, keepdims=False)
        ).astype(jnp.bfloat16)
        result = jnp.einsum(
            "rs,st->rt", upper, inverse_blk, preferred_element_type=jnp.float32
        ).astype(jnp.bfloat16)
        couple = lax.dynamic_index_in_dim(coupling, jnp.maximum(place - 1, 0), 0, keepdims=False)
        push = jnp.einsum("rs,st->rt", result, couple, preferred_element_type=jnp.float32) * (
            place > 0
        ).astype(jnp.float32)
        target = lax.dynamic_index_in_dim(carry, link, 0, keepdims=False)
        carry = lax.dynamic_update_index_in_dim(carry, target + push, link, 0)
        return (carry, result)

    empty = jnp.zeros((blocks_n, nrhs_here, block_w), jnp.float32)
    _, solved = lax.scan(backward, empty, (store, diag_inverse, parent, places), reverse=True)
    return solved.transpose(1, 0, 2).reshape(nrhs_here, width_ext)


def pick_slot(padded, axis_pos, coord, slot_id):
    where_at = [1, 1, 1]
    where_at[axis_pos] = coord
    return padded[where_at[0], where_at[1], where_at[2], slot_id]


def per_device(
    residual, diag_inverse, coupling, parent, send_rows, counts, deflation, coarse_inverse
):
    nrhs_here, owned_n = residual.shape
    slots_n, face_w = send_rows.shape
    kmax_here = deflation.shape[0]
    outgoing = jnp.moveaxis(jnp.take(residual, send_rows, axis=1), 1, 0)
    mask = (lax.iota(jnp.int32, kmax_here) < counts[0]).astype(jnp.float32)
    vectors = deflation * mask[:, None]
    coeffs = jnp.dot(
        residual, vectors.T, precision=lax.Precision.HIGHEST, preferred_element_type=jnp.float32
    )
    padded = with_halo(outgoing[None, None, None], (("gx", 0), ("gy", 1), ("gz", 2)), 1)
    incoming = []
    for axis_pos in range(3):
        incoming.append(pick_slot(padded, axis_pos, 2, 2 * axis_pos))
        incoming.append(pick_slot(padded, axis_pos, 0, 2 * axis_pos + 1))
    extended = jnp.concatenate([residual] + incoming, axis=1)
    solved = solve_local(extended, diag_inverse, coupling, parent)
    corrections = jnp.moveaxis(solved[:, owned_n:].reshape(nrhs_here, slots_n, face_w), 1, 0)
    back = with_halo(corrections[None, None, None], (("gx", 0), ("gy", 1), ("gz", 2)), 1)
    returned = []
    for axis_pos in range(3):
        returned.append(pick_slot(back, axis_pos, 0, 2 * axis_pos))
        returned.append(pick_slot(back, axis_pos, 2, 2 * axis_pos + 1))
    solved_coarse = lax.dot_general(
        lax.all_gather(coeffs, ("gx", "gy", "gz"), axis=1, tiled=True),
        coarse_inverse,
        (((1,), (1,)), ((), ())),
        precision=lax.Precision.HIGHEST,
        preferred_element_type=jnp.float32,
    )
    total = solved[:, :owned_n].astype(jnp.float32)
    for slot_id in range(6):
        total = total.at[:, send_rows[slot_id]].add(returned[slot_id].astype(jnp.float32))
    total = total + jnp.dot(
        solved_coarse, vectors, precision=lax.Precision.HIGHEST, preferred_element_type=jnp.float32
    )
    return total


def solution(mesh):
    return jax.shard_map(
        per_device,
        mesh=mesh,
        in_specs=(
            P(None, ("gx", "gy", "gz")),
            P(("gx", "gy", "gz"), None, None),
            P(("gx", "gy", "gz"), None, None),
            P(("gx", "gy", "gz")),
            P(("gx", "gy", "gz"), None),
            P(("gx", "gy", "gz")),
            P(None, ("gx", "gy", "gz")),
            P(("gx", "gy", "gz"), None),
        ),
        out_specs=P(None, ("gx", "gy", "gz")),
        check_vma=False,
    )
```

profile of v0, /device:TPU:0, one launch (start us, length us, event | category | flops | bytes accessed | tf_op | source)
XLA Modules:
  0.0 555.2 jit_solution(16365458862300856485)
XLA Ops:
  6.5 5.6 %collective-permute-start.1 = (f32[1,1,1,6,128,128]{4,5,3,2,1,0:T(8,128)S(1)}, f32[1,1,1,6,128,128]{4,5,3,2,1,0:T(8,128)S(1)}, u32[]{:S(2)}, u32[]{:S(2)}) collective-permute-start(f32[1,1,1,6,128,128]{4,5,3,2,1,0:T(8,128)S(1)} %select_bitcast_fusion), channel_id=1, source_target_pairs={{0,8},{8,16},{16,24},{1,9},{9,17},{17,25},{2,10},{10,18},{18,26},{... | collective-permute-start | bytes 1179656 | tf_op jit(solution)/shard_map/ppermute | solution.py:12
  12.1 7.1 %collective-permute-done = f32[1,1,1,6,128,128]{4,5,3,2,1,0:T(8,128)S(1)} collective-permute-done((f32[1,1,1,6,128,128]{4,5,3,2,1,0:T(8,128)S(1)}, f32[1,1,1,6,128,128]{4,5,3,2,1,0:T(8,128)S(1)}, u32[]{:S(2)}, u32[]{:S(2)}) %collective-permute-start) | collective-permute-done | bytes 393248 | tf_op jit(solution)/shard_map/ppermute | solution.py:15
  21.8 4.6 collective-permute-start.3
  26.4 24.9 %collective-permute-done.2 = f32[3,1,1,6,128,128]{4,5,3,2,1,0:T(8,128)S(1)} collective-permute-done((f32[3,1,1,6,128,128]{4,5,3,2,1,0:T(8,128)S(1)}, f32[3,1,1,6,128,128]{4,5,3,2,1,0:T(8,128)S(1)}, u32[]{:S(2)}, u32[]{:S(2)}) %collective-permute-start.2) | collective-permute-done | bytes 1179680 | tf_op jit(solution)/shard_map/ppermute | solution.py:15
  55.2 6.7 %collective-permute-start.5 = (f32[3,3,1,6,128,128]{4,5,3,2,1,0:T(8,128)}, f32[3,3,1,6,128,128]{4,5,3,2,1,0:T(8,128)}, u32[]{:S(2)}, u32[]{:S(2)}) collective-permute-start(f32[3,3,1,6,128,128]{4,5,3,2,1,0:T(8,128)} %pad_maximum_fusion), channel_id=1, source_target_pairs={{0,1},{2,3},{4,5},{6,7},{8,9},{10,11},{12,13},{14,15},{16,17},{18,... | collective-permute-start | bytes 10616840 | tf_op jit(solution)/shard_map/ppermute | solution.py:12
  61.8 3.4 slice.108
  71.5 148.3 %while.28 = (s32[]{:T(128)}, bf16[20,128,256]{2,1,0:T(8,128)(2,1)}, f32[19,128,256]{1,2,0:T(8,128)S(1)}, s32[19]{0:T(128)S(1)}, bf16[19,256,256]{2,1,0:T(8,128)(...) while((s32[]{:T(128)}, bf16[20,128,256]{2,1,0:T(8,128)(2,1)}, ...), condition=%wide.region_1.2_spmd, body=%wide.region_0.1_spmd.sunk | while | flops 33652744 | bytes 1180877 | solution.py:44
  221.4 183.8 %while.29 = (s32[]{:T(128)}, f32[20,128,256]{2,1,0:T(8,128)S(1)}, bf16[20,128,256]{1,2,0:T(8,128)(2,1)}, s32[20]{0:T(128)S(1)}, bf16[20,128,256]{2,1,0:T(8,128)(...) while((s32[]{:T(128)}, f32[20,128,256]{2,1,0:T(8,128)S(1)}, ...), condition=%wide.region_3.4_spmd, body=%wide.region_2.3_spmd.sunk | while | flops 33751048 | bytes 1378079 | solution.py:65
  406.1 4.7 collective-permute-start.6
  414.0 4.4 collective-permute-done.7
  418.4 24.2 %collective-permute-start.8 = (bf16[3,1,1,6,128,128]{4,5,3,2,1,0:T(8,128)(2,1)S(1)}, bf16[3,1,1,6,128,128]{4,5,3,2,1,0:T(8,128)(2,1)S(1)}, u32[]{:S(2)}, u32[]{:S(2)}) collective-permute-start(bf16[3,1,1,6,128,128]{4,5,3,2,1,0:T(8,128)(2,1)S(1)} %pad_maximum_fusion.3), channel_id=1, source_target_pairs={{0,2},{2,4},{4,6},{1,3},{3,5},{5,7},{8,10},{10,12},{12,14},{9,11},... | collective-permute-start | bytes 1769480 | tf_op jit(solution)/shard_map/ppermute | solution.py:12
  444.0 8.4 %collective-permute-done.8 = bf16[3,1,1,6,128,128]{4,5,3,2,1,0:T(8,128)(2,1)S(1)} collective-permute-done((bf16[3,1,1,6,128,128]{4,5,3,2,1,0:T(8,128)(2,1)S(1)}, bf16[3,1,1,6,128,128]{4,5,3,2,1,0:T(8,128)(2,1)S(1)}, u32[]{:S(2)}, u32[]{:S(2)}) %collective-permute-start.8) | collective-permute-done | bytes 589856 | tf_op jit(solution)/shard_map/ppermute | solution.py:12
  452.4 16.5 %collective-permute-done.9 = bf16[3,1,1,6,128,128]{4,5,3,2,1,0:T(8,128)(2,1)S(1)} collective-permute-done((bf16[3,1,1,6,128,128]{4,5,3,2,1,0:T(8,128)(2,1)S(1)}, bf16[3,1,1,6,128,128]{4,5,3,2,1,0:T(8,128)(2,1)S(1)}, u32[]{:S(2)}, u32[]{:S(2)}) %collective-permute-start.9) | collective-permute-done | bytes 589856 | tf_op jit(solution)/shard_map/ppermute | solution.py:15
  470.3 2.5 collective-permute-start.10
  475.4 2.4 convolution_bitcast_fusion
  477.8 40.4 %all_gather.3 = f32[128,1280]{0,1:T(8,128)S(1)} all-gather(f32[128,40]{0,1:T(8,128)S(1)} %convolution_bitcast_fusion), channel_id=1, replica_groups=mesh['gx'=4,'gy'=4,'gz'=2] {'gx','gy','gz'}, dimensions={1}, use_global_device_ids=true | all-gather | bytes 675840 | tf_op jit(solution)/shard_map/all_gather | solution.py:101
  520.8 3.1 convolution_add_fusion
  525.9 4.4 scatter_custom_fusion
  530.3 4.4 scatter_custom_fusion.1
  534.7 4.4 scatter_custom_fusion.2
  539.1 4.4 scatter_custom_fusion.3
  543.5 4.4 scatter_custom_fusion.4
  547.9 4.4 scatter_custom_fusion.5
  552.2 3.0 copy.21
  (324 shorter events, 196.4 us)
Async XLA Ops:
  0.0 518.2 %copy-start = (f32[40,1280]{1,0:T(8,128)S(1)}, f32[40,1280]{1,0:T(8,128)}, u32[]{:S(2)}) copy-start(f32[40,1280]{1,0:T(8,128)} %param.21) | copy-start | bytes 614404
  5.2 14.0 %collective-permute-start = (f32[1,1,1,6,128,128]{4,5,3,2,1,0:T(8,128)S(1)}, f32[1,1,1,6,128,128]{4,5,3,2,1,0:T(8,128)S(1)}, u32[]{:S(2)}, u32[]{:S(2)}) collective-permute-start(f32[1,1,1,6,128,128]{4,5,3,2,1,0:T(8,128)S(1)} %select_bitcast_fusion), channel_id=1, source_target_pairs={{8,0},{16,8},{24,16},{9,1},{17,9},{25,17},{10,2},{18,10},{26,18},{... | collective-permute-start | bytes 1179656 | tf_op jit(solution)/shard_map/ppermute | solution.py:15
  6.5 13.9 %collective-permute-start.1 = (f32[1,1,1,6,128,128]{4,5,3,2,1,0:T(8,128)S(1)}, f32[1,1,1,6,128,128]{4,5,3,2,1,0:T(8,128)S(1)}, u32[]{:S(2)}, u32[]{:S(2)}) collective-permute-start(f32[1,1,1,6,128,128]{4,5,3,2,1,0:T(8,128)S(1)} %select_bitcast_fusion), channel_id=1, source_target_pairs={{0,8},{8,16},{16,24},{1,9},{9,17},{17,25},{2,10},{10,18},{18,26},{... | collective-permute-start | bytes 1179656 | tf_op jit(solution)/shard_map/ppermute | solution.py:12
  20.5 30.8 %collective-permute-start.2 = (f32[3,1,1,6,128,128]{4,5,3,2,1,0:T(8,128)S(1)}, f32[3,1,1,6,128,128]{4,5,3,2,1,0:T(8,128)S(1)}, u32[]{:S(2)}, u32[]{:S(2)}) collective-permute-start(f32[3,1,1,6,128,128]{4,5,3,2,1,0:T(8,128)S(1)} %pad_maximum_fusion.2), channel_id=1, source_target_pairs={{2,0},{4,2},{6,4},{3,1},{5,3},{7,5},{10,8},{12,10},{14,12},{11,9},... | collective-permute-start | bytes 3538952 | tf_op jit(solution)/shard_map/ppermute | solution.py:15
  21.8 29.5 %collective-permute-start.3 = (f32[3,1,1,6,128,128]{4,5,3,2,1,0:T(8,128)S(1)}, f32[3,1,1,6,128,128]{4,5,3,2,1,0:T(8,128)S(1)}, u32[]{:S(2)}, u32[]{:S(2)}) collective-permute-start(f32[3,1,1,6,128,128]{4,5,3,2,1,0:T(8,128)S(1)} %pad_maximum_fusion.2), channel_id=1, source_target_pairs={{0,2},{2,4},{4,6},{1,3},{3,5},{5,7},{8,10},{10,12},{12,14},{9,11},... | collective-permute-start | bytes 3538952 | tf_op jit(solution)/shard_map/ppermute | solution.py:12
  51.3 2.2 copy-start.4
  51.3 2.6 copy-start.5
  53.9 13.4 %collective-permute-start.4 = (f32[3,3,1,6,128,128]{4,5,3,2,1,0:T(8,128)}, f32[3,3,1,6,128,128]{4,5,3,2,1,0:T(8,128)}, u32[]{:S(2)}, u32[]{:S(2)}) collective-permute-start(f32[3,3,1,6,128,128]{4,5,3,2,1,0:T(8,128)} %pad_maximum_fusion), channel_id=1, source_target_pairs={{1,0},{3,2},{5,4},{7,6},{9,8},{11,10},{13,12},{15,14},{17,16},{19,... | collective-permute-start | bytes 10616840 | tf_op jit(solution)/shard_map/ppermute | solution.py:15
  55.2 13.0 %collective-permute-start.5 = (f32[3,3,1,6,128,128]{4,5,3,2,1,0:T(8,128)}, f32[3,3,1,6,128,128]{4,5,3,2,1,0:T(8,128)}, u32[]{:S(2)}, u32[]{:S(2)}) collective-permute-start(f32[3,3,1,6,128,128]{4,5,3,2,1,0:T(8,128)} %pad_maximum_fusion), channel_id=1, source_target_pairs={{0,1},{2,3},{4,5},{6,7},{8,9},{10,11},{12,13},{14,15},{16,17},{18,... | collective-permute-start | bytes 10616840 | tf_op jit(solution)/shard_map/ppermute | solution.py:12
  61.8 3.5 copy-start.11
  406.1 68.7 %copy-start.10 = (s32[6,128]{1,0:T(8,128)S(1)}, s32[6,128]{1,0:T(8,128)}, u32[]{:S(2)}) copy-start(s32[6,128]{1,0:T(8,128)} %param.18) | copy-start | bytes 9220
  406.1 69.3 %copy-start.1 = (f32[128,4352]{1,0:T(8,128)S(1)}, f32[128,4352]{1,0:T(8,128)}, u32[]{:S(2)}) copy-start(f32[128,4352]{1,0:T(8,128)} %param.14) | copy-start | bytes 6684676
  406.1 69.3 %copy-start.3 = (f32[40,4352]{1,0:T(8,128)S(1)}, f32[40,4352]{1,0:T(8,128)}, u32[]{:S(2)}) copy-start(f32[40,4352]{1,0:T(8,128)} %param.20) | copy-start | bytes 2088964
  406.1 7.8 %collective-permute-start.6 = (bf16[1,1,1,6,128,128]{4,5,3,2,1,0:T(8,128)(2,1)S(1)}, bf16[1,1,1,6,128,128]{4,5,3,2,1,0:T(8,128)(2,1)S(1)}, u32[]{:S(2)}, u32[]{:S(2)}) collective-permute-start(bf16[1,1,1,6,128,128]{4,5,3,2,1,0:T(8,128)(2,1)S(1)} %bitcast.215), channel_id=1, source_target_pairs={{0,8},{8,16},{16,24},{1,9},{9,17},{17,25},{2,10},{10,18},{18,26},{... | collective-permute-start | bytes 589832 | tf_op jit(solution)/shard_map/ppermute | solution.py:12
  410.8 7.6 %collective-permute-start.7 = (bf16[1,1,1,6,128,128]{4,5,3,2,1,0:T(8,128)(2,1)S(1)}, bf16[1,1,1,6,128,128]{4,5,3,2,1,0:T(8,128)(2,1)S(1)}, u32[]{:S(2)}, u32[]{:S(2)}) collective-permute-start(bf16[1,1,1,6,128,128]{4,5,3,2,1,0:T(8,128)(2,1)S(1)} %bitcast.216), channel_id=1, source_target_pairs={{8,0},{16,8},{24,16},{9,1},{17,9},{25,17},{10,2},{18,10},{26,18},{... | collective-permute-start | bytes 589832 | tf_op jit(solution)/shard_map/ppermute | solution.py:15
  414.0 56.3 %copy-start.6 = (bf16[1,1,1,6,128,128]{4,5,3,2,1,0:T(8,128)(2,1)}, bf16[1,1,1,6,128,128]{4,5,3,2,1,0:T(8,128)(2,1)S(1)}, u32[]{:S(2)}) copy-start(bf16[1,1,1,6,128,128]{4,5,3,2,1,0:T(8,128)(2,1)S(1)} %collective-permute-done.6) | copy-start | bytes 589828
  418.4 51.9 %copy-start.7 = (bf16[1,1,1,6,128,128]{4,5,3,2,1,0:T(8,128)(2,1)}, bf16[1,1,1,6,128,128]{4,5,3,2,1,0:T(8,128)(2,1)S(1)}, u32[]{:S(2)}) copy-start(bf16[1,1,1,6,128,128]{4,5,3,2,1,0:T(8,128)(2,1)S(1)} %collective-permute-done.7) | copy-start | bytes 589828
  418.4 34.0 %collective-permute-start.8 = (bf16[3,1,1,6,128,128]{4,5,3,2,1,0:T(8,128)(2,1)S(1)}, bf16[3,1,1,6,128,128]{4,5,3,2,1,0:T(8,128)(2,1)S(1)}, u32[]{:S(2)}, u32[]{:S(2)}) collective-permute-start(bf16[3,1,1,6,128,128]{4,5,3,2,1,0:T(8,128)(2,1)S(1)} %pad_maximum_fusion.3), channel_id=1, source_target_pairs={{0,2},{2,4},{4,6},{1,3},{3,5},{5,7},{8,10},{10,12},{12,14},{9,11},... | collective-permute-start | bytes 1769480 | tf_op jit(solution)/shard_map/ppermute | solution.py:12
  442.7 26.2 %collective-permute-start.9 = (bf16[3,1,1,6,128,128]{4,5,3,2,1,0:T(8,128)(2,1)S(1)}, bf16[3,1,1,6,128,128]{4,5,3,2,1,0:T(8,128)(2,1)S(1)}, u32[]{:S(2)}, u32[]{:S(2)}) collective-permute-start(bf16[3,1,1,6,128,128]{4,5,3,2,1,0:T(8,128)(2,1)S(1)} %pad_maximum_fusion.3), channel_id=1, source_target_pairs={{2,0},{4,2},{6,4},{3,1},{5,3},{7,5},{10,8},{12,10},{14,12},{11,9},... | collective-permute-start | bytes 1769480 | tf_op jit(solution)/shard_map/ppermute | solution.py:15
  452.4 25.3 %copy-start.8 = (bf16[3,1,1,6,128,128]{4,5,3,2,1,0:T(8,128)(2,1)}, bf16[3,1,1,6,128,128]{4,5,3,2,1,0:T(8,128)(2,1)S(1)}, u32[]{:S(2)}) copy-start(bf16[3,1,1,6,128,128]{4,5,3,2,1,0:T(8,128)(2,1)S(1)} %collective-permute-done.8) | copy-start | bytes 1769476
  468.9 8.9 %copy-start.9 = (bf16[3,1,1,6,128,128]{4,5,3,2,1,0:T(8,128)(2,1)}, bf16[3,1,1,6,128,128]{4,5,3,2,1,0:T(8,128)(2,1)S(1)}, u32[]{:S(2)}) copy-start(bf16[3,1,1,6,128,128]{4,5,3,2,1,0:T(8,128)(2,1)S(1)} %collective-permute-done.9) | copy-start | bytes 1769476
  470.3 73.2 %collective-permute-start.10 = (bf16[3,3,1,6,128,128]{4,5,3,2,1,0:T(8,128)(2,1)}, bf16[3,3,1,6,128,128]{4,5,3,2,1,0:T(8,128)(2,1)}, u32[]{:S(2)}, u32[]{:S(2)}) collective-permute-start(bf16[3,3,1,6,128,128]{4,5,3,2,1,0:T(8,128)(2,1)} %pad_maximum_fusion.1), channel_id=1, source_target_pairs={{0,1},{2,3},{4,5},{6,7},{8,9},{10,11},{12,13},{14,15},{16,17},{18,... | collective-permute-start | bytes 5308424 | tf_op jit(solution)/shard_map/ppermute | solution.py:12
  472.8 75.0 %collective-permute-start.11 = (bf16[3,3,1,6,128,128]{4,5,3,2,1,0:T(8,128)(2,1)}, bf16[3,3,1,6,128,128]{4,5,3,2,1,0:T(8,128)(2,1)}, u32[]{:S(2)}, u32[]{:S(2)}) collective-permute-start(bf16[3,3,1,6,128,128]{4,5,3,2,1,0:T(8,128)(2,1)} %pad_maximum_fusion.1), channel_id=1, source_target_pairs={{1,0},{3,2},{5,4},{7,6},{9,8},{11,10},{13,12},{15,14},{17,16},{19,... | collective-permute-start | bytes 5308424 | tf_op jit(solution)/shard_map/ppermute | solution.py:15
  475.4 44.7 %copy-start.2 = (bf16[20,128,256]{1,2,0:T(8,128)(2,1)S(1)}, bf16[20,128,256]{1,2,0:T(8,128)(2,1)}, u32[]{:S(2)}) copy-start(bf16[20,128,256]{1,2,0:T(8,128)(2,1)} %get-tuple-element.237) | copy-start | bytes 3932164
where the time goes:
time: 561 us; the launch traced here: 555 us
  loops' own time  170 us (30%)
  local copies, waits for them, and re-layouts  103 us (18%)
  matrix products  89.1 us (16%)
  waiting for transfers between devices  64.4 us (11%)
  starting transfers between devices  56 us (10%)
  blocking collectives  40.4 us (7%)
  other arithmetic  32.2 us (6%)
    another operation x1, loops' own time, solve_local(): lax.scan(backward, empty, (store, diag_inverse, parent, places), reverse=...  99.9 us
    another operation x1, loops' own time, solve_local(): lax.scan(forward, store, (blocks[1:], diag_inverse[1:], coupling, parent[...  69.8 us
    ppermute x6, waiting for transfers between devices, with_halo(): lax.ppermute(lax.slice_in_dim(block, 0, width, axis=dim), axis, backward)  52.9 us
    ppermute x6, starting transfers between devices, with_halo(): lax.ppermute(lax.slice_in_dim(block, block.shape[dim] - width, None, axis...  48.3 us
    all_gather x1, blocking collectives, per_device(): lax.all_gather(coeffs, ('gx', 'gy', 'gz'), axis=1, tiled=True)  40.4 us
    dot_general x19, matrix products, forward(): jnp.einsum('rs,ts->rt', lower, inverse_blk, preferred_element_type=jnp.fl...  37 us
    scatter-add x6, other arithmetic, per_device(): total.at[:, send_rows[slot_id]].add(returned[slot_id].astype(jnp.float32))  26.3 us
    dynamic_slice x76, local copies, waits for them, and re-layouts, solve_local(): lax.scan(forward, store, (blocks[1:], diag_inverse[1:], coupling, parent[...  25.4 us
  transfers between devices with their start and end apart: 12, of which 7 were waited for; matrix products, arithmetic and copies ran while one was open for 7% of the time, Pallas kernels for 0%

commit v1 on v0

v1 whole, which is shorter than its diff:
```python
import functools

import jax
import jax.numpy as jnp
from jax import lax
from jax.experimental import pallas as pl
from jax.experimental.pallas import tpu as pltpu
from jax.sharding import PartitionSpec as P

AXES = ("gx", "gy", "gz")
NT = (((1,), (1,)), ((), ()))


def solve_kernel(parent_ref, res_ref, slot_ref, inv_ref, cpl_ref, own_ref, zslot_ref, y_ref, carry_ref):
    blocks_n, block_w, _ = inv_ref.shape
    owned_blocks = res_ref.shape[1] // block_w

    def columns(b):
        if b < owned_blocks:
            return res_ref, pl.ds(b * block_w, block_w)
        return slot_ref, pl.ds((b - owned_blocks) * block_w, block_w)

    def link(b):
        return jnp.clip(parent_ref[b], 0, blocks_n - 1)

    for b in range(blocks_n):
        ref, cols = columns(b)
        x = ref[:, cols]
        if b == 0:
            lower = x.astype(jnp.bfloat16)
        else:
            prior = y_ref[link(b)]
            lower = (
                x - lax.dot_general(prior, cpl_ref[b - 1], NT, preferred_element_type=jnp.float32)
            ).astype(jnp.bfloat16)
        y_ref[b] = lax.dot_general(
            lower, inv_ref[b], NT, preferred_element_type=jnp.float32
        ).astype(jnp.bfloat16)

    carry_ref[...] = jnp.zeros(carry_ref.shape, carry_ref.dtype)
    for b in reversed(range(blocks_n)):
        upper = (y_ref[b].astype(jnp.float32) - carry_ref[b]).astype(jnp.bfloat16)
        result = jnp.dot(upper, inv_ref[b], preferred_element_type=jnp.float32).astype(jnp.bfloat16)
        if b < owned_blocks:
            own_ref[:, pl.ds(b * block_w, block_w)] = result
        else:
            zslot_ref[:, pl.ds((b - owned_blocks) * block_w, block_w)] = result
        if b > 0:
            push = jnp.dot(result, cpl_ref[b - 1], preferred_element_type=jnp.float32)
            p = link(b)
            carry_ref[p] = carry_ref[p] + push


def local_solve(parent, residual, slots, diag_inverse, coupling):
    nrhs_here, owned_n = residual.shape
    blocks_n, block_w, _ = diag_inverse.shape
    vmem = pltpu.VMEM
    return pl.pallas_call(
        solve_kernel,
        out_shape=(
            jax.ShapeDtypeStruct((nrhs_here, owned_n), jnp.bfloat16),
            jax.ShapeDtypeStruct(slots.shape, jnp.bfloat16),
        ),
        in_specs=[
            pl.BlockSpec(memory_space=pltpu.SMEM),
            pl.BlockSpec(memory_space=vmem),
            pl.BlockSpec(memory_space=vmem),
            pl.BlockSpec(memory_space=vmem),
            pl.BlockSpec(memory_space=vmem),
        ],
        out_specs=(pl.BlockSpec(memory_space=vmem), pl.BlockSpec(memory_space=vmem)),
        scratch_shapes=[
            pltpu.VMEM((blocks_n, nrhs_here, block_w), jnp.bfloat16),
            pltpu.VMEM((blocks_n, nrhs_here, block_w), jnp.float32),
        ],
        compiler_params=pltpu.CompilerParams(vmem_limit_bytes=48 * 1024 * 1024),
    )(parent, residual, slots, diag_inverse, coupling)


def shift(value, axis, up):
    count = lax.axis_size(axis)
    if up:
        pairs = [(i, i + 1) for i in range(count - 1)]
    else:
        pairs = [(i + 1, i) for i in range(count - 1)]
    return lax.ppermute(value, axis, pairs)


def per_device(
    residual, diag_inverse, coupling, parent, send_rows, counts, deflation, coarse_inverse
):
    nrhs_here, owned_n = residual.shape
    slots_n, face_w = send_rows.shape
    kmax_here = deflation.shape[0]
    mask = (lax.iota(jnp.int32, kmax_here) < counts[0]).astype(jnp.float32)
    vectors = deflation * mask[:, None]
    coeffs = jnp.dot(
        residual, vectors.T, precision=lax.Precision.HIGHEST, preferred_element_type=jnp.float32
    )
    gathered = lax.all_gather(coeffs, AXES, axis=1, tiled=True)
    solved_coarse = lax.dot_general(
        gathered,
        coarse_inverse,
        (((1,), (1,)), ((), ())),
        precision=lax.Precision.HIGHEST,
        preferred_element_type=jnp.float32,
    )

    outgoing = jnp.take(residual, send_rows, axis=1)
    incoming = []
    for axis_pos, axis in enumerate(AXES):
        incoming.append(shift(outgoing[:, 2 * axis_pos], axis, up=False))
        incoming.append(shift(outgoing[:, 2 * axis_pos + 1], axis, up=True))
    slots = jnp.concatenate(incoming, axis=1)

    own, zslots = local_solve(parent, residual, slots, diag_inverse, coupling)

    returned = []
    for axis_pos, axis in enumerate(AXES):
        lo = zslots[:, (2 * axis_pos) * face_w : (2 * axis_pos + 1) * face_w]
        hi = zslots[:, (2 * axis_pos + 1) * face_w : (2 * axis_pos + 2) * face_w]
        returned.append(shift(lo, axis, up=True))
        returned.append(shift(hi, axis, up=False))
    returned = jnp.concatenate(returned, axis=1)
    onehot = (
        send_rows.reshape(slots_n * face_w, 1) == lax.iota(jnp.int32, owned_n)[None, :]
    ).astype(jnp.bfloat16)
    faces = jnp.dot(returned, onehot, preferred_element_type=jnp.float32)
    coarse = jnp.dot(
        solved_coarse, vectors, precision=lax.Precision.HIGHEST, preferred_element_type=jnp.float32
    )
    return own.astype(jnp.float32) + faces + coarse


def solution(mesh):
    return jax.shard_map(
        per_device,
        mesh=mesh,
        in_specs=(
            P(None, AXES),
            P(AXES, None, None),
            P(AXES, None, None),
            P(AXES),
            P(AXES, None),
            P(AXES),
            P(None, AXES),
            P(AXES, None),
        ),
        out_specs=P(None, AXES),
        check_vma=False,
    )
```

time: 561 us -> 101 us (0.18)
  loops' own time: 170 us -> 0 us
  local copies, waits for them, and re-layouts: 103 us -> 4.69 us
  matrix products: 89.1 us -> 10.1 us
  waiting for transfers between devices: 64.4 us -> 2.29 us
  starting transfers between devices: 56 us -> 25.1 us
  other arithmetic: 32.2 us -> 2.46 us
  Pallas kernels: 0 us -> 13.1 us
    another operation x2 -> x0, loops' own time: 170 us -> none  [the longest x1 99.9 us: solve_local(): lax.scan(backward, empty, (store, diag_inverse, parent, places), reverse=...]
    dot_general x61 -> x2, matrix products: 83.6 us -> 5.82 us  [the longest x1 4.61 us: per_device(): faces = jnp.dot(returned, onehot, preferred_element_type=jnp.float32)]
    dynamic_slice x155 -> x0, local copies, waits for them, and re-layouts: 66.9 us -> none  [the longest x76 25.4 us: solve_local(): lax.scan(forward, store, (blocks[1:], diag_inverse[1:], coupling, parent[...]
    ppermute x12, waiting for transfers between devices: 64.4 us -> 2.29 us  [shift(): return lax.ppermute(value, axis, pairs)]
    ppermute x12, starting transfers between devices: 56 us -> 25.1 us  [shift(): return lax.ppermute(value, axis, pairs)]
    scatter-add x6 -> x0, other arithmetic: 26.3 us -> none  [per_device(): total.at[:, send_rows[slot_id]].add(returned[slot_id].astype(jnp.float32))]
    dynamic_update_slice x40 -> x0, local copies, waits for them, and re-layouts: 14.9 us -> none  [solve_local(): lax.scan(backward, empty, (store, diag_inverse, parent, places), reverse=...]
    pallas_call x0 -> x1, Pallas kernels: none -> 13.1 us  [local_solve(): pl.pallas_call(solve_kernel, out_shape=(jax.ShapeDtypeStruct((nrhs_here,...]
  transfers between devices with their start and end apart: 12 -> 12, of which waited for: 7 -> 3; matrix products, arithmetic and copies ran while one was open for 7% -> 6% of each run, Pallas kernels for 0% -> 0%
where the time goes in v1:
time: 101 us; the launch traced here: 99.8 us
  blocking collectives  41 us (41%)
  starting transfers between devices  25.1 us (25%)
  Pallas kernels  13.1 us (13%)
  matrix products  10.1 us (10%)
  local copies, waits for them, and re-layouts  4.69 us (5%)
  other arithmetic  2.46 us (2%)
  waiting for transfers between devices  2.29 us (2%)
  between operations  1.01 us (1%)
    all_gather x1, blocking collectives, per_device(): gathered = lax.all_gather(coeffs, AXES, axis=1, tiled=True)  41 us
    ppermute x12, starting transfers between devices, shift(): return lax.ppermute(value, axis, pairs)  25.1 us
    pallas_call x1, Pallas kernels, local_solve(): pl.pallas_call(solve_kernel, out_shape=(jax.ShapeDtypeStruct((nrhs_here,...  13.1 us
    dot_general x1, matrix products, per_device(): faces = jnp.dot(returned, onehot, preferred_element_type=jnp.float32)  4.61 us
    gather x2, local copies, waits for them, and re-layouts, per_device(): outgoing = jnp.take(residual, send_rows, axis=1)  2.49 us
    dot_general x1, matrix products, per_device(): jnp.dot(residual, vectors.T, precision=lax.Precision.HIGHEST, preferred_e...  2.35 us
    ppermute x12, waiting for transfers between devices, shift(): return lax.ppermute(value, axis, pairs)  2.29 us
    unnamed x21, local copies, waits for them, and re-layouts  2.12 us
  transfers between devices with their start and end apart: 12, of which 3 were waited for; matrix products, arithmetic and copies ran while one was open for 6% of the time, Pallas kernels for 0%

profile of v1, /device:TPU:0, one launch (start us, length us, event | category | flops | bytes accessed | tf_op | source)
XLA Modules:
  0.0 99.8 jit_solution(7228386739228844370)
XLA Ops:
  1.4 2.0 %copy.10 = f32[128,4352]{0,1:T(8,128)S(1)} copy(f32[128,4352]{1,0:T(8,128)} %res_ref.1) | data formatting | bytes 4456448 | tf_op args[0]
  3.5 1.6 %gather_fusion = f32[768,128]{1,0:T(8,128)S(1)} fusion(f32[128,4352]{0,1:T(8,128)S(1)} %copy.10, s32[1024]{0:T(1024)S(1)} %pad_clamp_fusion), kind=kCustom, calls=%fused_computation | custom fusion | bytes 789504 | tf_op jit(solution)/shard_map/jit(_take)/gather | solution.py:109
  5.1 0.9 copy.11
  6.0 1.0 %select_bitcast_fusion = f32[128,6,128]{2,0,1:T(8,128)S(1)} fusion(f32[6,128,128]{1,2,0:T(8,128)} %copy.11, pred[6,128]{1,0:T(8,128)(4,1)S(1)} %compare_and_fusion), kind=kLoop, calls=%fused_computation.9 | loop fusion | flops 98304 | bytes 787200 | tf_op jit(solution)/shard_map/jit(_take)/select_n | solution.py:109
  7.0 1.3 %collective-permute-start = (f32[128,128]{1,0:T(8,128)S(1)}, f32[128,128]{1,0:T(8,128)S(1)}, u32[]{:S(2)}, u32[]{:S(2)}) collective-permute-start(f32[128,128]{1,0:T(8,128)S(1)} %get-tuple-element.14), channel_id=1, source_target_pairs={{8,0},{16,8},{24,16},{9,1},{17,9},{25,17},{10,2},{18,10},{26,18},{... | collective-permute-start | bytes 196616 | tf_op jit(solution)/shard_map/ppermute | solution.py:86
  8.3 5.6 %collective-permute-start.1 = (f32[128,128]{1,0:T(8,128)S(1)}, f32[128,128]{1,0:T(8,128)S(1)}, u32[]{:S(2)}, u32[]{:S(2)}) collective-permute-start(f32[128,128]{1,0:T(8,128)S(1)} %get-tuple-element.13), channel_id=1, source_target_pairs={{0,8},{8,16},{16,24},{1,9},{9,17},{17,25},{2,10},{10,18},{18,26},{... | collective-permute-start | bytes 196616 | tf_op jit(solution)/shard_map/ppermute | solution.py:86
  13.9 1.3 %collective-permute-start.2 = (f32[128,128]{1,0:T(8,128)S(1)}, f32[128,128]{1,0:T(8,128)S(1)}, u32[]{:S(2)}, u32[]{:S(2)}) collective-permute-start(f32[128,128]{1,0:T(8,128)S(1)} %get-tuple-element.12), channel_id=1, source_target_pairs={{2,0},{4,2},{6,4},{3,1},{5,3},{7,5},{10,8},{12,10},{14,12},{11,9},... | collective-permute-start | bytes 196616 | tf_op jit(solution)/shard_map/ppermute | solution.py:86
  15.2 4.5 %collective-permute-start.3 = (f32[128,128]{1,0:T(8,128)S(1)}, f32[128,128]{1,0:T(8,128)S(1)}, u32[]{:S(2)}, u32[]{:S(2)}) collective-permute-start(f32[128,128]{1,0:T(8,128)S(1)} %get-tuple-element.11), channel_id=1, source_target_pairs={{0,2},{2,4},{4,6},{1,3},{3,5},{5,7},{8,10},{10,12},{12,14},{9,11},... | collective-permute-start | bytes 196616 | tf_op jit(solution)/shard_map/ppermute | solution.py:86
  19.8 1.3 %collective-permute-start.4 = (f32[128,128]{1,0:T(8,128)S(1)}, f32[128,128]{1,0:T(8,128)S(1)}, u32[]{:S(2)}, u32[]{:S(2)}) collective-permute-start(f32[128,128]{1,0:T(8,128)S(1)} %get-tuple-element.10), channel_id=1, source_target_pairs={{1,0},{3,2},{5,4},{7,6},{9,8},{11,10},{13,12},{15,14},{17,16},{19,... | collective-permute-start | bytes 196616 | tf_op jit(solution)/shard_map/ppermute | solution.py:86
  21.7 2.4 %convolution_bitcast_fusion = f32[128,40]{0,1:T(8,128)S(1)} fusion(f32[128,4352]{1,0:T(8,128)S(1)} %copy-done.1, f32[40,4352]{1,0:T(8,128)S(1)} %copy-done.3, f32[40]{0:T(128)S(1)} %compare_convert_fusion), kind=kOutput, calls=%fused_computation.5 | convolution fusion | flops 267560960 | bytes 2945184 | tf_op jit(solution)/shard_map/dot_general | solution.py:97
  24.1 41.0 %all_gather.3 = f32[128,1280]{0,1:T(8,128)S(1)} all-gather(f32[128,40]{0,1:T(8,128)S(1)} %convolution_bitcast_fusion), channel_id=1, replica_groups=mesh['gx'=4,'gy'=4,'gz'=2] {'gx','gy','gz'}, dimensions={1}, use_global_device_ids=true | all-gather | bytes 675840 | tf_op jit(solution)/shard_map/all_gather | solution.py:100
  65.1 1.2 %fusion.9 = f32[128,40]{1,0:T(8,128)S(1)} fusion(f32[128,1280]{0,1:T(8,128)S(1)} %all_gather.3, f32[40,1280]{1,0:T(8,128)S(1)} %copy-done), kind=kOutput, calls=%fused_computation.36 | convolution fusion | flops 78643200 | bytes 880640 | tf_op jit(solution)/shard_map/dot_general | solution.py:101
  66.3 2.3 %collective-permute-start.5 = (f32[128,128]{1,0:T(8,128)S(1)}, f32[128,128]{1,0:T(8,128)S(1)}, u32[]{:S(2)}, u32[]{:S(2)}) collective-permute-start(f32[128,128]{1,0:T(8,128)S(1)} %get-tuple-element.9), channel_id=1, source_target_pairs={{0,1},{2,3},{4,5},{6,7},{8,9},{10,11},{12,13},{14,15},{16,17},{18,... | collective-permute-start | bytes 196616 | tf_op jit(solution)/shard_map/ppermute | solution.py:86
  68.7 0.8 collective-permute-done.5
  69.5 13.1 %shard_map.82 = (bf16[128,4352]{1,0:T(8,128)(2,1)S(1)}, bf16[128,768]{1,0:T(8,128)(2,1)S(1)}) custom-call(s32[20]{0:T(128)S(1)} %copy-done.2, f32[128,4352]{1,0:T(8,128)S(1)} %copy-done.1, f32[128,768]{1,0:T(8,128)S(1)} %constant_dynamic-update-slice_fusion.slot_ref, bf16[20,256,256]{2,1,0:T(8,128)(2,1)} %inv_ref.1, bf16[19,256,256]{2,1,0:T(8,128)(2,1)} %cpl_ref.1), custom_call_target="tpu_custom_call" | custom-call | tf_op jit(solution)/shard_map/pallas_call | solution.py:58
  82.7 1.3 %collective-permute-start.6 = (bf16[128,128]{1,0:T(8,128)(2,1)S(1)}, bf16[128,128]{1,0:T(8,128)(2,1)S(1)}, u32[]{:S(2)}, u32[]{:S(2)}) collective-permute-start(bf16[128,128]{1,0:T(8,128)(2,1)S(1)} %get-tuple-element.20), channel_id=1, source_target_pairs={{0,8},{8,16},{16,24},{1,9},{9,17},{17,25},{2,10},{10,18},{18,26},{... | collective-permute-start | bytes 98312 | tf_op jit(solution)/shard_map/ppermute | solution.py:86
  84.0 1.9 %fusion.2 = f32[128,4352]{1,0:T(8,128)S(1)} fusion(f32[128,40]{1,0:T(8,128)S(1)} %fusion.9, f32[40,4352]{1,0:T(8,128)S(1)} %copy-done.3, f32[40]{0:T(128)S(1)} %compare_convert_fusion), kind=kOutput, calls=%fused_computation.6 | convolution fusion | flops 267560960 | bytes 2945184 | tf_op jit(solution)/shard_map/dot_general | solution.py:129
  85.9 1.3 %collective-permute-start.7 = (bf16[128,128]{1,0:T(8,128)(2,1)S(1)}, bf16[128,128]{1,0:T(8,128)(2,1)S(1)}, u32[]{:S(2)}, u32[]{:S(2)}) collective-permute-start(bf16[128,128]{1,0:T(8,128)(2,1)S(1)} %get-tuple-element.19), channel_id=1, source_target_pairs={{8,0},{16,8},{24,16},{9,1},{17,9},{25,17},{10,2},{18,10},{26,18},{... | collective-permute-start | bytes 98312 | tf_op jit(solution)/shard_map/ppermute | solution.py:86
  87.2 1.3 %collective-permute-start.8 = (bf16[128,128]{1,0:T(8,128)(2,1)S(1)}, bf16[128,128]{1,0:T(8,128)(2,1)S(1)}, u32[]{:S(2)}, u32[]{:S(2)}) collective-permute-start(bf16[128,128]{1,0:T(8,128)(2,1)S(1)} %get-tuple-element.18), channel_id=1, source_target_pairs={{0,2},{2,4},{4,6},{1,3},{3,5},{5,7},{8,10},{10,12},{12,14},{9,11},... | collective-permute-start | bytes 98312 | tf_op jit(solution)/shard_map/ppermute | solution.py:86
  88.5 1.3 %collective-permute-start.9 = (bf16[128,128]{1,0:T(8,128)(2,1)S(1)}, bf16[128,128]{1,0:T(8,128)(2,1)S(1)}, u32[]{:S(2)}, u32[]{:S(2)}) collective-permute-start(bf16[128,128]{1,0:T(8,128)(2,1)S(1)} %get-tuple-element.17), channel_id=1, source_target_pairs={{2,0},{4,2},{6,4},{3,1},{5,3},{7,5},{10,8},{12,10},{14,12},{11,9},... | collective-permute-start | bytes 98312 | tf_op jit(solution)/shard_map/ppermute | solution.py:86
  89.8 2.3 %collective-permute-start.10 = (bf16[128,128]{1,0:T(8,128)(2,1)S(1)}, bf16[128,128]{1,0:T(8,128)(2,1)S(1)}, u32[]{:S(2)}, u32[]{:S(2)}) collective-permute-start(bf16[128,128]{1,0:T(8,128)(2,1)S(1)} %get-tuple-element.16), channel_id=1, source_target_pairs={{0,1},{2,3},{4,5},{6,7},{8,9},{10,11},{12,13},{14,15},{16,17},{18,... | collective-permute-start | bytes 98312 | tf_op jit(solution)/shard_map/ppermute | solution.py:86
  92.1 1.5 %collective-permute-start.11 = (bf16[128,128]{1,0:T(8,128)(2,1)S(1)}, bf16[128,128]{1,0:T(8,128)(2,1)S(1)}, u32[]{:S(2)}, u32[]{:S(2)}) collective-permute-start(bf16[128,128]{1,0:T(8,128)(2,1)S(1)} %get-tuple-element.15), channel_id=1, source_target_pairs={{1,0},{3,2},{5,4},{7,6},{9,8},{11,10},{13,12},{15,14},{17,16},{19,... | collective-permute-start | bytes 98312 | tf_op jit(solution)/shard_map/ppermute | solution.py:86
  94.4 0.8 collective-permute-done.11
  95.2 4.6 %add_add_fusion = f32[128,4352]{1,0:T(8,128)} fusion(f32[128,4352]{1,0:T(8,128)S(1)} %fusion.2, bf16[128,4352]{1,0:T(8,128)(2,1)S(1)} %get-tuple-element.7, bf16[128,768]{1,0:T(8,128)(2,1)S(1)} %constant_dynamic-update-slice_fusion.6, s32[768]{0:T(1024)S(1)} %bitcast.28), kind=kOutput, calls=%fused_computation.4 | convolution fusion | flops 860651520 | bytes 5770240 | tf_op jit(solution)/shard_map/dot_general | solution.py:128
  (38 shorter events, 2.4 us)
Async XLA Ops:
  0.0 65.1 %copy-start = (f32[40,1280]{1,0:T(8,128)S(1)}, f32[40,1280]{1,0:T(8,128)}, u32[]{:S(2)}) copy-start(f32[40,1280]{1,0:T(8,128)} %param.15) | copy-start | bytes 614404
  3.4 18.3 %copy-start.3 = (f32[40,4352]{1,0:T(8,128)S(1)}, f32[40,4352]{1,0:T(8,128)}, u32[]{:S(2)}) copy-start(f32[40,4352]{1,0:T(8,128)} %param.14) | copy-start | bytes 2088964
  5.0 16.7 %copy-start.1 = (f32[128,4352]{1,0:T(8,128)S(1)}, f32[128,4352]{1,0:T(8,128)}, u32[]{:S(2)}) copy-start(f32[128,4352]{1,0:T(8,128)} %res_ref.1) | copy-start | bytes 6684676
  7.0 59.3 %collective-permute-start = (f32[128,128]{1,0:T(8,128)S(1)}, f32[128,128]{1,0:T(8,128)S(1)}, u32[]{:S(2)}, u32[]{:S(2)}) collective-permute-start(f32[128,128]{1,0:T(8,128)S(1)} %get-tuple-element.14), channel_id=1, source_target_pairs={{8,0},{16,8},{24,16},{9,1},{17,9},{25,17},{10,2},{18,10},{26,18},{... | collective-permute-start | bytes 196616 | tf_op jit(solution)/shard_map/ppermute | solution.py:86
  8.3 60.3 %collective-permute-start.1 = (f32[128,128]{1,0:T(8,128)S(1)}, f32[128,128]{1,0:T(8,128)S(1)}, u32[]{:S(2)}, u32[]{:S(2)}) collective-permute-start(f32[128,128]{1,0:T(8,128)S(1)} %get-tuple-element.13), channel_id=1, source_target_pairs={{0,8},{8,16},{16,24},{1,9},{9,17},{17,25},{2,10},{10,18},{18,26},{... | collective-permute-start | bytes 196616 | tf_op jit(solution)/shard_map/ppermute | solution.py:86
  13.9 54.7 %collective-permute-start.2 = (f32[128,128]{1,0:T(8,128)S(1)}, f32[128,128]{1,0:T(8,128)S(1)}, u32[]{:S(2)}, u32[]{:S(2)}) collective-permute-start(f32[128,128]{1,0:T(8,128)S(1)} %get-tuple-element.12), channel_id=1, source_target_pairs={{2,0},{4,2},{6,4},{3,1},{5,3},{7,5},{10,8},{12,10},{14,12},{11,9},... | collective-permute-start | bytes 196616 | tf_op jit(solution)/shard_map/ppermute | solution.py:86
  15.2 53.4 %collective-permute-start.3 = (f32[128,128]{1,0:T(8,128)S(1)}, f32[128,128]{1,0:T(8,128)S(1)}, u32[]{:S(2)}, u32[]{:S(2)}) collective-permute-start(f32[128,128]{1,0:T(8,128)S(1)} %get-tuple-element.11), channel_id=1, source_target_pairs={{0,2},{2,4},{4,6},{1,3},{3,5},{5,7},{8,10},{10,12},{12,14},{9,11},... | collective-permute-start | bytes 196616 | tf_op jit(solution)/shard_map/ppermute | solution.py:86
  19.8 48.9 %collective-permute-start.4 = (f32[128,128]{1,0:T(8,128)S(1)}, f32[128,128]{1,0:T(8,128)S(1)}, u32[]{:S(2)}, u32[]{:S(2)}) collective-permute-start(f32[128,128]{1,0:T(8,128)S(1)} %get-tuple-element.10), channel_id=1, source_target_pairs={{1,0},{3,2},{5,4},{7,6},{9,8},{11,10},{13,12},{15,14},{17,16},{19,... | collective-permute-start | bytes 196616 | tf_op jit(solution)/shard_map/ppermute | solution.py:86
  21.7 47.7 %copy-start.2 = (s32[20]{0:T(128)S(1)}, s32[20]{0:T(128)}, u32[]{:S(2)}) copy-start(s32[20]{0:T(128)} %parent_ref.1) | copy-start | bytes 244
  66.3 3.1 %collective-permute-start.5 = (f32[128,128]{1,0:T(8,128)S(1)}, f32[128,128]{1,0:T(8,128)S(1)}, u32[]{:S(2)}, u32[]{:S(2)}) collective-permute-start(f32[128,128]{1,0:T(8,128)S(1)} %get-tuple-element.9), channel_id=1, source_target_pairs={{0,1},{2,3},{4,5},{6,7},{8,9},{10,11},{12,13},{14,15},{16,17},{18,... | collective-permute-start | bytes 196616 | tf_op jit(solution)/shard_map/ppermute | solution.py:86
  82.6 12.6 %copy-start.4 = (s32[6,128]{1,0:T(8,128)S(1)}, s32[6,128]{1,0:T(8,128)}, u32[]{:S(2)}) copy-start(s32[6,128]{1,0:T(8,128)} %param.12) | copy-start | bytes 9220
  82.7 9.4 %collective-permute-start.6 = (bf16[128,128]{1,0:T(8,128)(2,1)S(1)}, bf16[128,128]{1,0:T(8,128)(2,1)S(1)}, u32[]{:S(2)}, u32[]{:S(2)}) collective-permute-start(bf16[128,128]{1,0:T(8,128)(2,1)S(1)} %get-tuple-element.20), channel_id=1, source_target_pairs={{0,8},{8,16},{16,24},{1,9},{9,17},{17,25},{2,10},{10,18},{18,26},{... | collective-permute-start | bytes 98312 | tf_op jit(solution)/shard_map/ppermute | solution.py:86
  85.9 7.7 %collective-permute-start.7 = (bf16[128,128]{1,0:T(8,128)(2,1)S(1)}, bf16[128,128]{1,0:T(8,128)(2,1)S(1)}, u32[]{:S(2)}, u32[]{:S(2)}) collective-permute-start(bf16[128,128]{1,0:T(8,128)(2,1)S(1)} %get-tuple-element.19), channel_id=1, source_target_pairs={{8,0},{16,8},{24,16},{9,1},{17,9},{25,17},{10,2},{18,10},{26,18},{... | collective-permute-start | bytes 98312 | tf_op jit(solution)/shard_map/ppermute | solution.py:86
  87.2 6.4 %collective-permute-start.8 = (bf16[128,128]{1,0:T(8,128)(2,1)S(1)}, bf16[128,128]{1,0:T(8,128)(2,1)S(1)}, u32[]{:S(2)}, u32[]{:S(2)}) collective-permute-start(bf16[128,128]{1,0:T(8,128)(2,1)S(1)} %get-tuple-element.18), channel_id=1, source_target_pairs={{0,2},{2,4},{4,6},{1,3},{3,5},{5,7},{8,10},{10,12},{12,14},{9,11},... | collective-permute-start | bytes 98312 | tf_op jit(solution)/shard_map/ppermute | solution.py:86
  88.5 5.8 %collective-permute-start.9 = (bf16[128,128]{1,0:T(8,128)(2,1)S(1)}, bf16[128,128]{1,0:T(8,128)(2,1)S(1)}, u32[]{:S(2)}, u32[]{:S(2)}) collective-permute-start(bf16[128,128]{1,0:T(8,128)(2,1)S(1)} %get-tuple-element.17), channel_id=1, source_target_pairs={{2,0},{4,2},{6,4},{3,1},{5,3},{7,5},{10,8},{12,10},{14,12},{11,9},... | collective-permute-start | bytes 98312 | tf_op jit(solution)/shard_map/ppermute | solution.py:86
  89.8 4.5 %collective-permute-start.10 = (bf16[128,128]{1,0:T(8,128)(2,1)S(1)}, bf16[128,128]{1,0:T(8,128)(2,1)S(1)}, u32[]{:S(2)}, u32[]{:S(2)}) collective-permute-start(bf16[128,128]{1,0:T(8,128)(2,1)S(1)} %get-tuple-element.16), channel_id=1, source_target_pairs={{0,1},{2,3},{4,5},{6,7},{8,9},{10,11},{12,13},{14,15},{16,17},{18,... | collective-permute-start | bytes 98312 | tf_op jit(solution)/shard_map/ppermute | solution.py:86
  92.1 3.1 %collective-permute-start.11 = (bf16[128,128]{1,0:T(8,128)(2,1)S(1)}, bf16[128,128]{1,0:T(8,128)(2,1)S(1)}, u32[]{:S(2)}, u32[]{:S(2)}) collective-permute-start(bf16[128,128]{1,0:T(8,128)(2,1)S(1)} %get-tuple-element.15), channel_id=1, source_target_pairs={{1,0},{3,2},{5,4},{7,6},{9,8},{11,10},{13,12},{15,14},{17,16},{19,... | collective-permute-start | bytes 98312 | tf_op jit(solution)/shard_map/ppermute | solution.py:86

commit v2 on v1

--- a/solution.py
+++ b/solution.py
@@ -94,16 +94,15 @@
     kmax_here = deflation.shape[0]
     mask = (lax.iota(jnp.int32, kmax_here) < counts[0]).astype(jnp.float32)
     vectors = deflation * mask[:, None]
-    coeffs = jnp.dot(
-        residual, vectors.T, precision=lax.Precision.HIGHEST, preferred_element_type=jnp.float32
+    coeffs_t = lax.dot_general(
+        vectors, residual, NT, precision=lax.Precision.HIGHEST, preferred_element_type=jnp.float32
     )
-    gathered = lax.all_gather(coeffs, AXES, axis=1, tiled=True)
-    solved_coarse = lax.dot_general(
-        gathered,
-        coarse_inverse,
-        (((1,), (1,)), ((), ())),
-        precision=lax.Precision.HIGHEST,
-        preferred_element_type=jnp.float32,
+    me = lax.axis_index(AXES)
+    placed = jnp.zeros((coarse_inverse.shape[1], coeffs_t.shape[1]), jnp.float32)
+    placed = lax.dynamic_update_slice_in_dim(placed, coeffs_t, me * kmax_here, axis=0)
+    gathered = lax.psum(placed, AXES)
+    solved_t = jnp.dot(
+        coarse_inverse, gathered, precision=lax.Precision.HIGHEST, preferred_element_type=jnp.float32
     )
 
     outgoing = jnp.take(residual, send_rows, axis=1)
@@ -126,8 +125,12 @@
         send_rows.reshape(slots_n * face_w, 1) == lax.iota(jnp.int32, owned_n)[None, :]
     ).astype(jnp.bfloat16)
     faces = jnp.dot(returned, onehot, preferred_element_type=jnp.float32)
-    coarse = jnp.dot(
-        solved_coarse, vectors, precision=lax.Precision.HIGHEST, preferred_element_type=jnp.float32
+    coarse = lax.dot_general(
+        solved_t,
+        vectors,
+        (((0,), (0,)), ((), ())),
+        precision=lax.Precision.HIGHEST,
+        preferred_element_type=jnp.float32,
     )
     return own.astype(jnp.float32) + faces + coarse
 

time: 101 us -> 197 us (1.95)
  waiting for transfers between devices: 2.29 us -> 117 us
  blocking collectives: 41 us -> 0 us
  between operations: 1.01 us -> 14.4 us
  starting transfers between devices: 25.1 us -> 31.9 us
    psum x0 -> x1, waiting for transfers between devices: none -> 115 us  [per_device(): gathered = lax.psum(placed, AXES)]
    all_gather x1 -> x0, blocking collectives: 41 us -> none  [per_device(): gathered = lax.all_gather(coeffs, AXES, axis=1, tiled=True)]
    ppermute x12, starting transfers between devices: 25.1 us -> 31.9 us  [shift(): return lax.ppermute(value, axis, pairs)]
  transfers between devices with their start and end apart: 12 -> 13, of which waited for: 3 -> 4; matrix products, arithmetic and copies ran while one was open for 6% -> 2% of each run, Pallas kernels for 0% -> 0%
where the time goes in v2:
time: 197 us; the launch traced here: 196 us
  waiting for transfers between devices  117 us (59%)
  starting transfers between devices  31.9 us (16%)
  between operations  14.4 us (7%)
  Pallas kernels  13.2 us (7%)
  matrix products  11.8 us (6%)
  local copies, waits for them, and re-layouts  6.24 us (3%)
    psum x1, waiting for transfers between devices, per_device(): gathered = lax.psum(placed, AXES)  115 us
    ppermute x12, starting transfers between devices, shift(): return lax.ppermute(value, axis, pairs)  31.9 us
    pallas_call x1, Pallas kernels, local_solve(): pl.pallas_call(solve_kernel, out_shape=(jax.ShapeDtypeStruct((nrhs_here,...  13.2 us
    dot_general x1, matrix products, per_device(): faces = jnp.dot(returned, onehot, preferred_element_type=jnp.float32)  4.61 us
  transfers between devices with their start and end apart: 13, of which 4 were waited for; matrix products, arithmetic and copies ran while one was open for 2% of the time, Pallas kernels for 0%

profile of v2, /device:TPU:0, one launch (start us, length us, event | category | flops | bytes accessed | tf_op | source)
XLA Modules:
  0.0 196.0 jit_solution(17991139520927639370)
XLA Ops:
  8.0 2.0 %copy.10 = f32[128,4352]{0,1:T(8,128)S(1)} copy(f32[128,4352]{1,0:T(8,128)} %res_ref.1) | data formatting | bytes 4456448 | tf_op args[0]
  10.0 1.6 gather_fusion
  11.8 1.4 collective-permute-start
  13.3 5.6 %collective-permute-start.1 = (f32[128,128]{1,0:T(8,128)S(1)}, f32[128,128]{1,0:T(8,128)S(1)}, u32[]{:S(2)}, u32[]{:S(2)}) collective-permute-start(f32[128,128]{1,0:T(8,128)S(1)} %get-tuple-element.13), channel_id=1, source_target_pairs={{0,8},{8,16},{16,24},{1,9},{9,17},{17,25},{2,10},{10,18},{18,26},{... | collective-permute-start | bytes 196616 | tf_op jit(solution)/shard_map/ppermute | solution.py:86
  18.8 1.3 collective-permute-start.2
  20.1 4.5 %collective-permute-start.3 = (f32[128,128]{1,0:T(8,128)S(1)}, f32[128,128]{1,0:T(8,128)S(1)}, u32[]{:S(2)}, u32[]{:S(2)}) collective-permute-start(f32[128,128]{1,0:T(8,128)S(1)} %get-tuple-element.11), channel_id=1, source_target_pairs={{0,2},{2,4},{4,6},{1,3},{3,5},{5,7},{8,10},{10,12},{12,14},{9,11},... | collective-permute-start | bytes 196616 | tf_op jit(solution)/shard_map/ppermute | solution.py:86
  24.7 1.3 collective-permute-start.4
  26.7 3.0 %collective-permute-start.5 = (f32[128,128]{1,0:T(8,128)S(1)}, f32[128,128]{1,0:T(8,128)S(1)}, u32[]{:S(2)}, u32[]{:S(2)}) collective-permute-start(f32[128,128]{1,0:T(8,128)S(1)} %get-tuple-element.9), channel_id=1, source_target_pairs={{0,1},{2,3},{4,5},{6,7},{8,9},{10,11},{12,13},{14,15},{16,17},{18,... | collective-permute-start | bytes 196616 | tf_op jit(solution)/shard_map/ppermute | solution.py:86
  29.8 0.8 collective-permute-done.5
  30.6 13.2 %shard_map.82 = (bf16[128,4352]{1,0:T(8,128)(2,1)S(1)}, bf16[128,768]{1,0:T(8,128)(2,1)S(1)}) custom-call(s32[20]{0:T(128)S(1)} %copy-done.2, f32[128,4352]{1,0:T(8,128)S(1)} %copy-done.1, f32[128,768]{1,0:T(8,128)S(1)} %constant_dynamic-update-slice_fusion.slot_ref, bf16[20,256,256]{2,1,0:T(8,128)(2,1)} %inv_ref.1, bf16[19,256,256]{2,1,0:T(8,128)(2,1)} %cpl_ref.1), custom_call_target="tpu_custom_call" | custom-call | tf_op jit(solution)/shard_map/pallas_call | solution.py:58
  44.5 4.5 %collective-permute-start.6 = (bf16[128,128]{1,0:T(8,128)(2,1)}, bf16[128,128]{1,0:T(8,128)(2,1)}, u32[]{:S(2)}, u32[]{:S(2)}) collective-permute-start(bf16[128,128]{1,0:T(8,128)(2,1)} %get-tuple-element.20), channel_id=1, source_target_pairs={{0,8},{8,16},{16,24},{1,9},{9,17},{17,25},{2,10},{10,18},{18,26},{... | collective-permute-start | bytes 98312 | tf_op jit(solution)/shard_map/ppermute | solution.py:86
  49.1 0.9 broadcast_in_dim.20
  49.9 3.0 %convolution_dynamic-update-slice_fusion = f32[1280,128]{1,0:T(8,128)} fusion(f32[1280,128]{1,0:T(8,128)} %broadcast_in_dim.20, s32[]{:T(128)S(6)} %select_n.14, f32[128,4352]{1,0:T(8,128)S(1)} %copy-done.1, f32[40,4352]{1,0:T(8,128)S(1)} %copy-done.3, f32[40]{0:T(128)S(1)} %compare_convert_fusion), kind=kOutput, calls=%fused_computation.5 | convolution fusion | flops 267560960 | bytes 2945188 | tf_op jit(solution)/shard_map/dot_general | solution.py:97
  52.9 1.4 collective-permute-start.7
  54.4 4.3 %collective-permute-start.8 = (bf16[128,128]{1,0:T(8,128)(2,1)}, bf16[128,128]{1,0:T(8,128)(2,1)S(1)}, u32[]{:S(2)}, u32[]{:S(2)}) collective-permute-start(bf16[128,128]{1,0:T(8,128)(2,1)} %get-tuple-element.18), channel_id=1, source_target_pairs={{0,2},{2,4},{4,6},{1,3},{3,5},{5,7},{8,10},{10,12},{12,14},{9,11},... | collective-permute-start | bytes 98312 | tf_op jit(solution)/shard_map/ppermute | solution.py:86
  58.7 1.3 collective-permute-start.9
  60.0 1.7 collective-permute-start.10
  61.7 1.5 collective-permute-start.11
  63.2 0.8 constant_dynamic-update-slice_fusion.11
  64.0 0.8 collective-permute-done.9
  65.0 115.3 %all-reduce.2.cloned.1.call-done = f32[1280,128]{1,0:T(8,128)} async-done(((f32[1280,128]{1,0:T(8,128)}), f32[1280,128]{1,0:T(8,128)}) %all-reduce.2.cloned.1.call-update) | async-done | bytes 655376 | tf_op jit(solution)/shard_map/psum | solution.py:103
  180.3 2.3 %fusion.9 = f32[128,40]{1,0:T(8,128)S(1)} fusion(f32[1280,128]{1,0:T(8,128)} %all-reduce.2.cloned.1.call-done, f32[40,1280]{1,0:T(8,128)S(1)} %copy-done), kind=kOutput, calls=%fused_computation.36 | convolution fusion | flops 78643200 | bytes 880640 | tf_op jit(solution)/shard_map/dot_general | solution.py:104
  182.6 1.9 fusion.2
  184.6 4.6 %add_add_fusion = f32[128,4352]{1,0:T(8,128)} fusion(f32[128,4352]{1,0:T(8,128)S(1)} %fusion.2, bf16[128,4352]{1,0:T(8,128)(2,1)S(1)} %get-tuple-element.7, bf16[128,768]{1,0:T(8,128)(2,1)S(1)} %constant_dynamic-update-slice_fusion.6, s32[768]{0:T(1024)S(1)} %bitcast.26), kind=kOutput, calls=%fused_computation.4 | convolution fusion | flops 860651520 | bytes 5770240 | tf_op jit(solution)/shard_map/dot_general | solution.py:127
  (43 shorter events, 2.7 us)
Async XLA Ops:
  6.5 173.8 %copy-start = (f32[40,1280]{1,0:T(8,128)S(1)}, f32[40,1280]{1,0:T(8,128)}, u32[]{:S(2)}) copy-start(f32[40,1280]{1,0:T(8,128)} %param.15) | copy-start | bytes 614404
  6.5 173.8 %all-reduce.2.cloned.1.call-start = ((), (), s32[]{:S(2)}) async-start(), calls=%async_computation | async-start | bytes 1310720 | tf_op jit(solution)/shard_map/psum | solution.py:103
  11.6 19.0 %copy-start.1 = (f32[128,4352]{1,0:T(8,128)S(1)}, f32[128,4352]{1,0:T(8,128)}, u32[]{:S(2)}) copy-start(f32[128,4352]{1,0:T(8,128)} %res_ref.1) | copy-start | bytes 6684676
  11.6 19.0 %copy-start.2 = (s32[20]{0:T(128)S(1)}, s32[20]{0:T(128)}, u32[]{:S(2)}) copy-start(s32[20]{0:T(128)} %parent_ref.1) | copy-start | bytes 244
  11.8 14.8 %collective-permute-start = (f32[128,128]{1,0:T(8,128)S(1)}, f32[128,128]{1,0:T(8,128)S(1)}, u32[]{:S(2)}, u32[]{:S(2)}) collective-permute-start(f32[128,128]{1,0:T(8,128)S(1)} %get-tuple-element.14), channel_id=1, source_target_pairs={{8,0},{16,8},{24,16},{9,1},{17,9},{25,17},{10,2},{18,10},{26,18},{... | collective-permute-start | bytes 196616 | tf_op jit(solution)/shard_map/ppermute | solution.py:86
  13.3 16.5 %collective-permute-start.1 = (f32[128,128]{1,0:T(8,128)S(1)}, f32[128,128]{1,0:T(8,128)S(1)}, u32[]{:S(2)}, u32[]{:S(2)}) collective-permute-start(f32[128,128]{1,0:T(8,128)S(1)} %get-tuple-element.13), channel_id=1, source_target_pairs={{0,8},{8,16},{16,24},{1,9},{9,17},{17,25},{2,10},{10,18},{18,26},{... | collective-permute-start | bytes 196616 | tf_op jit(solution)/shard_map/ppermute | solution.py:86
  18.8 10.9 %collective-permute-start.2 = (f32[128,128]{1,0:T(8,128)S(1)}, f32[128,128]{1,0:T(8,128)S(1)}, u32[]{:S(2)}, u32[]{:S(2)}) collective-permute-start(f32[128,128]{1,0:T(8,128)S(1)} %get-tuple-element.12), channel_id=1, source_target_pairs={{2,0},{4,2},{6,4},{3,1},{5,3},{7,5},{10,8},{12,10},{14,12},{11,9},... | collective-permute-start | bytes 196616 | tf_op jit(solution)/shard_map/ppermute | solution.py:86
  20.1 9.6 %collective-permute-start.3 = (f32[128,128]{1,0:T(8,128)S(1)}, f32[128,128]{1,0:T(8,128)S(1)}, u32[]{:S(2)}, u32[]{:S(2)}) collective-permute-start(f32[128,128]{1,0:T(8,128)S(1)} %get-tuple-element.11), channel_id=1, source_target_pairs={{0,2},{2,4},{4,6},{1,3},{3,5},{5,7},{8,10},{10,12},{12,14},{9,11},... | collective-permute-start | bytes 196616 | tf_op jit(solution)/shard_map/ppermute | solution.py:86
  24.7 5.1 %collective-permute-start.4 = (f32[128,128]{1,0:T(8,128)S(1)}, f32[128,128]{1,0:T(8,128)S(1)}, u32[]{:S(2)}, u32[]{:S(2)}) collective-permute-start(f32[128,128]{1,0:T(8,128)S(1)} %get-tuple-element.10), channel_id=1, source_target_pairs={{1,0},{3,2},{5,4},{7,6},{9,8},{11,10},{13,12},{15,14},{17,16},{19,... | collective-permute-start | bytes 196616 | tf_op jit(solution)/shard_map/ppermute | solution.py:86
  26.7 3.9 %collective-permute-start.5 = (f32[128,128]{1,0:T(8,128)S(1)}, f32[128,128]{1,0:T(8,128)S(1)}, u32[]{:S(2)}, u32[]{:S(2)}) collective-permute-start(f32[128,128]{1,0:T(8,128)S(1)} %get-tuple-element.9), channel_id=1, source_target_pairs={{0,1},{2,3},{4,5},{6,7},{8,9},{10,11},{12,13},{14,15},{16,17},{18,... | collective-permute-start | bytes 196616 | tf_op jit(solution)/shard_map/ppermute | solution.py:86
  30.6 19.3 %copy-start.3 = (f32[40,4352]{1,0:T(8,128)S(1)}, f32[40,4352]{1,0:T(8,128)}, u32[]{:S(2)}) copy-start(f32[40,4352]{1,0:T(8,128)} %param.14) | copy-start | bytes 2088964
  44.5 17.1 %collective-permute-start.6 = (bf16[128,128]{1,0:T(8,128)(2,1)}, bf16[128,128]{1,0:T(8,128)(2,1)}, u32[]{:S(2)}, u32[]{:S(2)}) collective-permute-start(bf16[128,128]{1,0:T(8,128)(2,1)} %get-tuple-element.20), channel_id=1, source_target_pairs={{0,8},{8,16},{16,24},{1,9},{9,17},{17,25},{2,10},{10,18},{18,26},{... | collective-permute-start | bytes 98312 | tf_op jit(solution)/shard_map/ppermute | solution.py:86
  52.9 129.7 %copy-start.4 = (f32[40,4352]{1,0:T(8,128)S(1)}, f32[40,4352]{1,0:T(8,128)}, u32[]{:S(2)}) copy-start(f32[40,4352]{1,0:T(8,128)} %param.14) | copy-start | bytes 2088964
  52.9 131.6 %copy-start.5 = (s32[6,128]{1,0:T(8,128)S(1)}, s32[6,128]{1,0:T(8,128)}, u32[]{:S(2)}) copy-start(s32[6,128]{1,0:T(8,128)} %param.12) | copy-start | bytes 9220
  52.9 11.0 %collective-permute-start.7 = (bf16[128,128]{1,0:T(8,128)(2,1)}, bf16[128,128]{1,0:T(8,128)(2,1)S(1)}, u32[]{:S(2)}, u32[]{:S(2)}) collective-permute-start(bf16[128,128]{1,0:T(8,128)(2,1)} %get-tuple-element.19), channel_id=1, source_target_pairs={{8,0},{16,8},{24,16},{9,1},{17,9},{25,17},{10,2},{18,10},{26,18},{... | collective-permute-start | bytes 98312 | tf_op jit(solution)/shard_map/ppermute | solution.py:86
  54.4 9.6 %collective-permute-start.8 = (bf16[128,128]{1,0:T(8,128)(2,1)}, bf16[128,128]{1,0:T(8,128)(2,1)S(1)}, u32[]{:S(2)}, u32[]{:S(2)}) collective-permute-start(bf16[128,128]{1,0:T(8,128)(2,1)} %get-tuple-element.18), channel_id=1, source_target_pairs={{0,2},{2,4},{4,6},{1,3},{3,5},{5,7},{8,10},{10,12},{12,14},{9,11},... | collective-permute-start | bytes 98312 | tf_op jit(solution)/shard_map/ppermute | solution.py:86
  58.7 6.1 %collective-permute-start.9 = (bf16[128,128]{1,0:T(8,128)(2,1)}, bf16[128,128]{1,0:T(8,128)(2,1)S(1)}, u32[]{:S(2)}, u32[]{:S(2)}) collective-permute-start(bf16[128,128]{1,0:T(8,128)(2,1)} %get-tuple-element.17), channel_id=1, source_target_pairs={{2,0},{4,2},{6,4},{3,1},{5,3},{7,5},{10,8},{12,10},{14,12},{11,9},... | collective-permute-start | bytes 98312 | tf_op jit(solution)/shard_map/ppermute | solution.py:86
  60.0 4.8 %collective-permute-start.10 = (bf16[128,128]{1,0:T(8,128)(2,1)}, bf16[128,128]{1,0:T(8,128)(2,1)S(1)}, u32[]{:S(2)}, u32[]{:S(2)}) collective-permute-start(bf16[128,128]{1,0:T(8,128)(2,1)} %get-tuple-element.16), channel_id=1, source_target_pairs={{0,1},{2,3},{4,5},{6,7},{8,9},{10,11},{12,13},{14,15},{16,17},{18,... | collective-permute-start | bytes 98312 | tf_op jit(solution)/shard_map/ppermute | solution.py:86
  61.7 3.3 %collective-permute-start.11 = (bf16[128,128]{1,0:T(8,128)(2,1)}, bf16[128,128]{1,0:T(8,128)(2,1)S(1)}, u32[]{:S(2)}, u32[]{:S(2)}) collective-permute-start(bf16[128,128]{1,0:T(8,128)(2,1)} %get-tuple-element.15), channel_id=1, source_target_pairs={{1,0},{3,2},{5,4},{7,6},{9,8},{11,10},{13,12},{15,14},{17,16},{19,... | collective-permute-start | bytes 98312 | tf_op jit(solution)/shard_map/ppermute | solution.py:86
Sparse Core Ops, SparseCore 0:
  53.1 127.1 all-reduce.1

commit v3 on v2

--- a/solution.py
+++ b/solution.py
@@ -86,6 +86,28 @@
     return lax.ppermute(value, axis, pairs)
 
 
+def gather_axis(value, axis):
+    count = lax.axis_size(axis)
+    if count & (count - 1):
+        return lax.all_gather(value, axis, axis=0, tiled=False)
+    me = lax.axis_index(axis)
+    held = value[None]
+    step = 1
+    while step < count:
+        pairs = [(i, i ^ step) for i in range(count)]
+        other = lax.ppermute(held, axis, pairs)
+        low = (me // step) % 2 == 0
+        held = jnp.where(low, jnp.concatenate([held, other]), jnp.concatenate([other, held]))
+        step *= 2
+    return held
+
+
+def gather_all(value):
+    for axis in reversed(AXES):
+        value = gather_axis(value, axis)
+    return value
+
+
 def per_device(
     residual, diag_inverse, coupling, parent, send_rows, counts, deflation, coarse_inverse
 ):
@@ -97,10 +119,7 @@
     coeffs_t = lax.dot_general(
         vectors, residual, NT, precision=lax.Precision.HIGHEST, preferred_element_type=jnp.float32
     )
-    me = lax.axis_index(AXES)
-    placed = jnp.zeros((coarse_inverse.shape[1], coeffs_t.shape[1]), jnp.float32)
-    placed = lax.dynamic_update_slice_in_dim(placed, coeffs_t, me * kmax_here, axis=0)
-    gathered = lax.psum(placed, AXES)
+    gathered = gather_all(coeffs_t).reshape(-1, coeffs_t.shape[1])
     solved_t = jnp.dot(
         coarse_inverse, gathered, precision=lax.Precision.HIGHEST, preferred_element_type=jnp.float32
     )

time: 197 us -> 91 us (0.46)
  waiting for transfers between devices: 117 us -> 19.6 us
  between operations: 14.4 us -> 1.32 us
  starting transfers between devices: 31.9 us -> 38.3 us
    psum x1 -> x0, waiting for transfers between devices: 115 us -> none  [per_device(): gathered = lax.psum(placed, AXES)]
    ppermute x0 -> x5, waiting for transfers between devices: none -> 19.6 us  [gather_axis(): other = lax.ppermute(held, axis, pairs)]
    ppermute x0 -> x5, starting transfers between devices: none -> 10.4 us  [gather_axis(): other = lax.ppermute(held, axis, pairs)]
    ppermute x12, starting transfers between devices: 31.9 us -> 27.9 us  [shift(): return lax.ppermute(value, axis, pairs)]
  transfers between devices with their start and end apart: 13 -> 17, of which waited for: 4 -> 2; matrix products, arithmetic and copies ran while one was open for 2% -> 6% of each run, Pallas kernels for 0% -> 15%
where the time goes in v3:
time: 91 us; the launch traced here: 90 us
  starting transfers between devices  38.3 us (42%)
  waiting for transfers between devices  19.6 us (22%)
  Pallas kernels  13.2 us (15%)
  matrix products  12 us (13%)
  local copies, waits for them, and re-layouts  5.46 us (6%)
  between operations  1.32 us (1%)
    ppermute x12, starting transfers between devices, shift(): return lax.ppermute(value, axis, pairs)  27.9 us
    ppermute x5, waiting for transfers between devices, gather_axis(): other = lax.ppermute(held, axis, pairs)  19.6 us
    pallas_call x1, Pallas kernels, local_solve(): pl.pallas_call(solve_kernel, out_shape=(jax.ShapeDtypeStruct((nrhs_here,...  13.2 us
    ppermute x5, starting transfers between devices, gather_axis(): other = lax.ppermute(held, axis, pairs)  10.4 us
    dot_general x1, matrix products, per_device(): faces = jnp.dot(returned, onehot, preferred_element_type=jnp.float32)  4.61 us
    dot_general x1, matrix products, per_device(): lax.dot_general(vectors, residual, NT, precision=lax.Precision.HIGHEST, p...  4.2 us
    gather x2, local copies, waits for them, and re-layouts, per_device(): outgoing = jnp.take(residual, send_rows, axis=1)  3.36 us
    unnamed x21, local copies, waits for them, and re-layouts  2.02 us
  transfers between devices with their start and end apart: 17, of which 2 were waited for; matrix products, arithmetic and copies ran while one was open for 6% of the time, Pallas kernels for 15%

profile of v3, /device:TPU:0, one launch (start us, length us, event | category | flops | bytes accessed | tf_op | source)
XLA Modules:
  0.0 90.0 jit_solution(8031139360629344032)
XLA Ops:
  0.8 4.2 %fusion.4 = f32[40,128]{1,0:T(8,128)S(1)} fusion(f32[128,4352]{1,0:T(8,128)} %res_ref.1, f32[40,4352]{1,0:T(8,128)} %param.14, f32[40]{0:T(128)S(1)} %compare_convert_fusion), kind=kOutput, calls=%fused_computation.8 | convolution fusion | flops 267560960 | bytes 2945184 | tf_op jit(solution)/shard_map/dot_general | solution.py:119
  5.6 1.9 %copy.10 = f32[128,4352]{0,1:T(8,128)} copy(f32[128,4352]{1,0:T(8,128)S(1)} %copy-done.1) | data formatting | bytes 4456448 | tf_op args[0]
  7.5 3.2 %gather_fusion = f32[768,128]{1,0:T(8,128)S(1)} fusion(f32[128,4352]{0,1:T(8,128)} %copy.10, s32[1024]{0:T(1024)S(1)} %pad_clamp_fusion), kind=kCustom, calls=%fused_computation | custom fusion | bytes 789504 | tf_op jit(solution)/shard_map/jit(_take)/gather | solution.py:127
  10.9 2.6 %collective-permute-start.13 = (f32[1,2,40,128]{3,2,1,0:T(8,128)S(1)}, f32[1,2,40,128]{3,2,1,0:T(8,128)S(1)}, u32[]{:S(2)}, u32[]{:S(2)}) collective-permute-start(f32[1,2,40,128]{3,2,1,0:T(8,128)S(1)} %maximum_select_fusion.4), channel_id=1, source_target_pairs={{0,2},{2,0},{4,6},{6,4},{1,3},{3,1},{5,7},{7,5},{8,10},{10,8},{12,... | collective-permute-start | bytes 122888 | tf_op jit(solution)/shard_map/ppermute | solution.py:98
  13.6 1.3 %collective-permute-start = (f32[128,128]{1,0:T(8,128)S(1)}, f32[128,128]{1,0:T(8,128)S(1)}, u32[]{:S(2)}, u32[]{:S(2)}) collective-permute-start(f32[128,128]{1,0:T(8,128)S(1)} %get-tuple-element.14), channel_id=1, source_target_pairs={{8,0},{16,8},{24,16},{9,1},{17,9},{25,17},{10,2},{18,10},{26,18},{... | collective-permute-start | bytes 196616 | tf_op jit(solution)/shard_map/ppermute | solution.py:86
  14.9 4.5 %collective-permute-start.1 = (f32[128,128]{1,0:T(8,128)S(1)}, f32[128,128]{1,0:T(8,128)S(1)}, u32[]{:S(2)}, u32[]{:S(2)}) collective-permute-start(f32[128,128]{1,0:T(8,128)S(1)} %get-tuple-element.13), channel_id=1, source_target_pairs={{0,8},{8,16},{16,24},{1,9},{9,17},{17,25},{2,10},{10,18},{18,26},{... | collective-permute-start | bytes 196616 | tf_op jit(solution)/shard_map/ppermute | solution.py:86
  19.4 1.3 %collective-permute-start.2 = (f32[128,128]{1,0:T(8,128)S(1)}, f32[128,128]{1,0:T(8,128)S(1)}, u32[]{:S(2)}, u32[]{:S(2)}) collective-permute-start(f32[128,128]{1,0:T(8,128)S(1)} %get-tuple-element.12), channel_id=1, source_target_pairs={{2,0},{4,2},{6,4},{3,1},{5,3},{7,5},{10,8},{12,10},{14,12},{11,9},... | collective-permute-start | bytes 196616 | tf_op jit(solution)/shard_map/ppermute | solution.py:86
  20.7 4.5 %collective-permute-start.3 = (f32[128,128]{1,0:T(8,128)S(1)}, f32[128,128]{1,0:T(8,128)S(1)}, u32[]{:S(2)}, u32[]{:S(2)}) collective-permute-start(f32[128,128]{1,0:T(8,128)S(1)} %get-tuple-element.11), channel_id=1, source_target_pairs={{0,2},{2,4},{4,6},{1,3},{3,5},{5,7},{8,10},{10,12},{12,14},{9,11},... | collective-permute-start | bytes 196616 | tf_op jit(solution)/shard_map/ppermute | solution.py:86
  25.4 1.3 %collective-permute-start.4 = (f32[128,128]{1,0:T(8,128)S(1)}, f32[128,128]{1,0:T(8,128)S(1)}, u32[]{:S(2)}, u32[]{:S(2)}) collective-permute-start(f32[128,128]{1,0:T(8,128)S(1)} %get-tuple-element.10), channel_id=1, source_target_pairs={{1,0},{3,2},{5,4},{7,6},{9,8},{11,10},{13,12},{15,14},{17,16},{19,... | collective-permute-start | bytes 196616 | tf_op jit(solution)/shard_map/ppermute | solution.py:86
  26.7 3.0 %collective-permute-start.5 = (f32[128,128]{1,0:T(8,128)S(1)}, f32[128,128]{1,0:T(8,128)S(1)}, u32[]{:S(2)}, u32[]{:S(2)}) collective-permute-start(f32[128,128]{1,0:T(8,128)S(1)} %get-tuple-element.9), channel_id=1, source_target_pairs={{0,1},{2,3},{4,5},{6,7},{8,9},{10,11},{12,13},{14,15},{16,17},{18,... | collective-permute-start | bytes 196616 | tf_op jit(solution)/shard_map/ppermute | solution.py:86
  29.7 1.6 %collective-permute-start.14 = (f32[2,2,40,128]{3,2,1,0:T(8,128)S(1)}, f32[2,2,40,128]{3,2,1,0:T(8,128)S(1)}, u32[]{:S(2)}, u32[]{:S(2)}) collective-permute-start(f32[2,2,40,128]{3,2,1,0:T(8,128)S(1)} %maximum_select_fusion.3), channel_id=1, source_target_pairs={{0,4},{2,6},{4,0},{6,2},{1,5},{3,7},{5,1},{7,3},{8,12},{10,14},{12... | collective-permute-start | bytes 245768 | tf_op jit(solution)/shard_map/ppermute | solution.py:98
  31.4 13.2 %shard_map.82 = (bf16[128,4352]{1,0:T(8,128)(2,1)S(1)}, bf16[128,768]{1,0:T(8,128)(2,1)S(1)}) custom-call(s32[20]{0:T(128)S(1)} %copy-done.2, f32[128,4352]{1,0:T(8,128)S(1)} %copy-done.1, f32[128,768]{1,0:T(8,128)S(1)} %constant_dynamic-update-slice_fusion.slot_ref, bf16[20,256,256]{2,1,0:T(8,128)(2,1)} %inv_ref.1, bf16[19,256,256]{2,1,0:T(8,128)(2,1)} %cpl_ref.1), custom_call_target="tpu_custom_call" | custom-call | tf_op jit(solution)/shard_map/pallas_call | solution.py:58
  44.7 3.6 %collective-permute-start.6 = (bf16[128,128]{1,0:T(8,128)(2,1)S(1)}, bf16[128,128]{1,0:T(8,128)(2,1)S(1)}, u32[]{:S(2)}, u32[]{:S(2)}) collective-permute-start(bf16[128,128]{1,0:T(8,128)(2,1)S(1)} %get-tuple-element.20), channel_id=1, source_target_pairs={{0,8},{8,16},{16,24},{1,9},{9,17},{17,25},{2,10},{10,18},{18,26},{... | collective-permute-start | bytes 98312 | tf_op jit(solution)/shard_map/ppermute | solution.py:86
  48.3 1.3 %collective-permute-start.7 = (bf16[128,128]{1,0:T(8,128)(2,1)S(1)}, bf16[128,128]{1,0:T(8,128)(2,1)S(1)}, u32[]{:S(2)}, u32[]{:S(2)}) collective-permute-start(bf16[128,128]{1,0:T(8,128)(2,1)S(1)} %get-tuple-element.19), channel_id=1, source_target_pairs={{8,0},{16,8},{24,16},{9,1},{17,9},{25,17},{10,2},{18,10},{26,18},{... | collective-permute-start | bytes 98312 | tf_op jit(solution)/shard_map/ppermute | solution.py:86
  49.6 2.5 %collective-permute-start.8 = (bf16[128,128]{1,0:T(8,128)(2,1)S(1)}, bf16[128,128]{1,0:T(8,128)(2,1)S(1)}, u32[]{:S(2)}, u32[]{:S(2)}) collective-permute-start(bf16[128,128]{1,0:T(8,128)(2,1)S(1)} %get-tuple-element.18), channel_id=1, source_target_pairs={{0,2},{2,4},{4,6},{1,3},{3,5},{5,7},{8,10},{10,12},{12,14},{9,11},... | collective-permute-start | bytes 98312 | tf_op jit(solution)/shard_map/ppermute | solution.py:86
  52.1 1.3 %collective-permute-start.9 = (bf16[128,128]{1,0:T(8,128)(2,1)S(1)}, bf16[128,128]{1,0:T(8,128)(2,1)S(1)}, u32[]{:S(2)}, u32[]{:S(2)}) collective-permute-start(bf16[128,128]{1,0:T(8,128)(2,1)S(1)} %get-tuple-element.17), channel_id=1, source_target_pairs={{2,0},{4,2},{6,4},{3,1},{5,3},{7,5},{10,8},{12,10},{14,12},{11,9},... | collective-permute-start | bytes 98312 | tf_op jit(solution)/shard_map/ppermute | solution.py:86
  53.4 1.7 %collective-permute-start.10 = (bf16[128,128]{1,0:T(8,128)(2,1)S(1)}, bf16[128,128]{1,0:T(8,128)(2,1)S(1)}, u32[]{:S(2)}, u32[]{:S(2)}) collective-permute-start(bf16[128,128]{1,0:T(8,128)(2,1)S(1)} %get-tuple-element.16), channel_id=1, source_target_pairs={{0,1},{2,3},{4,5},{6,7},{8,9},{10,11},{12,13},{14,15},{16,17},{18,... | collective-permute-start | bytes 98312 | tf_op jit(solution)/shard_map/ppermute | solution.py:86
  55.2 1.5 %collective-permute-start.11 = (bf16[128,128]{1,0:T(8,128)(2,1)S(1)}, bf16[128,128]{1,0:T(8,128)(2,1)S(1)}, u32[]{:S(2)}, u32[]{:S(2)}) collective-permute-start(bf16[128,128]{1,0:T(8,128)(2,1)S(1)} %get-tuple-element.15), channel_id=1, source_target_pairs={{1,0},{3,2},{5,4},{7,6},{9,8},{11,10},{13,12},{15,14},{17,16},{19,... | collective-permute-start | bytes 98312 | tf_op jit(solution)/shard_map/ppermute | solution.py:86
  56.7 2.4 %collective-permute-start.15 = (f32[1,4,2,40,128]{4,3,2,1,0:T(8,128)S(1)}, f32[1,4,2,40,128]{4,3,2,1,0:T(8,128)S(1)}, u32[]{:S(2)}, u32[]{:S(2)}) collective-permute-start(f32[1,4,2,40,128]{4,3,2,1,0:T(8,128)S(1)} %maximum_select_fusion.2), channel_id=1, source_target_pairs={{0,8},{8,0},{16,24},{24,16},{1,9},{9,1},{17,25},{25,17},{2,10},{10... | collective-permute-start | bytes 491528 | tf_op jit(solution)/shard_map/ppermute | solution.py:98
  59.1 4.7 %collective-permute-done.15 = f32[1,4,2,40,128]{4,3,2,1,0:T(8,128)S(1)} collective-permute-done((f32[1,4,2,40,128]{4,3,2,1,0:T(8,128)S(1)}, f32[1,4,2,40,128]{4,3,2,1,0:T(8,128)S(1)}, u32[]{:S(2)}, u32[]{:S(2)}) %collective-permute-start.15) | collective-permute-done | bytes 163872 | tf_op jit(solution)/shard_map/ppermute | solution.py:98
  63.8 3.3 %collective-permute-start.16 = (f32[2,4,2,40,128]{4,3,2,1,0:T(8,128)S(1)}, f32[2,4,2,40,128]{4,3,2,1,0:T(8,128)S(1)}, u32[]{:S(2)}, u32[]{:S(2)}) collective-permute-start(f32[2,4,2,40,128]{4,3,2,1,0:T(8,128)S(1)} %maximum_select_fusion.1), channel_id=1, source_target_pairs={{0,16},{8,24},{16,0},{24,8},{1,17},{9,25},{17,1},{25,9},{2,18},{10... | collective-permute-start | bytes 983048 | tf_op jit(solution)/shard_map/ppermute | solution.py:98
  67.2 14.9 %collective-permute-done.16 = f32[2,4,2,40,128]{4,3,2,1,0:T(8,128)S(1)} collective-permute-done((f32[2,4,2,40,128]{4,3,2,1,0:T(8,128)S(1)}, f32[2,4,2,40,128]{4,3,2,1,0:T(8,128)S(1)}, u32[]{:S(2)}, u32[]{:S(2)}) %collective-permute-start.16) | collective-permute-done | bytes 327712 | tf_op jit(solution)/shard_map/ppermute | solution.py:98
  83.4 2.0 %fusion.2 = f32[128,4352]{1,0:T(8,128)S(1)} fusion(f32[128,40]{1,0:T(8,128)S(1)} %fusion.10, f32[40,4352]{1,0:T(8,128)S(1)} %copy-done.3, f32[40]{0:T(128)S(1)} %compare_convert_fusion), kind=kOutput, calls=%fused_computation.6 | convolution fusion | flops 267560960 | bytes 2945184 | tf_op jit(solution)/shard_map/dot_general | solution.py:147
  85.4 4.6 %add_add_fusion = f32[128,4352]{1,0:T(8,128)} fusion(f32[128,4352]{1,0:T(8,128)S(1)} %fusion.2, bf16[128,4352]{1,0:T(8,128)(2,1)S(1)} %get-tuple-element.7, bf16[128,768]{1,0:T(8,128)(2,1)S(1)} %constant_dynamic-update-slice_fusion.6, s32[768]{0:T(1024)S(1)} %bitcast.38), kind=kOutput, calls=%fused_computation.4 | convolution fusion | flops 860651520 | bytes 5770240 | tf_op jit(solution)/shard_map/dot_general | solution.py:146
  (53 shorter events, 2.3 us)
Async XLA Ops:
  0.0 82.2 %copy-start = (f32[40,1280]{1,0:T(8,128)S(1)}, f32[40,1280]{1,0:T(8,128)}, u32[]{:S(2)}) copy-start(f32[40,1280]{1,0:T(8,128)} %param.15) | copy-start | bytes 614404
  0.0 5.5 %copy-start.1 = (f32[128,4352]{1,0:T(8,128)S(1)}, f32[128,4352]{1,0:T(8,128)}, u32[]{:S(2)}) copy-start(f32[128,4352]{1,0:T(8,128)} %res_ref.1) | copy-start | bytes 6684676
  5.0 2.4 %copy-start.4 = (s32[6,128]{1,0:T(8,128)S(1)}, s32[6,128]{1,0:T(8,128)}, u32[]{:S(2)}) copy-start(s32[6,128]{1,0:T(8,128)} %param.12) | copy-start | bytes 9220
  5.0 5.9 %collective-permute-start.12 = (f32[1,40,128]{2,1,0:T(8,128)S(1)}, f32[1,40,128]{2,1,0:T(8,128)S(1)}, u32[]{:S(2)}, u32[]{:S(2)}) collective-permute-start(f32[1,40,128]{2,1,0:T(8,128)S(1)} %bitcast.34), channel_id=1, source_target_pairs={{0,1},{1,0},{2,3},{3,2},{4,5},{5,4},{6,7},{7,6},{8,9},{9,8},{10,11... | collective-permute-start | bytes 61448 | tf_op jit(solution)/shard_map/ppermute | solution.py:98
  10.7 20.8 %copy-start.2 = (s32[20]{0:T(128)S(1)}, s32[20]{0:T(128)}, u32[]{:S(2)}) copy-start(s32[20]{0:T(128)} %parent_ref.1) | copy-start | bytes 244
  10.9 14.4 %collective-permute-start.13 = (f32[1,2,40,128]{3,2,1,0:T(8,128)S(1)}, f32[1,2,40,128]{3,2,1,0:T(8,128)S(1)}, u32[]{:S(2)}, u32[]{:S(2)}) collective-permute-start(f32[1,2,40,128]{3,2,1,0:T(8,128)S(1)} %maximum_select_fusion.4), channel_id=1, source_target_pairs={{0,2},{2,0},{4,6},{6,4},{1,3},{3,1},{5,7},{7,5},{8,10},{10,8},{12,... | collective-permute-start | bytes 122888 | tf_op jit(solution)/shard_map/ppermute | solution.py:98
  13.6 13.1 %collective-permute-start = (f32[128,128]{1,0:T(8,128)S(1)}, f32[128,128]{1,0:T(8,128)S(1)}, u32[]{:S(2)}, u32[]{:S(2)}) collective-permute-start(f32[128,128]{1,0:T(8,128)S(1)} %get-tuple-element.14), channel_id=1, source_target_pairs={{8,0},{16,8},{24,16},{9,1},{17,9},{25,17},{10,2},{18,10},{26,18},{... | collective-permute-start | bytes 196616 | tf_op jit(solution)/shard_map/ppermute | solution.py:86
  14.9 14.9 %collective-permute-start.1 = (f32[128,128]{1,0:T(8,128)S(1)}, f32[128,128]{1,0:T(8,128)S(1)}, u32[]{:S(2)}, u32[]{:S(2)}) collective-permute-start(f32[128,128]{1,0:T(8,128)S(1)} %get-tuple-element.13), channel_id=1, source_target_pairs={{0,8},{8,16},{16,24},{1,9},{9,17},{17,25},{2,10},{10,18},{18,26},{... | collective-permute-start | bytes 196616 | tf_op jit(solution)/shard_map/ppermute | solution.py:86
  19.4 11.9 %collective-permute-start.2 = (f32[128,128]{1,0:T(8,128)S(1)}, f32[128,128]{1,0:T(8,128)S(1)}, u32[]{:S(2)}, u32[]{:S(2)}) collective-permute-start(f32[128,128]{1,0:T(8,128)S(1)} %get-tuple-element.12), channel_id=1, source_target_pairs={{2,0},{4,2},{6,4},{3,1},{5,3},{7,5},{10,8},{12,10},{14,12},{11,9},... | collective-permute-start | bytes 196616 | tf_op jit(solution)/shard_map/ppermute | solution.py:86
  20.7 10.6 %collective-permute-start.3 = (f32[128,128]{1,0:T(8,128)S(1)}, f32[128,128]{1,0:T(8,128)S(1)}, u32[]{:S(2)}, u32[]{:S(2)}) collective-permute-start(f32[128,128]{1,0:T(8,128)S(1)} %get-tuple-element.11), channel_id=1, source_target_pairs={{0,2},{2,4},{4,6},{1,3},{3,5},{5,7},{8,10},{10,12},{12,14},{9,11},... | collective-permute-start | bytes 196616 | tf_op jit(solution)/shard_map/ppermute | solution.py:86
  25.4 6.0 %collective-permute-start.4 = (f32[128,128]{1,0:T(8,128)S(1)}, f32[128,128]{1,0:T(8,128)S(1)}, u32[]{:S(2)}, u32[]{:S(2)}) collective-permute-start(f32[128,128]{1,0:T(8,128)S(1)} %get-tuple-element.10), channel_id=1, source_target_pairs={{1,0},{3,2},{5,4},{7,6},{9,8},{11,10},{13,12},{15,14},{17,16},{19,... | collective-permute-start | bytes 196616 | tf_op jit(solution)/shard_map/ppermute | solution.py:86
  26.7 4.7 %collective-permute-start.5 = (f32[128,128]{1,0:T(8,128)S(1)}, f32[128,128]{1,0:T(8,128)S(1)}, u32[]{:S(2)}, u32[]{:S(2)}) collective-permute-start(f32[128,128]{1,0:T(8,128)S(1)} %get-tuple-element.9), channel_id=1, source_target_pairs={{0,1},{2,3},{4,5},{6,7},{8,9},{10,11},{12,13},{14,15},{16,17},{18,... | collective-permute-start | bytes 196616 | tf_op jit(solution)/shard_map/ppermute | solution.py:86
  29.7 25.4 %collective-permute-start.14 = (f32[2,2,40,128]{3,2,1,0:T(8,128)S(1)}, f32[2,2,40,128]{3,2,1,0:T(8,128)S(1)}, u32[]{:S(2)}, u32[]{:S(2)}) collective-permute-start(f32[2,2,40,128]{3,2,1,0:T(8,128)S(1)} %maximum_select_fusion.3), channel_id=1, source_target_pairs={{0,4},{2,6},{4,0},{6,2},{1,5},{3,7},{5,1},{7,3},{8,12},{10,14},{12... | collective-permute-start | bytes 245768 | tf_op jit(solution)/shard_map/ppermute | solution.py:98
  44.6 38.8 %copy-start.3 = (f32[40,4352]{1,0:T(8,128)S(1)}, f32[40,4352]{1,0:T(8,128)}, u32[]{:S(2)}) copy-start(f32[40,4352]{1,0:T(8,128)} %param.14) | copy-start | bytes 2088964
  44.7 8.8 %collective-permute-start.6 = (bf16[128,128]{1,0:T(8,128)(2,1)S(1)}, bf16[128,128]{1,0:T(8,128)(2,1)S(1)}, u32[]{:S(2)}, u32[]{:S(2)}) collective-permute-start(bf16[128,128]{1,0:T(8,128)(2,1)S(1)} %get-tuple-element.20), channel_id=1, source_target_pairs={{0,8},{8,16},{16,24},{1,9},{9,17},{17,25},{2,10},{10,18},{18,26},{... | collective-permute-start | bytes 98312 | tf_op jit(solution)/shard_map/ppermute | solution.py:86
  48.3 8.4 %collective-permute-start.7 = (bf16[128,128]{1,0:T(8,128)(2,1)S(1)}, bf16[128,128]{1,0:T(8,128)(2,1)S(1)}, u32[]{:S(2)}, u32[]{:S(2)}) collective-permute-start(bf16[128,128]{1,0:T(8,128)(2,1)S(1)} %get-tuple-element.19), channel_id=1, source_target_pairs={{8,0},{16,8},{24,16},{9,1},{17,9},{25,17},{10,2},{18,10},{26,18},{... | collective-permute-start | bytes 98312 | tf_op jit(solution)/shard_map/ppermute | solution.py:86
  49.6 9.5 %collective-permute-start.8 = (bf16[128,128]{1,0:T(8,128)(2,1)S(1)}, bf16[128,128]{1,0:T(8,128)(2,1)S(1)}, u32[]{:S(2)}, u32[]{:S(2)}) collective-permute-start(bf16[128,128]{1,0:T(8,128)(2,1)S(1)} %get-tuple-element.18), channel_id=1, source_target_pairs={{0,2},{2,4},{4,6},{1,3},{3,5},{5,7},{8,10},{10,12},{12,14},{9,11},... | collective-permute-start | bytes 98312 | tf_op jit(solution)/shard_map/ppermute | solution.py:86
  52.1 15.0 %collective-permute-start.9 = (bf16[128,128]{1,0:T(8,128)(2,1)S(1)}, bf16[128,128]{1,0:T(8,128)(2,1)S(1)}, u32[]{:S(2)}, u32[]{:S(2)}) collective-permute-start(bf16[128,128]{1,0:T(8,128)(2,1)S(1)} %get-tuple-element.17), channel_id=1, source_target_pairs={{2,0},{4,2},{6,4},{3,1},{5,3},{7,5},{10,8},{12,10},{14,12},{11,9},... | collective-permute-start | bytes 98312 | tf_op jit(solution)/shard_map/ppermute | solution.py:86
  53.4 13.7 %collective-permute-start.10 = (bf16[128,128]{1,0:T(8,128)(2,1)S(1)}, bf16[128,128]{1,0:T(8,128)(2,1)S(1)}, u32[]{:S(2)}, u32[]{:S(2)}) collective-permute-start(bf16[128,128]{1,0:T(8,128)(2,1)S(1)} %get-tuple-element.16), channel_id=1, source_target_pairs={{0,1},{2,3},{4,5},{6,7},{8,9},{10,11},{12,13},{14,15},{16,17},{18,... | collective-permute-start | bytes 98312 | tf_op jit(solution)/shard_map/ppermute | solution.py:86
  55.2 12.0 %collective-permute-start.11 = (bf16[128,128]{1,0:T(8,128)(2,1)S(1)}, bf16[128,128]{1,0:T(8,128)(2,1)S(1)}, u32[]{:S(2)}, u32[]{:S(2)}) collective-permute-start(bf16[128,128]{1,0:T(8,128)(2,1)S(1)} %get-tuple-element.15), channel_id=1, source_target_pairs={{1,0},{3,2},{5,4},{7,6},{9,8},{11,10},{13,12},{15,14},{17,16},{19,... | collective-permute-start | bytes 98312 | tf_op jit(solution)/shard_map/ppermute | solution.py:86
  56.7 7.1 %collective-permute-start.15 = (f32[1,4,2,40,128]{4,3,2,1,0:T(8,128)S(1)}, f32[1,4,2,40,128]{4,3,2,1,0:T(8,128)S(1)}, u32[]{:S(2)}, u32[]{:S(2)}) collective-permute-start(f32[1,4,2,40,128]{4,3,2,1,0:T(8,128)S(1)} %maximum_select_fusion.2), channel_id=1, source_target_pairs={{0,8},{8,0},{16,24},{24,16},{1,9},{9,1},{17,25},{25,17},{2,10},{10... | collective-permute-start | bytes 491528 | tf_op jit(solution)/shard_map/ppermute | solution.py:98
  63.8 18.3 %collective-permute-start.16 = (f32[2,4,2,40,128]{4,3,2,1,0:T(8,128)S(1)}, f32[2,4,2,40,128]{4,3,2,1,0:T(8,128)S(1)}, u32[]{:S(2)}, u32[]{:S(2)}) collective-permute-start(f32[2,4,2,40,128]{4,3,2,1,0:T(8,128)S(1)} %maximum_select_fusion.1), channel_id=1, source_target_pairs={{0,16},{8,24},{16,0},{24,8},{1,17},{9,25},{17,1},{25,9},{2,18},{10... | collective-permute-start | bytes 983048 | tf_op jit(solution)/shard_map/ppermute | solution.py:98

commit v4 on v3

--- a/solution.py
+++ b/solution.py
@@ -86,27 +86,30 @@
     return lax.ppermute(value, axis, pairs)
 
 
-def gather_axis(value, axis):
+def gather_axis(held, axis, dim):
     count = lax.axis_size(axis)
     if count & (count - 1):
-        return lax.all_gather(value, axis, axis=0, tiled=False)
+        return lax.all_gather(held, axis, axis=dim, tiled=True)
     me = lax.axis_index(axis)
-    held = value[None]
     step = 1
     while step < count:
         pairs = [(i, i ^ step) for i in range(count)]
         other = lax.ppermute(held, axis, pairs)
         low = (me // step) % 2 == 0
-        held = jnp.where(low, jnp.concatenate([held, other]), jnp.concatenate([other, held]))
+        held = jnp.where(
+            low,
+            jnp.concatenate([held, other], axis=dim),
+            jnp.concatenate([other, held], axis=dim),
+        )
         step *= 2
     return held
 
 
 def gather_all(value):
-    for axis in reversed(AXES):
-        value = gather_axis(value, axis)
-    return value
-
+    held = value.reshape((1,) * len(AXES) + value.shape)
+    for dim, axis in enumerate(AXES):
+        held = gather_axis(held, axis, dim)
+    return held
 
 def per_device(
     residual, diag_inverse, coupling, parent, send_rows, counts, deflation, coarse_inverse

time: 91 us -> 80.3 us (0.88)
  waiting for transfers between devices: 19.6 us -> 8.37 us
    ppermute x5, waiting for transfers between devices: 19.6 us -> 8.34 us  [gather_axis(): other = lax.ppermute(held, axis, pairs)]
  transfers between devices with their start and end apart: 17 -> 17, of which waited for: 2 -> 3; matrix products, arithmetic and copies ran while one was open for 6% -> 7% of each run, Pallas kernels for 15% -> 17%
where the time goes in v4:
time: 80.3 us; the launch traced here: 78.9 us
  starting transfers between devices  38.4 us (48%)
  Pallas kernels  13.2 us (16%)
  matrix products  12 us (15%)
  waiting for transfers between devices  8.37 us (10%)
  local copies, waits for them, and re-layouts  5.46 us (7%)
  between operations  1.31 us (2%)
    ppermute x12, starting transfers between devices, shift(): return lax.ppermute(value, axis, pairs)  27.5 us
    pallas_call x1, Pallas kernels, local_solve(): pl.pallas_call(solve_kernel, out_shape=(jax.ShapeDtypeStruct((nrhs_here,...  13.2 us
    ppermute x5, starting transfers between devices, gather_axis(): other = lax.ppermute(held, axis, pairs)  10.9 us
    ppermute x5, waiting for transfers between devices, gather_axis(): other = lax.ppermute(held, axis, pairs)  8.34 us
    dot_general x1, matrix products, per_device(): faces = jnp.dot(returned, onehot, preferred_element_type=jnp.float32)  4.61 us
    dot_general x1, matrix products, per_device(): lax.dot_general(vectors, residual, NT, precision=lax.Precision.HIGHEST, p...  4.2 us
    gather x2, local copies, waits for them, and re-layouts, per_device(): outgoing = jnp.take(residual, send_rows, axis=1)  3.36 us
    unnamed x21, local copies, waits for them, and re-layouts  2.02 us
  transfers between devices with their start and end apart: 17, of which 3 were waited for; matrix products, arithmetic and copies ran while one was open for 7% of the time, Pallas kernels for 17%

profile of v4, /device:TPU:0, one launch (start us, length us, event | category | flops | bytes accessed | tf_op | source)
XLA Modules:
  0.0 78.9 jit_solution(9673793036962039429)
XLA Ops:
  0.8 4.2 %fusion.4 = f32[40,128]{1,0:T(8,128)S(1)} fusion(f32[128,4352]{1,0:T(8,128)} %res_ref.1, f32[40,4352]{1,0:T(8,128)} %param.14, f32[40]{0:T(128)S(1)} %compare_convert_fusion), kind=kOutput, calls=%fused_computation.8 | convolution fusion | flops 267560960 | bytes 2945184 | tf_op jit(solution)/shard_map/dot_general | solution.py:122
  5.0 3.1 %collective-permute-start.12 = (f32[1,1,1,40,128]{4,3,2,1,0:T(8,128)S(1)}, f32[1,1,1,40,128]{4,3,2,1,0:T(8,128)S(1)}, u32[]{:S(2)}, u32[]{:S(2)}) collective-permute-start(f32[1,1,1,40,128]{4,3,2,1,0:T(8,128)S(1)} %bitcast.57), channel_id=1, source_target_pairs={{0,8},{8,0},{16,24},{24,16},{1,9},{9,1},{17,25},{25,17},{2,10},{10... | collective-permute-start | bytes 61448 | tf_op jit(solution)/shard_map/ppermute | solution.py:97
  8.1 1.9 %copy.16 = f32[128,4352]{0,1:T(8,128)} copy(f32[128,4352]{1,0:T(8,128)S(1)} %copy-done.1) | data formatting | bytes 4456448 | tf_op args[0]
  10.0 3.2 %gather_fusion = f32[768,128]{1,0:T(8,128)S(1)} fusion(f32[128,4352]{0,1:T(8,128)} %copy.16, s32[1024]{0:T(1024)S(1)} %pad_clamp_fusion), kind=kCustom, calls=%fused_computation | custom fusion | bytes 789504 | tf_op jit(solution)/shard_map/jit(_take)/gather | solution.py:130
  13.5 1.3 %collective-permute-start = (f32[128,128]{1,0:T(8,128)S(1)}, f32[128,128]{1,0:T(8,128)S(1)}, u32[]{:S(2)}, u32[]{:S(2)}) collective-permute-start(f32[128,128]{1,0:T(8,128)S(1)} %get-tuple-element.14), channel_id=1, source_target_pairs={{8,0},{16,8},{24,16},{9,1},{17,9},{25,17},{10,2},{18,10},{26,18},{... | collective-permute-start | bytes 196616 | tf_op jit(solution)/shard_map/ppermute | solution.py:86
  14.8 4.5 %collective-permute-start.1 = (f32[128,128]{1,0:T(8,128)S(1)}, f32[128,128]{1,0:T(8,128)S(1)}, u32[]{:S(2)}, u32[]{:S(2)}) collective-permute-start(f32[128,128]{1,0:T(8,128)S(1)} %get-tuple-element.13), channel_id=1, source_target_pairs={{0,8},{8,16},{16,24},{1,9},{9,17},{17,25},{2,10},{10,18},{18,26},{... | collective-permute-start | bytes 196616 | tf_op jit(solution)/shard_map/ppermute | solution.py:86
  19.4 1.3 %collective-permute-start.2 = (f32[128,128]{1,0:T(8,128)S(1)}, f32[128,128]{1,0:T(8,128)S(1)}, u32[]{:S(2)}, u32[]{:S(2)}) collective-permute-start(f32[128,128]{1,0:T(8,128)S(1)} %get-tuple-element.12), channel_id=1, source_target_pairs={{2,0},{4,2},{6,4},{3,1},{5,3},{7,5},{10,8},{12,10},{14,12},{11,9},... | collective-permute-start | bytes 196616 | tf_op jit(solution)/shard_map/ppermute | solution.py:86
  20.7 4.5 %collective-permute-start.3 = (f32[128,128]{1,0:T(8,128)S(1)}, f32[128,128]{1,0:T(8,128)S(1)}, u32[]{:S(2)}, u32[]{:S(2)}) collective-permute-start(f32[128,128]{1,0:T(8,128)S(1)} %get-tuple-element.11), channel_id=1, source_target_pairs={{0,2},{2,4},{4,6},{1,3},{3,5},{5,7},{8,10},{10,12},{12,14},{9,11},... | collective-permute-start | bytes 196616 | tf_op jit(solution)/shard_map/ppermute | solution.py:86
  25.3 2.7 %collective-permute-start.13 = (f32[2,1,1,40,128]{4,3,2,1,0:T(8,128)S(1)}, f32[2,1,1,40,128]{4,3,2,1,0:T(8,128)S(1)}, u32[]{:S(2)}, u32[]{:S(2)}) collective-permute-start(f32[2,1,1,40,128]{4,3,2,1,0:T(8,128)S(1)} %maximum_select_fusion.6), channel_id=1, source_target_pairs={{0,16},{8,24},{16,0},{24,8},{1,17},{9,25},{17,1},{25,9},{2,18},{10... | collective-permute-start | bytes 122888 | tf_op jit(solution)/shard_map/ppermute | solution.py:97
  28.0 2.3 %collective-permute-done.13 = f32[2,1,1,40,128]{4,3,2,1,0:T(8,128)S(1)} collective-permute-done((f32[2,1,1,40,128]{4,3,2,1,0:T(8,128)S(1)}, f32[2,1,1,40,128]{4,3,2,1,0:T(8,128)S(1)}, u32[]{:S(2)}, u32[]{:S(2)}) %collective-permute-start.13) | collective-permute-done | bytes 40992 | tf_op jit(solution)/shard_map/ppermute | solution.py:97
  31.6 3.0 %collective-permute-start.5 = (f32[128,128]{1,0:T(8,128)S(1)}, f32[128,128]{1,0:T(8,128)S(1)}, u32[]{:S(2)}, u32[]{:S(2)}) collective-permute-start(f32[128,128]{1,0:T(8,128)S(1)} %get-tuple-element.9), channel_id=1, source_target_pairs={{0,1},{2,3},{4,5},{6,7},{8,9},{10,11},{12,13},{14,15},{16,17},{18,... | collective-permute-start | bytes 196616 | tf_op jit(solution)/shard_map/ppermute | solution.py:86
  34.7 2.5 %collective-permute-start.14 = (f32[4,1,1,40,128]{4,3,2,1,0:T(8,128)S(1)}, f32[4,1,1,40,128]{4,3,2,1,0:T(8,128)S(1)}, u32[]{:S(2)}, u32[]{:S(2)}) collective-permute-start(f32[4,1,1,40,128]{4,3,2,1,0:T(8,128)S(1)} %fusion.9), channel_id=1, source_target_pairs={{0,2},{2,0},{4,6},{6,4},{1,3},{3,1},{5,7},{7,5},{8,10},{10,8},{12,... | collective-permute-start | bytes 245768 | tf_op jit(solution)/shard_map/ppermute | solution.py:97
  37.3 13.2 %shard_map.82 = (bf16[128,4352]{1,0:T(8,128)(2,1)S(1)}, bf16[128,768]{1,0:T(8,128)(2,1)S(1)}) custom-call(s32[20]{0:T(128)S(1)} %copy-done.2, f32[128,4352]{1,0:T(8,128)S(1)} %copy-done.1, f32[128,768]{1,0:T(8,128)S(1)} %constant_dynamic-update-slice_fusion.slot_ref, bf16[20,256,256]{2,1,0:T(8,128)(2,1)} %inv_ref.1, bf16[19,256,256]{2,1,0:T(8,128)(2,1)} %cpl_ref.1), custom_call_target="tpu_custom_call" | custom-call | tf_op jit(solution)/shard_map/pallas_call | solution.py:58
  50.5 3.2 %collective-permute-start.6 = (bf16[128,128]{1,0:T(8,128)(2,1)S(1)}, bf16[128,128]{1,0:T(8,128)(2,1)S(1)}, u32[]{:S(2)}, u32[]{:S(2)}) collective-permute-start(bf16[128,128]{1,0:T(8,128)(2,1)S(1)} %get-tuple-element.20), channel_id=1, source_target_pairs={{0,8},{8,16},{16,24},{1,9},{9,17},{17,25},{2,10},{10,18},{18,26},{... | collective-permute-start | bytes 98312 | tf_op jit(solution)/shard_map/ppermute | solution.py:86
  53.7 1.3 %collective-permute-start.7 = (bf16[128,128]{1,0:T(8,128)(2,1)S(1)}, bf16[128,128]{1,0:T(8,128)(2,1)S(1)}, u32[]{:S(2)}, u32[]{:S(2)}) collective-permute-start(bf16[128,128]{1,0:T(8,128)(2,1)S(1)} %get-tuple-element.19), channel_id=1, source_target_pairs={{8,0},{16,8},{24,16},{9,1},{17,9},{25,17},{10,2},{18,10},{26,18},{... | collective-permute-start | bytes 98312 | tf_op jit(solution)/shard_map/ppermute | solution.py:86
  55.0 2.6 %collective-permute-start.8 = (bf16[128,128]{1,0:T(8,128)(2,1)S(1)}, bf16[128,128]{1,0:T(8,128)(2,1)S(1)}, u32[]{:S(2)}, u32[]{:S(2)}) collective-permute-start(bf16[128,128]{1,0:T(8,128)(2,1)S(1)} %get-tuple-element.18), channel_id=1, source_target_pairs={{0,2},{2,4},{4,6},{1,3},{3,5},{5,7},{8,10},{10,12},{12,14},{9,11},... | collective-permute-start | bytes 98312 | tf_op jit(solution)/shard_map/ppermute | solution.py:86
  57.6 1.3 %collective-permute-start.9 = (bf16[128,128]{1,0:T(8,128)(2,1)S(1)}, bf16[128,128]{1,0:T(8,128)(2,1)S(1)}, u32[]{:S(2)}, u32[]{:S(2)}) collective-permute-start(bf16[128,128]{1,0:T(8,128)(2,1)S(1)} %get-tuple-element.17), channel_id=1, source_target_pairs={{2,0},{4,2},{6,4},{3,1},{5,3},{7,5},{10,8},{12,10},{14,12},{11,9},... | collective-permute-start | bytes 98312 | tf_op jit(solution)/shard_map/ppermute | solution.py:86
  58.9 1.7 %collective-permute-start.10 = (bf16[128,128]{1,0:T(8,128)(2,1)S(1)}, bf16[128,128]{1,0:T(8,128)(2,1)S(1)}, u32[]{:S(2)}, u32[]{:S(2)}) collective-permute-start(bf16[128,128]{1,0:T(8,128)(2,1)S(1)} %get-tuple-element.16), channel_id=1, source_target_pairs={{0,1},{2,3},{4,5},{6,7},{8,9},{10,11},{12,13},{14,15},{16,17},{18,... | collective-permute-start | bytes 98312 | tf_op jit(solution)/shard_map/ppermute | solution.py:86
  60.6 1.5 %collective-permute-start.11 = (bf16[128,128]{1,0:T(8,128)(2,1)S(1)}, bf16[128,128]{1,0:T(8,128)(2,1)S(1)}, u32[]{:S(2)}, u32[]{:S(2)}) collective-permute-start(bf16[128,128]{1,0:T(8,128)(2,1)S(1)} %get-tuple-element.15), channel_id=1, source_target_pairs={{1,0},{3,2},{5,4},{7,6},{9,8},{11,10},{13,12},{15,14},{17,16},{19,... | collective-permute-start | bytes 98312 | tf_op jit(solution)/shard_map/ppermute | solution.py:86
  62.2 2.5 %collective-permute-start.15 = (f32[4,2,1,40,128]{4,3,2,1,0:T(8,128)S(1)}, f32[4,2,1,40,128]{4,3,2,1,0:T(8,128)S(1)}, u32[]{:S(2)}, u32[]{:S(2)}) collective-permute-start(f32[4,2,1,40,128]{4,3,2,1,0:T(8,128)S(1)} %maximum_select_fusion.3), channel_id=1, source_target_pairs={{0,4},{2,6},{4,0},{6,2},{1,5},{3,7},{5,1},{7,3},{8,12},{10,14},{12... | collective-permute-start | bytes 491528 | tf_op jit(solution)/shard_map/ppermute | solution.py:97
  64.7 4.7 %collective-permute-done.15 = f32[4,2,1,40,128]{4,3,2,1,0:T(8,128)S(1)} collective-permute-done((f32[4,2,1,40,128]{4,3,2,1,0:T(8,128)S(1)}, f32[4,2,1,40,128]{4,3,2,1,0:T(8,128)S(1)}, u32[]{:S(2)}, u32[]{:S(2)}) %collective-permute-start.15) | collective-permute-done | bytes 163872 | tf_op jit(solution)/shard_map/ppermute | solution.py:97
  69.7 1.4 %collective-permute-done.16 = f32[4,4,1,40,128]{4,3,2,1,0:T(8,128)S(1)} collective-permute-done((f32[4,4,1,40,128]{4,3,2,1,0:T(8,128)S(1)}, f32[4,4,1,40,128]{4,3,2,1,0:T(8,128)S(1)}, u32[]{:S(2)}, u32[]{:S(2)}) %collective-permute-start.16) | collective-permute-done | bytes 327712 | tf_op jit(solution)/shard_map/ppermute | solution.py:97
  72.3 2.0 %fusion.2 = f32[128,4352]{1,0:T(8,128)S(1)} fusion(f32[128,40]{1,0:T(8,128)S(1)} %fusion.15, f32[40,4352]{1,0:T(8,128)S(1)} %copy-done.3, f32[40]{0:T(128)S(1)} %compare_convert_fusion), kind=kOutput, calls=%fused_computation.6 | convolution fusion | flops 267560960 | bytes 2945184 | tf_op jit(solution)/shard_map/dot_general | solution.py:150
  74.3 4.6 %add_add_fusion = f32[128,4352]{1,0:T(8,128)} fusion(f32[128,4352]{1,0:T(8,128)S(1)} %fusion.2, bf16[128,4352]{1,0:T(8,128)(2,1)S(1)} %get-tuple-element.7, bf16[128,768]{1,0:T(8,128)(2,1)S(1)} %constant_dynamic-update-slice_fusion.6, s32[768]{0:T(1024)S(1)} %bitcast.61), kind=kOutput, calls=%fused_computation.4 | convolution fusion | flops 860651520 | bytes 5770240 | tf_op jit(solution)/shard_map/dot_general | solution.py:149
  (55 shorter events, 3.3 us)
Async XLA Ops:
  0.0 71.1 %copy-start = (f32[40,1280]{1,0:T(8,128)S(1)}, f32[40,1280]{1,0:T(8,128)}, u32[]{:S(2)}) copy-start(f32[40,1280]{1,0:T(8,128)} %param.15) | copy-start | bytes 614404
  0.0 8.1 %copy-start.1 = (f32[128,4352]{1,0:T(8,128)S(1)}, f32[128,4352]{1,0:T(8,128)}, u32[]{:S(2)}) copy-start(f32[128,4352]{1,0:T(8,128)} %res_ref.1) | copy-start | bytes 6684676
  5.0 5.0 %copy-start.4 = (s32[6,128]{1,0:T(8,128)S(1)}, s32[6,128]{1,0:T(8,128)}, u32[]{:S(2)}) copy-start(s32[6,128]{1,0:T(8,128)} %param.12) | copy-start | bytes 9220
  5.0 20.3 %collective-permute-start.12 = (f32[1,1,1,40,128]{4,3,2,1,0:T(8,128)S(1)}, f32[1,1,1,40,128]{4,3,2,1,0:T(8,128)S(1)}, u32[]{:S(2)}, u32[]{:S(2)}) collective-permute-start(f32[1,1,1,40,128]{4,3,2,1,0:T(8,128)S(1)} %bitcast.57), channel_id=1, source_target_pairs={{0,8},{8,0},{16,24},{24,16},{1,9},{9,1},{17,25},{25,17},{2,10},{10... | collective-permute-start | bytes 61448 | tf_op jit(solution)/shard_map/ppermute | solution.py:97
  13.3 24.0 %copy-start.2 = (s32[20]{0:T(128)S(1)}, s32[20]{0:T(128)}, u32[]{:S(2)}) copy-start(s32[20]{0:T(128)} %parent_ref.1) | copy-start | bytes 244
  13.5 18.1 %collective-permute-start = (f32[128,128]{1,0:T(8,128)S(1)}, f32[128,128]{1,0:T(8,128)S(1)}, u32[]{:S(2)}, u32[]{:S(2)}) collective-permute-start(f32[128,128]{1,0:T(8,128)S(1)} %get-tuple-element.14), channel_id=1, source_target_pairs={{8,0},{16,8},{24,16},{9,1},{17,9},{25,17},{10,2},{18,10},{26,18},{... | collective-permute-start | bytes 196616 | tf_op jit(solution)/shard_map/ppermute | solution.py:86
  14.8 19.9 %collective-permute-start.1 = (f32[128,128]{1,0:T(8,128)S(1)}, f32[128,128]{1,0:T(8,128)S(1)}, u32[]{:S(2)}, u32[]{:S(2)}) collective-permute-start(f32[128,128]{1,0:T(8,128)S(1)} %get-tuple-element.13), channel_id=1, source_target_pairs={{0,8},{8,16},{16,24},{1,9},{9,17},{17,25},{2,10},{10,18},{18,26},{... | collective-permute-start | bytes 196616 | tf_op jit(solution)/shard_map/ppermute | solution.py:86
  19.4 17.8 %collective-permute-start.2 = (f32[128,128]{1,0:T(8,128)S(1)}, f32[128,128]{1,0:T(8,128)S(1)}, u32[]{:S(2)}, u32[]{:S(2)}) collective-permute-start(f32[128,128]{1,0:T(8,128)S(1)} %get-tuple-element.12), channel_id=1, source_target_pairs={{2,0},{4,2},{6,4},{3,1},{5,3},{7,5},{10,8},{12,10},{14,12},{11,9},... | collective-permute-start | bytes 196616 | tf_op jit(solution)/shard_map/ppermute | solution.py:86
  20.7 16.5 %collective-permute-start.3 = (f32[128,128]{1,0:T(8,128)S(1)}, f32[128,128]{1,0:T(8,128)S(1)}, u32[]{:S(2)}, u32[]{:S(2)}) collective-permute-start(f32[128,128]{1,0:T(8,128)S(1)} %get-tuple-element.11), channel_id=1, source_target_pairs={{0,2},{2,4},{4,6},{1,3},{3,5},{5,7},{8,10},{10,12},{12,14},{9,11},... | collective-permute-start | bytes 196616 | tf_op jit(solution)/shard_map/ppermute | solution.py:86
  25.3 5.0 %collective-permute-start.13 = (f32[2,1,1,40,128]{4,3,2,1,0:T(8,128)S(1)}, f32[2,1,1,40,128]{4,3,2,1,0:T(8,128)S(1)}, u32[]{:S(2)}, u32[]{:S(2)}) collective-permute-start(f32[2,1,1,40,128]{4,3,2,1,0:T(8,128)S(1)} %maximum_select_fusion.6), channel_id=1, source_target_pairs={{0,16},{8,24},{16,0},{24,8},{1,17},{9,25},{17,1},{25,9},{2,18},{10... | collective-permute-start | bytes 122888 | tf_op jit(solution)/shard_map/ppermute | solution.py:97
  30.3 6.9 %collective-permute-start.4 = (f32[128,128]{1,0:T(8,128)S(1)}, f32[128,128]{1,0:T(8,128)S(1)}, u32[]{:S(2)}, u32[]{:S(2)}) collective-permute-start(f32[128,128]{1,0:T(8,128)S(1)} %get-tuple-element.10), channel_id=1, source_target_pairs={{1,0},{3,2},{5,4},{7,6},{9,8},{11,10},{13,12},{15,14},{17,16},{19,... | collective-permute-start | bytes 196616 | tf_op jit(solution)/shard_map/ppermute | solution.py:86
  31.6 5.6 %collective-permute-start.5 = (f32[128,128]{1,0:T(8,128)S(1)}, f32[128,128]{1,0:T(8,128)S(1)}, u32[]{:S(2)}, u32[]{:S(2)}) collective-permute-start(f32[128,128]{1,0:T(8,128)S(1)} %get-tuple-element.9), channel_id=1, source_target_pairs={{0,1},{2,3},{4,5},{6,7},{8,9},{10,11},{12,13},{14,15},{16,17},{18,... | collective-permute-start | bytes 196616 | tf_op jit(solution)/shard_map/ppermute | solution.py:86
  34.7 27.4 %collective-permute-start.14 = (f32[4,1,1,40,128]{4,3,2,1,0:T(8,128)S(1)}, f32[4,1,1,40,128]{4,3,2,1,0:T(8,128)S(1)}, u32[]{:S(2)}, u32[]{:S(2)}) collective-permute-start(f32[4,1,1,40,128]{4,3,2,1,0:T(8,128)S(1)} %fusion.9), channel_id=1, source_target_pairs={{0,2},{2,0},{4,6},{6,4},{1,3},{3,1},{5,7},{7,5},{8,10},{10,8},{12,... | collective-permute-start | bytes 245768 | tf_op jit(solution)/shard_map/ppermute | solution.py:97
  50.5 21.9 %copy-start.3 = (f32[40,4352]{1,0:T(8,128)S(1)}, f32[40,4352]{1,0:T(8,128)}, u32[]{:S(2)}) copy-start(f32[40,4352]{1,0:T(8,128)} %param.14) | copy-start | bytes 2088964
  50.5 8.4 %collective-permute-start.6 = (bf16[128,128]{1,0:T(8,128)(2,1)S(1)}, bf16[128,128]{1,0:T(8,128)(2,1)S(1)}, u32[]{:S(2)}, u32[]{:S(2)}) collective-permute-start(bf16[128,128]{1,0:T(8,128)(2,1)S(1)} %get-tuple-element.20), channel_id=1, source_target_pairs={{0,8},{8,16},{16,24},{1,9},{9,17},{17,25},{2,10},{10,18},{18,26},{... | collective-permute-start | bytes 98312 | tf_op jit(solution)/shard_map/ppermute | solution.py:86
  53.7 6.9 %collective-permute-start.7 = (bf16[128,128]{1,0:T(8,128)(2,1)S(1)}, bf16[128,128]{1,0:T(8,128)(2,1)S(1)}, u32[]{:S(2)}, u32[]{:S(2)}) collective-permute-start(bf16[128,128]{1,0:T(8,128)(2,1)S(1)} %get-tuple-element.19), channel_id=1, source_target_pairs={{8,0},{16,8},{24,16},{9,1},{17,9},{25,17},{10,2},{18,10},{26,18},{... | collective-permute-start | bytes 98312 | tf_op jit(solution)/shard_map/ppermute | solution.py:86
  55.0 9.6 %collective-permute-start.8 = (bf16[128,128]{1,0:T(8,128)(2,1)S(1)}, bf16[128,128]{1,0:T(8,128)(2,1)S(1)}, u32[]{:S(2)}, u32[]{:S(2)}) collective-permute-start(bf16[128,128]{1,0:T(8,128)(2,1)S(1)} %get-tuple-element.18), channel_id=1, source_target_pairs={{0,2},{2,4},{4,6},{1,3},{3,5},{5,7},{8,10},{10,12},{12,14},{9,11},... | collective-permute-start | bytes 98312 | tf_op jit(solution)/shard_map/ppermute | solution.py:86
  57.6 12.0 %collective-permute-start.9 = (bf16[128,128]{1,0:T(8,128)(2,1)S(1)}, bf16[128,128]{1,0:T(8,128)(2,1)S(1)}, u32[]{:S(2)}, u32[]{:S(2)}) collective-permute-start(bf16[128,128]{1,0:T(8,128)(2,1)S(1)} %get-tuple-element.17), channel_id=1, source_target_pairs={{2,0},{4,2},{6,4},{3,1},{5,3},{7,5},{10,8},{12,10},{14,12},{11,9},... | collective-permute-start | bytes 98312 | tf_op jit(solution)/shard_map/ppermute | solution.py:86
  58.9 10.7 %collective-permute-start.10 = (bf16[128,128]{1,0:T(8,128)(2,1)S(1)}, bf16[128,128]{1,0:T(8,128)(2,1)S(1)}, u32[]{:S(2)}, u32[]{:S(2)}) collective-permute-start(bf16[128,128]{1,0:T(8,128)(2,1)S(1)} %get-tuple-element.16), channel_id=1, source_target_pairs={{0,1},{2,3},{4,5},{6,7},{8,9},{10,11},{12,13},{14,15},{16,17},{18,... | collective-permute-start | bytes 98312 | tf_op jit(solution)/shard_map/ppermute | solution.py:86
  60.6 9.0 %collective-permute-start.11 = (bf16[128,128]{1,0:T(8,128)(2,1)S(1)}, bf16[128,128]{1,0:T(8,128)(2,1)S(1)}, u32[]{:S(2)}, u32[]{:S(2)}) collective-permute-start(bf16[128,128]{1,0:T(8,128)(2,1)S(1)} %get-tuple-element.15), channel_id=1, source_target_pairs={{1,0},{3,2},{5,4},{7,6},{9,8},{11,10},{13,12},{15,14},{17,16},{19,... | collective-permute-start | bytes 98312 | tf_op jit(solution)/shard_map/ppermute | solution.py:86
  62.2 7.2 %collective-permute-start.15 = (f32[4,2,1,40,128]{4,3,2,1,0:T(8,128)S(1)}, f32[4,2,1,40,128]{4,3,2,1,0:T(8,128)S(1)}, u32[]{:S(2)}, u32[]{:S(2)}) collective-permute-start(f32[4,2,1,40,128]{4,3,2,1,0:T(8,128)S(1)} %maximum_select_fusion.3), channel_id=1, source_target_pairs={{0,4},{2,6},{4,0},{6,2},{1,5},{3,7},{5,1},{7,3},{8,12},{10,14},{12... | collective-permute-start | bytes 491528 | tf_op jit(solution)/shard_map/ppermute | solution.py:97
  69.3 1.7 %collective-permute-start.16 = (f32[4,4,1,40,128]{4,3,2,1,0:T(8,128)S(1)}, f32[4,4,1,40,128]{4,3,2,1,0:T(8,128)S(1)}, u32[]{:S(2)}, u32[]{:S(2)}) collective-permute-start(f32[4,4,1,40,128]{4,3,2,1,0:T(8,128)S(1)} %maximum_select_fusion.1), channel_id=1, source_target_pairs={{0,1},{1,0},{2,3},{3,2},{4,5},{5,4},{6,7},{7,6},{8,9},{9,8},{10,11... | collective-permute-start | bytes 983048 | tf_op jit(solution)/shard_map/ppermute | solution.py:97

commit v5 on v4

--- a/solution.py
+++ b/solution.py
@@ -122,7 +122,8 @@
     coeffs_t = lax.dot_general(
         vectors, residual, NT, precision=lax.Precision.HIGHEST, preferred_element_type=jnp.float32
     )
-    gathered = gather_all(coeffs_t).reshape(-1, coeffs_t.shape[1])
+    gathered = lax.all_gather(coeffs_t.reshape(1, -1), AXES, axis=0, tiled=True)
+    gathered = gathered.reshape(-1, coeffs_t.shape[1])
     solved_t = jnp.dot(
         coarse_inverse, gathered, precision=lax.Precision.HIGHEST, preferred_element_type=jnp.float32
     )

time: 80.3 us -> 100 us (1.25)
  blocking collectives: 0 us -> 41 us
  starting transfers between devices: 38.4 us -> 25.1 us
  waiting for transfers between devices: 8.37 us -> 2.29 us
  matrix products: 12 us -> 9.42 us
  other arithmetic: 0.2 us -> 2.46 us
    all_gather x0 -> x1, blocking collectives: none -> 41 us  [per_device(): gathered = lax.all_gather(coeffs_t.reshape(1, -1), AXES, axis=0, tiled=True)]
    ppermute x5 -> x0, starting transfers between devices: 10.9 us -> none  [gather_axis(): other = lax.ppermute(held, axis, pairs)]
    ppermute x5 -> x0, waiting for transfers between devices: 8.34 us -> none  [gather_axis(): other = lax.ppermute(held, axis, pairs)]
    ppermute x12, starting transfers between devices: 27.5 us -> 25.1 us  [shift(): return lax.ppermute(value, axis, pairs)]
    ppermute x12, waiting for transfers between devices: 0.03 us -> 2.29 us  [shift(): return lax.ppermute(value, axis, pairs)]
    dot_general x1, matrix products: 4.2 us -> 2.35 us  [per_device(): lax.dot_general(vectors, residual, NT, precision=lax.Precision.HIGHEST, p...]
  transfers between devices with their start and end apart: 17 -> 12, of which waited for: 3 -> 3; matrix products, arithmetic and copies ran while one was open for 7% -> 5% of each run, Pallas kernels for 17% -> 0%
where the time goes in v5:
time: 100 us; the launch traced here: 99.1 us
  blocking collectives  41 us (41%)
  starting transfers between devices  25.1 us (25%)
  Pallas kernels  13.1 us (13%)
  matrix products  9.42 us (9%)
  local copies, waits for them, and re-layouts  4.69 us (5%)
  other arithmetic  2.46 us (2%)
  waiting for transfers between devices  2.29 us (2%)
  between operations  1.02 us (1%)
    all_gather x1, blocking collectives, per_device(): gathered = lax.all_gather(coeffs_t.reshape(1, -1), AXES, axis=0, tiled=True)  41 us
    ppermute x12, starting transfers between devices, shift(): return lax.ppermute(value, axis, pairs)  25.1 us
    pallas_call x1, Pallas kernels, local_solve(): pl.pallas_call(solve_kernel, out_shape=(jax.ShapeDtypeStruct((nrhs_here,...  13.1 us
    dot_general x1, matrix products, per_device(): faces = jnp.dot(returned, onehot, preferred_element_type=jnp.float32)  4.61 us
    gather x2, local copies, waits for them, and re-layouts, per_device(): outgoing = jnp.take(residual, send_rows, axis=1)  2.49 us
    dot_general x1, matrix products, per_device(): lax.dot_general(vectors, residual, NT, precision=lax.Precision.HIGHEST, p...  2.35 us
    ppermute x12, waiting for transfers between devices, shift(): return lax.ppermute(value, axis, pairs)  2.29 us
    unnamed x21, local copies, waits for them, and re-layouts  2.12 us
  transfers between devices with their start and end apart: 12, of which 3 were waited for; matrix products, arithmetic and copies ran while one was open for 5% of the time, Pallas kernels for 0%

profile of v5, /device:TPU:0, one launch (start us, length us, event | category | flops | bytes accessed | tf_op | source)
XLA Modules:
  0.0 99.1 jit_solution(9553092395587415821)
XLA Ops:
  0.0 0.7 fusion.8
  1.4 2.0 %copy.12 = f32[128,4352]{0,1:T(8,128)S(1)} copy(f32[128,4352]{1,0:T(8,128)} %res_ref.1) | data formatting | bytes 4456448 | tf_op args[0]
  3.5 1.6 %gather_fusion = f32[768,128]{1,0:T(8,128)S(1)} fusion(f32[128,4352]{0,1:T(8,128)S(1)} %copy.12, s32[1024]{0:T(1024)S(1)} %pad_clamp_fusion), kind=kCustom, calls=%fused_computation | custom fusion | bytes 789504 | tf_op jit(solution)/shard_map/jit(_take)/gather | solution.py:131
  5.1 0.9 copy.13
  6.0 1.0 %select_bitcast_fusion = f32[128,6,128]{2,0,1:T(8,128)S(1)} fusion(f32[6,128,128]{1,2,0:T(8,128)} %copy.13, pred[6,128]{1,0:T(8,128)(4,1)S(1)} %compare_and_fusion), kind=kLoop, calls=%fused_computation.9 | loop fusion | flops 98304 | bytes 787200 | tf_op jit(solution)/shard_map/jit(_take)/select_n | solution.py:131
  7.0 1.3 %collective-permute-start = (f32[128,128]{1,0:T(8,128)S(1)}, f32[128,128]{1,0:T(8,128)S(1)}, u32[]{:S(2)}, u32[]{:S(2)}) collective-permute-start(f32[128,128]{1,0:T(8,128)S(1)} %get-tuple-element.14), channel_id=1, source_target_pairs={{8,0},{16,8},{24,16},{9,1},{17,9},{25,17},{10,2},{18,10},{26,18},{... | collective-permute-start | bytes 196616 | tf_op jit(solution)/shard_map/ppermute | solution.py:86
  8.3 5.6 %collective-permute-start.1 = (f32[128,128]{1,0:T(8,128)S(1)}, f32[128,128]{1,0:T(8,128)S(1)}, u32[]{:S(2)}, u32[]{:S(2)}) collective-permute-start(f32[128,128]{1,0:T(8,128)S(1)} %get-tuple-element.13), channel_id=1, source_target_pairs={{0,8},{8,16},{16,24},{1,9},{9,17},{17,25},{2,10},{10,18},{18,26},{... | collective-permute-start | bytes 196616 | tf_op jit(solution)/shard_map/ppermute | solution.py:86
  13.9 1.3 %collective-permute-start.2 = (f32[128,128]{1,0:T(8,128)S(1)}, f32[128,128]{1,0:T(8,128)S(1)}, u32[]{:S(2)}, u32[]{:S(2)}) collective-permute-start(f32[128,128]{1,0:T(8,128)S(1)} %get-tuple-element.12), channel_id=1, source_target_pairs={{2,0},{4,2},{6,4},{3,1},{5,3},{7,5},{10,8},{12,10},{14,12},{11,9},... | collective-permute-start | bytes 196616 | tf_op jit(solution)/shard_map/ppermute | solution.py:86
  15.2 4.5 %collective-permute-start.3 = (f32[128,128]{1,0:T(8,128)S(1)}, f32[128,128]{1,0:T(8,128)S(1)}, u32[]{:S(2)}, u32[]{:S(2)}) collective-permute-start(f32[128,128]{1,0:T(8,128)S(1)} %get-tuple-element.11), channel_id=1, source_target_pairs={{0,2},{2,4},{4,6},{1,3},{3,5},{5,7},{8,10},{10,12},{12,14},{9,11},... | collective-permute-start | bytes 196616 | tf_op jit(solution)/shard_map/ppermute | solution.py:86
  19.8 1.3 %collective-permute-start.4 = (f32[128,128]{1,0:T(8,128)S(1)}, f32[128,128]{1,0:T(8,128)S(1)}, u32[]{:S(2)}, u32[]{:S(2)}) collective-permute-start(f32[128,128]{1,0:T(8,128)S(1)} %get-tuple-element.10), channel_id=1, source_target_pairs={{1,0},{3,2},{5,4},{7,6},{9,8},{11,10},{13,12},{15,14},{17,16},{19,... | collective-permute-start | bytes 196616 | tf_op jit(solution)/shard_map/ppermute | solution.py:86
  21.7 2.4 %fusion.4 = f32[40,128]{1,0:T(8,128)S(1)} fusion(f32[128,4352]{1,0:T(8,128)S(1)} %copy-done.1, f32[40,4352]{1,0:T(8,128)S(1)} %copy-done.3, f32[40]{0:T(128)S(1)} %compare_convert_fusion), kind=kOutput, calls=%fused_computation.7 | convolution fusion | flops 267560960 | bytes 2945184 | tf_op jit(solution)/shard_map/dot_general | solution.py:122
  24.1 41.0 %all-gather = f32[32,1,5120]{2,1,0:T(1,128)S(1)} all-gather(f32[1,1,5120]{2,1,0:T(1,128)S(1)} %bitcast.29), channel_id=1, replica_groups=mesh['gx'=4,'gy'=4,'gz'=2] {'gx','gy','gz'}, dimensions={0}, use_global_device_ids=true | all-gather | bytes 675840 | tf_op jit(solution)/shard_map/all_gather | solution.py:125
  65.6 2.3 %collective-permute-start.5 = (f32[128,128]{1,0:T(8,128)S(1)}, f32[128,128]{1,0:T(8,128)S(1)}, u32[]{:S(2)}, u32[]{:S(2)}) collective-permute-start(f32[128,128]{1,0:T(8,128)S(1)} %get-tuple-element.9), channel_id=1, source_target_pairs={{0,1},{2,3},{4,5},{6,7},{8,9},{10,11},{12,13},{14,15},{16,17},{18,... | collective-permute-start | bytes 196616 | tf_op jit(solution)/shard_map/ppermute | solution.py:86
  68.0 0.8 collective-permute-done.5
  68.7 13.1 %shard_map.82 = (bf16[128,4352]{1,0:T(8,128)(2,1)S(1)}, bf16[128,768]{1,0:T(8,128)(2,1)S(1)}) custom-call(s32[20]{0:T(128)S(1)} %copy-done.2, f32[128,4352]{1,0:T(8,128)S(1)} %copy-done.1, f32[128,768]{1,0:T(8,128)S(1)} %constant_dynamic-update-slice_fusion.slot_ref, bf16[20,256,256]{2,1,0:T(8,128)(2,1)} %inv_ref.1, bf16[19,256,256]{2,1,0:T(8,128)(2,1)} %cpl_ref.1), custom_call_target="tpu_custom_call" | custom-call | tf_op jit(solution)/shard_map/pallas_call | solution.py:58
  81.9 1.3 %collective-permute-start.6 = (bf16[128,128]{1,0:T(8,128)(2,1)S(1)}, bf16[128,128]{1,0:T(8,128)(2,1)S(1)}, u32[]{:S(2)}, u32[]{:S(2)}) collective-permute-start(bf16[128,128]{1,0:T(8,128)(2,1)S(1)} %get-tuple-element.20), channel_id=1, source_target_pairs={{0,8},{8,16},{16,24},{1,9},{9,17},{17,25},{2,10},{10,18},{18,26},{... | collective-permute-start | bytes 98312 | tf_op jit(solution)/shard_map/ppermute | solution.py:86
  83.2 2.0 %fusion.2 = f32[128,4352]{1,0:T(8,128)S(1)} fusion(f32[128,40]{0,1:T(8,128)S(1)} %fusion.10, f32[40,4352]{1,0:T(8,128)S(1)} %copy-done.3, f32[40]{0:T(128)S(1)} %compare_convert_fusion), kind=kOutput, calls=%fused_computation.5 | convolution fusion | flops 267560960 | bytes 2945184 | tf_op jit(solution)/shard_map/dot_general | solution.py:151
  85.2 1.3 %collective-permute-start.7 = (bf16[128,128]{1,0:T(8,128)(2,1)S(1)}, bf16[128,128]{1,0:T(8,128)(2,1)S(1)}, u32[]{:S(2)}, u32[]{:S(2)}) collective-permute-start(bf16[128,128]{1,0:T(8,128)(2,1)S(1)} %get-tuple-element.19), channel_id=1, source_target_pairs={{8,0},{16,8},{24,16},{9,1},{17,9},{25,17},{10,2},{18,10},{26,18},{... | collective-permute-start | bytes 98312 | tf_op jit(solution)/shard_map/ppermute | solution.py:86
  86.5 1.3 %collective-permute-start.8 = (bf16[128,128]{1,0:T(8,128)(2,1)S(1)}, bf16[128,128]{1,0:T(8,128)(2,1)S(1)}, u32[]{:S(2)}, u32[]{:S(2)}) collective-permute-start(bf16[128,128]{1,0:T(8,128)(2,1)S(1)} %get-tuple-element.18), channel_id=1, source_target_pairs={{0,2},{2,4},{4,6},{1,3},{3,5},{5,7},{8,10},{10,12},{12,14},{9,11},... | collective-permute-start | bytes 98312 | tf_op jit(solution)/shard_map/ppermute | solution.py:86
  87.8 1.3 %collective-permute-start.9 = (bf16[128,128]{1,0:T(8,128)(2,1)S(1)}, bf16[128,128]{1,0:T(8,128)(2,1)S(1)}, u32[]{:S(2)}, u32[]{:S(2)}) collective-permute-start(bf16[128,128]{1,0:T(8,128)(2,1)S(1)} %get-tuple-element.17), channel_id=1, source_target_pairs={{2,0},{4,2},{6,4},{3,1},{5,3},{7,5},{10,8},{12,10},{14,12},{11,9},... | collective-permute-start | bytes 98312 | tf_op jit(solution)/shard_map/ppermute | solution.py:86
  89.1 2.3 %collective-permute-start.10 = (bf16[128,128]{1,0:T(8,128)(2,1)S(1)}, bf16[128,128]{1,0:T(8,128)(2,1)S(1)}, u32[]{:S(2)}, u32[]{:S(2)}) collective-permute-start(bf16[128,128]{1,0:T(8,128)(2,1)S(1)} %get-tuple-element.16), channel_id=1, source_target_pairs={{0,1},{2,3},{4,5},{6,7},{8,9},{10,11},{12,13},{14,15},{16,17},{18,... | collective-permute-start | bytes 98312 | tf_op jit(solution)/shard_map/ppermute | solution.py:86
  91.4 1.5 %collective-permute-start.11 = (bf16[128,128]{1,0:T(8,128)(2,1)S(1)}, bf16[128,128]{1,0:T(8,128)(2,1)S(1)}, u32[]{:S(2)}, u32[]{:S(2)}) collective-permute-start(bf16[128,128]{1,0:T(8,128)(2,1)S(1)} %get-tuple-element.15), channel_id=1, source_target_pairs={{1,0},{3,2},{5,4},{7,6},{9,8},{11,10},{13,12},{15,14},{17,16},{19,... | collective-permute-start | bytes 98312 | tf_op jit(solution)/shard_map/ppermute | solution.py:86
  93.7 0.8 collective-permute-done.11
  94.5 4.6 %add_add_fusion = f32[128,4352]{1,0:T(8,128)} fusion(f32[128,4352]{1,0:T(8,128)S(1)} %fusion.2, bf16[128,4352]{1,0:T(8,128)(2,1)S(1)} %get-tuple-element.7, bf16[128,768]{1,0:T(8,128)(2,1)S(1)} %constant_dynamic-update-slice_fusion.6, s32[768]{0:T(1024)S(1)} %bitcast.30), kind=kOutput, calls=%fused_computation.4 | convolution fusion | flops 860651520 | bytes 5770240 | tf_op jit(solution)/shard_map/dot_general | solution.py:150
  (38 shorter events, 2.1 us)
Async XLA Ops:
  0.0 65.1 %copy-start = (f32[40,1280]{1,0:T(8,128)S(1)}, f32[40,1280]{1,0:T(8,128)}, u32[]{:S(2)}) copy-start(f32[40,1280]{1,0:T(8,128)} %param.15) | copy-start | bytes 614404
  3.4 18.3 %copy-start.3 = (f32[40,4352]{1,0:T(8,128)S(1)}, f32[40,4352]{1,0:T(8,128)}, u32[]{:S(2)}) copy-start(f32[40,4352]{1,0:T(8,128)} %param.14) | copy-start | bytes 2088964
  5.0 16.7 %copy-start.1 = (f32[128,4352]{1,0:T(8,128)S(1)}, f32[128,4352]{1,0:T(8,128)}, u32[]{:S(2)}) copy-start(f32[128,4352]{1,0:T(8,128)} %res_ref.1) | copy-start | bytes 6684676
  7.0 58.5 %collective-permute-start = (f32[128,128]{1,0:T(8,128)S(1)}, f32[128,128]{1,0:T(8,128)S(1)}, u32[]{:S(2)}, u32[]{:S(2)}) collective-permute-start(f32[128,128]{1,0:T(8,128)S(1)} %get-tuple-element.14), channel_id=1, source_target_pairs={{8,0},{16,8},{24,16},{9,1},{17,9},{25,17},{10,2},{18,10},{26,18},{... | collective-permute-start | bytes 196616 | tf_op jit(solution)/shard_map/ppermute | solution.py:86
  8.3 59.5 %collective-permute-start.1 = (f32[128,128]{1,0:T(8,128)S(1)}, f32[128,128]{1,0:T(8,128)S(1)}, u32[]{:S(2)}, u32[]{:S(2)}) collective-permute-start(f32[128,128]{1,0:T(8,128)S(1)} %get-tuple-element.13), channel_id=1, source_target_pairs={{0,8},{8,16},{16,24},{1,9},{9,17},{17,25},{2,10},{10,18},{18,26},{... | collective-permute-start | bytes 196616 | tf_op jit(solution)/shard_map/ppermute | solution.py:86
  13.9 54.0 %collective-permute-start.2 = (f32[128,128]{1,0:T(8,128)S(1)}, f32[128,128]{1,0:T(8,128)S(1)}, u32[]{:S(2)}, u32[]{:S(2)}) collective-permute-start(f32[128,128]{1,0:T(8,128)S(1)} %get-tuple-element.12), channel_id=1, source_target_pairs={{2,0},{4,2},{6,4},{3,1},{5,3},{7,5},{10,8},{12,10},{14,12},{11,9},... | collective-permute-start | bytes 196616 | tf_op jit(solution)/shard_map/ppermute | solution.py:86
  15.2 52.7 %collective-permute-start.3 = (f32[128,128]{1,0:T(8,128)S(1)}, f32[128,128]{1,0:T(8,128)S(1)}, u32[]{:S(2)}, u32[]{:S(2)}) collective-permute-start(f32[128,128]{1,0:T(8,128)S(1)} %get-tuple-element.11), channel_id=1, source_target_pairs={{0,2},{2,4},{4,6},{1,3},{3,5},{5,7},{8,10},{10,12},{12,14},{9,11},... | collective-permute-start | bytes 196616 | tf_op jit(solution)/shard_map/ppermute | solution.py:86
  19.8 48.2 %collective-permute-start.4 = (f32[128,128]{1,0:T(8,128)S(1)}, f32[128,128]{1,0:T(8,128)S(1)}, u32[]{:S(2)}, u32[]{:S(2)}) collective-permute-start(f32[128,128]{1,0:T(8,128)S(1)} %get-tuple-element.10), channel_id=1, source_target_pairs={{1,0},{3,2},{5,4},{7,6},{9,8},{11,10},{13,12},{15,14},{17,16},{19,... | collective-permute-start | bytes 196616 | tf_op jit(solution)/shard_map/ppermute | solution.py:86
  21.7 47.0 %copy-start.2 = (s32[20]{0:T(128)S(1)}, s32[20]{0:T(128)}, u32[]{:S(2)}) copy-start(s32[20]{0:T(128)} %parent_ref.1) | copy-start | bytes 244
  65.6 3.1 %collective-permute-start.5 = (f32[128,128]{1,0:T(8,128)S(1)}, f32[128,128]{1,0:T(8,128)S(1)}, u32[]{:S(2)}, u32[]{:S(2)}) collective-permute-start(f32[128,128]{1,0:T(8,128)S(1)} %get-tuple-element.9), channel_id=1, source_target_pairs={{0,1},{2,3},{4,5},{6,7},{8,9},{10,11},{12,13},{14,15},{16,17},{18,... | collective-permute-start | bytes 196616 | tf_op jit(solution)/shard_map/ppermute | solution.py:86
  81.9 12.6 %copy-start.4 = (s32[6,128]{1,0:T(8,128)S(1)}, s32[6,128]{1,0:T(8,128)}, u32[]{:S(2)}) copy-start(s32[6,128]{1,0:T(8,128)} %param.12) | copy-start | bytes 9220
  81.9 9.5 %collective-permute-start.6 = (bf16[128,128]{1,0:T(8,128)(2,1)S(1)}, bf16[128,128]{1,0:T(8,128)(2,1)S(1)}, u32[]{:S(2)}, u32[]{:S(2)}) collective-permute-start(bf16[128,128]{1,0:T(8,128)(2,1)S(1)} %get-tuple-element.20), channel_id=1, source_target_pairs={{0,8},{8,16},{16,24},{1,9},{9,17},{17,25},{2,10},{10,18},{18,26},{... | collective-permute-start | bytes 98312 | tf_op jit(solution)/shard_map/ppermute | solution.py:86
  85.2 7.7 %collective-permute-start.7 = (bf16[128,128]{1,0:T(8,128)(2,1)S(1)}, bf16[128,128]{1,0:T(8,128)(2,1)S(1)}, u32[]{:S(2)}, u32[]{:S(2)}) collective-permute-start(bf16[128,128]{1,0:T(8,128)(2,1)S(1)} %get-tuple-element.19), channel_id=1, source_target_pairs={{8,0},{16,8},{24,16},{9,1},{17,9},{25,17},{10,2},{18,10},{26,18},{... | collective-permute-start | bytes 98312 | tf_op jit(solution)/shard_map/ppermute | solution.py:86
  86.5 6.4 %collective-permute-start.8 = (bf16[128,128]{1,0:T(8,128)(2,1)S(1)}, bf16[128,128]{1,0:T(8,128)(2,1)S(1)}, u32[]{:S(2)}, u32[]{:S(2)}) collective-permute-start(bf16[128,128]{1,0:T(8,128)(2,1)S(1)} %get-tuple-element.18), channel_id=1, source_target_pairs={{0,2},{2,4},{4,6},{1,3},{3,5},{5,7},{8,10},{10,12},{12,14},{9,11},... | collective-permute-start | bytes 98312 | tf_op jit(solution)/shard_map/ppermute | solution.py:86
  87.8 5.8 %collective-permute-start.9 = (bf16[128,128]{1,0:T(8,128)(2,1)S(1)}, bf16[128,128]{1,0:T(8,128)(2,1)S(1)}, u32[]{:S(2)}, u32[]{:S(2)}) collective-permute-start(bf16[128,128]{1,0:T(8,128)(2,1)S(1)} %get-tuple-element.17), channel_id=1, source_target_pairs={{2,0},{4,2},{6,4},{3,1},{5,3},{7,5},{10,8},{12,10},{14,12},{11,9},... | collective-permute-start | bytes 98312 | tf_op jit(solution)/shard_map/ppermute | solution.py:86
  89.1 4.5 %collective-permute-start.10 = (bf16[128,128]{1,0:T(8,128)(2,1)S(1)}, bf16[128,128]{1,0:T(8,128)(2,1)S(1)}, u32[]{:S(2)}, u32[]{:S(2)}) collective-permute-start(bf16[128,128]{1,0:T(8,128)(2,1)S(1)} %get-tuple-element.16), channel_id=1, source_target_pairs={{0,1},{2,3},{4,5},{6,7},{8,9},{10,11},{12,13},{14,15},{16,17},{18,... | collective-permute-start | bytes 98312 | tf_op jit(solution)/shard_map/ppermute | solution.py:86
  91.4 3.1 %collective-permute-start.11 = (bf16[128,128]{1,0:T(8,128)(2,1)S(1)}, bf16[128,128]{1,0:T(8,128)(2,1)S(1)}, u32[]{:S(2)}, u32[]{:S(2)}) collective-permute-start(bf16[128,128]{1,0:T(8,128)(2,1)S(1)} %get-tuple-element.15), channel_id=1, source_target_pairs={{1,0},{3,2},{5,4},{7,6},{9,8},{11,10},{13,12},{15,14},{17,16},{19,... | collective-permute-start | bytes 98312 | tf_op jit(solution)/shard_map/ppermute | solution.py:86

commit v6 on v4

--- a/solution.py
+++ b/solution.py
@@ -11,8 +11,20 @@
 NT = (((1,), (1,)), ((), ()))
 
 
-def solve_kernel(parent_ref, res_ref, slot_ref, inv_ref, cpl_ref, own_ref, zslot_ref, y_ref, carry_ref):
+def solve_kernel(
+    parent_ref, res_ref, slot_ref, inv_hbm, cpl_hbm, own_ref, zslot_ref,
+    inv_ref, cpl_ref, sems, y_ref, carry_ref,
+):
     blocks_n, block_w, _ = inv_ref.shape
+    inv_copies, cpl_copies = [], []
+    for b in range(blocks_n):
+        if b > 0:
+            cpl_copies.append(
+                pltpu.make_async_copy(cpl_hbm.at[b - 1], cpl_ref.at[b - 1], sems.at[blocks_n + b - 1])
+            )
+            cpl_copies[-1].start()
+        inv_copies.append(pltpu.make_async_copy(inv_hbm.at[b], inv_ref.at[b], sems.at[b]))
+        inv_copies[-1].start()
     owned_blocks = res_ref.shape[1] // block_w
 
     def columns(b):
@@ -29,10 +41,12 @@
         if b == 0:
             lower = x.astype(jnp.bfloat16)
         else:
+            cpl_copies[b - 1].wait()
             prior = y_ref[link(b)]
             lower = (
                 x - lax.dot_general(prior, cpl_ref[b - 1], NT, preferred_element_type=jnp.float32)
             ).astype(jnp.bfloat16)
+        inv_copies[b].wait()
         y_ref[b] = lax.dot_general(
             lower, inv_ref[b], NT, preferred_element_type=jnp.float32
         ).astype(jnp.bfloat16)
@@ -65,11 +79,14 @@
             pl.BlockSpec(memory_space=pltpu.SMEM),
             pl.BlockSpec(memory_space=vmem),
             pl.BlockSpec(memory_space=vmem),
-            pl.BlockSpec(memory_space=vmem),
-            pl.BlockSpec(memory_space=vmem),
+            pl.BlockSpec(memory_space=pl.ANY),
+            pl.BlockSpec(memory_space=pl.ANY),
         ],
         out_specs=(pl.BlockSpec(memory_space=vmem), pl.BlockSpec(memory_space=vmem)),
         scratch_shapes=[
+            pltpu.VMEM(diag_inverse.shape, diag_inverse.dtype),
+            pltpu.VMEM(coupling.shape, coupling.dtype),
+            pltpu.SemaphoreType.DMA((2 * blocks_n - 1,)),
             pltpu.VMEM((blocks_n, nrhs_here, block_w), jnp.bfloat16),
             pltpu.VMEM((blocks_n, nrhs_here, block_w), jnp.float32),
         ],

time: 80.3 us -> 82.7 us (1.030)
  Pallas kernels: 13.2 us -> 15.6 us
    pallas_call x1, Pallas kernels: 13.2 us -> 15.6 us  [local_solve(): pl.pallas_call(solve_kernel, out_shape=(jax.ShapeDtypeStruct((nrhs_here,...]
  transfers between devices with their start and end apart: 17 -> 17, of which waited for: 3 -> 3; matrix products, arithmetic and copies ran while one was open for 7% -> 7% of each run, Pallas kernels for 17% -> 19%
where the time goes in v6:
time: 82.7 us; the launch traced here: 81.4 us
  starting transfers between devices  38.4 us (46%)
  Pallas kernels  15.6 us (19%)
  matrix products  12 us (15%)
  waiting for transfers between devices  8.37 us (10%)
  local copies, waits for them, and re-layouts  5.46 us (7%)
  between operations  1.32 us (2%)
    ppermute x12, starting transfers between devices, shift(): return lax.ppermute(value, axis, pairs)  27.5 us
    pallas_call x1, Pallas kernels, local_solve(): pl.pallas_call(solve_kernel, out_shape=(jax.ShapeDtypeStruct((nrhs_here,...  15.6 us
    ppermute x5, starting transfers between devices, gather_axis(): other = lax.ppermute(held, axis, pairs)  10.9 us
    ppermute x5, waiting for transfers between devices, gather_axis(): other = lax.ppermute(held, axis, pairs)  8.34 us
    dot_general x1, matrix products, per_device(): faces = jnp.dot(returned, onehot, preferred_element_type=jnp.float32)  4.62 us
    dot_general x1, matrix products, per_device(): lax.dot_general(vectors, residual, NT, precision=lax.Precision.HIGHEST, p...  4.2 us
    gather x2, local copies, waits for them, and re-layouts, per_device(): outgoing = jnp.take(residual, send_rows, axis=1)  3.36 us
    unnamed x21, local copies, waits for them, and re-layouts  2.02 us
  transfers between devices with their start and end apart: 17, of which 3 were waited for; matrix products, arithmetic and copies ran while one was open for 7% of the time, Pallas kernels for 19%

profile of v6, /device:TPU:0, one launch (start us, length us, event | category | flops | bytes accessed | tf_op | source)
XLA Modules:
  0.0 81.4 jit_solution(15324235157960201405)
XLA Ops:
  0.8 4.2 %fusion.4 = f32[40,128]{1,0:T(8,128)S(1)} fusion(f32[128,4352]{1,0:T(8,128)} %res_ref.1, f32[40,4352]{1,0:T(8,128)} %param.14, f32[40]{0:T(128)S(1)} %compare_convert_fusion), kind=kOutput, calls=%fused_computation.8 | convolution fusion | flops 267560960 | bytes 2945184 | tf_op jit(solution)/shard_map/dot_general | solution.py:139
  5.0 3.1 %collective-permute-start.12 = (f32[1,1,1,40,128]{4,3,2,1,0:T(8,128)S(1)}, f32[1,1,1,40,128]{4,3,2,1,0:T(8,128)S(1)}, u32[]{:S(2)}, u32[]{:S(2)}) collective-permute-start(f32[1,1,1,40,128]{4,3,2,1,0:T(8,128)S(1)} %bitcast.57), channel_id=1, source_target_pairs={{0,8},{8,0},{16,24},{24,16},{1,9},{9,1},{17,25},{25,17},{2,10},{10... | collective-permute-start | bytes 61448 | tf_op jit(solution)/shard_map/ppermute | solution.py:114
  8.1 1.9 %copy.16 = f32[128,4352]{0,1:T(8,128)} copy(f32[128,4352]{1,0:T(8,128)S(1)} %copy-done.1) | data formatting | bytes 4456448 | tf_op args[0]
  10.0 3.2 %gather_fusion = f32[768,128]{1,0:T(8,128)S(1)} fusion(f32[128,4352]{0,1:T(8,128)} %copy.16, s32[1024]{0:T(1024)S(1)} %pad_clamp_fusion), kind=kCustom, calls=%fused_computation | custom fusion | bytes 789504 | tf_op jit(solution)/shard_map/jit(_take)/gather | solution.py:147
  13.5 1.3 %collective-permute-start = (f32[128,128]{1,0:T(8,128)S(1)}, f32[128,128]{1,0:T(8,128)S(1)}, u32[]{:S(2)}, u32[]{:S(2)}) collective-permute-start(f32[128,128]{1,0:T(8,128)S(1)} %get-tuple-element.14), channel_id=1, source_target_pairs={{8,0},{16,8},{24,16},{9,1},{17,9},{25,17},{10,2},{18,10},{26,18},{... | collective-permute-start | bytes 196616 | tf_op jit(solution)/shard_map/ppermute | solution.py:103
  14.8 4.5 %collective-permute-start.1 = (f32[128,128]{1,0:T(8,128)S(1)}, f32[128,128]{1,0:T(8,128)S(1)}, u32[]{:S(2)}, u32[]{:S(2)}) collective-permute-start(f32[128,128]{1,0:T(8,128)S(1)} %get-tuple-element.13), channel_id=1, source_target_pairs={{0,8},{8,16},{16,24},{1,9},{9,17},{17,25},{2,10},{10,18},{18,26},{... | collective-permute-start | bytes 196616 | tf_op jit(solution)/shard_map/ppermute | solution.py:103
  19.4 1.3 %collective-permute-start.2 = (f32[128,128]{1,0:T(8,128)S(1)}, f32[128,128]{1,0:T(8,128)S(1)}, u32[]{:S(2)}, u32[]{:S(2)}) collective-permute-start(f32[128,128]{1,0:T(8,128)S(1)} %get-tuple-element.12), channel_id=1, source_target_pairs={{2,0},{4,2},{6,4},{3,1},{5,3},{7,5},{10,8},{12,10},{14,12},{11,9},... | collective-permute-start | bytes 196616 | tf_op jit(solution)/shard_map/ppermute | solution.py:103
  20.7 4.5 %collective-permute-start.3 = (f32[128,128]{1,0:T(8,128)S(1)}, f32[128,128]{1,0:T(8,128)S(1)}, u32[]{:S(2)}, u32[]{:S(2)}) collective-permute-start(f32[128,128]{1,0:T(8,128)S(1)} %get-tuple-element.11), channel_id=1, source_target_pairs={{0,2},{2,4},{4,6},{1,3},{3,5},{5,7},{8,10},{10,12},{12,14},{9,11},... | collective-permute-start | bytes 196616 | tf_op jit(solution)/shard_map/ppermute | solution.py:103
  25.3 2.7 %collective-permute-start.13 = (f32[2,1,1,40,128]{4,3,2,1,0:T(8,128)S(1)}, f32[2,1,1,40,128]{4,3,2,1,0:T(8,128)S(1)}, u32[]{:S(2)}, u32[]{:S(2)}) collective-permute-start(f32[2,1,1,40,128]{4,3,2,1,0:T(8,128)S(1)} %maximum_select_fusion.6), channel_id=1, source_target_pairs={{0,16},{8,24},{16,0},{24,8},{1,17},{9,25},{17,1},{25,9},{2,18},{10... | collective-permute-start | bytes 122888 | tf_op jit(solution)/shard_map/ppermute | solution.py:114
  28.0 2.3 %collective-permute-done.13 = f32[2,1,1,40,128]{4,3,2,1,0:T(8,128)S(1)} collective-permute-done((f32[2,1,1,40,128]{4,3,2,1,0:T(8,128)S(1)}, f32[2,1,1,40,128]{4,3,2,1,0:T(8,128)S(1)}, u32[]{:S(2)}, u32[]{:S(2)}) %collective-permute-start.13) | collective-permute-done | bytes 40992 | tf_op jit(solution)/shard_map/ppermute | solution.py:114
  31.6 3.0 %collective-permute-start.5 = (f32[128,128]{1,0:T(8,128)S(1)}, f32[128,128]{1,0:T(8,128)S(1)}, u32[]{:S(2)}, u32[]{:S(2)}) collective-permute-start(f32[128,128]{1,0:T(8,128)S(1)} %get-tuple-element.9), channel_id=1, source_target_pairs={{0,1},{2,3},{4,5},{6,7},{8,9},{10,11},{12,13},{14,15},{16,17},{18,... | collective-permute-start | bytes 196616 | tf_op jit(solution)/shard_map/ppermute | solution.py:103
  34.7 2.5 %collective-permute-start.14 = (f32[4,1,1,40,128]{4,3,2,1,0:T(8,128)S(1)}, f32[4,1,1,40,128]{4,3,2,1,0:T(8,128)S(1)}, u32[]{:S(2)}, u32[]{:S(2)}) collective-permute-start(f32[4,1,1,40,128]{4,3,2,1,0:T(8,128)S(1)} %fusion.9), channel_id=1, source_target_pairs={{0,2},{2,0},{4,6},{6,4},{1,3},{3,1},{5,7},{7,5},{8,10},{10,8},{12,... | collective-permute-start | bytes 245768 | tf_op jit(solution)/shard_map/ppermute | solution.py:114
  37.3 15.6 %shard_map.82 = (bf16[128,4352]{1,0:T(8,128)(2,1)S(1)}, bf16[128,768]{1,0:T(8,128)(2,1)S(1)}) custom-call(s32[20]{0:T(128)S(1)} %copy-done.2, f32[128,4352]{1,0:T(8,128)S(1)} %copy-done.1, f32[128,768]{1,0:T(8,128)S(1)} %constant_dynamic-update-slice_fusion.slot_ref, bf16[20,256,256]{2,1,0:T(8,128)(2,1)} %inv_hbm.1, bf16[19,256,256]{2,1,0:T(8,128)(2,1)} %cpl_hbm.1), custom_call_target="tpu_custom_call" | custom-call | tf_op jit(solution)/shard_map/pallas_call | solution.py:72
  53.0 3.2 %collective-permute-start.6 = (bf16[128,128]{1,0:T(8,128)(2,1)S(1)}, bf16[128,128]{1,0:T(8,128)(2,1)S(1)}, u32[]{:S(2)}, u32[]{:S(2)}) collective-permute-start(bf16[128,128]{1,0:T(8,128)(2,1)S(1)} %get-tuple-element.20), channel_id=1, source_target_pairs={{0,8},{8,16},{16,24},{1,9},{9,17},{17,25},{2,10},{10,18},{18,26},{... | collective-permute-start | bytes 98312 | tf_op jit(solution)/shard_map/ppermute | solution.py:103
  56.2 1.3 %collective-permute-start.7 = (bf16[128,128]{1,0:T(8,128)(2,1)S(1)}, bf16[128,128]{1,0:T(8,128)(2,1)S(1)}, u32[]{:S(2)}, u32[]{:S(2)}) collective-permute-start(bf16[128,128]{1,0:T(8,128)(2,1)S(1)} %get-tuple-element.19), channel_id=1, source_target_pairs={{8,0},{16,8},{24,16},{9,1},{17,9},{25,17},{10,2},{18,10},{26,18},{... | collective-permute-start | bytes 98312 | tf_op jit(solution)/shard_map/ppermute | solution.py:103
  57.5 2.6 %collective-permute-start.8 = (bf16[128,128]{1,0:T(8,128)(2,1)S(1)}, bf16[128,128]{1,0:T(8,128)(2,1)S(1)}, u32[]{:S(2)}, u32[]{:S(2)}) collective-permute-start(bf16[128,128]{1,0:T(8,128)(2,1)S(1)} %get-tuple-element.18), channel_id=1, source_target_pairs={{0,2},{2,4},{4,6},{1,3},{3,5},{5,7},{8,10},{10,12},{12,14},{9,11},... | collective-permute-start | bytes 98312 | tf_op jit(solution)/shard_map/ppermute | solution.py:103
  60.1 1.3 %collective-permute-start.9 = (bf16[128,128]{1,0:T(8,128)(2,1)S(1)}, bf16[128,128]{1,0:T(8,128)(2,1)S(1)}, u32[]{:S(2)}, u32[]{:S(2)}) collective-permute-start(bf16[128,128]{1,0:T(8,128)(2,1)S(1)} %get-tuple-element.17), channel_id=1, source_target_pairs={{2,0},{4,2},{6,4},{3,1},{5,3},{7,5},{10,8},{12,10},{14,12},{11,9},... | collective-permute-start | bytes 98312 | tf_op jit(solution)/shard_map/ppermute | solution.py:103
  61.4 1.7 %collective-permute-start.10 = (bf16[128,128]{1,0:T(8,128)(2,1)S(1)}, bf16[128,128]{1,0:T(8,128)(2,1)S(1)}, u32[]{:S(2)}, u32[]{:S(2)}) collective-permute-start(bf16[128,128]{1,0:T(8,128)(2,1)S(1)} %get-tuple-element.16), channel_id=1, source_target_pairs={{0,1},{2,3},{4,5},{6,7},{8,9},{10,11},{12,13},{14,15},{16,17},{18,... | collective-permute-start | bytes 98312 | tf_op jit(solution)/shard_map/ppermute | solution.py:103
  63.1 1.5 %collective-permute-start.11 = (bf16[128,128]{1,0:T(8,128)(2,1)S(1)}, bf16[128,128]{1,0:T(8,128)(2,1)S(1)}, u32[]{:S(2)}, u32[]{:S(2)}) collective-permute-start(bf16[128,128]{1,0:T(8,128)(2,1)S(1)} %get-tuple-element.15), channel_id=1, source_target_pairs={{1,0},{3,2},{5,4},{7,6},{9,8},{11,10},{13,12},{15,14},{17,16},{19,... | collective-permute-start | bytes 98312 | tf_op jit(solution)/shard_map/ppermute | solution.py:103
  64.6 2.5 %collective-permute-start.15 = (f32[4,2,1,40,128]{4,3,2,1,0:T(8,128)S(1)}, f32[4,2,1,40,128]{4,3,2,1,0:T(8,128)S(1)}, u32[]{:S(2)}, u32[]{:S(2)}) collective-permute-start(f32[4,2,1,40,128]{4,3,2,1,0:T(8,128)S(1)} %maximum_select_fusion.3), channel_id=1, source_target_pairs={{0,4},{2,6},{4,0},{6,2},{1,5},{3,7},{5,1},{7,3},{8,12},{10,14},{12... | collective-permute-start | bytes 491528 | tf_op jit(solution)/shard_map/ppermute | solution.py:114
  67.1 4.7 %collective-permute-done.15 = f32[4,2,1,40,128]{4,3,2,1,0:T(8,128)S(1)} collective-permute-done((f32[4,2,1,40,128]{4,3,2,1,0:T(8,128)S(1)}, f32[4,2,1,40,128]{4,3,2,1,0:T(8,128)S(1)}, u32[]{:S(2)}, u32[]{:S(2)}) %collective-permute-start.15) | collective-permute-done | bytes 163872 | tf_op jit(solution)/shard_map/ppermute | solution.py:114
  72.1 1.4 %collective-permute-done.16 = f32[4,4,1,40,128]{4,3,2,1,0:T(8,128)S(1)} collective-permute-done((f32[4,4,1,40,128]{4,3,2,1,0:T(8,128)S(1)}, f32[4,4,1,40,128]{4,3,2,1,0:T(8,128)S(1)}, u32[]{:S(2)}, u32[]{:S(2)}) %collective-permute-start.16) | collective-permute-done | bytes 327712 | tf_op jit(solution)/shard_map/ppermute | solution.py:114
  74.8 2.0 %fusion.2 = f32[128,4352]{1,0:T(8,128)S(1)} fusion(f32[128,40]{1,0:T(8,128)S(1)} %fusion.15, f32[40,4352]{1,0:T(8,128)S(1)} %copy-done.3, f32[40]{0:T(128)S(1)} %compare_convert_fusion), kind=kOutput, calls=%fused_computation.6 | convolution fusion | flops 267560960 | bytes 2945184 | tf_op jit(solution)/shard_map/dot_general | solution.py:167
  76.8 4.6 %add_add_fusion = f32[128,4352]{1,0:T(8,128)} fusion(f32[128,4352]{1,0:T(8,128)S(1)} %fusion.2, bf16[128,4352]{1,0:T(8,128)(2,1)S(1)} %get-tuple-element.7, bf16[128,768]{1,0:T(8,128)(2,1)S(1)} %constant_dynamic-update-slice_fusion.6, s32[768]{0:T(1024)S(1)} %bitcast.61), kind=kOutput, calls=%fused_computation.4 | convolution fusion | flops 860651520 | bytes 5770240 | tf_op jit(solution)/shard_map/dot_general | solution.py:166
  (55 shorter events, 3.3 us)
Async XLA Ops:
  0.0 73.6 %copy-start = (f32[40,1280]{1,0:T(8,128)S(1)}, f32[40,1280]{1,0:T(8,128)}, u32[]{:S(2)}) copy-start(f32[40,1280]{1,0:T(8,128)} %param.15) | copy-start | bytes 614404
  0.0 8.1 %copy-start.1 = (f32[128,4352]{1,0:T(8,128)S(1)}, f32[128,4352]{1,0:T(8,128)}, u32[]{:S(2)}) copy-start(f32[128,4352]{1,0:T(8,128)} %res_ref.1) | copy-start | bytes 6684676
  5.0 5.0 %copy-start.4 = (s32[6,128]{1,0:T(8,128)S(1)}, s32[6,128]{1,0:T(8,128)}, u32[]{:S(2)}) copy-start(s32[6,128]{1,0:T(8,128)} %param.12) | copy-start | bytes 9220
  5.0 20.3 %collective-permute-start.12 = (f32[1,1,1,40,128]{4,3,2,1,0:T(8,128)S(1)}, f32[1,1,1,40,128]{4,3,2,1,0:T(8,128)S(1)}, u32[]{:S(2)}, u32[]{:S(2)}) collective-permute-start(f32[1,1,1,40,128]{4,3,2,1,0:T(8,128)S(1)} %bitcast.57), channel_id=1, source_target_pairs={{0,8},{8,0},{16,24},{24,16},{1,9},{9,1},{17,25},{25,17},{2,10},{10... | collective-permute-start | bytes 61448 | tf_op jit(solution)/shard_map/ppermute | solution.py:114
  13.3 24.0 %copy-start.2 = (s32[20]{0:T(128)S(1)}, s32[20]{0:T(128)}, u32[]{:S(2)}) copy-start(s32[20]{0:T(128)} %parent_ref.1) | copy-start | bytes 244
  13.5 18.1 %collective-permute-start = (f32[128,128]{1,0:T(8,128)S(1)}, f32[128,128]{1,0:T(8,128)S(1)}, u32[]{:S(2)}, u32[]{:S(2)}) collective-permute-start(f32[128,128]{1,0:T(8,128)S(1)} %get-tuple-element.14), channel_id=1, source_target_pairs={{8,0},{16,8},{24,16},{9,1},{17,9},{25,17},{10,2},{18,10},{26,18},{... | collective-permute-start | bytes 196616 | tf_op jit(solution)/shard_map/ppermute | solution.py:103
  14.8 19.9 %collective-permute-start.1 = (f32[128,128]{1,0:T(8,128)S(1)}, f32[128,128]{1,0:T(8,128)S(1)}, u32[]{:S(2)}, u32[]{:S(2)}) collective-permute-start(f32[128,128]{1,0:T(8,128)S(1)} %get-tuple-element.13), channel_id=1, source_target_pairs={{0,8},{8,16},{16,24},{1,9},{9,17},{17,25},{2,10},{10,18},{18,26},{... | collective-permute-start | bytes 196616 | tf_op jit(solution)/shard_map/ppermute | solution.py:103
  19.4 17.8 %collective-permute-start.2 = (f32[128,128]{1,0:T(8,128)S(1)}, f32[128,128]{1,0:T(8,128)S(1)}, u32[]{:S(2)}, u32[]{:S(2)}) collective-permute-start(f32[128,128]{1,0:T(8,128)S(1)} %get-tuple-element.12), channel_id=1, source_target_pairs={{2,0},{4,2},{6,4},{3,1},{5,3},{7,5},{10,8},{12,10},{14,12},{11,9},... | collective-permute-start | bytes 196616 | tf_op jit(solution)/shard_map/ppermute | solution.py:103
  20.7 16.5 %collective-permute-start.3 = (f32[128,128]{1,0:T(8,128)S(1)}, f32[128,128]{1,0:T(8,128)S(1)}, u32[]{:S(2)}, u32[]{:S(2)}) collective-permute-start(f32[128,128]{1,0:T(8,128)S(1)} %get-tuple-element.11), channel_id=1, source_target_pairs={{0,2},{2,4},{4,6},{1,3},{3,5},{5,7},{8,10},{10,12},{12,14},{9,11},... | collective-permute-start | bytes 196616 | tf_op jit(solution)/shard_map/ppermute | solution.py:103
  25.3 5.0 %collective-permute-start.13 = (f32[2,1,1,40,128]{4,3,2,1,0:T(8,128)S(1)}, f32[2,1,1,40,128]{4,3,2,1,0:T(8,128)S(1)}, u32[]{:S(2)}, u32[]{:S(2)}) collective-permute-start(f32[2,1,1,40,128]{4,3,2,1,0:T(8,128)S(1)} %maximum_select_fusion.6), channel_id=1, source_target_pairs={{0,16},{8,24},{16,0},{24,8},{1,17},{9,25},{17,1},{25,9},{2,18},{10... | collective-permute-start | bytes 122888 | tf_op jit(solution)/shard_map/ppermute | solution.py:114
  30.3 6.9 %collective-permute-start.4 = (f32[128,128]{1,0:T(8,128)S(1)}, f32[128,128]{1,0:T(8,128)S(1)}, u32[]{:S(2)}, u32[]{:S(2)}) collective-permute-start(f32[128,128]{1,0:T(8,128)S(1)} %get-tuple-element.10), channel_id=1, source_target_pairs={{1,0},{3,2},{5,4},{7,6},{9,8},{11,10},{13,12},{15,14},{17,16},{19,... | collective-permute-start | bytes 196616 | tf_op jit(solution)/shard_map/ppermute | solution.py:103
  31.6 5.6 %collective-permute-start.5 = (f32[128,128]{1,0:T(8,128)S(1)}, f32[128,128]{1,0:T(8,128)S(1)}, u32[]{:S(2)}, u32[]{:S(2)}) collective-permute-start(f32[128,128]{1,0:T(8,128)S(1)} %get-tuple-element.9), channel_id=1, source_target_pairs={{0,1},{2,3},{4,5},{6,7},{8,9},{10,11},{12,13},{14,15},{16,17},{18,... | collective-permute-start | bytes 196616 | tf_op jit(solution)/shard_map/ppermute | solution.py:103
  34.7 29.9 %collective-permute-start.14 = (f32[4,1,1,40,128]{4,3,2,1,0:T(8,128)S(1)}, f32[4,1,1,40,128]{4,3,2,1,0:T(8,128)S(1)}, u32[]{:S(2)}, u32[]{:S(2)}) collective-permute-start(f32[4,1,1,40,128]{4,3,2,1,0:T(8,128)S(1)} %fusion.9), channel_id=1, source_target_pairs={{0,2},{2,0},{4,6},{6,4},{1,3},{3,1},{5,7},{7,5},{8,10},{10,8},{12,... | collective-permute-start | bytes 245768 | tf_op jit(solution)/shard_map/ppermute | solution.py:114
  53.0 21.8 %copy-start.3 = (f32[40,4352]{1,0:T(8,128)S(1)}, f32[40,4352]{1,0:T(8,128)}, u32[]{:S(2)}) copy-start(f32[40,4352]{1,0:T(8,128)} %param.14) | copy-start | bytes 2088964
  53.0 8.4 %collective-permute-start.6 = (bf16[128,128]{1,0:T(8,128)(2,1)S(1)}, bf16[128,128]{1,0:T(8,128)(2,1)S(1)}, u32[]{:S(2)}, u32[]{:S(2)}) collective-permute-start(bf16[128,128]{1,0:T(8,128)(2,1)S(1)} %get-tuple-element.20), channel_id=1, source_target_pairs={{0,8},{8,16},{16,24},{1,9},{9,17},{17,25},{2,10},{10,18},{18,26},{... | collective-permute-start | bytes 98312 | tf_op jit(solution)/shard_map/ppermute | solution.py:103
  56.2 6.9 %collective-permute-start.7 = (bf16[128,128]{1,0:T(8,128)(2,1)S(1)}, bf16[128,128]{1,0:T(8,128)(2,1)S(1)}, u32[]{:S(2)}, u32[]{:S(2)}) collective-permute-start(bf16[128,128]{1,0:T(8,128)(2,1)S(1)} %get-tuple-element.19), channel_id=1, source_target_pairs={{8,0},{16,8},{24,16},{9,1},{17,9},{25,17},{10,2},{18,10},{26,18},{... | collective-permute-start | bytes 98312 | tf_op jit(solution)/shard_map/ppermute | solution.py:103
  57.5 9.6 %collective-permute-start.8 = (bf16[128,128]{1,0:T(8,128)(2,1)S(1)}, bf16[128,128]{1,0:T(8,128)(2,1)S(1)}, u32[]{:S(2)}, u32[]{:S(2)}) collective-permute-start(bf16[128,128]{1,0:T(8,128)(2,1)S(1)} %get-tuple-element.18), channel_id=1, source_target_pairs={{0,2},{2,4},{4,6},{1,3},{3,5},{5,7},{8,10},{10,12},{12,14},{9,11},... | collective-permute-start | bytes 98312 | tf_op jit(solution)/shard_map/ppermute | solution.py:103
  60.1 12.0 %collective-permute-start.9 = (bf16[128,128]{1,0:T(8,128)(2,1)S(1)}, bf16[128,128]{1,0:T(8,128)(2,1)S(1)}, u32[]{:S(2)}, u32[]{:S(2)}) collective-permute-start(bf16[128,128]{1,0:T(8,128)(2,1)S(1)} %get-tuple-element.17), channel_id=1, source_target_pairs={{2,0},{4,2},{6,4},{3,1},{5,3},{7,5},{10,8},{12,10},{14,12},{11,9},... | collective-permute-start | bytes 98312 | tf_op jit(solution)/shard_map/ppermute | solution.py:103
  61.4 10.7 %collective-permute-start.10 = (bf16[128,128]{1,0:T(8,128)(2,1)S(1)}, bf16[128,128]{1,0:T(8,128)(2,1)S(1)}, u32[]{:S(2)}, u32[]{:S(2)}) collective-permute-start(bf16[128,128]{1,0:T(8,128)(2,1)S(1)} %get-tuple-element.16), channel_id=1, source_target_pairs={{0,1},{2,3},{4,5},{6,7},{8,9},{10,11},{12,13},{14,15},{16,17},{18,... | collective-permute-start | bytes 98312 | tf_op jit(solution)/shard_map/ppermute | solution.py:103
  63.1 9.0 %collective-permute-start.11 = (bf16[128,128]{1,0:T(8,128)(2,1)S(1)}, bf16[128,128]{1,0:T(8,128)(2,1)S(1)}, u32[]{:S(2)}, u32[]{:S(2)}) collective-permute-start(bf16[128,128]{1,0:T(8,128)(2,1)S(1)} %get-tuple-element.15), channel_id=1, source_target_pairs={{1,0},{3,2},{5,4},{7,6},{9,8},{11,10},{13,12},{15,14},{17,16},{19,... | collective-permute-start | bytes 98312 | tf_op jit(solution)/shard_map/ppermute | solution.py:103
  64.6 7.2 %collective-permute-start.15 = (f32[4,2,1,40,128]{4,3,2,1,0:T(8,128)S(1)}, f32[4,2,1,40,128]{4,3,2,1,0:T(8,128)S(1)}, u32[]{:S(2)}, u32[]{:S(2)}) collective-permute-start(f32[4,2,1,40,128]{4,3,2,1,0:T(8,128)S(1)} %maximum_select_fusion.3), channel_id=1, source_target_pairs={{0,4},{2,6},{4,0},{6,2},{1,5},{3,7},{5,1},{7,3},{8,12},{10,14},{12... | collective-permute-start | bytes 491528 | tf_op jit(solution)/shard_map/ppermute | solution.py:114
  71.8 1.7 %collective-permute-start.16 = (f32[4,4,1,40,128]{4,3,2,1,0:T(8,128)S(1)}, f32[4,4,1,40,128]{4,3,2,1,0:T(8,128)S(1)}, u32[]{:S(2)}, u32[]{:S(2)}) collective-permute-start(f32[4,4,1,40,128]{4,3,2,1,0:T(8,128)S(1)} %maximum_select_fusion.1), channel_id=1, source_target_pairs={{0,1},{1,0},{2,3},{3,2},{4,5},{5,4},{6,7},{7,6},{8,9},{9,8},{10,11... | collective-permute-start | bytes 983048 | tf_op jit(solution)/shard_map/ppermute | solution.py:114

commit v7 on v2

--- a/solution.py
+++ b/solution.py
@@ -77,13 +77,66 @@
     )(parent, residual, slots, diag_inverse, coupling)
 
 
-def shift(value, axis, up):
+def matchings(count):
+    first = [(i, i + 1) for i in range(0, count - 1, 2)] + [(i + 1, i) for i in range(0, count - 1, 2)]
+    second = [(i, i + 1) for i in range(1, count - 1, 2)] + [(i + 1, i) for i in range(1, count - 1, 2)]
+    return first, second
+
+
+def swap(value, axis, pairs, extra=None):
+    if not pairs:
+        return jnp.zeros_like(value), None
+    if extra is None:
+        return lax.ppermute(value, axis, pairs), None
+    rows = value.shape[0]
+    packed = jnp.concatenate([value.astype(extra.dtype), extra], axis=0)
+    got = lax.ppermute(packed, axis, pairs)
+    return got[:rows].astype(value.dtype), got[rows:]
+
+
+def halo_out(down, up, axis, extra=None):
+    even = lax.axis_index(axis) % 2 == 0
+    first, second = matchings(lax.axis_size(axis))
+    r1, got = swap(jnp.where(even, up, down), axis, first, extra)
+    r2, _ = swap(jnp.where(even, down, up), axis, second)
+    return jnp.where(even, r1, r2), jnp.where(even, r2, r1), got
+
+
+def halo_back(lo, hi, axis, extra=None):
+    even = lax.axis_index(axis) % 2 == 0
+    first, second = matchings(lax.axis_size(axis))
+    r1, got = swap(jnp.where(even, lo, hi), axis, first, extra)
+    r2, _ = swap(jnp.where(even, hi, lo), axis, second)
+    return jnp.where(even, r2, r1), jnp.where(even, r1, r2), got
+
+
+def doubling(axis):
     count = lax.axis_size(axis)
-    if up:
-        pairs = [(i, i + 1) for i in range(count - 1)]
-    else:
-        pairs = [(i + 1, i) for i in range(count - 1)]
-    return lax.ppermute(value, axis, pairs)
+    return count > 1 and not count & (count - 1)
+
+
+def merge(held, other, axis, dim, step):
+    low = (lax.axis_index(axis) // step) % 2 == 0
+    return jnp.where(
+        low,
+        jnp.concatenate([held, other], axis=dim),
+        jnp.concatenate([other, held], axis=dim),
+    )
+
+
+def gather_axis(held, axis, dim, step=1):
+    count = lax.axis_size(axis)
+    if not doubling(axis):
+        return lax.all_gather(held, axis, axis=dim, tiled=True)
+    while step < count:
+        pairs = [(i, i ^ step) for i in range(count)]
+        held = merge(held, lax.ppermute(held, axis, pairs), axis, dim, step)
+        step *= 2
+    return held
+
+
+def rows_of(held):
+    return held.reshape(-1, held.shape[-1])
 
 
 def per_device(
@@ -97,30 +150,51 @@
     coeffs_t = lax.dot_general(
         vectors, residual, NT, precision=lax.Precision.HIGHEST, preferred_element_type=jnp.float32
     )
-    me = lax.axis_index(AXES)
-    placed = jnp.zeros((coarse_inverse.shape[1], coeffs_t.shape[1]), jnp.float32)
-    placed = lax.dynamic_update_slice_in_dim(placed, coeffs_t, me * kmax_here, axis=0)
-    gathered = lax.psum(placed, AXES)
-    solved_t = jnp.dot(
-        coarse_inverse, gathered, precision=lax.Precision.HIGHEST, preferred_element_type=jnp.float32
-    )
+    held = coeffs_t.reshape((1,) * len(AXES) + coeffs_t.shape)
 
     outgoing = jnp.take(residual, send_rows, axis=1)
     incoming = []
     for axis_pos, axis in enumerate(AXES):
-        incoming.append(shift(outgoing[:, 2 * axis_pos], axis, up=False))
-        incoming.append(shift(outgoing[:, 2 * axis_pos + 1], axis, up=True))
+        ride = axis_pos == 0 and doubling(axis)
+        low, high, got = halo_out(
+            outgoing[:, 2 * axis_pos],
+            outgoing[:, 2 * axis_pos + 1],
+            axis,
+            rows_of(held) if ride else None,
+        )
+        incoming += [low, high]
+        if axis_pos == 0:
+            if ride:
+                held = gather_axis(merge(held, got.reshape(held.shape), axis, 0, 1), axis, 0, 2)
+            else:
+                held = gather_axis(held, axis, 0)
+    for axis_pos in range(1, len(AXES) - 1):
+        held = gather_axis(held, AXES[axis_pos], axis_pos)
+    last = len(AXES) - 1
+    late = lax.axis_size(AXES[last]) == 2
+    if not late:
+        held = gather_axis(held, AXES[last], last)
     slots = jnp.concatenate(incoming, axis=1)
 
     own, zslots = local_solve(parent, residual, slots, diag_inverse, coupling)
 
     returned = []
     for axis_pos, axis in enumerate(AXES):
-        lo = zslots[:, (2 * axis_pos) * face_w : (2 * axis_pos + 1) * face_w]
-        hi = zslots[:, (2 * axis_pos + 1) * face_w : (2 * axis_pos + 2) * face_w]
-        returned.append(shift(lo, axis, up=True))
-        returned.append(shift(hi, axis, up=False))
+        ride = axis_pos == last and late
+        low, high, got = halo_back(
+            zslots[:, (2 * axis_pos) * face_w : (2 * axis_pos + 1) * face_w],
+            zslots[:, (2 * axis_pos + 1) * face_w : (2 * axis_pos + 2) * face_w],
+            axis,
+            rows_of(held) if ride else None,
+        )
+        returned += [low, high]
+        if ride:
+            held = merge(held, got.reshape(held.shape), axis, last, 1)
     returned = jnp.concatenate(returned, axis=1)
+
+    solved_t = jnp.dot(
+        coarse_inverse, rows_of(held), precision=lax.Precision.HIGHEST, preferred_element_type=jnp.float32
+    )
     onehot = (
         send_rows.reshape(slots_n * face_w, 1) == lax.iota(jnp.int32, owned_n)[None, :]
     ).astype(jnp.bfloat16)

time: 197 us -> 70.5 us (0.36)
  waiting for transfers between devices: 117 us -> 9.9 us
  between operations: 14.4 us -> 1.09 us
  starting transfers between devices: 31.9 us -> 25.3 us
    psum x1 -> x0, waiting for transfers between devices: 115 us -> none  [per_device(): gathered = lax.psum(placed, AXES)]
    ppermute x12 -> x13, waiting for transfers between devices: 1.76 us -> 9.9 us  [the longest x3 7.24 us: gather_axis(): held = merge(held, lax.ppermute(held, axis, pairs), axis, dim, step)]
    ppermute x12 -> x13, starting transfers between devices: 31.9 us -> 25.3 us  [the longest x8 15.7 us: swap(): return (lax.ppermute(value, axis, pairs), None)]
    gather x2, local copies, waits for them, and re-layouts: 1.74 us -> 4.26 us  [per_device(): outgoing = jnp.take(residual, send_rows, axis=1)]
  transfers between devices with their start and end apart: 13 -> 13, of which waited for: 4 -> 4; matrix products, arithmetic and copies ran while one was open for 2% -> 0% of each run, Pallas kernels for 0% -> 19%
where the time goes in v7:
time: 70.5 us; the launch traced here: 70.3 us
  starting transfers between devices  25.3 us (36%)
  Pallas kernels  13.2 us (19%)
  matrix products  10.2 us (14%)
  waiting for transfers between devices  9.9 us (14%)
  local copies, waits for them, and re-layouts  7.37 us (10%)
  other arithmetic  3.23 us (5%)
  between operations  1.09 us (2%)
    ppermute x8, starting transfers between devices, swap(): return (lax.ppermute(value, axis, pairs), None)  15.7 us
    pallas_call x1, Pallas kernels, local_solve(): pl.pallas_call(solve_kernel, out_shape=(jax.ShapeDtypeStruct((nrhs_here,...  13.2 us
    ppermute x3, waiting for transfers between devices, gather_axis(): held = merge(held, lax.ppermute(held, axis, pairs), axis, dim, step)  7.24 us
    ppermute x3, starting transfers between devices, gather_axis(): held = merge(held, lax.ppermute(held, axis, pairs), axis, dim, step)  6.51 us
    gather x2, local copies, waits for them, and re-layouts, per_device(): outgoing = jnp.take(residual, send_rows, axis=1)  4.26 us
    dot_general x1, matrix products, per_device(): lax.dot_general(solved_t, vectors, (((0,), (0,)), ((), ())), precision=la...  3.6 us
    ppermute x2, starting transfers between devices, swap(): got = lax.ppermute(packed, axis, pairs)  3.1 us
    dot_general x1, matrix products, per_device(): faces = jnp.dot(returned, onehot, preferred_element_type=jnp.float32)  3.02 us
  transfers between devices with their start and end apart: 13, of which 4 were waited for; matrix products, arithmetic and copies ran while one was open for 0% of the time, Pallas kernels for 19%

profile of v7, /device:TPU:0, one launch (start us, length us, event | category | flops | bytes accessed | tf_op | source)
XLA Modules:
  0.0 70.3 jit_solution(12877323479016893322)
XLA Ops:
  0.0 0.7 %compare_and_fusion = pred[6,128]{1,0:T(8,128)(4,1)S(1)} fusion(s32[6,128]{1,0:T(8,128)} %param.12), kind=kLoop, calls=%fused_computation.59 | loop fusion | flops 4608 | bytes 3840 | tf_op jit(solution)/shard_map/jit(_take)/and | solution.py:155
  0.7 0.7 fusion.15
  2.1 3.0 %copy.18 = f32[128,4352]{0,1:T(8,128)} copy(f32[128,4352]{1,0:T(8,128)} %res_ref.1) | data formatting | bytes 4456448 | tf_op args[0]
  5.1 3.3 %gather_fusion = f32[768,128]{1,0:T(8,128)S(1)} fusion(f32[128,4352]{0,1:T(8,128)} %copy.18, s32[1024]{0:T(1024)S(1)} %pad_clamp_fusion), kind=kCustom, calls=%fused_computation | custom fusion | bytes 789504 | tf_op jit(solution)/shard_map/jit(_take)/gather | solution.py:155
  8.4 0.9 %copy.19 = f32[6,128,128]{1,2,0:T(8,128)} copy(f32[6,128,128]{2,1,0:T(8,128)S(1)} %bitcast.52) | data formatting | bytes 786432 | tf_op jit(solution)/shard_map/jit(_take)/gather | solution.py:155
  9.4 2.4 %fusion.3 = f32[40,128]{1,0:T(8,128)S(1)} fusion(f32[128,4352]{1,0:T(8,128)S(1)} %copy-done.1, f32[40,4352]{1,0:T(8,128)S(1)} %copy-done.3, f32[40]{0:T(128)S(1)} %compare_convert_fusion), kind=kOutput, calls=%fused_computation.7 | convolution fusion | flops 267560960 | bytes 2945184 | tf_op jit(solution)/shard_map/dot_general | solution.py:150
  11.8 0.7 %fusion.11 = (f32[128,128]{1,0:T(8,128)}, f32[128,128]{1,0:T(8,128)}, f32[128,128]{1,0:T(8,128)}, f32[128,128]{1,0:T(8,128)S(1)}, f32[128,128]{1,0:T(8,128)}) fusion(f32[128,6,128]{2,0,1:T(8,128)S(1)} %select_bitcast_fusion, pred[]{:T(512)S(6)} %eq.50, pred[]{:T(512)S(6)} %eq.49, pred[]{:T(512)S(6)} %eq.48), kind=kLoop, calls=%fused_computation.28 | loop fusion | flops 81920 | bytes 720899 | tf_op jit(solution)/shard_map/jit(_where)/select_n | solution.py:100
  13.2 3.0 %collective-permute-start = (f32[168,128]{1,0:T(8,128)}, f32[168,128]{1,0:T(8,128)S(1)}, u32[]{:S(2)}, u32[]{:S(2)}) collective-permute-start(f32[168,128]{1,0:T(8,128)} %pad_maximum_fusion.5), channel_id=1, source_target_pairs={{0,8},{16,24},{8,0},{24,16},{1,9},{17,25},{9,1},{25,17},{2,10},{18... | collective-permute-start | bytes 258056 | tf_op jit(solution)/shard_map/ppermute | solution.py:93
  16.2 1.5 %collective-permute-start.2 = (f32[128,128]{1,0:T(8,128)}, f32[128,128]{1,0:T(8,128)S(1)}, u32[]{:S(2)}, u32[]{:S(2)}) collective-permute-start(f32[128,128]{1,0:T(8,128)} %get-tuple-element.10), channel_id=1, source_target_pairs={{0,2},{4,6},{2,0},{6,4},{1,3},{5,7},{3,1},{7,5},{8,10},{12,14},{10... | collective-permute-start | bytes 196616 | tf_op jit(solution)/shard_map/ppermute | solution.py:90
  18.3 0.7 collective-permute-start.1
  19.1 3.9 %collective-permute-start.9 = (f32[2,1,1,40,128]{4,3,2,1,0:T(8,128)S(1)}, f32[2,1,1,40,128]{4,3,2,1,0:T(8,128)S(1)}, u32[]{:S(2)}, u32[]{:S(2)}) collective-permute-start(f32[2,1,1,40,128]{4,3,2,1,0:T(8,128)S(1)} %maximum_select_fusion.5), channel_id=1, source_target_pairs={{0,16},{8,24},{16,0},{24,8},{1,17},{9,25},{17,1},{25,9},{2,18},{10... | collective-permute-start | bytes 122888 | tf_op jit(solution)/shard_map/ppermute | solution.py:133
  23.2 13.2 %shard_map.82 = (bf16[128,4352]{1,0:T(8,128)(2,1)S(1)}, bf16[128,768]{1,0:T(8,128)(2,1)S(1)}) custom-call(s32[20]{0:T(128)S(1)} %copy-done.2, f32[128,4352]{1,0:T(8,128)S(1)} %copy-done.1, f32[128,768]{1,0:T(8,128)S(1)} %select_dynamic-update-slice_fusion.slot_ref, bf16[20,256,256]{2,1,0:T(8,128)(2,1)} %inv_ref.1, bf16[19,256,256]{2,1,0:T(8,128)(2,1)} %cpl_ref.1), custom_call_target="tpu_custom_call" | custom-call | tf_op jit(solution)/shard_map/pallas_call | solution.py:58
  36.4 4.3 %collective-permute-start.8 = (bf16[128,128]{1,0:T(8,128)(2,1)S(1)}, bf16[128,128]{1,0:T(8,128)(2,1)S(1)}, u32[]{:S(2)}, u32[]{:S(2)}) collective-permute-start(bf16[128,128]{1,0:T(8,128)(2,1)S(1)} %get-tuple-element.14), channel_id=1, source_target_pairs={{0,2},{4,6},{2,0},{6,4},{1,3},{5,7},{3,1},{7,5},{8,10},{12,14},{10... | collective-permute-start | bytes 98312 | tf_op jit(solution)/shard_map/ppermute | solution.py:90
  41.3 7.1 %collective-permute-start.6 = (bf16[128,128]{1,0:T(8,128)(2,1)S(1)}, bf16[128,128]{1,0:T(8,128)(2,1)S(1)}, u32[]{:S(2)}, u32[]{:S(2)}) collective-permute-start(bf16[128,128]{1,0:T(8,128)(2,1)S(1)} %get-tuple-element.17), channel_id=1, source_target_pairs={{0,8},{16,24},{8,0},{24,16},{1,9},{17,25},{9,1},{25,17},{2,10},{18... | collective-permute-start | bytes 98312 | tf_op jit(solution)/shard_map/ppermute | solution.py:90
  48.5 0.8 %collective-permute-start.7 = (bf16[128,128]{1,0:T(8,128)(2,1)S(1)}, bf16[128,128]{1,0:T(8,128)(2,1)S(1)}, u32[]{:S(2)}, u32[]{:S(2)}) collective-permute-start(bf16[128,128]{1,0:T(8,128)(2,1)S(1)} %get-tuple-element.18), channel_id=1, source_target_pairs={{2,4},{4,2},{3,5},{5,3},{10,12},{12,10},{11,13},{13,11},{18,20},{2... | collective-permute-start | bytes 98312 | tf_op jit(solution)/shard_map/ppermute | solution.py:90
  49.3 1.0 %collective-permute-done.6 = bf16[128,128]{1,0:T(8,128)(2,1)S(1)} collective-permute-done((bf16[128,128]{1,0:T(8,128)(2,1)S(1)}, bf16[128,128]{1,0:T(8,128)(2,1)S(1)}, u32[]{:S(2)}, u32[]{:S(2)}) %collective-permute-start.6) | collective-permute-done | bytes 32800 | tf_op jit(solution)/shard_map/ppermute | solution.py:90
  50.4 0.8 %collective-permute-start.10 = (f32[4,1,1,40,128]{4,3,2,1,0:T(8,128)S(1)}, f32[4,1,1,40,128]{4,3,2,1,0:T(8,128)S(1)}, u32[]{:S(2)}, u32[]{:S(2)}) collective-permute-start(f32[4,1,1,40,128]{4,3,2,1,0:T(8,128)S(1)} %fusion.10), channel_id=1, source_target_pairs={{0,2},{2,0},{4,6},{6,4},{1,3},{3,1},{5,7},{7,5},{8,10},{10,8},{12,... | collective-permute-start | bytes 245768 | tf_op jit(solution)/shard_map/ppermute | solution.py:133
  51.2 3.7 %collective-permute-done.10 = f32[4,1,1,40,128]{4,3,2,1,0:T(8,128)S(1)} collective-permute-done((f32[4,1,1,40,128]{4,3,2,1,0:T(8,128)S(1)}, f32[4,1,1,40,128]{4,3,2,1,0:T(8,128)S(1)}, u32[]{:S(2)}, u32[]{:S(2)}) %collective-permute-start.10) | collective-permute-done | bytes 81952 | tf_op jit(solution)/shard_map/ppermute | solution.py:133
  54.9 1.8 %collective-permute-start.11 = (f32[4,2,1,40,128]{4,3,0,1,2:T(8,128)S(1)}, f32[4,2,1,40,128]{4,3,0,1,2:T(8,128)S(1)}, u32[]{:S(2)}, u32[]{:S(2)}) collective-permute-start(f32[4,2,1,40,128]{4,3,0,1,2:T(8,128)S(1)} %maximum_select_fusion.1), channel_id=1, source_target_pairs={{0,4},{2,6},{4,0},{6,2},{1,5},{3,7},{5,1},{7,3},{8,12},{10,14},{12... | collective-permute-start | bytes 491528 | tf_op jit(solution)/shard_map/ppermute | solution.py:133
  56.8 3.5 %collective-permute-done.11 = f32[4,2,1,40,128]{4,3,0,1,2:T(8,128)S(1)} collective-permute-done((f32[4,2,1,40,128]{4,3,0,1,2:T(8,128)S(1)}, f32[4,2,1,40,128]{4,3,0,1,2:T(8,128)S(1)}, u32[]{:S(2)}, u32[]{:S(2)}) %collective-permute-start.11) | collective-permute-done | bytes 163872 | tf_op jit(solution)/shard_map/ppermute | solution.py:133
  60.6 1.6 %collective-permute-done.12 = f32[768,128]{1,0:T(8,128)S(1)} collective-permute-done((f32[768,128]{1,0:T(8,128)S(1)}, f32[768,128]{1,0:T(8,128)S(1)}, u32[]{:S(2)}, u32[]{:S(2)}) %collective-permute-start.12) | collective-permute-done | bytes 393248 | tf_op jit(solution)/shard_map/ppermute | solution.py:93
  62.4 1.2 %fusion.16 = f32[128,40]{1,0:T(8,128)S(1)} fusion(f32[1280,128]{1,0:T(8,128)S(1)} %bitcast.51, f32[40,1280]{1,0:T(8,128)S(1)} %copy-done), kind=kOutput, calls=%fused_computation.62 | convolution fusion | flops 78643200 | bytes 880640 | tf_op jit(solution)/shard_map/dot_general | solution.py:195
  63.6 3.0 %fusion = f32[128,4352]{1,0:T(8,128)S(1)} fusion(bf16[128,768]{1,0:T(8,128)(2,1)S(1)} %select_dynamic-update-slice_fusion.6, s32[768]{0:T(1024)S(1)} %bitcast.62), kind=kOutput, calls=%fused_computation.2 | convolution fusion | flops 858980352 | bytes 2427904 | tf_op jit(solution)/shard_map/dot_general | solution.py:201
  66.7 3.6 %convolution_add_fusion = f32[128,4352]{1,0:T(8,128)} fusion(f32[128,40]{1,0:T(8,128)S(1)} %fusion.16, f32[128,4352]{1,0:T(8,128)S(1)} %fusion, bf16[128,4352]{1,0:T(8,128)(2,1)S(1)} %get-tuple-element.7, f32[40,4352]{1,0:T(8,128)S(1)} %copy-done.3, f32[40]{0:T(128)S(1)} %compare_convert_fusion), kind=kOutput, calls=%fused_computation.4 | convolution fusion | flops 269232128 | bytes 6287520 | tf_op jit(solution)/shard_map/dot_general | solution.py:202
  (55 shorter events, 2.6 us)
Async XLA Ops:
  0.0 62.4 %copy-start = (f32[40,1280]{1,0:T(8,128)S(1)}, f32[40,1280]{1,0:T(8,128)}, u32[]{:S(2)}) copy-start(f32[40,1280]{1,0:T(8,128)} %param.15) | copy-start | bytes 614404
  5.1 4.3 %copy-start.1 = (f32[128,4352]{1,0:T(8,128)S(1)}, f32[128,4352]{1,0:T(8,128)}, u32[]{:S(2)}) copy-start(f32[128,4352]{1,0:T(8,128)} %res_ref.1) | copy-start | bytes 6684676
  5.1 4.3 %copy-start.3 = (f32[40,4352]{1,0:T(8,128)S(1)}, f32[40,4352]{1,0:T(8,128)}, u32[]{:S(2)}) copy-start(f32[40,4352]{1,0:T(8,128)} %param.14) | copy-start | bytes 2088964
  9.4 2.4 %copy-start.4 = (f32[6,128,128]{1,2,0:T(8,128)S(1)}, f32[6,128,128]{1,2,0:T(8,128)}, u32[]{:S(2)}) copy-start(f32[6,128,128]{1,2,0:T(8,128)} %copy.19) | copy-start | bytes 1179652
  9.4 13.8 %copy-start.2 = (s32[20]{0:T(128)S(1)}, s32[20]{0:T(128)}, u32[]{:S(2)}) copy-start(s32[20]{0:T(128)} %parent_ref.1) | copy-start | bytes 244
  13.2 5.9 %collective-permute-start = (f32[168,128]{1,0:T(8,128)}, f32[168,128]{1,0:T(8,128)S(1)}, u32[]{:S(2)}, u32[]{:S(2)}) collective-permute-start(f32[168,128]{1,0:T(8,128)} %pad_maximum_fusion.5), channel_id=1, source_target_pairs={{0,8},{16,24},{8,0},{24,16},{1,9},{17,25},{9,1},{25,17},{2,10},{18... | collective-permute-start | bytes 258056 | tf_op jit(solution)/shard_map/ppermute | solution.py:93
  16.2 6.9 %collective-permute-start.4 = (f32[128,128]{1,0:T(8,128)}, f32[128,128]{1,0:T(8,128)S(1)}, u32[]{:S(2)}, u32[]{:S(2)}) collective-permute-start(f32[128,128]{1,0:T(8,128)} %get-tuple-element.9), channel_id=1, source_target_pairs={{0,1},{1,0},{2,3},{3,2},{4,5},{5,4},{6,7},{7,6},{8,9},{9,8},{10,11... | collective-permute-start | bytes 196616 | tf_op jit(solution)/shard_map/ppermute | solution.py:90
  16.2 6.9 %collective-permute-start.2 = (f32[128,128]{1,0:T(8,128)}, f32[128,128]{1,0:T(8,128)S(1)}, u32[]{:S(2)}, u32[]{:S(2)}) collective-permute-start(f32[128,128]{1,0:T(8,128)} %get-tuple-element.10), channel_id=1, source_target_pairs={{0,2},{4,6},{2,0},{6,4},{1,3},{5,7},{3,1},{7,5},{8,10},{12,14},{10... | collective-permute-start | bytes 196616 | tf_op jit(solution)/shard_map/ppermute | solution.py:90
  17.7 5.4 %collective-permute-start.3 = (f32[128,128]{1,0:T(8,128)}, f32[128,128]{1,0:T(8,128)S(1)}, u32[]{:S(2)}, u32[]{:S(2)}) collective-permute-start(f32[128,128]{1,0:T(8,128)} %get-tuple-element.11), channel_id=1, source_target_pairs={{2,4},{4,2},{3,5},{5,3},{10,12},{12,10},{11,13},{13,11},{18,20},{2... | collective-permute-start | bytes 196616 | tf_op jit(solution)/shard_map/ppermute | solution.py:90
  18.3 4.7 %collective-permute-start.1 = (f32[128,128]{1,0:T(8,128)}, f32[128,128]{1,0:T(8,128)S(1)}, u32[]{:S(2)}, u32[]{:S(2)}) collective-permute-start(f32[128,128]{1,0:T(8,128)} %get-tuple-element.13), channel_id=1, source_target_pairs={{8,16},{16,8},{9,17},{17,9},{10,18},{18,10},{11,19},{19,11},{12,20... | collective-permute-start | bytes 196616 | tf_op jit(solution)/shard_map/ppermute | solution.py:90
  19.1 31.3 %collective-permute-start.9 = (f32[2,1,1,40,128]{4,3,2,1,0:T(8,128)S(1)}, f32[2,1,1,40,128]{4,3,2,1,0:T(8,128)S(1)}, u32[]{:S(2)}, u32[]{:S(2)}) collective-permute-start(f32[2,1,1,40,128]{4,3,2,1,0:T(8,128)S(1)} %maximum_select_fusion.5), channel_id=1, source_target_pairs={{0,16},{8,24},{16,0},{24,8},{1,17},{9,25},{17,1},{25,9},{2,18},{10... | collective-permute-start | bytes 122888 | tf_op jit(solution)/shard_map/ppermute | solution.py:133
  36.4 24.1 %collective-permute-start.8 = (bf16[128,128]{1,0:T(8,128)(2,1)S(1)}, bf16[128,128]{1,0:T(8,128)(2,1)S(1)}, u32[]{:S(2)}, u32[]{:S(2)}) collective-permute-start(bf16[128,128]{1,0:T(8,128)(2,1)S(1)} %get-tuple-element.14), channel_id=1, source_target_pairs={{0,2},{4,6},{2,0},{6,4},{1,3},{5,7},{3,1},{7,5},{8,10},{12,14},{10... | collective-permute-start | bytes 98312 | tf_op jit(solution)/shard_map/ppermute | solution.py:90
  40.7 8.7 %collective-permute-start.5 = (bf16[128,128]{1,0:T(8,128)(2,1)S(1)}, bf16[128,128]{1,0:T(8,128)(2,1)S(1)}, u32[]{:S(2)}, u32[]{:S(2)}) collective-permute-start(bf16[128,128]{1,0:T(8,128)(2,1)S(1)} %get-tuple-element.16), channel_id=1, source_target_pairs={{8,16},{16,8},{9,17},{17,9},{10,18},{18,10},{11,19},{19,11},{12,20... | collective-permute-start | bytes 98312 | tf_op jit(solution)/shard_map/ppermute | solution.py:90
  41.3 9.0 %collective-permute-start.6 = (bf16[128,128]{1,0:T(8,128)(2,1)S(1)}, bf16[128,128]{1,0:T(8,128)(2,1)S(1)}, u32[]{:S(2)}, u32[]{:S(2)}) collective-permute-start(bf16[128,128]{1,0:T(8,128)(2,1)S(1)} %get-tuple-element.17), channel_id=1, source_target_pairs={{0,8},{16,24},{8,0},{24,16},{1,9},{17,25},{9,1},{25,17},{2,10},{18... | collective-permute-start | bytes 98312 | tf_op jit(solution)/shard_map/ppermute | solution.py:90
  48.5 12.1 %collective-permute-start.7 = (bf16[128,128]{1,0:T(8,128)(2,1)S(1)}, bf16[128,128]{1,0:T(8,128)(2,1)S(1)}, u32[]{:S(2)}, u32[]{:S(2)}) collective-permute-start(bf16[128,128]{1,0:T(8,128)(2,1)S(1)} %get-tuple-element.18), channel_id=1, source_target_pairs={{2,4},{4,2},{3,5},{5,3},{10,12},{12,10},{11,13},{13,11},{18,20},{2... | collective-permute-start | bytes 98312 | tf_op jit(solution)/shard_map/ppermute | solution.py:90
  50.4 4.5 %collective-permute-start.10 = (f32[4,1,1,40,128]{4,3,2,1,0:T(8,128)S(1)}, f32[4,1,1,40,128]{4,3,2,1,0:T(8,128)S(1)}, u32[]{:S(2)}, u32[]{:S(2)}) collective-permute-start(f32[4,1,1,40,128]{4,3,2,1,0:T(8,128)S(1)} %fusion.10), channel_id=1, source_target_pairs={{0,2},{2,0},{4,6},{6,4},{1,3},{3,1},{5,7},{7,5},{8,10},{10,8},{12,... | collective-permute-start | bytes 245768 | tf_op jit(solution)/shard_map/ppermute | solution.py:133
  54.9 5.4 %collective-permute-start.11 = (f32[4,2,1,40,128]{4,3,0,1,2:T(8,128)S(1)}, f32[4,2,1,40,128]{4,3,0,1,2:T(8,128)S(1)}, u32[]{:S(2)}, u32[]{:S(2)}) collective-permute-start(f32[4,2,1,40,128]{4,3,0,1,2:T(8,128)S(1)} %maximum_select_fusion.1), channel_id=1, source_target_pairs={{0,4},{2,6},{4,0},{6,2},{1,5},{3,7},{5,1},{7,3},{8,12},{10,14},{12... | collective-permute-start | bytes 491528 | tf_op jit(solution)/shard_map/ppermute | solution.py:133
  60.4 1.8 %collective-permute-start.12 = (f32[768,128]{1,0:T(8,128)S(1)}, f32[768,128]{1,0:T(8,128)S(1)}, u32[]{:S(2)}, u32[]{:S(2)}) collective-permute-start(f32[768,128]{1,0:T(8,128)S(1)} %pad_maximum_fusion), channel_id=1, source_target_pairs={{0,1},{1,0},{2,3},{3,2},{4,5},{5,4},{6,7},{7,6},{8,9},{9,8},{10,11... | collective-permute-start | bytes 1179656 | tf_op jit(solution)/shard_map/ppermute | solution.py:93
  60.6 3.1 %copy-start.5 = (s32[6,128]{1,0:T(8,128)S(1)}, s32[6,128]{1,0:T(8,128)}, u32[]{:S(2)}) copy-start(s32[6,128]{1,0:T(8,128)} %param.12) | copy-start | bytes 9220

commit v8 on v7

--- a/solution.py
+++ b/solution.py
@@ -11,7 +11,10 @@
 NT = (((1,), (1,)), ((), ()))
 
 
-def solve_kernel(parent_ref, res_ref, slot_ref, inv_ref, cpl_ref, own_ref, zslot_ref, y_ref, carry_ref):
+def solve_kernel(
+    parent_ref, res_ref, slot_ref, inv_ref, cpl_ref, after_ref, own_ref, zslot_ref, y_ref, carry_ref
+):
+    del after_ref
     blocks_n, block_w, _ = inv_ref.shape
     owned_blocks = res_ref.shape[1] // block_w
 
@@ -51,7 +54,7 @@
             carry_ref[p] = carry_ref[p] + push
 
 
-def local_solve(parent, residual, slots, diag_inverse, coupling):
+def local_solve(parent, residual, slots, diag_inverse, coupling, after):
     nrhs_here, owned_n = residual.shape
     blocks_n, block_w, _ = diag_inverse.shape
     vmem = pltpu.VMEM
@@ -67,6 +70,7 @@
             pl.BlockSpec(memory_space=vmem),
             pl.BlockSpec(memory_space=vmem),
             pl.BlockSpec(memory_space=vmem),
+            pl.BlockSpec(memory_space=pl.ANY),
         ],
         out_specs=(pl.BlockSpec(memory_space=vmem), pl.BlockSpec(memory_space=vmem)),
         scratch_shapes=[
@@ -74,7 +78,7 @@
             pltpu.VMEM((blocks_n, nrhs_here, block_w), jnp.float32),
         ],
         compiler_params=pltpu.CompilerParams(vmem_limit_bytes=48 * 1024 * 1024),
-    )(parent, residual, slots, diag_inverse, coupling)
+    )(parent, residual, slots, diag_inverse, coupling, after)
 
 
 def matchings(count):
@@ -168,15 +172,22 @@
                 held = gather_axis(merge(held, got.reshape(held.shape), axis, 0, 1), axis, 0, 2)
             else:
                 held = gather_axis(held, axis, 0)
+    after = held
     for axis_pos in range(1, len(AXES) - 1):
-        held = gather_axis(held, AXES[axis_pos], axis_pos)
+        axis = AXES[axis_pos]
+        if doubling(axis):
+            held = merge(held, lax.ppermute(held, axis, matchings(lax.axis_size(axis))[0]), axis, axis_pos, 1)
+            after = held
+            held = gather_axis(held, axis, axis_pos, 2)
+        else:
+            held = gather_axis(held, axis, axis_pos)
     last = len(AXES) - 1
     late = lax.axis_size(AXES[last]) == 2
     if not late:
         held = gather_axis(held, AXES[last], last)
     slots = jnp.concatenate(incoming, axis=1)
 
-    own, zslots = local_solve(parent, residual, slots, diag_inverse, coupling)
+    own, zslots = local_solve(parent, residual, slots, diag_inverse, coupling, after)
 
     returned = []
     for axis_pos, axis in enumerate(AXES):

time: 70.5 us -> 67.2 us (0.953)
  the two profiles are of different devices: /device:TPU:0 before, /device:TPU:4 now
where the time goes in v8:
time: 67.2 us; the launch traced here: 67 us
  starting transfers between devices  20.7 us (31%)
  Pallas kernels  13.2 us (20%)
  waiting for transfers between devices  11.2 us (17%)
  matrix products  10.2 us (15%)
  local copies, waits for them, and re-layouts  7.31 us (11%)
  other arithmetic  3.25 us (5%)
  between operations  1.08 us (2%)
    ppermute x8, starting transfers between devices, swap(): return (lax.ppermute(value, axis, pairs), None)  14.1 us
    pallas_call x1, Pallas kernels, local_solve(): pl.pallas_call(solve_kernel, out_shape=(jax.ShapeDtypeStruct((nrhs_here,...  13.2 us
    ppermute x2, starting transfers between devices, gather_axis(): held = merge(held, lax.ppermute(held, axis, pairs), axis, dim, step)  4.96 us
    ppermute x1, waiting for transfers between devices, per_device(): lax.ppermute(held, axis, matchings(lax.axis_size(axis))[0])  4.41 us
    gather x2, local copies, waits for them, and re-layouts, per_device(): outgoing = jnp.take(residual, send_rows, axis=1)  4.26 us
    ppermute x8, waiting for transfers between devices, swap(): return (lax.ppermute(value, axis, pairs), None)  4.02 us
    dot_general x1, matrix products, per_device(): lax.dot_general(solved_t, vectors, (((0,), (0,)), ((), ())), precision=la...  3.6 us
    unnamed x13, local copies, waits for them, and re-layouts  3.02 us
  transfers between devices with their start and end apart: 13, of which 4 were waited for; matrix products, arithmetic and copies ran while one was open for 0% of the time, Pallas kernels for 20%

profile of v8, /device:TPU:4, one launch (start us, length us, event | category | flops | bytes accessed | tf_op | source)
XLA Modules:
  0.0 67.0 jit_solution(10120030271612771203)
XLA Ops:
  0.0 0.7 %compare_and_fusion = pred[6,128]{1,0:T(8,128)(4,1)S(1)} fusion(s32[6,128]{1,0:T(8,128)} %param.12), kind=kLoop, calls=%fused_computation.62 | loop fusion | flops 4608 | bytes 3840 | tf_op jit(solution)/shard_map/jit(_take)/and | solution.py:159
  0.7 0.7 %fusion.15 = s32[768]{0:T(1024)S(1)} fusion(s32[6,128]{1,0:T(8,128)} %param.12), kind=kLoop, calls=%fused_computation.63 | loop fusion | flops 2304 | bytes 6144 | tf_op jit(solution)/shard_map/jit(_take)/broadcast_in_dim | solution.py:159
  2.1 3.0 %copy.15 = f32[128,4352]{0,1:T(8,128)} copy(f32[128,4352]{1,0:T(8,128)} %res_ref.1) | data formatting | bytes 4456448 | tf_op args[0]
  5.1 3.3 %gather_fusion = f32[768,128]{1,0:T(8,128)S(1)} fusion(f32[128,4352]{0,1:T(8,128)} %copy.15, s32[1024]{0:T(1024)S(1)} %pad_clamp_fusion), kind=kCustom, calls=%fused_computation | custom fusion | bytes 789504 | tf_op jit(solution)/shard_map/jit(_take)/gather | solution.py:159
  8.4 0.9 %copy.16 = f32[6,128,128]{1,2,0:T(8,128)} copy(f32[6,128,128]{2,1,0:T(8,128)S(1)} %bitcast.52) | data formatting | bytes 786432 | tf_op jit(solution)/shard_map/jit(_take)/gather | solution.py:159
  9.4 2.4 %fusion.3 = f32[40,128]{1,0:T(8,128)S(1)} fusion(f32[128,4352]{1,0:T(8,128)S(1)} %copy-done.1, f32[40,4352]{1,0:T(8,128)S(1)} %copy-done.3, f32[40]{0:T(128)S(1)} %compare_convert_fusion), kind=kOutput, calls=%fused_computation.7 | convolution fusion | flops 267560960 | bytes 2945184 | tf_op jit(solution)/shard_map/dot_general | solution.py:154
  11.8 0.7 %fusion.11 = (f32[128,128]{1,0:T(8,128)}, f32[128,128]{1,0:T(8,128)}, f32[128,128]{1,0:T(8,128)}, f32[128,128]{1,0:T(8,128)S(1)}, f32[128,128]{1,0:T(8,128)}) fusion(f32[128,6,128]{2,0,1:T(8,128)S(1)} %select_bitcast_fusion, pred[]{:T(512)S(6)} %eq.50, pred[]{:T(512)S(6)} %eq.49, pred[]{:T(512)S(6)} %eq.48), kind=kLoop, calls=%fused_computation.31 | loop fusion | flops 81920 | bytes 720899 | tf_op jit(solution)/shard_map/jit(_where)/select_n | solution.py:104
  13.2 1.6 %collective-permute-start = (f32[168,128]{1,0:T(8,128)}, f32[168,128]{1,0:T(8,128)S(1)}, u32[]{:S(2)}, u32[]{:S(2)}) collective-permute-start(f32[168,128]{1,0:T(8,128)} %pad_maximum_fusion.7), channel_id=1, source_target_pairs={{0,8},{16,24},{8,0},{24,16},{1,9},{17,25},{9,1},{25,17},{2,10},{18... | collective-permute-start | bytes 258056 | tf_op jit(solution)/shard_map/ppermute | solution.py:97
  14.7 1.5 %collective-permute-start.2 = (f32[128,128]{1,0:T(8,128)}, f32[128,128]{1,0:T(8,128)S(1)}, u32[]{:S(2)}, u32[]{:S(2)}) collective-permute-start(f32[128,128]{1,0:T(8,128)} %get-tuple-element.10), channel_id=1, source_target_pairs={{0,2},{4,6},{2,0},{6,4},{1,3},{5,7},{3,1},{7,5},{8,10},{12,14},{10... | collective-permute-start | bytes 196616 | tf_op jit(solution)/shard_map/ppermute | solution.py:94
  16.2 2.4 %collective-permute-start.3 = (f32[128,128]{1,0:T(8,128)}, f32[128,128]{1,0:T(8,128)S(1)}, u32[]{:S(2)}, u32[]{:S(2)}) collective-permute-start(f32[128,128]{1,0:T(8,128)} %get-tuple-element.11), channel_id=1, source_target_pairs={{2,4},{4,2},{3,5},{5,3},{10,12},{12,10},{11,13},{13,11},{18,20},{2... | collective-permute-start | bytes 196616 | tf_op jit(solution)/shard_map/ppermute | solution.py:94
  18.6 0.7 collective-permute-start.1
  19.4 3.9 %collective-permute-start.5 = (f32[2,1,1,40,128]{4,3,0,2,1:T(8,128)S(1)}, f32[2,1,1,40,128]{4,3,0,2,1:T(8,128)S(1)}, u32[]{:S(2)}, u32[]{:S(2)}) collective-permute-start(f32[2,1,1,40,128]{4,3,0,2,1:T(8,128)S(1)} %fusion.12), channel_id=1, source_target_pairs={{0,16},{8,24},{16,0},{24,8},{1,17},{9,25},{17,1},{25,9},{2,18},{10... | collective-permute-start | bytes 122888 | tf_op jit(solution)/shard_map/ppermute | solution.py:137
  23.6 2.8 %collective-permute-done.5 = f32[2,1,1,40,128]{4,3,0,2,1:T(8,128)S(1)} collective-permute-done((f32[2,1,1,40,128]{4,3,0,2,1:T(8,128)S(1)}, f32[2,1,1,40,128]{4,3,0,2,1:T(8,128)S(1)}, u32[]{:S(2)}, u32[]{:S(2)}) %collective-permute-start.5) | collective-permute-done | bytes 40992 | tf_op jit(solution)/shard_map/ppermute | solution.py:137
  26.5 4.4 %collective-permute-done.6 = f32[4,1,1,40,128]{4,3,0,2,1:T(8,128)S(1)} collective-permute-done((f32[4,1,1,40,128]{4,3,0,2,1:T(8,128)S(1)}, f32[4,1,1,40,128]{4,3,0,2,1:T(8,128)S(1)}, u32[]{:S(2)}, u32[]{:S(2)}) %collective-permute-start.6) | collective-permute-done | bytes 81952 | tf_op jit(solution)/shard_map/ppermute | solution.py:179
  31.0 1.1 %collective-permute-start.11 = (f32[4,2,1,40,128]{4,3,2,1,0:T(8,128)S(1)}, f32[4,2,1,40,128]{4,3,2,1,0:T(8,128)S(1)}, u32[]{:S(2)}, u32[]{:S(2)}) collective-permute-start(f32[4,2,1,40,128]{4,3,2,1,0:T(8,128)S(1)} %copy_select_fusion.after_ref), channel_id=1, source_target_pairs={{0,4},{2,6},{4,0},{6,2},{1,5},{3,7},{5,1},{7,3},{8,12},{10,14},{12... | collective-permute-start | bytes 491528 | tf_op jit(solution)/shard_map/ppermute | solution.py:137
  32.0 13.2 %shard_map.82 = (bf16[128,4352]{1,0:T(8,128)(2,1)S(1)}, bf16[128,768]{1,0:T(8,128)(2,1)S(1)}) custom-call(s32[20]{0:T(128)S(1)} %copy-done.2, f32[128,4352]{1,0:T(8,128)S(1)} %copy-done.1, f32[128,768]{1,0:T(8,128)S(1)} %select_dynamic-update-slice_fusion.slot_ref, bf16[20,256,256]{2,1,0:T(8,128)(2,1)} %inv_ref.1, bf16[19,256,256]{2,1,0:T(8,128)(2,1)} %cpl_ref.1, ...), custom_call_target="tpu_custom_call" | custom-call | tf_op jit(solution)/shard_map/pallas_call | solution.py:61
  45.2 0.7 collective-permute-start.7
  45.9 4.2 %collective-permute-start.8 = (bf16[128,128]{1,0:T(8,128)(2,1)S(1)}, bf16[128,128]{1,0:T(8,128)(2,1)S(1)}, u32[]{:S(2)}, u32[]{:S(2)}) collective-permute-start(bf16[128,128]{1,0:T(8,128)(2,1)S(1)} %get-tuple-element.17), channel_id=1, source_target_pairs={{0,8},{16,24},{8,0},{24,16},{1,9},{17,25},{9,1},{25,17},{2,10},{18... | collective-permute-start | bytes 98312 | tf_op jit(solution)/shard_map/ppermute | solution.py:94
  50.1 2.1 %collective-permute-start.10 = (bf16[128,128]{1,0:T(8,128)(2,1)S(1)}, bf16[128,128]{1,0:T(8,128)(2,1)S(1)}, u32[]{:S(2)}, u32[]{:S(2)}) collective-permute-start(bf16[128,128]{1,0:T(8,128)(2,1)S(1)} %get-tuple-element.14), channel_id=1, source_target_pairs={{0,2},{4,6},{2,0},{6,4},{1,3},{5,7},{3,1},{7,5},{8,10},{12,14},{10... | collective-permute-start | bytes 98312 | tf_op jit(solution)/shard_map/ppermute | solution.py:94
  52.2 2.6 %collective-permute-start.9 = (bf16[128,128]{1,0:T(8,128)(2,1)S(1)}, bf16[128,128]{1,0:T(8,128)(2,1)S(1)}, u32[]{:S(2)}, u32[]{:S(2)}) collective-permute-start(bf16[128,128]{1,0:T(8,128)(2,1)S(1)} %get-tuple-element.18), channel_id=1, source_target_pairs={{2,4},{4,2},{3,5},{5,3},{10,12},{12,10},{11,13},{13,11},{18,20},{2... | collective-permute-start | bytes 98312 | tf_op jit(solution)/shard_map/ppermute | solution.py:94
  55.1 3.9 %collective-permute-done.9 = bf16[128,128]{1,0:T(8,128)(2,1)S(1)} collective-permute-done((bf16[128,128]{1,0:T(8,128)(2,1)S(1)}, bf16[128,128]{1,0:T(8,128)(2,1)S(1)}, u32[]{:S(2)}, u32[]{:S(2)}) %collective-permute-start.9) | collective-permute-done | bytes 32800 | tf_op jit(solution)/shard_map/ppermute | solution.py:94
  59.1 1.2 %fusion.16 = f32[128,40]{1,0:T(8,128)S(1)} fusion(f32[1280,128]{1,0:T(8,128)S(1)} %bitcast.51, f32[40,1280]{1,0:T(8,128)S(1)} %copy-done), kind=kOutput, calls=%fused_computation.65 | convolution fusion | flops 78643200 | bytes 880640 | tf_op jit(solution)/shard_map/dot_general | solution.py:206
  60.3 3.0 %fusion = f32[128,4352]{1,0:T(8,128)S(1)} fusion(bf16[128,768]{1,0:T(8,128)(2,1)S(1)} %select_dynamic-update-slice_fusion.6, s32[768]{0:T(1024)S(1)} %bitcast.60), kind=kOutput, calls=%fused_computation.2 | convolution fusion | flops 858980352 | bytes 2427904 | tf_op jit(solution)/shard_map/dot_general | solution.py:212
  63.4 3.6 %convolution_add_fusion = f32[128,4352]{1,0:T(8,128)} fusion(f32[128,40]{1,0:T(8,128)S(1)} %fusion.16, f32[128,4352]{1,0:T(8,128)S(1)} %fusion, bf16[128,4352]{1,0:T(8,128)(2,1)S(1)} %get-tuple-element.7, f32[40,4352]{1,0:T(8,128)S(1)} %copy-done.3, f32[40]{0:T(128)S(1)} %compare_convert_fusion), kind=kOutput, calls=%fused_computation.4 | convolution fusion | flops 269232128 | bytes 6287520 | tf_op jit(solution)/shard_map/dot_general | solution.py:213
  (54 shorter events, 1.5 us)
Async XLA Ops:
  0.0 59.1 %copy-start = (f32[40,1280]{1,0:T(8,128)S(1)}, f32[40,1280]{1,0:T(8,128)}, u32[]{:S(2)}) copy-start(f32[40,1280]{1,0:T(8,128)} %param.15) | copy-start | bytes 614404
  5.1 4.3 %copy-start.1 = (f32[128,4352]{1,0:T(8,128)S(1)}, f32[128,4352]{1,0:T(8,128)}, u32[]{:S(2)}) copy-start(f32[128,4352]{1,0:T(8,128)} %res_ref.1) | copy-start | bytes 6684676
  5.1 4.3 %copy-start.3 = (f32[40,4352]{1,0:T(8,128)S(1)}, f32[40,4352]{1,0:T(8,128)}, u32[]{:S(2)}) copy-start(f32[40,4352]{1,0:T(8,128)} %param.14) | copy-start | bytes 2088964
  9.4 2.4 %copy-start.4 = (f32[6,128,128]{1,2,0:T(8,128)S(1)}, f32[6,128,128]{1,2,0:T(8,128)}, u32[]{:S(2)}) copy-start(f32[6,128,128]{1,2,0:T(8,128)} %copy.16) | copy-start | bytes 1179652
  11.7 20.3 %copy-start.2 = (s32[20]{0:T(128)S(1)}, s32[20]{0:T(128)}, u32[]{:S(2)}) copy-start(s32[20]{0:T(128)} %parent_ref.1) | copy-start | bytes 244
  13.2 6.2 %collective-permute-start = (f32[168,128]{1,0:T(8,128)}, f32[168,128]{1,0:T(8,128)S(1)}, u32[]{:S(2)}, u32[]{:S(2)}) collective-permute-start(f32[168,128]{1,0:T(8,128)} %pad_maximum_fusion.7), channel_id=1, source_target_pairs={{0,8},{16,24},{8,0},{24,16},{1,9},{17,25},{9,1},{25,17},{2,10},{18... | collective-permute-start | bytes 258056 | tf_op jit(solution)/shard_map/ppermute | solution.py:97
  14.7 8.8 %collective-permute-start.4 = (f32[128,128]{1,0:T(8,128)}, f32[128,128]{1,0:T(8,128)S(1)}, u32[]{:S(2)}, u32[]{:S(2)}) collective-permute-start(f32[128,128]{1,0:T(8,128)} %get-tuple-element.9), channel_id=1, source_target_pairs={{0,1},{1,0},{2,3},{3,2},{4,5},{5,4},{6,7},{7,6},{8,9},{9,8},{10,11... | collective-permute-start | bytes 196616 | tf_op jit(solution)/shard_map/ppermute | solution.py:94
  14.7 8.6 %collective-permute-start.2 = (f32[128,128]{1,0:T(8,128)}, f32[128,128]{1,0:T(8,128)S(1)}, u32[]{:S(2)}, u32[]{:S(2)}) collective-permute-start(f32[128,128]{1,0:T(8,128)} %get-tuple-element.10), channel_id=1, source_target_pairs={{0,2},{4,6},{2,0},{6,4},{1,3},{5,7},{3,1},{7,5},{8,10},{12,14},{10... | collective-permute-start | bytes 196616 | tf_op jit(solution)/shard_map/ppermute | solution.py:94
  16.2 7.3 %collective-permute-start.3 = (f32[128,128]{1,0:T(8,128)}, f32[128,128]{1,0:T(8,128)S(1)}, u32[]{:S(2)}, u32[]{:S(2)}) collective-permute-start(f32[128,128]{1,0:T(8,128)} %get-tuple-element.11), channel_id=1, source_target_pairs={{2,4},{4,2},{3,5},{5,3},{10,12},{12,10},{11,13},{13,11},{18,20},{2... | collective-permute-start | bytes 196616 | tf_op jit(solution)/shard_map/ppermute | solution.py:94
  18.6 4.7 %collective-permute-start.1 = (f32[128,128]{1,0:T(8,128)}, f32[128,128]{1,0:T(8,128)S(1)}, u32[]{:S(2)}, u32[]{:S(2)}) collective-permute-start(f32[128,128]{1,0:T(8,128)} %get-tuple-element.13), channel_id=1, source_target_pairs={{8,16},{16,8},{9,17},{17,9},{10,18},{18,10},{11,19},{19,11},{12,20... | collective-permute-start | bytes 196616 | tf_op jit(solution)/shard_map/ppermute | solution.py:94
  19.4 7.0 %collective-permute-start.5 = (f32[2,1,1,40,128]{4,3,0,2,1:T(8,128)S(1)}, f32[2,1,1,40,128]{4,3,0,2,1:T(8,128)S(1)}, u32[]{:S(2)}, u32[]{:S(2)}) collective-permute-start(f32[2,1,1,40,128]{4,3,0,2,1:T(8,128)S(1)} %fusion.12), channel_id=1, source_target_pairs={{0,16},{8,24},{16,0},{24,8},{1,17},{9,25},{17,1},{25,9},{2,18},{10... | collective-permute-start | bytes 122888 | tf_op jit(solution)/shard_map/ppermute | solution.py:137
  26.4 4.5 %collective-permute-start.6 = (f32[4,1,1,40,128]{4,3,0,2,1:T(8,128)S(1)}, f32[4,1,1,40,128]{4,3,0,2,1:T(8,128)S(1)}, u32[]{:S(2)}, u32[]{:S(2)}) collective-permute-start(f32[4,1,1,40,128]{4,3,0,2,1:T(8,128)S(1)} %maximum_select_fusion.2), channel_id=1, source_target_pairs={{0,2},{4,6},{2,0},{6,4},{1,3},{5,7},{3,1},{7,5},{8,10},{12,14},{10... | collective-permute-start | bytes 245768 | tf_op jit(solution)/shard_map/ppermute | solution.py:179
  31.0 23.9 %collective-permute-start.11 = (f32[4,2,1,40,128]{4,3,2,1,0:T(8,128)S(1)}, f32[4,2,1,40,128]{4,3,2,1,0:T(8,128)S(1)}, u32[]{:S(2)}, u32[]{:S(2)}) collective-permute-start(f32[4,2,1,40,128]{4,3,2,1,0:T(8,128)S(1)} %copy_select_fusion.after_ref), channel_id=1, source_target_pairs={{0,4},{2,6},{4,0},{6,2},{1,5},{3,7},{5,1},{7,3},{8,12},{10,14},{12... | collective-permute-start | bytes 491528 | tf_op jit(solution)/shard_map/ppermute | solution.py:137
  45.2 9.6 %collective-permute-start.7 = (bf16[128,128]{1,0:T(8,128)(2,1)S(1)}, bf16[128,128]{1,0:T(8,128)(2,1)S(1)}, u32[]{:S(2)}, u32[]{:S(2)}) collective-permute-start(bf16[128,128]{1,0:T(8,128)(2,1)S(1)} %get-tuple-element.16), channel_id=1, source_target_pairs={{8,16},{16,8},{9,17},{17,9},{10,18},{18,10},{11,19},{19,11},{12,20... | collective-permute-start | bytes 98312 | tf_op jit(solution)/shard_map/ppermute | solution.py:94
  45.9 8.9 %collective-permute-start.8 = (bf16[128,128]{1,0:T(8,128)(2,1)S(1)}, bf16[128,128]{1,0:T(8,128)(2,1)S(1)}, u32[]{:S(2)}, u32[]{:S(2)}) collective-permute-start(bf16[128,128]{1,0:T(8,128)(2,1)S(1)} %get-tuple-element.17), channel_id=1, source_target_pairs={{0,8},{16,24},{8,0},{24,16},{1,9},{17,25},{9,1},{25,17},{2,10},{18... | collective-permute-start | bytes 98312 | tf_op jit(solution)/shard_map/ppermute | solution.py:94
  50.1 4.9 %collective-permute-start.10 = (bf16[128,128]{1,0:T(8,128)(2,1)S(1)}, bf16[128,128]{1,0:T(8,128)(2,1)S(1)}, u32[]{:S(2)}, u32[]{:S(2)}) collective-permute-start(bf16[128,128]{1,0:T(8,128)(2,1)S(1)} %get-tuple-element.14), channel_id=1, source_target_pairs={{0,2},{4,6},{2,0},{6,4},{1,3},{5,7},{3,1},{7,5},{8,10},{12,14},{10... | collective-permute-start | bytes 98312 | tf_op jit(solution)/shard_map/ppermute | solution.py:94
  52.2 6.7 %collective-permute-start.9 = (bf16[128,128]{1,0:T(8,128)(2,1)S(1)}, bf16[128,128]{1,0:T(8,128)(2,1)S(1)}, u32[]{:S(2)}, u32[]{:S(2)}) collective-permute-start(bf16[128,128]{1,0:T(8,128)(2,1)S(1)} %get-tuple-element.18), channel_id=1, source_target_pairs={{2,4},{4,2},{3,5},{5,3},{10,12},{12,10},{11,13},{13,11},{18,20},{2... | collective-permute-start | bytes 98312 | tf_op jit(solution)/shard_map/ppermute | solution.py:94
  54.9 5.4 %copy-start.5 = (s32[6,128]{1,0:T(8,128)S(1)}, s32[6,128]{1,0:T(8,128)}, u32[]{:S(2)}) copy-start(s32[6,128]{1,0:T(8,128)} %param.12) | copy-start | bytes 9220
  55.0 4.0 %collective-permute-start.12 = (f32[768,128]{1,0:T(8,128)S(1)}, f32[768,128]{1,0:T(8,128)S(1)}, u32[]{:S(2)}, u32[]{:S(2)}) collective-permute-start(f32[768,128]{1,0:T(8,128)S(1)} %pad_maximum_fusion), channel_id=1, source_target_pairs={{0,1},{1,0},{2,3},{3,2},{4,5},{5,4},{6,7},{7,6},{8,9},{9,8},{10,11... | collective-permute-start | bytes 1179656 | tf_op jit(solution)/shard_map/ppermute | solution.py:97

commit v9 on v8

--- a/solution.py
+++ b/solution.py
@@ -154,53 +154,28 @@
     coeffs_t = lax.dot_general(
         vectors, residual, NT, precision=lax.Precision.HIGHEST, preferred_element_type=jnp.float32
     )
-    held = coeffs_t.reshape((1,) * len(AXES) + coeffs_t.shape)
+    total_dev = coarse_inverse.shape[1] // kmax_here
+    spread = jnp.broadcast_to(coeffs_t[None], (total_dev,) + coeffs_t.shape)
+    held = lax.all_to_all(spread, AXES, 0, 0, tiled=True)
 
     outgoing = jnp.take(residual, send_rows, axis=1)
     incoming = []
     for axis_pos, axis in enumerate(AXES):
-        ride = axis_pos == 0 and doubling(axis)
-        low, high, got = halo_out(
-            outgoing[:, 2 * axis_pos],
-            outgoing[:, 2 * axis_pos + 1],
-            axis,
-            rows_of(held) if ride else None,
-        )
+        low, high, _ = halo_out(outgoing[:, 2 * axis_pos], outgoing[:, 2 * axis_pos + 1], axis)
         incoming += [low, high]
-        if axis_pos == 0:
-            if ride:
-                held = gather_axis(merge(held, got.reshape(held.shape), axis, 0, 1), axis, 0, 2)
-            else:
-                held = gather_axis(held, axis, 0)
-    after = held
-    for axis_pos in range(1, len(AXES) - 1):
-        axis = AXES[axis_pos]
-        if doubling(axis):
-            held = merge(held, lax.ppermute(held, axis, matchings(lax.axis_size(axis))[0]), axis, axis_pos, 1)
-            after = held
-            held = gather_axis(held, axis, axis_pos, 2)
-        else:
-            held = gather_axis(held, axis, axis_pos)
-    last = len(AXES) - 1
-    late = lax.axis_size(AXES[last]) == 2
-    if not late:
-        held = gather_axis(held, AXES[last], last)
     slots = jnp.concatenate(incoming, axis=1)
+    after = coeffs_t
 
     own, zslots = local_solve(parent, residual, slots, diag_inverse, coupling, after)
 
     returned = []
     for axis_pos, axis in enumerate(AXES):
-        ride = axis_pos == last and late
-        low, high, got = halo_back(
+        low, high, _ = halo_back(
             zslots[:, (2 * axis_pos) * face_w : (2 * axis_pos + 1) * face_w],
             zslots[:, (2 * axis_pos + 1) * face_w : (2 * axis_pos + 2) * face_w],
             axis,
-            rows_of(held) if ride else None,
         )
         returned += [low, high]
-        if ride:
-            held = merge(held, got.reshape(held.shape), axis, last, 1)
     returned = jnp.concatenate(returned, axis=1)
 
     solved_t = jnp.dot(

time: 67.2 us -> 70.4 us (1.048)
  the two profiles are of different devices: /device:TPU:4 before, /device:TPU:0 now
where the time goes in v9:
time: 70.4 us; the launch traced here: 70 us
  starting transfers between devices  25.3 us (36%)
  Pallas kernels  13.1 us (19%)
  waiting for transfers between devices  12.4 us (18%)
  matrix products  10.1 us (14%)
  local copies, waits for them, and re-layouts  5.4 us (8%)
  other arithmetic  2.69 us (4%)
  between operations  0.98 us (1%)
    ppermute x10, starting transfers between devices, swap(): return (lax.ppermute(value, axis, pairs), None)  17.9 us
    pallas_call x1, Pallas kernels, local_solve(): pl.pallas_call(solve_kernel, out_shape=(jax.ShapeDtypeStruct((nrhs_here,...  13.1 us
    all_to_all x1, waiting for transfers between devices, per_device(): held = lax.all_to_all(spread, AXES, 0, 0, tiled=True)  7.78 us
    all_to_all x1, starting transfers between devices, per_device(): held = lax.all_to_all(spread, AXES, 0, 0, tiled=True)  7.42 us
    dot_general x1, matrix products, per_device(): faces = jnp.dot(returned, onehot, preferred_element_type=jnp.float32)  4.6 us
    ppermute x10, waiting for transfers between devices, swap(): return (lax.ppermute(value, axis, pairs), None)  4.57 us
    gather x2, local copies, waits for them, and re-layouts, per_device(): outgoing = jnp.take(residual, send_rows, axis=1)  2.49 us
    dot_general x1, matrix products, per_device(): lax.dot_general(vectors, residual, NT, precision=lax.Precision.HIGHEST, p...  2.35 us
  transfers between devices with their start and end apart: 11, of which 2 were waited for; matrix products, arithmetic and copies ran while one was open for 5% of the time, Pallas kernels for 0%

profile of v9, /device:TPU:0, one launch (start us, length us, event | category | flops | bytes accessed | tf_op | source)
XLA Modules:
  0.0 70.0 jit_solution(8108988972036392561)
XLA Ops:
  0.0 0.7 %fusion.9 = s32[768]{0:T(1024)S(1)} fusion(s32[6,128]{1,0:T(8,128)} %param.12), kind=kLoop, calls=%fused_computation.38 | loop fusion | flops 2304 | bytes 6144 | tf_op jit(solution)/shard_map/jit(_take)/broadcast_in_dim | solution.py:161
  0.7 0.7 compare_and_fusion
  1.4 2.0 %copy.10 = f32[128,4352]{0,1:T(8,128)S(1)} copy(f32[128,4352]{1,0:T(8,128)} %res_ref.1) | data formatting | bytes 4456448 | tf_op args[0]
  3.5 1.6 %gather_fusion = f32[768,128]{1,0:T(8,128)S(1)} fusion(f32[128,4352]{0,1:T(8,128)S(1)} %copy.10, s32[1024]{0:T(1024)S(1)} %pad_clamp_fusion), kind=kCustom, calls=%fused_computation | custom fusion | bytes 789504 | tf_op jit(solution)/shard_map/jit(_take)/gather | solution.py:161
  5.1 0.9 %copy.11 = f32[6,128,128]{1,2,0:T(8,128)} copy(f32[6,128,128]{2,1,0:T(8,128)S(1)} %bitcast.25) | data formatting | bytes 786432 | tf_op jit(solution)/shard_map/jit(_take)/gather | solution.py:161
  6.0 1.0 %select_bitcast_fusion = f32[128,6,128]{2,0,1:T(8,128)S(1)} fusion(f32[6,128,128]{1,2,0:T(8,128)} %copy.11, pred[6,128]{1,0:T(8,128)(4,1)S(1)} %compare_and_fusion), kind=kLoop, calls=%fused_computation.9 | loop fusion | flops 98304 | bytes 787200 | tf_op jit(solution)/shard_map/jit(_take)/select_n | solution.py:161
  7.0 3.1 %collective-permute-start = (f32[128,128]{1,0:T(8,128)S(1)}, f32[128,128]{1,0:T(8,128)S(1)}, u32[]{:S(2)}, u32[]{:S(2)}) collective-permute-start(f32[128,128]{1,0:T(8,128)S(1)} %get-tuple-element.12), channel_id=1, source_target_pairs={{0,8},{16,24},{8,0},{24,16},{1,9},{17,25},{9,1},{25,17},{2,10},{18... | collective-permute-start | bytes 196616 | tf_op jit(solution)/shard_map/ppermute | solution.py:94
  10.1 0.7 collective-permute-start.1
  10.8 1.6 %collective-permute-start.2 = (f32[128,128]{1,0:T(8,128)S(1)}, f32[128,128]{1,0:T(8,128)S(1)}, u32[]{:S(2)}, u32[]{:S(2)}) collective-permute-start(f32[128,128]{1,0:T(8,128)S(1)} %get-tuple-element.10), channel_id=1, source_target_pairs={{0,2},{4,6},{2,0},{6,4},{1,3},{5,7},{3,1},{7,5},{8,10},{12,14},{10... | collective-permute-start | bytes 196616 | tf_op jit(solution)/shard_map/ppermute | solution.py:94
  12.4 0.7 collective-permute-start.3
  13.0 0.1 collective-permute-start.4
  13.8 2.3 %fusion.4.after_ref = f32[40,128]{1,0:T(8,128)S(1)} fusion(f32[128,4352]{1,0:T(8,128)S(1)} %copy-done.1, f32[40,4352]{1,0:T(8,128)S(1)} %copy-done.3, f32[40]{0:T(128)S(1)} %compare_convert_fusion), kind=kOutput, calls=%fused_computation.7 | convolution fusion | flops 267560960 | bytes 2945184 | tf_op jit(solution)/shard_map/dot_general | solution.py:154
  16.3 13.1 %shard_map.82 = (bf16[128,4352]{1,0:T(8,128)(2,1)S(1)}, bf16[128,768]{1,0:T(8,128)(2,1)S(1)}) custom-call(s32[20]{0:T(128)S(1)} %copy-done.2, f32[128,4352]{1,0:T(8,128)S(1)} %copy-done.1, f32[128,768]{1,0:T(8,128)S(1)} %select_dynamic-update-slice_fusion.slot_ref, bf16[20,256,256]{2,1,0:T(8,128)(2,1)} %inv_ref.1, bf16[19,256,256]{2,1,0:T(8,128)(2,1)} %cpl_ref.1, ...), custom_call_target="tpu_custom_call" | custom-call | tf_op jit(solution)/shard_map/pallas_call | solution.py:61
  29.5 0.8 %collective-permute-start.5 = (bf16[128,128]{1,0:T(8,128)(2,1)S(1)}, bf16[128,128]{1,0:T(8,128)(2,1)S(1)}, u32[]{:S(2)}, u32[]{:S(2)}) collective-permute-start(bf16[128,128]{1,0:T(8,128)(2,1)S(1)} %get-tuple-element.17), channel_id=1, source_target_pairs={{8,16},{16,8},{9,17},{17,9},{10,18},{18,10},{11,19},{19,11},{12,20... | collective-permute-start | bytes 98312 | tf_op jit(solution)/shard_map/ppermute | solution.py:94
  30.3 5.7 %collective-permute-start.6 = (bf16[128,128]{1,0:T(8,128)(2,1)S(1)}, bf16[128,128]{1,0:T(8,128)(2,1)S(1)}, u32[]{:S(2)}, u32[]{:S(2)}) collective-permute-start(bf16[128,128]{1,0:T(8,128)(2,1)S(1)} %get-tuple-element.18), channel_id=1, source_target_pairs={{0,8},{16,24},{8,0},{24,16},{1,9},{17,25},{9,1},{25,17},{2,10},{18... | collective-permute-start | bytes 98312 | tf_op jit(solution)/shard_map/ppermute | solution.py:94
  36.0 0.9 %broadcast_in_dim.31 = f32[32,40,128]{2,1,0:T(8,128)} broadcast(f32[40,128]{1,0:T(8,128)S(1)} %fusion.4.after_ref), dimensions={1,2} | broadcast | bytes 675840 | tf_op jit(solution)/shard_map/broadcast_in_dim | solution.py:158
  36.9 7.4 %all-to-all-start = ((f32[32,40,128]{2,1,0:T(8,128)}), f32[32,40,128]{2,1,0:T(8,128)S(1)}, u32[]{:S(2)}, u32[]{:S(2)}) async-start(f32[32,40,128]{2,1,0:T(8,128)} %broadcast_in_dim.31), calls=%async_computation | async-start | bytes 1310720 | tf_op jit(solution)/shard_map/all_to_all | solution.py:159
  44.3 0.8 %collective-permute-start.7 = (bf16[128,128]{1,0:T(8,128)(2,1)S(1)}, bf16[128,128]{1,0:T(8,128)(2,1)S(1)}, u32[]{:S(2)}, u32[]{:S(2)}) collective-permute-start(bf16[128,128]{1,0:T(8,128)(2,1)S(1)} %get-tuple-element.15), channel_id=1, source_target_pairs={{2,4},{4,2},{3,5},{5,3},{10,12},{12,10},{11,13},{13,11},{18,20},{2... | collective-permute-start | bytes 98312 | tf_op jit(solution)/shard_map/ppermute | solution.py:94
  45.2 4.5 %collective-permute-start.8 = (bf16[128,128]{1,0:T(8,128)(2,1)S(1)}, bf16[128,128]{1,0:T(8,128)(2,1)S(1)}, u32[]{:S(2)}, u32[]{:S(2)}) collective-permute-start(bf16[128,128]{1,0:T(8,128)(2,1)S(1)} %get-tuple-element.16), channel_id=1, source_target_pairs={{0,2},{4,6},{2,0},{6,4},{1,3},{5,7},{3,1},{7,5},{8,10},{12,14},{10... | collective-permute-start | bytes 98312 | tf_op jit(solution)/shard_map/ppermute | solution.py:94
  49.8 4.5 %collective-permute-done.8 = bf16[128,128]{1,0:T(8,128)(2,1)S(1)} collective-permute-done((bf16[128,128]{1,0:T(8,128)(2,1)S(1)}, bf16[128,128]{1,0:T(8,128)(2,1)S(1)}, u32[]{:S(2)}, u32[]{:S(2)}) %collective-permute-start.8) | collective-permute-done | bytes 32800 | tf_op jit(solution)/shard_map/ppermute | solution.py:94
  54.4 7.8 %all-to-all-done = f32[32,40,128]{2,1,0:T(8,128)S(1)} async-done(((f32[32,40,128]{2,1,0:T(8,128)}), f32[32,40,128]{2,1,0:T(8,128)S(1)}, u32[]{:S(2)}, u32[]{:S(2)}) %all-to-all-start) | async-done | bytes 655392 | tf_op jit(solution)/shard_map/all_to_all | solution.py:159
  62.2 1.2 %fusion.10 = f32[128,40]{1,0:T(8,128)S(1)} fusion(f32[1280,128]{1,0:T(8,128)S(1)} %bitcast.24, f32[40,1280]{1,0:T(8,128)S(1)} %copy-done), kind=kOutput, calls=%fused_computation.40 | convolution fusion | flops 78643200 | bytes 880640 | tf_op jit(solution)/shard_map/dot_general | solution.py:181
  63.5 2.0 %fusion.2 = f32[128,4352]{1,0:T(8,128)S(1)} fusion(f32[128,40]{1,0:T(8,128)S(1)} %fusion.10, f32[40,4352]{1,0:T(8,128)S(1)} %copy-done.4, f32[40]{0:T(128)S(1)} %compare_convert_fusion), kind=kOutput, calls=%fused_computation.5 | convolution fusion | flops 267560960 | bytes 2945184 | tf_op jit(solution)/shard_map/dot_general | solution.py:188
  65.4 4.6 %add_add_fusion = f32[128,4352]{1,0:T(8,128)} fusion(f32[128,4352]{1,0:T(8,128)S(1)} %fusion.2, bf16[128,4352]{1,0:T(8,128)(2,1)S(1)} %get-tuple-element.7, bf16[128,768]{1,0:T(8,128)(2,1)S(1)} %select_dynamic-update-slice_fusion.6, s32[768]{0:T(1024)S(1)} %bitcast.26), kind=kOutput, calls=%fused_computation.4 | convolution fusion | flops 860651520 | bytes 5770240 | tf_op jit(solution)/shard_map/dot_general | solution.py:187
  (38 shorter events, 0.3 us)
Async XLA Ops:
  0.0 62.2 %copy-start = (f32[40,1280]{1,0:T(8,128)S(1)}, f32[40,1280]{1,0:T(8,128)}, u32[]{:S(2)}) copy-start(f32[40,1280]{1,0:T(8,128)} %param.15) | copy-start | bytes 614404
  3.4 10.3 %copy-start.3 = (f32[40,4352]{1,0:T(8,128)S(1)}, f32[40,4352]{1,0:T(8,128)}, u32[]{:S(2)}) copy-start(f32[40,4352]{1,0:T(8,128)} %param.14) | copy-start | bytes 2088964
  5.0 8.7 %copy-start.1 = (f32[128,4352]{1,0:T(8,128)S(1)}, f32[128,4352]{1,0:T(8,128)}, u32[]{:S(2)}) copy-start(f32[128,4352]{1,0:T(8,128)} %res_ref.1) | copy-start | bytes 6684676
  7.0 9.3 %copy-start.2 = (s32[20]{0:T(128)S(1)}, s32[20]{0:T(128)}, u32[]{:S(2)}) copy-start(s32[20]{0:T(128)} %parent_ref.1) | copy-start | bytes 244
  7.0 9.1 %collective-permute-start = (f32[128,128]{1,0:T(8,128)S(1)}, f32[128,128]{1,0:T(8,128)S(1)}, u32[]{:S(2)}, u32[]{:S(2)}) collective-permute-start(f32[128,128]{1,0:T(8,128)S(1)} %get-tuple-element.12), channel_id=1, source_target_pairs={{0,8},{16,24},{8,0},{24,16},{1,9},{17,25},{9,1},{25,17},{2,10},{18... | collective-permute-start | bytes 196616 | tf_op jit(solution)/shard_map/ppermute | solution.py:94
  10.1 6.0 %collective-permute-start.1 = (f32[128,128]{1,0:T(8,128)S(1)}, f32[128,128]{1,0:T(8,128)S(1)}, u32[]{:S(2)}, u32[]{:S(2)}) collective-permute-start(f32[128,128]{1,0:T(8,128)S(1)} %get-tuple-element.13), channel_id=1, source_target_pairs={{8,16},{16,8},{9,17},{17,9},{10,18},{18,10},{11,19},{19,11},{12,20... | collective-permute-start | bytes 196616 | tf_op jit(solution)/shard_map/ppermute | solution.py:94
  10.8 5.4 %collective-permute-start.2 = (f32[128,128]{1,0:T(8,128)S(1)}, f32[128,128]{1,0:T(8,128)S(1)}, u32[]{:S(2)}, u32[]{:S(2)}) collective-permute-start(f32[128,128]{1,0:T(8,128)S(1)} %get-tuple-element.10), channel_id=1, source_target_pairs={{0,2},{4,6},{2,0},{6,4},{1,3},{5,7},{3,1},{7,5},{8,10},{12,14},{10... | collective-permute-start | bytes 196616 | tf_op jit(solution)/shard_map/ppermute | solution.py:94
  12.4 3.8 %collective-permute-start.3 = (f32[128,128]{1,0:T(8,128)S(1)}, f32[128,128]{1,0:T(8,128)S(1)}, u32[]{:S(2)}, u32[]{:S(2)}) collective-permute-start(f32[128,128]{1,0:T(8,128)S(1)} %get-tuple-element.11), channel_id=1, source_target_pairs={{2,4},{4,2},{3,5},{5,3},{10,12},{12,10},{11,13},{13,11},{18,20},{2... | collective-permute-start | bytes 196616 | tf_op jit(solution)/shard_map/ppermute | solution.py:94
  13.0 3.2 %collective-permute-start.4 = (f32[128,128]{1,0:T(8,128)S(1)}, f32[128,128]{1,0:T(8,128)S(1)}, u32[]{:S(2)}, u32[]{:S(2)}) collective-permute-start(f32[128,128]{1,0:T(8,128)S(1)} %get-tuple-element.9), channel_id=1, source_target_pairs={{0,1},{1,0},{2,3},{3,2},{4,5},{5,4},{6,7},{7,6},{8,9},{9,8},{10,11... | collective-permute-start | bytes 196616 | tf_op jit(solution)/shard_map/ppermute | solution.py:94
  29.4 34.0 %copy-start.4 = (f32[40,4352]{1,0:T(8,128)S(1)}, f32[40,4352]{1,0:T(8,128)}, u32[]{:S(2)}) copy-start(f32[40,4352]{1,0:T(8,128)} %param.14) | copy-start | bytes 2088964
  29.5 20.2 %collective-permute-start.5 = (bf16[128,128]{1,0:T(8,128)(2,1)S(1)}, bf16[128,128]{1,0:T(8,128)(2,1)S(1)}, u32[]{:S(2)}, u32[]{:S(2)}) collective-permute-start(bf16[128,128]{1,0:T(8,128)(2,1)S(1)} %get-tuple-element.17), channel_id=1, source_target_pairs={{8,16},{16,8},{9,17},{17,9},{10,18},{18,10},{11,19},{19,11},{12,20... | collective-permute-start | bytes 98312 | tf_op jit(solution)/shard_map/ppermute | solution.py:94
  30.3 19.4 %collective-permute-start.6 = (bf16[128,128]{1,0:T(8,128)(2,1)S(1)}, bf16[128,128]{1,0:T(8,128)(2,1)S(1)}, u32[]{:S(2)}, u32[]{:S(2)}) collective-permute-start(bf16[128,128]{1,0:T(8,128)(2,1)S(1)} %get-tuple-element.18), channel_id=1, source_target_pairs={{0,8},{16,24},{8,0},{24,16},{1,9},{17,25},{9,1},{25,17},{2,10},{18... | collective-permute-start | bytes 98312 | tf_op jit(solution)/shard_map/ppermute | solution.py:94
  36.9 25.3 %all-to-all-start = ((f32[32,40,128]{2,1,0:T(8,128)}), f32[32,40,128]{2,1,0:T(8,128)S(1)}, u32[]{:S(2)}, u32[]{:S(2)}) async-start(f32[32,40,128]{2,1,0:T(8,128)} %broadcast_in_dim.31), calls=%async_computation | async-start | bytes 1310720 | tf_op jit(solution)/shard_map/all_to_all | solution.py:159
  44.3 21.1 %copy-start.5 = (s32[6,128]{1,0:T(8,128)S(1)}, s32[6,128]{1,0:T(8,128)}, u32[]{:S(2)}) copy-start(s32[6,128]{1,0:T(8,128)} %param.12) | copy-start | bytes 9220
  44.3 5.5 %collective-permute-start.7 = (bf16[128,128]{1,0:T(8,128)(2,1)S(1)}, bf16[128,128]{1,0:T(8,128)(2,1)S(1)}, u32[]{:S(2)}, u32[]{:S(2)}) collective-permute-start(bf16[128,128]{1,0:T(8,128)(2,1)S(1)} %get-tuple-element.15), channel_id=1, source_target_pairs={{2,4},{4,2},{3,5},{5,3},{10,12},{12,10},{11,13},{13,11},{18,20},{2... | collective-permute-start | bytes 98312 | tf_op jit(solution)/shard_map/ppermute | solution.py:94
  45.2 9.2 %collective-permute-start.8 = (bf16[128,128]{1,0:T(8,128)(2,1)S(1)}, bf16[128,128]{1,0:T(8,128)(2,1)S(1)}, u32[]{:S(2)}, u32[]{:S(2)}) collective-permute-start(bf16[128,128]{1,0:T(8,128)(2,1)S(1)} %get-tuple-element.16), channel_id=1, source_target_pairs={{0,2},{4,6},{2,0},{6,4},{1,3},{5,7},{3,1},{7,5},{8,10},{12,14},{10... | collective-permute-start | bytes 98312 | tf_op jit(solution)/shard_map/ppermute | solution.py:94
  49.7 4.7 %collective-permute-start.9 = (bf16[128,128]{1,0:T(8,128)(2,1)S(1)}, bf16[128,128]{1,0:T(8,128)(2,1)S(1)}, u32[]{:S(2)}, u32[]{:S(2)}) collective-permute-start(bf16[128,128]{1,0:T(8,128)(2,1)S(1)} %get-tuple-element.14), channel_id=1, source_target_pairs={{0,1},{1,0},{2,3},{3,2},{4,5},{5,4},{6,7},{7,6},{8,9},{9,8},{10,11... | collective-permute-start | bytes 98312 | tf_op jit(solution)/shard_map/ppermute | solution.py:94

commit v10 on v8

--- a/solution.py
+++ b/solution.py
@@ -78,6 +78,11 @@
             pltpu.VMEM((blocks_n, nrhs_here, block_w), jnp.float32),
         ],
         compiler_params=pltpu.CompilerParams(vmem_limit_bytes=48 * 1024 * 1024),
+        cost_estimate=pl.CostEstimate(
+            flops=4 * (2 * blocks_n - 1) * nrhs_here * block_w * block_w,
+            transcendentals=0,
+            bytes_accessed=2 * (diag_inverse.size + coupling.size) + 6 * residual.size,
+        ),
     )(parent, residual, slots, diag_inverse, coupling, after)
 
 
@@ -157,9 +162,11 @@
     held = coeffs_t.reshape((1,) * len(AXES) + coeffs_t.shape)
 
     outgoing = jnp.take(residual, send_rows, axis=1)
+    last = len(AXES) - 1
+    late = lax.axis_size(AXES[last]) == 2
     incoming = []
     for axis_pos, axis in enumerate(AXES):
-        ride = axis_pos == 0 and doubling(axis)
+        ride = axis_pos < last and doubling(axis)
         low, high, got = halo_out(
             outgoing[:, 2 * axis_pos],
             outgoing[:, 2 * axis_pos + 1],
@@ -167,24 +174,11 @@
             rows_of(held) if ride else None,
         )
         incoming += [low, high]
-        if axis_pos == 0:
-            if ride:
-                held = gather_axis(merge(held, got.reshape(held.shape), axis, 0, 1), axis, 0, 2)
-            else:
-                held = gather_axis(held, axis, 0)
-    after = held
-    for axis_pos in range(1, len(AXES) - 1):
-        axis = AXES[axis_pos]
-        if doubling(axis):
-            held = merge(held, lax.ppermute(held, axis, matchings(lax.axis_size(axis))[0]), axis, axis_pos, 1)
-            after = held
-            held = gather_axis(held, axis, axis_pos, 2)
-        else:
+        if ride:
+            held = gather_axis(merge(held, got.reshape(held.shape), axis, axis_pos, 1), axis, axis_pos, 2)
+        elif axis_pos < last or not late:
             held = gather_axis(held, axis, axis_pos)
-    last = len(AXES) - 1
-    late = lax.axis_size(AXES[last]) == 2
-    if not late:
-        held = gather_axis(held, AXES[last], last)
+    after = coeffs_t
     slots = jnp.concatenate(incoming, axis=1)
 
     own, zslots = local_solve(parent, residual, slots, diag_inverse, coupling, after)

time: 67.2 us -> 66.6 us (level)
  the two profiles are of different devices: /device:TPU:4 before, /device:TPU:0 now
where the time goes in v10:
time: 66.6 us; the launch traced here: 65.8 us
  starting transfers between devices  18.6 us (28%)
  Pallas kernels  13.2 us (20%)
  waiting for transfers between devices  12.2 us (18%)
  matrix products  10.2 us (15%)
  local copies, waits for them, and re-layouts  7.38 us (11%)
  other arithmetic  3.19 us (5%)
  between operations  1.03 us (2%)
    pallas_call x1, Pallas kernels, local_solve(): pl.pallas_call(solve_kernel, out_shape=(jax.ShapeDtypeStruct((nrhs_here,...  13.2 us
    ppermute x3, starting transfers between devices, swap(): got = lax.ppermute(packed, axis, pairs)  7.11 us
    ppermute x7, starting transfers between devices, swap(): return (lax.ppermute(value, axis, pairs), None)  6.4 us
    ppermute x3, waiting for transfers between devices, swap(): got = lax.ppermute(packed, axis, pairs)  6.3 us
    ppermute x2, waiting for transfers between devices, gather_axis(): held = merge(held, lax.ppermute(held, axis, pairs), axis, dim, step)  5.49 us
    ppermute x2, starting transfers between devices, gather_axis(): held = merge(held, lax.ppermute(held, axis, pairs), axis, dim, step)  5.09 us
    gather x2, local copies, waits for them, and re-layouts, per_device(): outgoing = jnp.take(residual, send_rows, axis=1)  4.26 us
    dot_general x1, matrix products, per_device(): lax.dot_general(solved_t, vectors, (((0,), (0,)), ((), ())), precision=la...  3.6 us
  transfers between devices with their start and end apart: 12, of which 6 were waited for; matrix products, arithmetic and copies ran while one was open for 0% of the time, Pallas kernels for 0%

profile of v10, /device:TPU:0, one launch (start us, length us, event | category | flops | bytes accessed | tf_op | source)
XLA Modules:
  0.0 65.8 jit_solution(5697594640161042341)
XLA Ops:
  0.0 0.7 %compare_and_fusion = pred[6,128]{1,0:T(8,128)(4,1)S(1)} fusion(s32[6,128]{1,0:T(8,128)} %param.12), kind=kLoop, calls=%fused_computation.57 | loop fusion | flops 4608 | bytes 3840 | tf_op jit(solution)/shard_map/jit(_take)/and | solution.py:164
  0.7 0.7 %fusion.12 = s32[768]{0:T(1024)S(1)} fusion(s32[6,128]{1,0:T(8,128)} %param.12), kind=kLoop, calls=%fused_computation.58 | loop fusion | flops 2304 | bytes 6144 | tf_op jit(solution)/shard_map/jit(_take)/broadcast_in_dim | solution.py:164
  2.1 3.0 %copy.13 = f32[128,4352]{0,1:T(8,128)} copy(f32[128,4352]{1,0:T(8,128)} %res_ref.1) | data formatting | bytes 4456448 | tf_op args[0]
  5.1 3.3 %gather_fusion = f32[768,128]{1,0:T(8,128)S(1)} fusion(f32[128,4352]{0,1:T(8,128)} %copy.13, s32[1024]{0:T(1024)S(1)} %pad_clamp_fusion), kind=kCustom, calls=%fused_computation | custom fusion | bytes 789504 | tf_op jit(solution)/shard_map/jit(_take)/gather | solution.py:164
  8.4 0.9 %copy.14 = f32[6,128,128]{1,2,0:T(8,128)} copy(f32[6,128,128]{2,1,0:T(8,128)S(1)} %bitcast.44) | data formatting | bytes 786432 | tf_op jit(solution)/shard_map/jit(_take)/gather | solution.py:164
  9.4 2.3 %fusion.3.after_ref = f32[40,128]{1,0:T(8,128)S(1)} fusion(f32[128,4352]{1,0:T(8,128)S(1)} %copy-done.1, f32[40,4352]{1,0:T(8,128)S(1)} %copy-done.3, f32[40]{0:T(128)S(1)} %compare_convert_fusion), kind=kOutput, calls=%fused_computation.7 | convolution fusion | flops 267560960 | bytes 2945184 | tf_op jit(solution)/shard_map/dot_general | solution.py:159
  11.8 0.7 %fusion.10 = (f32[128,128]{1,0:T(8,128)}, f32[128,128]{1,0:T(8,128)S(1)}, f32[128,128]{1,0:T(8,128)}, f32[128,128]{1,0:T(8,128)S(1)}, f32[128,128]{1,0:T(8,128)}) fusion(f32[128,6,128]{2,0,1:T(8,128)S(1)} %select_bitcast_fusion, pred[]{:T(512)S(6)} %eq.51, pred[]{:T(512)S(6)} %eq.49, pred[]{:T(512)S(6)} %eq.48), kind=kLoop, calls=%fused_computation.28 | loop fusion | flops 81920 | bytes 720899 | tf_op jit(solution)/shard_map/jit(_where)/select_n | solution.py:109
  13.1 3.0 %collective-permute-start = (f32[168,128]{1,0:T(8,128)}, f32[168,128]{1,0:T(8,128)S(1)}, u32[]{:S(2)}, u32[]{:S(2)}) collective-permute-start(f32[168,128]{1,0:T(8,128)} %pad_maximum_fusion.6), channel_id=1, source_target_pairs={{0,8},{16,24},{8,0},{24,16},{1,9},{17,25},{9,1},{25,17},{2,10},{18... | collective-permute-start | bytes 258056 | tf_op jit(solution)/shard_map/ppermute | solution.py:102
  16.8 0.7 %collective-permute-start.1 = (f32[128,128]{1,0:T(8,128)}, f32[128,128]{1,0:T(8,128)S(1)}, u32[]{:S(2)}, u32[]{:S(2)}) collective-permute-start(f32[128,128]{1,0:T(8,128)} %get-tuple-element.13), channel_id=1, source_target_pairs={{8,16},{16,8},{9,17},{17,9},{10,18},{18,10},{11,19},{19,11},{12,20... | collective-permute-start | bytes 196616 | tf_op jit(solution)/shard_map/ppermute | solution.py:99
  17.5 1.3 %collective-permute-done = f32[168,128]{1,0:T(8,128)S(1)} collective-permute-done((f32[168,128]{1,0:T(8,128)}, f32[168,128]{1,0:T(8,128)S(1)}, u32[]{:S(2)}, u32[]{:S(2)}) %collective-permute-start) | collective-permute-done | bytes 86048 | tf_op jit(solution)/shard_map/ppermute | solution.py:102
  18.9 3.0 %collective-permute-start.2 = (f32[2,1,1,40,128]{4,3,0,2,1:T(8,128)S(1)}, f32[2,1,1,40,128]{4,3,0,2,1:T(8,128)S(1)}, u32[]{:S(2)}, u32[]{:S(2)}) collective-permute-start(f32[2,1,1,40,128]{4,3,0,2,1:T(8,128)S(1)} %maximum_select_fusion.5), channel_id=1, source_target_pairs={{0,16},{8,24},{16,0},{24,8},{1,17},{9,25},{17,1},{25,9},{2,18},{10... | collective-permute-start | bytes 122888 | tf_op jit(solution)/shard_map/ppermute | solution.py:142
  22.0 3.2 %collective-permute-done.2 = f32[2,1,1,40,128]{4,3,0,2,1:T(8,128)S(1)} collective-permute-done((f32[2,1,1,40,128]{4,3,0,2,1:T(8,128)S(1)}, f32[2,1,1,40,128]{4,3,0,2,1:T(8,128)S(1)}, u32[]{:S(2)}, u32[]{:S(2)}) %collective-permute-start.2) | collective-permute-done | bytes 40992 | tf_op jit(solution)/shard_map/ppermute | solution.py:142
  25.2 4.0 %collective-permute-start.3 = (f32[288,128]{1,0:T(8,128)S(1)}, f32[288,128]{1,0:T(8,128)S(1)}, u32[]{:S(2)}, u32[]{:S(2)}) collective-permute-start(f32[288,128]{1,0:T(8,128)S(1)} %pad_maximum_fusion.5), channel_id=1, source_target_pairs={{0,2},{4,6},{2,0},{6,4},{1,3},{5,7},{3,1},{7,5},{8,10},{12,14},{10... | collective-permute-start | bytes 442376 | tf_op jit(solution)/shard_map/ppermute | solution.py:102
  29.2 3.7 %collective-permute-done.3 = f32[288,128]{1,0:T(8,128)S(1)} collective-permute-done((f32[288,128]{1,0:T(8,128)S(1)}, f32[288,128]{1,0:T(8,128)S(1)}, u32[]{:S(2)}, u32[]{:S(2)}) %collective-permute-start.3) | collective-permute-done | bytes 147488 | tf_op jit(solution)/shard_map/ppermute | solution.py:102
  33.0 13.2 %shard_map.82 = (bf16[128,4352]{1,0:T(8,128)(2,1)S(1)}, bf16[128,768]{1,0:T(8,128)(2,1)S(1)}) custom-call(s32[20]{0:T(128)S(1)} %copy-done.2, f32[128,4352]{1,0:T(8,128)S(1)} %copy-done.1, f32[128,768]{1,0:T(8,128)S(1)} %select_dynamic-update-slice_fusion.slot_ref, bf16[20,256,256]{2,1,0:T(8,128)(2,1)} %inv_ref.1, bf16[19,256,256]{2,1,0:T(8,128)(2,1)} %cpl_ref.1, ...), custom_call_target="tpu_custom_call" | custom-call | flops 1308622848 | bytes 8454144 | tf_op jit(solution)/shard_map/pallas_call | solution.py:61
  46.2 0.7 %collective-permute-start.6 = (bf16[128,128]{1,0:T(8,128)(2,1)S(1)}, bf16[128,128]{1,0:T(8,128)(2,1)S(1)}, u32[]{:S(2)}, u32[]{:S(2)}) collective-permute-start(bf16[128,128]{1,0:T(8,128)(2,1)S(1)} %get-tuple-element.16), channel_id=1, source_target_pairs={{8,16},{16,8},{9,17},{17,9},{10,18},{18,10},{11,19},{19,11},{12,20... | collective-permute-start | bytes 98312 | tf_op jit(solution)/shard_map/ppermute | solution.py:99
  46.9 3.5 %collective-permute-start.7 = (bf16[128,128]{1,0:T(8,128)(2,1)S(1)}, bf16[128,128]{1,0:T(8,128)(2,1)S(1)}, u32[]{:S(2)}, u32[]{:S(2)}) collective-permute-start(bf16[128,128]{1,0:T(8,128)(2,1)S(1)} %get-tuple-element.17), channel_id=1, source_target_pairs={{0,8},{16,24},{8,0},{24,16},{1,9},{17,25},{9,1},{25,17},{2,10},{18... | collective-permute-start | bytes 98312 | tf_op jit(solution)/shard_map/ppermute | solution.py:99
  50.4 2.1 %collective-permute-start.10 = (f32[4,2,1,40,128]{4,3,0,1,2:T(8,128)S(1)}, f32[4,2,1,40,128]{4,3,0,1,2:T(8,128)S(1)}, u32[]{:S(2)}, u32[]{:S(2)}) collective-permute-start(f32[4,2,1,40,128]{4,3,0,1,2:T(8,128)S(1)} %maximum_select_fusion.1), channel_id=1, source_target_pairs={{0,4},{2,6},{4,0},{6,2},{1,5},{3,7},{5,1},{7,3},{8,12},{10,14},{12... | collective-permute-start | bytes 491528 | tf_op jit(solution)/shard_map/ppermute | solution.py:142
  52.6 0.8 %collective-permute-start.8 = (bf16[128,128]{1,0:T(8,128)(2,1)S(1)}, bf16[128,128]{1,0:T(8,128)(2,1)S(1)}, u32[]{:S(2)}, u32[]{:S(2)}) collective-permute-start(bf16[128,128]{1,0:T(8,128)(2,1)S(1)} %get-tuple-element.18), channel_id=1, source_target_pairs={{2,4},{4,2},{3,5},{5,3},{10,12},{12,10},{11,13},{13,11},{18,20},{2... | collective-permute-start | bytes 98312 | tf_op jit(solution)/shard_map/ppermute | solution.py:99
  53.5 2.3 %collective-permute-done.10 = f32[4,2,1,40,128]{4,3,0,1,2:T(8,128)S(1)} collective-permute-done((f32[4,2,1,40,128]{4,3,0,1,2:T(8,128)S(1)}, f32[4,2,1,40,128]{4,3,0,1,2:T(8,128)S(1)}, u32[]{:S(2)}, u32[]{:S(2)}) %collective-permute-start.10) | collective-permute-done | bytes 163872 | tf_op jit(solution)/shard_map/ppermute | solution.py:142
  56.4 1.3 %collective-permute-done.11 = f32[768,128]{1,0:T(8,128)S(1)} collective-permute-done((f32[768,128]{1,0:T(8,128)S(1)}, f32[768,128]{1,0:T(8,128)S(1)}, u32[]{:S(2)}, u32[]{:S(2)}) %collective-permute-start.11) | collective-permute-done | bytes 393248 | tf_op jit(solution)/shard_map/ppermute | solution.py:102
  57.8 1.2 %fusion.13 = f32[128,40]{1,0:T(8,128)S(1)} fusion(f32[1280,128]{1,0:T(8,128)S(1)} %bitcast.43, f32[40,1280]{1,0:T(8,128)S(1)} %copy-done), kind=kOutput, calls=%fused_computation.60 | convolution fusion | flops 78643200 | bytes 880640 | tf_op jit(solution)/shard_map/dot_general | solution.py:200
  59.1 3.0 %fusion = f32[128,4352]{1,0:T(8,128)S(1)} fusion(bf16[128,768]{1,0:T(8,128)(2,1)S(1)} %select_dynamic-update-slice_fusion.6, s32[768]{0:T(1024)S(1)} %bitcast.52), kind=kOutput, calls=%fused_computation.2 | convolution fusion | flops 858980352 | bytes 2427904 | tf_op jit(solution)/shard_map/dot_general | solution.py:206
  62.2 3.6 %convolution_add_fusion = f32[128,4352]{1,0:T(8,128)} fusion(f32[128,40]{1,0:T(8,128)S(1)} %fusion.13, f32[128,4352]{1,0:T(8,128)S(1)} %fusion, bf16[128,4352]{1,0:T(8,128)(2,1)S(1)} %get-tuple-element.7, f32[40,4352]{1,0:T(8,128)S(1)} %copy-done.3, f32[40]{0:T(128)S(1)} %compare_convert_fusion), kind=kOutput, calls=%fused_computation.4 | convolution fusion | flops 269232128 | bytes 6287520 | tf_op jit(solution)/shard_map/dot_general | solution.py:207
  (55 shorter events, 2.5 us)
Async XLA Ops:
  0.0 57.8 %copy-start = (f32[40,1280]{1,0:T(8,128)S(1)}, f32[40,1280]{1,0:T(8,128)}, u32[]{:S(2)}) copy-start(f32[40,1280]{1,0:T(8,128)} %param.15) | copy-start | bytes 614404
  5.1 4.3 %copy-start.1 = (f32[128,4352]{1,0:T(8,128)S(1)}, f32[128,4352]{1,0:T(8,128)}, u32[]{:S(2)}) copy-start(f32[128,4352]{1,0:T(8,128)} %res_ref.1) | copy-start | bytes 6684676
  5.1 4.3 %copy-start.3 = (f32[40,4352]{1,0:T(8,128)S(1)}, f32[40,4352]{1,0:T(8,128)}, u32[]{:S(2)}) copy-start(f32[40,4352]{1,0:T(8,128)} %param.14) | copy-start | bytes 2088964
  9.4 2.4 %copy-start.4 = (f32[6,128,128]{1,2,0:T(8,128)S(1)}, f32[6,128,128]{1,2,0:T(8,128)}, u32[]{:S(2)}) copy-start(f32[6,128,128]{1,2,0:T(8,128)} %copy.14) | copy-start | bytes 1179652
  11.7 21.3 %copy-start.2 = (s32[20]{0:T(128)S(1)}, s32[20]{0:T(128)}, u32[]{:S(2)}) copy-start(s32[20]{0:T(128)} %parent_ref.1) | copy-start | bytes 244
  13.1 5.8 %collective-permute-start = (f32[168,128]{1,0:T(8,128)}, f32[168,128]{1,0:T(8,128)S(1)}, u32[]{:S(2)}, u32[]{:S(2)}) collective-permute-start(f32[168,128]{1,0:T(8,128)} %pad_maximum_fusion.6), channel_id=1, source_target_pairs={{0,8},{16,24},{8,0},{24,16},{1,9},{17,25},{9,1},{25,17},{2,10},{18... | collective-permute-start | bytes 258056 | tf_op jit(solution)/shard_map/ppermute | solution.py:102
  16.1 16.8 %collective-permute-start.5 = (f32[128,128]{1,0:T(8,128)}, f32[128,128]{1,0:T(8,128)S(1)}, u32[]{:S(2)}, u32[]{:S(2)}) collective-permute-start(f32[128,128]{1,0:T(8,128)} %get-tuple-element.9), channel_id=1, source_target_pairs={{0,1},{1,0},{2,3},{3,2},{4,5},{5,4},{6,7},{7,6},{8,9},{9,8},{10,11... | collective-permute-start | bytes 196616 | tf_op jit(solution)/shard_map/ppermute | solution.py:99
  16.1 13.1 %collective-permute-start.4 = (f32[128,128]{1,0:T(8,128)}, f32[128,128]{1,0:T(8,128)S(1)}, u32[]{:S(2)}, u32[]{:S(2)}) collective-permute-start(f32[128,128]{1,0:T(8,128)} %get-tuple-element.11), channel_id=1, source_target_pairs={{2,4},{4,2},{3,5},{5,3},{10,12},{12,10},{11,13},{13,11},{18,20},{2... | collective-permute-start | bytes 196616 | tf_op jit(solution)/shard_map/ppermute | solution.py:99
  16.8 5.1 %collective-permute-start.1 = (f32[128,128]{1,0:T(8,128)}, f32[128,128]{1,0:T(8,128)S(1)}, u32[]{:S(2)}, u32[]{:S(2)}) collective-permute-start(f32[128,128]{1,0:T(8,128)} %get-tuple-element.13), channel_id=1, source_target_pairs={{8,16},{16,8},{9,17},{17,9},{10,18},{18,10},{11,19},{19,11},{12,20... | collective-permute-start | bytes 196616 | tf_op jit(solution)/shard_map/ppermute | solution.py:99
  18.9 6.3 %collective-permute-start.2 = (f32[2,1,1,40,128]{4,3,0,2,1:T(8,128)S(1)}, f32[2,1,1,40,128]{4,3,0,2,1:T(8,128)S(1)}, u32[]{:S(2)}, u32[]{:S(2)}) collective-permute-start(f32[2,1,1,40,128]{4,3,0,2,1:T(8,128)S(1)} %maximum_select_fusion.5), channel_id=1, source_target_pairs={{0,16},{8,24},{16,0},{24,8},{1,17},{9,25},{17,1},{25,9},{2,18},{10... | collective-permute-start | bytes 122888 | tf_op jit(solution)/shard_map/ppermute | solution.py:142
  25.2 7.7 %collective-permute-start.3 = (f32[288,128]{1,0:T(8,128)S(1)}, f32[288,128]{1,0:T(8,128)S(1)}, u32[]{:S(2)}, u32[]{:S(2)}) collective-permute-start(f32[288,128]{1,0:T(8,128)S(1)} %pad_maximum_fusion.5), channel_id=1, source_target_pairs={{0,2},{4,6},{2,0},{6,4},{1,3},{5,7},{3,1},{7,5},{8,10},{12,14},{10... | collective-permute-start | bytes 442376 | tf_op jit(solution)/shard_map/ppermute | solution.py:102
  46.2 7.2 %collective-permute-start.6 = (bf16[128,128]{1,0:T(8,128)(2,1)S(1)}, bf16[128,128]{1,0:T(8,128)(2,1)S(1)}, u32[]{:S(2)}, u32[]{:S(2)}) collective-permute-start(bf16[128,128]{1,0:T(8,128)(2,1)S(1)} %get-tuple-element.16), channel_id=1, source_target_pairs={{8,16},{16,8},{9,17},{17,9},{10,18},{18,10},{11,19},{19,11},{12,20... | collective-permute-start | bytes 98312 | tf_op jit(solution)/shard_map/ppermute | solution.py:99
  46.9 6.5 %collective-permute-start.7 = (bf16[128,128]{1,0:T(8,128)(2,1)S(1)}, bf16[128,128]{1,0:T(8,128)(2,1)S(1)}, u32[]{:S(2)}, u32[]{:S(2)}) collective-permute-start(bf16[128,128]{1,0:T(8,128)(2,1)S(1)} %get-tuple-element.17), channel_id=1, source_target_pairs={{0,8},{16,24},{8,0},{24,16},{1,9},{17,25},{9,1},{25,17},{2,10},{18... | collective-permute-start | bytes 98312 | tf_op jit(solution)/shard_map/ppermute | solution.py:99
  50.4 5.4 %collective-permute-start.10 = (f32[4,2,1,40,128]{4,3,0,1,2:T(8,128)S(1)}, f32[4,2,1,40,128]{4,3,0,1,2:T(8,128)S(1)}, u32[]{:S(2)}, u32[]{:S(2)}) collective-permute-start(f32[4,2,1,40,128]{4,3,0,1,2:T(8,128)S(1)} %maximum_select_fusion.1), channel_id=1, source_target_pairs={{0,4},{2,6},{4,0},{6,2},{1,5},{3,7},{5,1},{7,3},{8,12},{10,14},{12... | collective-permute-start | bytes 491528 | tf_op jit(solution)/shard_map/ppermute | solution.py:142
  52.5 3.9 %collective-permute-start.9 = (bf16[128,128]{1,0:T(8,128)(2,1)S(1)}, bf16[128,128]{1,0:T(8,128)(2,1)S(1)}, u32[]{:S(2)}, u32[]{:S(2)}) collective-permute-start(bf16[128,128]{1,0:T(8,128)(2,1)S(1)} %get-tuple-element.14), channel_id=1, source_target_pairs={{0,2},{4,6},{2,0},{6,4},{1,3},{5,7},{3,1},{7,5},{8,10},{12,14},{10... | collective-permute-start | bytes 98312 | tf_op jit(solution)/shard_map/ppermute | solution.py:99
  52.6 3.8 %collective-permute-start.8 = (bf16[128,128]{1,0:T(8,128)(2,1)S(1)}, bf16[128,128]{1,0:T(8,128)(2,1)S(1)}, u32[]{:S(2)}, u32[]{:S(2)}) collective-permute-start(bf16[128,128]{1,0:T(8,128)(2,1)S(1)} %get-tuple-element.18), channel_id=1, source_target_pairs={{2,4},{4,2},{3,5},{5,3},{10,12},{12,10},{11,13},{13,11},{18,20},{2... | collective-permute-start | bytes 98312 | tf_op jit(solution)/shard_map/ppermute | solution.py:99
  55.9 1.8 %collective-permute-start.11 = (f32[768,128]{1,0:T(8,128)S(1)}, f32[768,128]{1,0:T(8,128)S(1)}, u32[]{:S(2)}, u32[]{:S(2)}) collective-permute-start(f32[768,128]{1,0:T(8,128)S(1)} %pad_maximum_fusion), channel_id=1, source_target_pairs={{0,1},{1,0},{2,3},{3,2},{4,5},{5,4},{6,7},{7,6},{8,9},{9,8},{10,11... | collective-permute-start | bytes 1179656 | tf_op jit(solution)/shard_map/ppermute | solution.py:102
  56.4 2.7 %copy-start.5 = (s32[6,128]{1,0:T(8,128)S(1)}, s32[6,128]{1,0:T(8,128)}, u32[]{:S(2)}) copy-start(s32[6,128]{1,0:T(8,128)} %param.12) | copy-start | bytes 9220

commit v11 on v10

--- a/solution.py
+++ b/solution.py
@@ -84,6 +84,43 @@
             bytes_accessed=2 * (diag_inverse.size + coupling.size) + 6 * residual.size,
         ),
     )(parent, residual, slots, diag_inverse, coupling, after)
+
+
+def split3(value):
+    first = value.astype(jnp.bfloat16)
+    rest = value - first.astype(jnp.float32)
+    second = rest.astype(jnp.bfloat16)
+    third = (rest - second.astype(jnp.float32)).astype(jnp.bfloat16)
+    return first, second, third
+
+
+def finish_kernel(rows_ref, own_ref, back_ref, solved_ref, vec_ref, out_ref):
+    owned_n = own_ref.shape[1]
+    chunk = 256
+    rows = rows_ref[...]
+    back = back_ref[...]
+    s1, s2, s3 = split3(solved_ref[...])
+    for start in range(0, owned_n, chunk):
+        cols = pl.ds(start, chunk)
+        here = lax.broadcasted_iota(jnp.int32, (rows.shape[0], chunk), 1) + start
+        onehot = (rows == here).astype(jnp.bfloat16)
+        total = own_ref[:, cols].astype(jnp.float32)
+        total += jnp.dot(back, onehot, preferred_element_type=jnp.float32)
+        v1, v2, v3 = split3(vec_ref[:, cols])
+        for left, right in ((s1, v1), (s1, v2), (s2, v1), (s1, v3), (s3, v1), (s2, v2)):
+            total += jnp.dot(left, right, preferred_element_type=jnp.float32)
+        out_ref[:, cols] = total
+
+
+def finish(send_rows, own, returned, solved, vectors):
+    vmem = pltpu.VMEM
+    return pl.pallas_call(
+        finish_kernel,
+        out_shape=jax.ShapeDtypeStruct(own.shape, jnp.float32),
+        in_specs=[pl.BlockSpec(memory_space=vmem)] * 5,
+        out_specs=pl.BlockSpec(memory_space=vmem),
+        compiler_params=pltpu.CompilerParams(vmem_limit_bytes=48 * 1024 * 1024),
+    )(send_rows.reshape(-1, 1), own, returned, solved, vectors)
 
 
 def matchings(count):
@@ -197,21 +234,14 @@
             held = merge(held, got.reshape(held.shape), axis, last, 1)
     returned = jnp.concatenate(returned, axis=1)
 
-    solved_t = jnp.dot(
-        coarse_inverse, rows_of(held), precision=lax.Precision.HIGHEST, preferred_element_type=jnp.float32
-    )
-    onehot = (
-        send_rows.reshape(slots_n * face_w, 1) == lax.iota(jnp.int32, owned_n)[None, :]
-    ).astype(jnp.bfloat16)
-    faces = jnp.dot(returned, onehot, preferred_element_type=jnp.float32)
-    coarse = lax.dot_general(
-        solved_t,
-        vectors,
-        (((0,), (0,)), ((), ())),
+    solved = lax.dot_general(
+        rows_of(held),
+        coarse_inverse,
+        (((0,), (1,)), ((), ())),
         precision=lax.Precision.HIGHEST,
         preferred_element_type=jnp.float32,
     )
-    return own.astype(jnp.float32) + faces + coarse
+    return finish(send_rows, own, returned, solved, vectors)
 
 
 def solution(mesh):

time: 66.6 us -> 70.1 us (1.053)
  matrix products: 10.2 us -> 3.55 us
  other arithmetic: 3.19 us -> 9.68 us
  waiting for transfers between devices: 12.2 us -> 6.67 us
  starting transfers between devices: 18.6 us -> 23 us
  Pallas kernels: 13.2 us -> 17.3 us
  local copies, waits for them, and re-layouts: 7.38 us -> 8.29 us
    dot_general x3 -> x1, matrix products: 7.84 us -> 1.21 us  [per_device(): lax.dot_general(rows_of(held), coarse_inverse, (((0,), (1,)), ((), ())),...]
    ppermute x7, starting transfers between devices: 6.4 us -> 11.1 us  [swap(): return (lax.ppermute(value, axis, pairs), None)]
    ppermute x2, waiting for transfers between devices: 5.49 us -> 0.99 us  [gather_axis(): held = merge(held, lax.ppermute(held, axis, pairs), axis, dim, step)]
    pallas_call x0 -> x1, Pallas kernels: none -> 4.18 us  [finish(): pl.pallas_call(finish_kernel, out_shape=jax.ShapeDtypeStruct(own.shape, j...]
    unnamed x10, other arithmetic: 0.16 us -> 3.57 us
    ppermute x3, waiting for transfers between devices: 6.3 us -> 3.79 us  [swap(): got = lax.ppermute(packed, axis, pairs)]
    ppermute x7, waiting for transfers between devices: 0.4 us -> 1.89 us  [swap(): return (lax.ppermute(value, axis, pairs), None)]
    mul x0 -> x1, other arithmetic: none -> 1.21 us  [per_device(): vectors = deflation * mask[:, None]]
  transfers between devices with their start and end apart: 12 -> 12, of which waited for: 6 -> 4; matrix products, arithmetic and copies ran while one was open for 0% -> 7% of each run, Pallas kernels for 0% -> 0%
where the time goes in v11:
time: 70.1 us; the launch traced here: 69.5 us
  starting transfers between devices  23 us (33%)
  Pallas kernels  17.3 us (25%)
  other arithmetic  9.68 us (14%)
  local copies, waits for them, and re-layouts  8.29 us (12%)
  waiting for transfers between devices  6.67 us (10%)
  matrix products  3.55 us (5%)
  between operations  0.93 us (1%)
    pallas_call x1, Pallas kernels, local_solve(): pl.pallas_call(solve_kernel, out_shape=(jax.ShapeDtypeStruct((nrhs_here,...  13.1 us
    ppermute x7, starting transfers between devices, swap(): return (lax.ppermute(value, axis, pairs), None)  11.1 us
    ppermute x3, starting transfers between devices, swap(): got = lax.ppermute(packed, axis, pairs)  6.51 us
    ppermute x2, starting transfers between devices, gather_axis(): held = merge(held, lax.ppermute(held, axis, pairs), axis, dim, step)  5.35 us
    pallas_call x1, Pallas kernels, finish(): pl.pallas_call(finish_kernel, out_shape=jax.ShapeDtypeStruct(own.shape, j...  4.18 us
    gather x2, local copies, waits for them, and re-layouts, per_device(): outgoing = jnp.take(residual, send_rows, axis=1)  4.11 us
    ppermute x3, waiting for transfers between devices, swap(): got = lax.ppermute(packed, axis, pairs)  3.79 us
    unnamed x10, other arithmetic  3.57 us
  transfers between devices with their start and end apart: 12, of which 4 were waited for; matrix products, arithmetic and copies ran while one was open for 7% of the time, Pallas kernels for 0%

profile of v11, /device:TPU:0, one launch (start us, length us, event | category | flops | bytes accessed | tf_op | source)
XLA Modules:
  0.0 69.5 jit_solution(11464486763175985386)
XLA Ops:
  2.1 3.1 %copy.16 = f32[128,4352]{0,1:T(8,128)} copy(f32[128,4352]{1,0:T(8,128)} %res_ref.1) | data formatting | bytes 4456448 | tf_op args[0]
  5.3 1.2 %broadcast_multiply_fusion.vec_ref = f32[40,4352]{1,0:T(8,128)S(1)} fusion(f32[40,4352]{1,0:T(8,128)} %param.14, f32[40]{0:T(128)S(1)} %compare_convert_fusion), kind=kLoop, calls=%fused_computation.8 | loop fusion | flops 174080 | bytes 1392800 | tf_op jit(solution)/shard_map/mul | solution.py:195
  6.5 2.3 %fusion.6.after_ref = f32[40,128]{1,0:T(8,128)S(1)} fusion(f32[40,4352]{1,0:T(8,128)S(1)} %broadcast_multiply_fusion.vec_ref, f32[128,4352]{1,0:T(8,128)S(1)} %copy-done.1), kind=kOutput, calls=%fused_computation.53 | convolution fusion | flops 267386880 | bytes 2945024 | tf_op jit(solution)/shard_map/dot_general | solution.py:196
  8.8 3.2 %gather_fusion = f32[768,128]{1,0:T(8,128)S(1)} fusion(f32[128,4352]{0,1:T(8,128)} %copy.16, s32[1024]{0:T(1024)S(1)} %pad_clamp_fusion), kind=kCustom, calls=%fused_computation | custom fusion | bytes 789504 | tf_op jit(solution)/shard_map/jit(_take)/gather | solution.py:201
  12.0 0.9 %copy.17 = f32[6,128,128]{1,2,0:T(8,128)} copy(f32[6,128,128]{2,1,0:T(8,128)S(1)} %bitcast.52) | data formatting | bytes 786432 | tf_op jit(solution)/shard_map/jit(_take)/gather | solution.py:201
  13.0 1.0 %select_bitcast_fusion = f32[128,6,128]{2,0,1:T(8,128)S(1)} fusion(f32[6,128,128]{1,2,0:T(8,128)} %copy.17, pred[6,128]{1,0:T(8,128)(4,1)S(1)} %compare_and_fusion), kind=kLoop, calls=%fused_computation.3 | loop fusion | flops 98304 | bytes 787200 | tf_op jit(solution)/shard_map/jit(_take)/select_n | solution.py:201
  15.4 3.0 %collective-permute-start = (f32[168,128]{1,0:T(8,128)}, f32[168,128]{1,0:T(8,128)}, u32[]{:S(2)}, u32[]{:S(2)}) collective-permute-start(f32[168,128]{1,0:T(8,128)} %pad_maximum_fusion.6), channel_id=1, source_target_pairs={{0,8},{16,24},{8,0},{24,16},{1,9},{17,25},{9,1},{25,17},{2,10},{18... | collective-permute-start | bytes 258056 | tf_op jit(solution)/shard_map/ppermute | solution.py:139
  18.4 1.3 %collective-permute-start.4 = (f32[128,128]{1,0:T(8,128)}, f32[128,128]{1,0:T(8,128)}, u32[]{:S(2)}, u32[]{:S(2)}) collective-permute-start(f32[128,128]{1,0:T(8,128)} %get-tuple-element.11), channel_id=1, source_target_pairs={{2,4},{4,2},{3,5},{5,3},{10,12},{12,10},{11,13},{13,11},{18,20},{2... | collective-permute-start | bytes 196616 | tf_op jit(solution)/shard_map/ppermute | solution.py:136
  19.7 1.3 %collective-permute-start.1 = (f32[128,128]{1,0:T(8,128)}, f32[128,128]{1,0:T(8,128)}, u32[]{:S(2)}, u32[]{:S(2)}) collective-permute-start(f32[128,128]{1,0:T(8,128)} %get-tuple-element.13), channel_id=1, source_target_pairs={{8,16},{16,8},{9,17},{17,9},{10,18},{18,10},{11,19},{19,11},{12,20... | collective-permute-start | bytes 196616 | tf_op jit(solution)/shard_map/ppermute | solution.py:136
  22.0 3.3 %collective-permute-start.2 = (f32[2,1,1,40,128]{4,3,0,2,1:T(8,128)S(1)}, f32[2,1,1,40,128]{4,3,0,2,1:T(8,128)S(1)}, u32[]{:S(2)}, u32[]{:S(2)}) collective-permute-start(f32[2,1,1,40,128]{4,3,0,2,1:T(8,128)S(1)} %maximum_select_fusion.5), channel_id=1, source_target_pairs={{0,16},{8,24},{16,0},{24,8},{1,17},{9,25},{17,1},{25,9},{2,18},{10... | collective-permute-start | bytes 122888 | tf_op jit(solution)/shard_map/ppermute | solution.py:179
  25.3 0.9 %select_dynamic-update-slice_fusion.5 = f32[128,768]{1,0:T(8,128)S(1)} fusion(f32[128,128]{1,0:T(8,128)} %collective-permute-done.1, f32[168,128]{1,0:T(8,128)} %collective-permute-done, pred[]{:T(512)S(6)} %eq.33), kind=kLoop, calls=%fused_computation.28 | loop fusion | flops 16383 | bytes 196609
  26.1 0.9 %select_dynamic-update-slice_fusion.4 = f32[128,768]{1,0:T(8,128)S(1)} fusion(f32[128,768]{1,0:T(8,128)S(1)} %select_dynamic-update-slice_fusion.5, f32[128,128]{1,0:T(8,128)} %collective-permute-done.1, f32[168,128]{1,0:T(8,128)} %collective-permute-done, pred[]{:T(512)S(6)} %eq.33), kind=kLoop, calls=%fused_computation.27 | loop fusion | flops 16384 | bytes 196609
  27.0 1.0 %collective-permute-done.2 = f32[2,1,1,40,128]{4,3,0,2,1:T(8,128)S(1)} collective-permute-done((f32[2,1,1,40,128]{4,3,0,2,1:T(8,128)S(1)}, f32[2,1,1,40,128]{4,3,0,2,1:T(8,128)S(1)}, u32[]{:S(2)}, u32[]{:S(2)}) %collective-permute-start.2) | collective-permute-done | bytes 40992 | tf_op jit(solution)/shard_map/ppermute | solution.py:179
  28.9 3.4 %collective-permute-start.3 = (f32[288,128]{1,0:T(8,128)S(1)}, f32[288,128]{1,0:T(8,128)S(1)}, u32[]{:S(2)}, u32[]{:S(2)}) collective-permute-start(f32[288,128]{1,0:T(8,128)S(1)} %pad_maximum_fusion.5), channel_id=1, source_target_pairs={{0,2},{4,6},{2,0},{6,4},{1,3},{5,7},{3,1},{7,5},{8,10},{12,14},{10... | collective-permute-start | bytes 442376 | tf_op jit(solution)/shard_map/ppermute | solution.py:139
  32.3 3.7 %collective-permute-done.3 = f32[288,128]{1,0:T(8,128)S(1)} collective-permute-done((f32[288,128]{1,0:T(8,128)S(1)}, f32[288,128]{1,0:T(8,128)S(1)}, u32[]{:S(2)}, u32[]{:S(2)}) %collective-permute-start.3) | collective-permute-done | bytes 147488 | tf_op jit(solution)/shard_map/ppermute | solution.py:139
  36.0 0.9 %select_dynamic-update-slice_fusion.2 = f32[128,768]{1,0:T(8,128)S(1)} fusion(f32[128,768]{1,0:T(8,128)S(1)} %select_dynamic-update-slice_fusion.3, f32[128,128]{1,0:T(8,128)} %collective-permute-done.4, f32[288,128]{1,0:T(8,128)S(1)} %collective-permute-done.3, pred[]{:T(512)S(6)} %eq.34), kind=kLoop, calls=%fused_computation.23 | loop fusion | flops 16384 | bytes 196609
  36.9 0.9 %select_dynamic-update-slice_fusion.1 = f32[128,768]{1,0:T(8,128)S(1)} fusion(f32[128,768]{1,0:T(8,128)S(1)} %select_dynamic-update-slice_fusion.2, f32[128,128]{1,0:T(8,128)} %collective-permute-done.5, pred[]{:T(512)S(6)} %eq.36), kind=kLoop, calls=%fused_computation.22 | loop fusion | flops 16384 | bytes 131073
  37.8 13.1 %shard_map.82 = (bf16[128,4352]{1,0:T(8,128)(2,1)S(1)}, bf16[128,768]{1,0:T(8,128)(2,1)S(1)}) custom-call(s32[20]{0:T(128)S(1)} %copy-done.2, f32[128,4352]{1,0:T(8,128)S(1)} %copy-done.1, f32[128,768]{1,0:T(8,128)S(1)} %select_dynamic-update-slice_fusion.slot_ref, bf16[20,256,256]{2,1,0:T(8,128)(2,1)} %inv_ref.1, bf16[19,256,256]{2,1,0:T(8,128)(2,1)} %cpl_ref.1, ...), custom_call_target="tpu_custom_call" | custom-call | flops 1308622848 | bytes 8454144 | tf_op jit(solution)/shard_map/pallas_call | solution.py:61
  51.6 4.5 %collective-permute-start.7 = (bf16[128,128]{1,0:T(8,128)(2,1)S(1)}, bf16[128,128]{1,0:T(8,128)(2,1)S(1)}, u32[]{:S(2)}, u32[]{:S(2)}) collective-permute-start(bf16[128,128]{1,0:T(8,128)(2,1)S(1)} %get-tuple-element.18), channel_id=1, source_target_pairs={{0,8},{16,24},{8,0},{24,16},{1,9},{17,25},{9,1},{25,17},{2,10},{18... | collective-permute-start | bytes 98312 | tf_op jit(solution)/shard_map/ppermute | solution.py:136
  56.1 2.1 %collective-permute-start.10 = (f32[4,2,1,40,128]{4,3,0,1,2:T(8,128)S(1)}, f32[4,2,1,40,128]{4,3,0,1,2:T(8,128)S(1)}, u32[]{:S(2)}, u32[]{:S(2)}) collective-permute-start(f32[4,2,1,40,128]{4,3,0,1,2:T(8,128)S(1)} %maximum_select_fusion.1), channel_id=1, source_target_pairs={{0,4},{2,6},{4,0},{6,2},{1,5},{3,7},{5,1},{7,3},{8,12},{10,14},{12... | collective-permute-start | bytes 491528 | tf_op jit(solution)/shard_map/ppermute | solution.py:179
  58.8 2.8 %collective-permute-start.9 = (bf16[128,128]{1,0:T(8,128)(2,1)S(1)}, bf16[128,128]{1,0:T(8,128)(2,1)S(1)}, u32[]{:S(2)}, u32[]{:S(2)}) collective-permute-start(bf16[128,128]{1,0:T(8,128)(2,1)S(1)} %get-tuple-element.16), channel_id=1, source_target_pairs={{0,2},{4,6},{2,0},{6,4},{1,3},{5,7},{3,1},{7,5},{8,10},{12,14},{10... | collective-permute-start | bytes 98312 | tf_op jit(solution)/shard_map/ppermute | solution.py:136
  61.9 1.9 %collective-permute-done.9 = bf16[128,128]{1,0:T(8,128)(2,1)S(1)} collective-permute-done((bf16[128,128]{1,0:T(8,128)(2,1)S(1)}, bf16[128,128]{1,0:T(8,128)(2,1)S(1)}, u32[]{:S(2)}, u32[]{:S(2)}) %collective-permute-start.9) | collective-permute-done | bytes 32800 | tf_op jit(solution)/shard_map/ppermute | solution.py:136
  64.0 1.2 %fusion.7.solved_ref = f32[128,40]{1,0:T(8,128)S(1)} fusion(f32[1280,128]{1,0:T(8,128)S(1)} %bitcast.51, f32[40,1280]{1,0:T(8,128)S(1)} %copy-done), kind=kOutput, calls=%fused_computation.54 | convolution fusion | flops 78643200 | bytes 880640 | tf_op jit(solution)/shard_map/dot_general | solution.py:237
  65.3 4.2 %shard_map.83 = f32[128,4352]{1,0:T(8,128)} custom-call(s32[768,1]{1,0:T(8,128)S(1)} %bitcast.48, bf16[128,4352]{1,0:T(8,128)(2,1)S(1)} %get-tuple-element.7.own_ref, bf16[128,768]{1,0:T(8,128)(2,1)S(1)} %select_dynamic-update-slice_fusion.6.back_ref, f32[128,40]{1,0:T(8,128)S(1)} %fusion.7.solved_ref, f32[40,4352]{1,0:T(8,128)S(1)} %broadcast_multiply_fusion.vec_ref), custom_call_target="tpu_custom_call" | custom-call | tf_op jit(solution)/shard_map/pallas_call | solution.py:117
  (53 shorter events, 6.5 us)
Async XLA Ops:
  0.0 64.0 %copy-start = (f32[40,1280]{1,0:T(8,128)S(1)}, f32[40,1280]{1,0:T(8,128)}, u32[]{:S(2)}) copy-start(f32[40,1280]{1,0:T(8,128)} %param.15) | copy-start | bytes 614404
  2.1 4.4 %copy-start.1 = (f32[128,4352]{1,0:T(8,128)S(1)}, f32[128,4352]{1,0:T(8,128)}, u32[]{:S(2)}) copy-start(f32[128,4352]{1,0:T(8,128)} %res_ref.1) | copy-start | bytes 6684676
  12.0 8.9 %copy-start.3 = (s32[6,128]{1,0:T(8,128)S(1)}, s32[6,128]{1,0:T(8,128)}, u32[]{:S(2)}) copy-start(s32[6,128]{1,0:T(8,128)} %param.12) | copy-start | bytes 9220
  13.0 24.8 %copy-start.2 = (s32[20]{0:T(128)S(1)}, s32[20]{0:T(128)}, u32[]{:S(2)}) copy-start(s32[20]{0:T(128)} %parent_ref.1) | copy-start | bytes 244
  15.4 5.9 %collective-permute-start = (f32[168,128]{1,0:T(8,128)}, f32[168,128]{1,0:T(8,128)}, u32[]{:S(2)}, u32[]{:S(2)}) collective-permute-start(f32[168,128]{1,0:T(8,128)} %pad_maximum_fusion.6), channel_id=1, source_target_pairs={{0,8},{16,24},{8,0},{24,16},{1,9},{17,25},{9,1},{25,17},{2,10},{18... | collective-permute-start | bytes 258056 | tf_op jit(solution)/shard_map/ppermute | solution.py:139
  18.4 18.5 %collective-permute-start.5 = (f32[128,128]{1,0:T(8,128)}, f32[128,128]{1,0:T(8,128)}, u32[]{:S(2)}, u32[]{:S(2)}) collective-permute-start(f32[128,128]{1,0:T(8,128)} %get-tuple-element.9), channel_id=1, source_target_pairs={{0,1},{1,0},{2,3},{3,2},{4,5},{5,4},{6,7},{7,6},{8,9},{9,8},{10,11... | collective-permute-start | bytes 196616 | tf_op jit(solution)/shard_map/ppermute | solution.py:136
  18.4 13.9 %collective-permute-start.4 = (f32[128,128]{1,0:T(8,128)}, f32[128,128]{1,0:T(8,128)}, u32[]{:S(2)}, u32[]{:S(2)}) collective-permute-start(f32[128,128]{1,0:T(8,128)} %get-tuple-element.11), channel_id=1, source_target_pairs={{2,4},{4,2},{3,5},{5,3},{10,12},{12,10},{11,13},{13,11},{18,20},{2... | collective-permute-start | bytes 196616 | tf_op jit(solution)/shard_map/ppermute | solution.py:136
  19.7 5.6 %collective-permute-start.1 = (f32[128,128]{1,0:T(8,128)}, f32[128,128]{1,0:T(8,128)}, u32[]{:S(2)}, u32[]{:S(2)}) collective-permute-start(f32[128,128]{1,0:T(8,128)} %get-tuple-element.13), channel_id=1, source_target_pairs={{8,16},{16,8},{9,17},{17,9},{10,18},{18,10},{11,19},{19,11},{12,20... | collective-permute-start | bytes 196616 | tf_op jit(solution)/shard_map/ppermute | solution.py:136
  22.0 6.0 %collective-permute-start.2 = (f32[2,1,1,40,128]{4,3,0,2,1:T(8,128)S(1)}, f32[2,1,1,40,128]{4,3,0,2,1:T(8,128)S(1)}, u32[]{:S(2)}, u32[]{:S(2)}) collective-permute-start(f32[2,1,1,40,128]{4,3,0,2,1:T(8,128)S(1)} %maximum_select_fusion.5), channel_id=1, source_target_pairs={{0,16},{8,24},{16,0},{24,8},{1,17},{9,25},{17,1},{25,9},{2,18},{10... | collective-permute-start | bytes 122888 | tf_op jit(solution)/shard_map/ppermute | solution.py:179
  28.9 7.2 %collective-permute-start.3 = (f32[288,128]{1,0:T(8,128)S(1)}, f32[288,128]{1,0:T(8,128)S(1)}, u32[]{:S(2)}, u32[]{:S(2)}) collective-permute-start(f32[288,128]{1,0:T(8,128)S(1)} %pad_maximum_fusion.5), channel_id=1, source_target_pairs={{0,2},{4,6},{2,0},{6,4},{1,3},{5,7},{3,1},{7,5},{8,10},{12,14},{10... | collective-permute-start | bytes 442376 | tf_op jit(solution)/shard_map/ppermute | solution.py:139
  50.9 10.7 %collective-permute-start.6 = (bf16[128,128]{1,0:T(8,128)(2,1)S(1)}, bf16[128,128]{1,0:T(8,128)(2,1)S(1)}, u32[]{:S(2)}, u32[]{:S(2)}) collective-permute-start(bf16[128,128]{1,0:T(8,128)(2,1)S(1)} %get-tuple-element.17), channel_id=1, source_target_pairs={{8,16},{16,8},{9,17},{17,9},{10,18},{18,10},{11,19},{19,11},{12,20... | collective-permute-start | bytes 98312 | tf_op jit(solution)/shard_map/ppermute | solution.py:136
  51.6 10.0 %collective-permute-start.7 = (bf16[128,128]{1,0:T(8,128)(2,1)S(1)}, bf16[128,128]{1,0:T(8,128)(2,1)S(1)}, u32[]{:S(2)}, u32[]{:S(2)}) collective-permute-start(bf16[128,128]{1,0:T(8,128)(2,1)S(1)} %get-tuple-element.18), channel_id=1, source_target_pairs={{0,8},{16,24},{8,0},{24,16},{1,9},{17,25},{9,1},{25,17},{2,10},{18... | collective-permute-start | bytes 98312 | tf_op jit(solution)/shard_map/ppermute | solution.py:136
  56.1 5.6 %collective-permute-start.10 = (f32[4,2,1,40,128]{4,3,0,1,2:T(8,128)S(1)}, f32[4,2,1,40,128]{4,3,0,1,2:T(8,128)S(1)}, u32[]{:S(2)}, u32[]{:S(2)}) collective-permute-start(f32[4,2,1,40,128]{4,3,0,1,2:T(8,128)S(1)} %maximum_select_fusion.1), channel_id=1, source_target_pairs={{0,4},{2,6},{4,0},{6,2},{1,5},{3,7},{5,1},{7,3},{8,12},{10,14},{12... | collective-permute-start | bytes 491528 | tf_op jit(solution)/shard_map/ppermute | solution.py:179
  58.2 3.7 %collective-permute-start.8 = (bf16[128,128]{1,0:T(8,128)(2,1)S(1)}, bf16[128,128]{1,0:T(8,128)(2,1)S(1)}, u32[]{:S(2)}, u32[]{:S(2)}) collective-permute-start(bf16[128,128]{1,0:T(8,128)(2,1)S(1)} %get-tuple-element.15), channel_id=1, source_target_pairs={{2,4},{4,2},{3,5},{5,3},{10,12},{12,10},{11,13},{13,11},{18,20},{2... | collective-permute-start | bytes 98312 | tf_op jit(solution)/shard_map/ppermute | solution.py:136
  58.8 5.0 %collective-permute-start.9 = (bf16[128,128]{1,0:T(8,128)(2,1)S(1)}, bf16[128,128]{1,0:T(8,128)(2,1)S(1)}, u32[]{:S(2)}, u32[]{:S(2)}) collective-permute-start(bf16[128,128]{1,0:T(8,128)(2,1)S(1)} %get-tuple-element.16), channel_id=1, source_target_pairs={{0,2},{4,6},{2,0},{6,4},{1,3},{5,7},{3,1},{7,5},{8,10},{12,14},{10... | collective-permute-start | bytes 98312 | tf_op jit(solution)/shard_map/ppermute | solution.py:136
  61.8 2.0 %collective-permute-start.11 = (f32[768,128]{1,0:T(8,128)S(1)}, f32[768,128]{1,0:T(8,128)S(1)}, u32[]{:S(2)}, u32[]{:S(2)}) collective-permute-start(f32[768,128]{1,0:T(8,128)S(1)} %pad_maximum_fusion), channel_id=1, source_target_pairs={{0,1},{1,0},{2,3},{3,2},{4,5},{5,4},{6,7},{7,6},{8,9},{9,8},{10,11... | collective-permute-start | bytes 1179656 | tf_op jit(solution)/shard_map/ppermute | solution.py:139

commit v12 on v11

--- a/solution.py
+++ b/solution.py
@@ -94,8 +94,10 @@
     return first, second, third
 
 
-def finish_kernel(rows_ref, own_ref, back_ref, solved_ref, vec_ref, out_ref):
+def finish_kernel(count_ref, rows_ref, own_ref, back_ref, solved_ref, vec_ref, out_ref):
     owned_n = own_ref.shape[1]
+    kmax_here = vec_ref.shape[0]
+    keep = lax.broadcasted_iota(jnp.int32, (kmax_here, 1), 0) < count_ref[0]
     chunk = 256
     rows = rows_ref[...]
     back = back_ref[...]
@@ -106,21 +108,21 @@
         onehot = (rows == here).astype(jnp.bfloat16)
         total = own_ref[:, cols].astype(jnp.float32)
         total += jnp.dot(back, onehot, preferred_element_type=jnp.float32)
-        v1, v2, v3 = split3(vec_ref[:, cols])
+        v1, v2, v3 = split3(jnp.where(keep, vec_ref[:, cols], 0.0))
         for left, right in ((s1, v1), (s1, v2), (s2, v1), (s1, v3), (s3, v1), (s2, v2)):
             total += jnp.dot(left, right, preferred_element_type=jnp.float32)
         out_ref[:, cols] = total
 
 
-def finish(send_rows, own, returned, solved, vectors):
+def finish(send_rows, counts, own, returned, solved, deflation):
     vmem = pltpu.VMEM
     return pl.pallas_call(
         finish_kernel,
         out_shape=jax.ShapeDtypeStruct(own.shape, jnp.float32),
-        in_specs=[pl.BlockSpec(memory_space=vmem)] * 5,
+        in_specs=[pl.BlockSpec(memory_space=pltpu.SMEM)] + [pl.BlockSpec(memory_space=vmem)] * 5,
         out_specs=pl.BlockSpec(memory_space=vmem),
         compiler_params=pltpu.CompilerParams(vmem_limit_bytes=48 * 1024 * 1024),
-    )(send_rows.reshape(-1, 1), own, returned, solved, vectors)
+    )(counts, send_rows.reshape(-1, 1), own, returned, solved, deflation)
 
 
 def matchings(count):
@@ -234,14 +236,10 @@
             held = merge(held, got.reshape(held.shape), axis, last, 1)
     returned = jnp.concatenate(returned, axis=1)
 
-    solved = lax.dot_general(
-        rows_of(held),
-        coarse_inverse,
-        (((0,), (1,)), ((), ())),
-        precision=lax.Precision.HIGHEST,
-        preferred_element_type=jnp.float32,
-    )
-    return finish(send_rows, own, returned, solved, vectors)
+    solved_t = jnp.dot(
+        coarse_inverse, rows_of(held), precision=lax.Precision.HIGHEST, preferred_element_type=jnp.float32
+    )
+    return finish(send_rows, counts, own, returned, solved_t.T, deflation)
 
 
 def solution(mesh):

time: 70.1 us -> 67.8 us (0.967)
  other arithmetic: 9.68 us -> 7.48 us
    mul x1 -> x0, other arithmetic: 1.21 us -> none  [per_device(): vectors = deflation * mask[:, None]]
    select_n x1, other arithmetic: 1.04 us -> 0.03 us  [per_device(): outgoing = jnp.take(residual, send_rows, axis=1)]
    unnamed x11 -> x15, local copies, waits for them, and re-layouts: 3.35 us -> 3.21 us
where the time goes in v12:
time: 67.8 us; the launch traced here: 67.3 us
  starting transfers between devices  23 us (34%)
  Pallas kernels  17.3 us (26%)
  local copies, waits for them, and re-layouts  8.29 us (12%)
  other arithmetic  7.48 us (11%)
  waiting for transfers between devices  6.67 us (10%)
  matrix products  3.56 us (5%)
  between operations  0.93 us (1%)
    pallas_call x1, Pallas kernels, local_solve(): pl.pallas_call(solve_kernel, out_shape=(jax.ShapeDtypeStruct((nrhs_here,...  13.1 us
    ppermute x7, starting transfers between devices, swap(): return (lax.ppermute(value, axis, pairs), None)  11.2 us
    ppermute x3, starting transfers between devices, swap(): got = lax.ppermute(packed, axis, pairs)  6.5 us
    ppermute x2, starting transfers between devices, gather_axis(): held = merge(held, lax.ppermute(held, axis, pairs), axis, dim, step)  5.36 us
    gather x2, local copies, waits for them, and re-layouts, per_device(): outgoing = jnp.take(residual, send_rows, axis=1)  4.26 us
    pallas_call x1, Pallas kernels, finish(): pl.pallas_call(finish_kernel, out_shape=jax.ShapeDtypeStruct(own.shape, j...  4.17 us
    ppermute x3, waiting for transfers between devices, swap(): got = lax.ppermute(packed, axis, pairs)  3.79 us
    unnamed x10, other arithmetic  3.57 us
  transfers between devices with their start and end apart: 12, of which 4 were waited for; matrix products, arithmetic and copies ran while one was open for 7% of the time, Pallas kernels for 0%

profile of v12, /device:TPU:0, one launch (start us, length us, event | category | flops | bytes accessed | tf_op | source)
XLA Modules:
  0.0 67.3 jit_solution(18229405343859989334)
XLA Ops:
  0.0 0.7 %compare_and_fusion = pred[6,128]{1,0:T(8,128)(4,1)S(1)} fusion(s32[6,128]{1,0:T(8,128)} %param.12), kind=kLoop, calls=%fused_computation.51 | loop fusion | flops 4608 | bytes 3840 | tf_op jit(solution)/shard_map/jit(_take)/and | solution.py:203
  2.1 3.0 %copy.16 = f32[128,4352]{0,1:T(8,128)} copy(f32[128,4352]{1,0:T(8,128)} %res_ref.1) | data formatting | bytes 4456448 | tf_op args[0]
  5.1 3.3 %gather_fusion = f32[768,128]{1,0:T(8,128)S(1)} fusion(f32[128,4352]{0,1:T(8,128)} %copy.16, s32[1024]{0:T(1024)S(1)} %pad_clamp_fusion), kind=kCustom, calls=%fused_computation | custom fusion | bytes 789504 | tf_op jit(solution)/shard_map/jit(_take)/gather | solution.py:203
  8.5 0.9 %copy.17 = f32[6,128,128]{1,2,0:T(8,128)} copy(f32[6,128,128]{2,1,0:T(8,128)S(1)} %bitcast.51) | data formatting | bytes 786432 | tf_op jit(solution)/shard_map/jit(_take)/gather | solution.py:203
  9.4 2.3 %fusion.after_ref = f32[40,128]{1,0:T(8,128)S(1)} fusion(f32[128,4352]{1,0:T(8,128)S(1)} %copy-done.1, f32[40,4352]{1,0:T(8,128)S(1)} %copy-done.2, f32[40]{0:T(128)S(1)} %compare_convert_fusion), kind=kOutput, calls=%fused_computation.1 | convolution fusion | flops 267560960 | bytes 2945184 | tf_op jit(solution)/shard_map/dot_general | solution.py:198
  13.2 3.0 %collective-permute-start = (f32[168,128]{1,0:T(8,128)}, f32[168,128]{1,0:T(8,128)}, u32[]{:S(2)}, u32[]{:S(2)}) collective-permute-start(f32[168,128]{1,0:T(8,128)} %pad_maximum_fusion.6), channel_id=1, source_target_pairs={{0,8},{16,24},{8,0},{24,16},{1,9},{17,25},{9,1},{25,17},{2,10},{18... | collective-permute-start | bytes 258056 | tf_op jit(solution)/shard_map/ppermute | solution.py:141
  16.2 1.3 %collective-permute-start.4 = (f32[128,128]{1,0:T(8,128)}, f32[128,128]{1,0:T(8,128)}, u32[]{:S(2)}, u32[]{:S(2)}) collective-permute-start(f32[128,128]{1,0:T(8,128)} %get-tuple-element.11), channel_id=1, source_target_pairs={{2,4},{4,2},{3,5},{5,3},{10,12},{12,10},{11,13},{13,11},{18,20},{2... | collective-permute-start | bytes 196616 | tf_op jit(solution)/shard_map/ppermute | solution.py:138
  17.5 1.3 %collective-permute-start.1 = (f32[128,128]{1,0:T(8,128)}, f32[128,128]{1,0:T(8,128)}, u32[]{:S(2)}, u32[]{:S(2)}) collective-permute-start(f32[128,128]{1,0:T(8,128)} %get-tuple-element.13), channel_id=1, source_target_pairs={{8,16},{16,8},{9,17},{17,9},{10,18},{18,10},{11,19},{19,11},{12,20... | collective-permute-start | bytes 196616 | tf_op jit(solution)/shard_map/ppermute | solution.py:138
  19.8 3.3 %collective-permute-start.2 = (f32[2,1,1,40,128]{4,3,0,2,1:T(8,128)S(1)}, f32[2,1,1,40,128]{4,3,0,2,1:T(8,128)S(1)}, u32[]{:S(2)}, u32[]{:S(2)}) collective-permute-start(f32[2,1,1,40,128]{4,3,0,2,1:T(8,128)S(1)} %maximum_select_fusion.5), channel_id=1, source_target_pairs={{0,16},{8,24},{16,0},{24,8},{1,17},{9,25},{17,1},{25,9},{2,18},{10... | collective-permute-start | bytes 122888 | tf_op jit(solution)/shard_map/ppermute | solution.py:181
  23.1 0.9 %select_dynamic-update-slice_fusion.5 = f32[128,768]{1,0:T(8,128)S(1)} fusion(f32[128,128]{1,0:T(8,128)} %collective-permute-done.1, f32[168,128]{1,0:T(8,128)} %collective-permute-done, pred[]{:T(512)S(6)} %eq.33), kind=kLoop, calls=%fused_computation.30 | loop fusion | flops 16383 | bytes 196609
  23.9 0.9 %select_dynamic-update-slice_fusion.4 = f32[128,768]{1,0:T(8,128)S(1)} fusion(f32[128,768]{1,0:T(8,128)S(1)} %select_dynamic-update-slice_fusion.5, f32[128,128]{1,0:T(8,128)} %collective-permute-done.1, f32[168,128]{1,0:T(8,128)} %collective-permute-done, pred[]{:T(512)S(6)} %eq.33), kind=kLoop, calls=%fused_computation.29 | loop fusion | flops 16384 | bytes 196609
  24.8 1.0 %collective-permute-done.2 = f32[2,1,1,40,128]{4,3,0,2,1:T(8,128)S(1)} collective-permute-done((f32[2,1,1,40,128]{4,3,0,2,1:T(8,128)S(1)}, f32[2,1,1,40,128]{4,3,0,2,1:T(8,128)S(1)}, u32[]{:S(2)}, u32[]{:S(2)}) %collective-permute-start.2) | collective-permute-done | bytes 40992 | tf_op jit(solution)/shard_map/ppermute | solution.py:181
  25.8 0.9 %pad_maximum_fusion.5 = f32[288,128]{1,0:T(8,128)S(1)} fusion(f32[160,128]{1,0:T(8,128)S(1)} %bitcast.57, f32[128,128]{1,0:T(8,128)} %get-tuple-element.10), kind=kLoop, calls=%fused_computation.16 | loop fusion | flops 36864 | bytes 294912 | tf_op jit(solution)/shard_map/concatenate | solution.py:140
  26.7 3.4 %collective-permute-start.3 = (f32[288,128]{1,0:T(8,128)S(1)}, f32[288,128]{1,0:T(8,128)S(1)}, u32[]{:S(2)}, u32[]{:S(2)}) collective-permute-start(f32[288,128]{1,0:T(8,128)S(1)} %pad_maximum_fusion.5), channel_id=1, source_target_pairs={{0,2},{4,6},{2,0},{6,4},{1,3},{5,7},{3,1},{7,5},{8,10},{12,14},{10... | collective-permute-start | bytes 442376 | tf_op jit(solution)/shard_map/ppermute | solution.py:141
  30.1 3.7 %collective-permute-done.3 = f32[288,128]{1,0:T(8,128)S(1)} collective-permute-done((f32[288,128]{1,0:T(8,128)S(1)}, f32[288,128]{1,0:T(8,128)S(1)}, u32[]{:S(2)}, u32[]{:S(2)}) %collective-permute-start.3) | collective-permute-done | bytes 147488 | tf_op jit(solution)/shard_map/ppermute | solution.py:141
  33.8 0.9 %select_dynamic-update-slice_fusion.2 = f32[128,768]{1,0:T(8,128)S(1)} fusion(f32[128,768]{1,0:T(8,128)S(1)} %select_dynamic-update-slice_fusion.3, f32[128,128]{1,0:T(8,128)} %collective-permute-done.4, f32[288,128]{1,0:T(8,128)S(1)} %collective-permute-done.3, pred[]{:T(512)S(6)} %eq.34), kind=kLoop, calls=%fused_computation.25 | loop fusion | flops 16384 | bytes 196609
  34.7 0.9 %select_dynamic-update-slice_fusion.1 = f32[128,768]{1,0:T(8,128)S(1)} fusion(f32[128,768]{1,0:T(8,128)S(1)} %select_dynamic-update-slice_fusion.2, f32[128,128]{1,0:T(8,128)} %collective-permute-done.5, pred[]{:T(512)S(6)} %eq.36), kind=kLoop, calls=%fused_computation.24 | loop fusion | flops 16384 | bytes 131073
  35.6 13.1 %shard_map.82 = (bf16[128,4352]{1,0:T(8,128)(2,1)S(1)}, bf16[128,768]{1,0:T(8,128)(2,1)S(1)}) custom-call(s32[20]{0:T(128)S(1)} %copy-done.3, f32[128,4352]{1,0:T(8,128)S(1)} %copy-done.1, f32[128,768]{1,0:T(8,128)S(1)} %select_dynamic-update-slice_fusion.slot_ref, bf16[20,256,256]{2,1,0:T(8,128)(2,1)} %inv_ref.1, bf16[19,256,256]{2,1,0:T(8,128)(2,1)} %cpl_ref.1, ...), custom_call_target="tpu_custom_call" | custom-call | flops 1308622848 | bytes 8454144 | tf_op jit(solution)/shard_map/pallas_call | solution.py:61
  49.4 4.5 %collective-permute-start.7 = (bf16[128,128]{1,0:T(8,128)(2,1)S(1)}, bf16[128,128]{1,0:T(8,128)(2,1)S(1)}, u32[]{:S(2)}, u32[]{:S(2)}) collective-permute-start(bf16[128,128]{1,0:T(8,128)(2,1)S(1)} %get-tuple-element.18), channel_id=1, source_target_pairs={{0,8},{16,24},{8,0},{24,16},{1,9},{17,25},{9,1},{25,17},{2,10},{18... | collective-permute-start | bytes 98312 | tf_op jit(solution)/shard_map/ppermute | solution.py:138
  53.9 2.1 %collective-permute-start.10 = (f32[4,2,1,40,128]{4,3,0,1,2:T(8,128)S(1)}, f32[4,2,1,40,128]{4,3,0,1,2:T(8,128)S(1)}, u32[]{:S(2)}, u32[]{:S(2)}) collective-permute-start(f32[4,2,1,40,128]{4,3,0,1,2:T(8,128)S(1)} %maximum_select_fusion.1), channel_id=1, source_target_pairs={{0,4},{2,6},{4,0},{6,2},{1,5},{3,7},{5,1},{7,3},{8,12},{10,14},{12... | collective-permute-start | bytes 491528 | tf_op jit(solution)/shard_map/ppermute | solution.py:181
  56.7 2.8 %collective-permute-start.9 = (bf16[128,128]{1,0:T(8,128)(2,1)S(1)}, bf16[128,128]{1,0:T(8,128)(2,1)S(1)}, u32[]{:S(2)}, u32[]{:S(2)}) collective-permute-start(bf16[128,128]{1,0:T(8,128)(2,1)S(1)} %get-tuple-element.16), channel_id=1, source_target_pairs={{0,2},{4,6},{2,0},{6,4},{1,3},{5,7},{3,1},{7,5},{8,10},{12,14},{10... | collective-permute-start | bytes 98312 | tf_op jit(solution)/shard_map/ppermute | solution.py:138
  59.7 1.9 %collective-permute-done.9 = bf16[128,128]{1,0:T(8,128)(2,1)S(1)} collective-permute-done((bf16[128,128]{1,0:T(8,128)(2,1)S(1)}, bf16[128,128]{1,0:T(8,128)(2,1)S(1)}, u32[]{:S(2)}, u32[]{:S(2)}) %collective-permute-start.9) | collective-permute-done | bytes 32800 | tf_op jit(solution)/shard_map/ppermute | solution.py:138
  61.8 1.2 %fusion.9.solved_ref = f32[128,40]{1,0:T(8,128)S(1)} fusion(f32[1280,128]{1,0:T(8,128)S(1)} %bitcast.50, f32[40,1280]{1,0:T(8,128)S(1)} %copy-done), kind=kOutput, calls=%fused_computation.55 | convolution fusion | flops 78643200 | bytes 880640 | tf_op jit(solution)/shard_map/dot_general | solution.py:239
  63.1 4.2 %shard_map.83 = f32[128,4352]{1,0:T(8,128)} custom-call(s32[1]{0:T(128)} %copy.43.count_ref, s32[768,1]{1,0:T(8,128)S(1)} %bitcast.47, bf16[128,4352]{1,0:T(8,128)(2,1)S(1)} %get-tuple-element.7.own_ref, bf16[128,768]{1,0:T(8,128)(2,1)S(1)} %select_dynamic-update-slice_fusion.6.back_ref, f32[128,40]{1,0:T(8,128)S(1)} %fusion.9.solved_ref, ...), custom_call_target="tpu_custom_call" | custom-call | tf_op jit(solution)/shard_map/pallas_call | solution.py:119
  (56 shorter events, 5.0 us)
Async XLA Ops:
  0.0 61.8 %copy-start = (f32[40,1280]{1,0:T(8,128)S(1)}, f32[40,1280]{1,0:T(8,128)}, u32[]{:S(2)}) copy-start(f32[40,1280]{1,0:T(8,128)} %param.15) | copy-start | bytes 614404
  5.1 4.3 %copy-start.1 = (f32[128,4352]{1,0:T(8,128)S(1)}, f32[128,4352]{1,0:T(8,128)}, u32[]{:S(2)}) copy-start(f32[128,4352]{1,0:T(8,128)} %res_ref.1) | copy-start | bytes 6684676
  5.1 4.3 %copy-start.2 = (f32[40,4352]{1,0:T(8,128)S(1)}, f32[40,4352]{1,0:T(8,128)}, u32[]{:S(2)}) copy-start(f32[40,4352]{1,0:T(8,128)} %vec_ref.1) | copy-start | bytes 2088964
  9.4 2.4 %copy-start.4 = (f32[6,128,128]{1,2,0:T(8,128)S(1)}, f32[6,128,128]{1,2,0:T(8,128)}, u32[]{:S(2)}) copy-start(f32[6,128,128]{1,2,0:T(8,128)} %copy.17) | copy-start | bytes 1179652
  9.4 9.4 %copy-start.5 = (s32[6,128]{1,0:T(8,128)S(1)}, s32[6,128]{1,0:T(8,128)}, u32[]{:S(2)}) copy-start(s32[6,128]{1,0:T(8,128)} %param.12) | copy-start | bytes 9220
  11.7 23.8 %copy-start.3 = (s32[20]{0:T(128)S(1)}, s32[20]{0:T(128)}, u32[]{:S(2)}) copy-start(s32[20]{0:T(128)} %parent_ref.1) | copy-start | bytes 244
  13.2 5.9 %collective-permute-start = (f32[168,128]{1,0:T(8,128)}, f32[168,128]{1,0:T(8,128)}, u32[]{:S(2)}, u32[]{:S(2)}) collective-permute-start(f32[168,128]{1,0:T(8,128)} %pad_maximum_fusion.6), channel_id=1, source_target_pairs={{0,8},{16,24},{8,0},{24,16},{1,9},{17,25},{9,1},{25,17},{2,10},{18... | collective-permute-start | bytes 258056 | tf_op jit(solution)/shard_map/ppermute | solution.py:141
  16.2 18.5 %collective-permute-start.5 = (f32[128,128]{1,0:T(8,128)}, f32[128,128]{1,0:T(8,128)}, u32[]{:S(2)}, u32[]{:S(2)}) collective-permute-start(f32[128,128]{1,0:T(8,128)} %get-tuple-element.9), channel_id=1, source_target_pairs={{0,1},{1,0},{2,3},{3,2},{4,5},{5,4},{6,7},{7,6},{8,9},{9,8},{10,11... | collective-permute-start | bytes 196616 | tf_op jit(solution)/shard_map/ppermute | solution.py:138
  16.2 13.9 %collective-permute-start.4 = (f32[128,128]{1,0:T(8,128)}, f32[128,128]{1,0:T(8,128)}, u32[]{:S(2)}, u32[]{:S(2)}) collective-permute-start(f32[128,128]{1,0:T(8,128)} %get-tuple-element.11), channel_id=1, source_target_pairs={{2,4},{4,2},{3,5},{5,3},{10,12},{12,10},{11,13},{13,11},{18,20},{2... | collective-permute-start | bytes 196616 | tf_op jit(solution)/shard_map/ppermute | solution.py:138
  17.5 5.6 %collective-permute-start.1 = (f32[128,128]{1,0:T(8,128)}, f32[128,128]{1,0:T(8,128)}, u32[]{:S(2)}, u32[]{:S(2)}) collective-permute-start(f32[128,128]{1,0:T(8,128)} %get-tuple-element.13), channel_id=1, source_target_pairs={{8,16},{16,8},{9,17},{17,9},{10,18},{18,10},{11,19},{19,11},{12,20... | collective-permute-start | bytes 196616 | tf_op jit(solution)/shard_map/ppermute | solution.py:138
  19.8 6.0 %collective-permute-start.2 = (f32[2,1,1,40,128]{4,3,0,2,1:T(8,128)S(1)}, f32[2,1,1,40,128]{4,3,0,2,1:T(8,128)S(1)}, u32[]{:S(2)}, u32[]{:S(2)}) collective-permute-start(f32[2,1,1,40,128]{4,3,0,2,1:T(8,128)S(1)} %maximum_select_fusion.5), channel_id=1, source_target_pairs={{0,16},{8,24},{16,0},{24,8},{1,17},{9,25},{17,1},{25,9},{2,18},{10... | collective-permute-start | bytes 122888 | tf_op jit(solution)/shard_map/ppermute | solution.py:181
  26.7 7.1 %collective-permute-start.3 = (f32[288,128]{1,0:T(8,128)S(1)}, f32[288,128]{1,0:T(8,128)S(1)}, u32[]{:S(2)}, u32[]{:S(2)}) collective-permute-start(f32[288,128]{1,0:T(8,128)S(1)} %pad_maximum_fusion.5), channel_id=1, source_target_pairs={{0,2},{4,6},{2,0},{6,4},{1,3},{5,7},{3,1},{7,5},{8,10},{12,14},{10... | collective-permute-start | bytes 442376 | tf_op jit(solution)/shard_map/ppermute | solution.py:141
  48.8 10.7 %collective-permute-start.6 = (bf16[128,128]{1,0:T(8,128)(2,1)S(1)}, bf16[128,128]{1,0:T(8,128)(2,1)S(1)}, u32[]{:S(2)}, u32[]{:S(2)}) collective-permute-start(bf16[128,128]{1,0:T(8,128)(2,1)S(1)} %get-tuple-element.17), channel_id=1, source_target_pairs={{8,16},{16,8},{9,17},{17,9},{10,18},{18,10},{11,19},{19,11},{12,20... | collective-permute-start | bytes 98312 | tf_op jit(solution)/shard_map/ppermute | solution.py:138
  49.4 10.0 %collective-permute-start.7 = (bf16[128,128]{1,0:T(8,128)(2,1)S(1)}, bf16[128,128]{1,0:T(8,128)(2,1)S(1)}, u32[]{:S(2)}, u32[]{:S(2)}) collective-permute-start(bf16[128,128]{1,0:T(8,128)(2,1)S(1)} %get-tuple-element.18), channel_id=1, source_target_pairs={{0,8},{16,24},{8,0},{24,16},{1,9},{17,25},{9,1},{25,17},{2,10},{18... | collective-permute-start | bytes 98312 | tf_op jit(solution)/shard_map/ppermute | solution.py:138
  53.9 5.6 %collective-permute-start.10 = (f32[4,2,1,40,128]{4,3,0,1,2:T(8,128)S(1)}, f32[4,2,1,40,128]{4,3,0,1,2:T(8,128)S(1)}, u32[]{:S(2)}, u32[]{:S(2)}) collective-permute-start(f32[4,2,1,40,128]{4,3,0,1,2:T(8,128)S(1)} %maximum_select_fusion.1), channel_id=1, source_target_pairs={{0,4},{2,6},{4,0},{6,2},{1,5},{3,7},{5,1},{7,3},{8,12},{10,14},{12... | collective-permute-start | bytes 491528 | tf_op jit(solution)/shard_map/ppermute | solution.py:181
  56.0 3.7 %collective-permute-start.8 = (bf16[128,128]{1,0:T(8,128)(2,1)S(1)}, bf16[128,128]{1,0:T(8,128)(2,1)S(1)}, u32[]{:S(2)}, u32[]{:S(2)}) collective-permute-start(bf16[128,128]{1,0:T(8,128)(2,1)S(1)} %get-tuple-element.15), channel_id=1, source_target_pairs={{2,4},{4,2},{3,5},{5,3},{10,12},{12,10},{11,13},{13,11},{18,20},{2... | collective-permute-start | bytes 98312 | tf_op jit(solution)/shard_map/ppermute | solution.py:138
  56.7 5.0 %collective-permute-start.9 = (bf16[128,128]{1,0:T(8,128)(2,1)S(1)}, bf16[128,128]{1,0:T(8,128)(2,1)S(1)}, u32[]{:S(2)}, u32[]{:S(2)}) collective-permute-start(bf16[128,128]{1,0:T(8,128)(2,1)S(1)} %get-tuple-element.16), channel_id=1, source_target_pairs={{0,2},{4,6},{2,0},{6,4},{1,3},{5,7},{3,1},{7,5},{8,10},{12,14},{10... | collective-permute-start | bytes 98312 | tf_op jit(solution)/shard_map/ppermute | solution.py:138
  59.6 2.0 %collective-permute-start.11 = (f32[768,128]{1,0:T(8,128)S(1)}, f32[768,128]{1,0:T(8,128)S(1)}, u32[]{:S(2)}, u32[]{:S(2)}) collective-permute-start(f32[768,128]{1,0:T(8,128)S(1)} %pad_maximum_fusion), channel_id=1, source_target_pairs={{0,1},{1,0},{2,3},{3,2},{4,5},{5,4},{6,7},{7,6},{8,9},{9,8},{10,11... | collective-permute-start | bytes 1179656 | tf_op jit(solution)/shard_map/ppermute | solution.py:141

commit v13 on v9

--- a/solution.py
+++ b/solution.py
@@ -167,6 +167,7 @@
     after = coeffs_t
 
     own, zslots = local_solve(parent, residual, slots, diag_inverse, coupling, after)
+    zslots, held = lax.optimization_barrier((zslots, held))
 
     returned = []
     for axis_pos, axis in enumerate(AXES):

time: 70.4 us -> 66.5 us (0.945)
  waiting for transfers between devices: 12.4 us -> 6.8 us
  matrix products: 10.1 us -> 11.2 us
  local copies, waits for them, and re-layouts: 5.4 us -> 6.4 us
  starting transfers between devices: 25.3 us -> 24.3 us
    all_to_all x1, waiting for transfers between devices: 7.78 us -> 0.01 us  [per_device(): held = lax.all_to_all(spread, AXES, 0, 0, tiled=True)]
    ppermute x10, waiting for transfers between devices: 4.57 us -> 6.8 us  [swap(): return (lax.ppermute(value, axis, pairs), None)]
    dot_general x1, matrix products: 1.21 us -> 2.3 us  [per_device(): jnp.dot(coarse_inverse, rows_of(held), precision=lax.Precision.HIGHEST, p...]
    unnamed x13 -> x15, local copies, waits for them, and re-layouts: 2.03 us -> 3.02 us
  transfers between devices with their start and end apart: 11 -> 11, of which waited for: 2 -> 1; matrix products, arithmetic and copies ran while one was open for 5% -> 12% of each run, Pallas kernels for 0% -> 20%
where the time goes in v13:
time: 66.5 us; the launch traced here: 66.1 us
  starting transfers between devices  24.3 us (37%)
  Pallas kernels  13.2 us (20%)
  matrix products  11.2 us (17%)
  waiting for transfers between devices  6.8 us (10%)
  local copies, waits for them, and re-layouts  6.4 us (10%)
  other arithmetic  3.31 us (5%)
  between operations  0.98 us (1%)
    ppermute x10, starting transfers between devices, swap(): return (lax.ppermute(value, axis, pairs), None)  17.5 us
    pallas_call x1, Pallas kernels, local_solve(): pl.pallas_call(solve_kernel, out_shape=(jax.ShapeDtypeStruct((nrhs_here,...  13.2 us
    ppermute x10, waiting for transfers between devices, swap(): return (lax.ppermute(value, axis, pairs), None)  6.8 us
    all_to_all x1, starting transfers between devices, per_device(): held = lax.all_to_all(spread, AXES, 0, 0, tiled=True)  6.76 us
    dot_general x1, matrix products, per_device(): faces = jnp.dot(returned, onehot, preferred_element_type=jnp.float32)  4.61 us
    unnamed x15, local copies, waits for them, and re-layouts  3.02 us
    gather x2, local copies, waits for them, and re-layouts, per_device(): outgoing = jnp.take(residual, send_rows, axis=1)  2.49 us
    dot_general x1, matrix products, per_device(): lax.dot_general(vectors, residual, NT, precision=lax.Precision.HIGHEST, p...  2.35 us
  transfers between devices with their start and end apart: 11, of which 1 were waited for; matrix products, arithmetic and copies ran while one was open for 12% of the time, Pallas kernels for 20%

profile of v13, /device:TPU:0, one launch (start us, length us, event | category | flops | bytes accessed | tf_op | source)
XLA Modules:
  0.0 66.1 jit_solution(121845189665030658)
XLA Ops:
  0.0 0.7 %compare_and_fusion = pred[6,128]{1,0:T(8,128)(4,1)S(1)} fusion(s32[6,128]{1,0:T(8,128)} %param.12), kind=kLoop, calls=%fused_computation.37 | loop fusion | flops 4608 | bytes 3840 | tf_op jit(solution)/shard_map/jit(_take)/and | solution.py:161
  0.7 0.7 %fusion.9 = s32[768]{0:T(1024)S(1)} fusion(s32[6,128]{1,0:T(8,128)} %param.12), kind=kLoop, calls=%fused_computation.38 | loop fusion | flops 2304 | bytes 6144 | tf_op jit(solution)/shard_map/jit(_take)/broadcast_in_dim | solution.py:161
  1.4 2.0 %copy.10 = f32[128,4352]{0,1:T(8,128)S(1)} copy(f32[128,4352]{1,0:T(8,128)} %res_ref.1) | data formatting | bytes 4456448 | tf_op args[0]
  3.5 1.6 %gather_fusion = f32[768,128]{1,0:T(8,128)S(1)} fusion(f32[128,4352]{0,1:T(8,128)S(1)} %copy.10, s32[1024]{0:T(1024)S(1)} %pad_clamp_fusion), kind=kCustom, calls=%fused_computation | custom fusion | bytes 789504 | tf_op jit(solution)/shard_map/jit(_take)/gather | solution.py:161
  5.0 0.9 %copy.11 = f32[6,128,128]{1,2,0:T(8,128)} copy(f32[6,128,128]{2,1,0:T(8,128)S(1)} %bitcast.24) | data formatting | bytes 786432 | tf_op jit(solution)/shard_map/jit(_take)/gather | solution.py:161
  6.0 1.0 %select_bitcast_fusion = f32[128,6,128]{2,0,1:T(8,128)S(1)} fusion(f32[6,128,128]{1,2,0:T(8,128)} %copy.11, pred[6,128]{1,0:T(8,128)(4,1)S(1)} %compare_and_fusion), kind=kLoop, calls=%fused_computation.9 | loop fusion | flops 98304 | bytes 787200 | tf_op jit(solution)/shard_map/jit(_take)/select_n | solution.py:161
  7.0 0.7 fusion.8
  7.6 3.0 %collective-permute-start = (f32[128,128]{1,0:T(8,128)}, f32[128,128]{1,0:T(8,128)S(1)}, u32[]{:S(2)}, u32[]{:S(2)}) collective-permute-start(f32[128,128]{1,0:T(8,128)} %get-tuple-element.16), channel_id=1, source_target_pairs={{0,8},{16,24},{8,0},{24,16},{1,9},{17,25},{9,1},{25,17},{2,10},{18... | collective-permute-start | bytes 196616 | tf_op jit(solution)/shard_map/ppermute | solution.py:94
  10.7 0.7 collective-permute-start.1
  12.0 2.4 %fusion.4.after_ref = f32[40,128]{1,0:T(8,128)S(1)} fusion(f32[128,4352]{1,0:T(8,128)S(1)} %copy-done.1, f32[40,4352]{1,0:T(8,128)S(1)} %copy-done.5, f32[40]{0:T(128)S(1)} %compare_convert_fusion), kind=kOutput, calls=%fused_computation.7 | convolution fusion | flops 267560960 | bytes 2945184 | tf_op jit(solution)/shard_map/dot_general | solution.py:154
  14.4 0.9 %broadcast_in_dim.30 = f32[32,40,128]{2,1,0:T(8,128)} broadcast(f32[40,128]{1,0:T(8,128)S(1)} %fusion.4.after_ref), dimensions={1,2} | broadcast | bytes 675840 | tf_op jit(solution)/shard_map/broadcast_in_dim | solution.py:158
  15.3 6.8 %all-to-all-start = ((f32[32,40,128]{2,1,0:T(8,128)}), f32[32,40,128]{2,1,0:T(8,128)}, u32[]{:S(2)}, u32[]{:S(2)}) async-start(f32[32,40,128]{2,1,0:T(8,128)} %broadcast_in_dim.30), calls=%async_computation | async-start | bytes 1310720 | tf_op jit(solution)/shard_map/all_to_all | solution.py:159
  22.3 1.7 %collective-permute-start.2 = (f32[128,128]{1,0:T(8,128)S(1)}, f32[128,128]{1,0:T(8,128)S(1)}, u32[]{:S(2)}, u32[]{:S(2)}) collective-permute-start(f32[128,128]{1,0:T(8,128)S(1)} %get-tuple-element.14), channel_id=1, source_target_pairs={{0,2},{4,6},{2,0},{6,4},{1,3},{5,7},{3,1},{7,5},{8,10},{12,14},{10... | collective-permute-start | bytes 196616 | tf_op jit(solution)/shard_map/ppermute | solution.py:94
  24.0 0.7 collective-permute-start.3
  24.7 6.8 %collective-permute-done.2 = f32[128,128]{1,0:T(8,128)S(1)} collective-permute-done((f32[128,128]{1,0:T(8,128)S(1)}, f32[128,128]{1,0:T(8,128)S(1)}, u32[]{:S(2)}, u32[]{:S(2)}) %collective-permute-start.2) | collective-permute-done | bytes 65568 | tf_op jit(solution)/shard_map/ppermute | solution.py:94
  31.6 13.2 %shard_map.82 = (bf16[128,4352]{1,0:T(8,128)(2,1)S(1)}, bf16[128,768]{1,0:T(8,128)(2,1)S(1)}) custom-call(s32[20]{0:T(128)S(1)} %copy-done.2, f32[128,4352]{1,0:T(8,128)S(1)} %copy-done.1, f32[128,768]{1,0:T(8,128)S(1)} %select_dynamic-update-slice_fusion.slot_ref, bf16[20,256,256]{2,1,0:T(8,128)(2,1)} %inv_ref.1, bf16[19,256,256]{2,1,0:T(8,128)(2,1)} %cpl_ref.1, ...), custom_call_target="tpu_custom_call" | custom-call | tf_op jit(solution)/shard_map/pallas_call | solution.py:61
  44.7 1.0 %copy-done.3 = bf16[128,4352]{1,0:T(8,128)(2,1)} copy-done((bf16[128,4352]{1,0:T(8,128)(2,1)}, bf16[128,4352]{1,0:T(8,128)(2,1)S(1)}, u32[]{:S(2)}) %copy-start.3) | copy-done | bytes 1114136
  45.9 0.8 %collective-permute-start.7 = (bf16[128,128]{1,0:T(8,128)(2,1)S(1)}, bf16[128,128]{1,0:T(8,128)(2,1)S(1)}, u32[]{:S(2)}, u32[]{:S(2)}) collective-permute-start(bf16[128,128]{1,0:T(8,128)(2,1)S(1)} %get-tuple-element.19), channel_id=1, source_target_pairs={{2,4},{4,2},{3,5},{5,3},{10,12},{12,10},{11,13},{13,11},{18,20},{2... | collective-permute-start | bytes 98312 | tf_op jit(solution)/shard_map/ppermute | solution.py:94
  46.7 5.9 %collective-permute-start.8 = (bf16[128,128]{1,0:T(8,128)(2,1)S(1)}, bf16[128,128]{1,0:T(8,128)(2,1)S(1)}, u32[]{:S(2)}, u32[]{:S(2)}) collective-permute-start(bf16[128,128]{1,0:T(8,128)(2,1)S(1)} %get-tuple-element.20), channel_id=1, source_target_pairs={{0,2},{4,6},{2,0},{6,4},{1,3},{5,7},{3,1},{7,5},{8,10},{12,14},{10... | collective-permute-start | bytes 98312 | tf_op jit(solution)/shard_map/ppermute | solution.py:94
  52.5 0.8 %collective-permute-start.5 = (bf16[128,128]{1,0:T(8,128)(2,1)S(1)}, bf16[128,128]{1,0:T(8,128)(2,1)S(1)}, u32[]{:S(2)}, u32[]{:S(2)}) collective-permute-start(bf16[128,128]{1,0:T(8,128)(2,1)S(1)} %get-tuple-element.21), channel_id=1, source_target_pairs={{8,16},{16,8},{9,17},{17,9},{10,18},{18,10},{11,19},{19,11},{12,20... | collective-permute-start | bytes 98312 | tf_op jit(solution)/shard_map/ppermute | solution.py:94
  53.4 3.7 %collective-permute-start.6 = (bf16[128,128]{1,0:T(8,128)(2,1)S(1)}, bf16[128,128]{1,0:T(8,128)(2,1)S(1)}, u32[]{:S(2)}, u32[]{:S(2)}) collective-permute-start(bf16[128,128]{1,0:T(8,128)(2,1)S(1)} %get-tuple-element.22), channel_id=1, source_target_pairs={{0,8},{16,24},{8,0},{24,16},{1,9},{17,25},{9,1},{25,17},{2,10},{18... | collective-permute-start | bytes 98312 | tf_op jit(solution)/shard_map/ppermute | solution.py:94
  57.0 2.3 %fusion.10 = f32[128,40]{1,0:T(8,128)S(1)} fusion(f32[1280,128]{1,0:T(8,128)} %bitcast.10, f32[40,1280]{1,0:T(8,128)S(1)} %copy-done), kind=kOutput, calls=%fused_computation.40 | convolution fusion | flops 78643200 | bytes 880640 | tf_op jit(solution)/shard_map/dot_general | solution.py:182
  59.3 1.9 %fusion.2 = f32[128,4352]{1,0:T(8,128)S(1)} fusion(f32[128,40]{1,0:T(8,128)S(1)} %fusion.10, f32[40,4352]{1,0:T(8,128)S(1)} %copy-done.5, f32[40]{0:T(128)S(1)} %compare_convert_fusion), kind=kOutput, calls=%fused_computation.5 | convolution fusion | flops 267560960 | bytes 2945184 | tf_op jit(solution)/shard_map/dot_general | solution.py:189
  61.5 4.6 %add_add_fusion = f32[128,4352]{1,0:T(8,128)} fusion(f32[128,4352]{1,0:T(8,128)S(1)} %fusion.2, bf16[128,4352]{1,0:T(8,128)(2,1)S(1)} %copy-done.4, bf16[128,768]{1,0:T(8,128)(2,1)S(1)} %select_dynamic-update-slice_fusion.6, s32[768]{0:T(1024)S(1)} %bitcast.25), kind=kOutput, calls=%fused_computation.4 | convolution fusion | flops 860651520 | bytes 5770240 | tf_op jit(solution)/shard_map/dot_general | solution.py:188
  (40 shorter events, 0.6 us)
Async XLA Ops:
  0.0 57.0 %copy-start = (f32[40,1280]{1,0:T(8,128)S(1)}, f32[40,1280]{1,0:T(8,128)}, u32[]{:S(2)}) copy-start(f32[40,1280]{1,0:T(8,128)} %param.15) | copy-start | bytes 614404
  3.4 8.6 %copy-start.5 = (f32[40,4352]{1,0:T(8,128)S(1)}, f32[40,4352]{1,0:T(8,128)}, u32[]{:S(2)}) copy-start(f32[40,4352]{1,0:T(8,128)} %param.14) | copy-start | bytes 2088964
  5.0 7.0 %copy-start.1 = (f32[128,4352]{1,0:T(8,128)S(1)}, f32[128,4352]{1,0:T(8,128)}, u32[]{:S(2)}) copy-start(f32[128,4352]{1,0:T(8,128)} %res_ref.1) | copy-start | bytes 6684676
  7.6 17.0 %collective-permute-start = (f32[128,128]{1,0:T(8,128)}, f32[128,128]{1,0:T(8,128)S(1)}, u32[]{:S(2)}, u32[]{:S(2)}) collective-permute-start(f32[128,128]{1,0:T(8,128)} %get-tuple-element.16), channel_id=1, source_target_pairs={{0,8},{16,24},{8,0},{24,16},{1,9},{17,25},{9,1},{25,17},{2,10},{18... | collective-permute-start | bytes 196616 | tf_op jit(solution)/shard_map/ppermute | solution.py:94
  10.7 14.0 %collective-permute-start.1 = (f32[128,128]{1,0:T(8,128)S(1)}, f32[128,128]{1,0:T(8,128)S(1)}, u32[]{:S(2)}, u32[]{:S(2)}) collective-permute-start(f32[128,128]{1,0:T(8,128)S(1)} %get-tuple-element.17), channel_id=1, source_target_pairs={{8,16},{16,8},{9,17},{17,9},{10,18},{18,10},{11,19},{19,11},{12,20... | collective-permute-start | bytes 196616 | tf_op jit(solution)/shard_map/ppermute | solution.py:94
  14.4 17.2 %copy-start.2 = (s32[20]{0:T(128)S(1)}, s32[20]{0:T(128)}, u32[]{:S(2)}) copy-start(s32[20]{0:T(128)} %parent_ref.1) | copy-start | bytes 244
  15.3 30.5 %all-to-all-start = ((f32[32,40,128]{2,1,0:T(8,128)}), f32[32,40,128]{2,1,0:T(8,128)}, u32[]{:S(2)}, u32[]{:S(2)}) async-start(f32[32,40,128]{2,1,0:T(8,128)} %broadcast_in_dim.30), calls=%async_computation | async-start | bytes 1310720 | tf_op jit(solution)/shard_map/all_to_all | solution.py:159
  22.0 9.5 %collective-permute-start.4 = (f32[128,128]{1,0:T(8,128)S(1)}, f32[128,128]{1,0:T(8,128)S(1)}, u32[]{:S(2)}, u32[]{:S(2)}) collective-permute-start(f32[128,128]{1,0:T(8,128)S(1)} %get-tuple-element.13), channel_id=1, source_target_pairs={{0,1},{1,0},{2,3},{3,2},{4,5},{5,4},{6,7},{7,6},{8,9},{9,8},{10,11... | collective-permute-start | bytes 196616 | tf_op jit(solution)/shard_map/ppermute | solution.py:94
  22.3 9.2 %collective-permute-start.2 = (f32[128,128]{1,0:T(8,128)S(1)}, f32[128,128]{1,0:T(8,128)S(1)}, u32[]{:S(2)}, u32[]{:S(2)}) collective-permute-start(f32[128,128]{1,0:T(8,128)S(1)} %get-tuple-element.14), channel_id=1, source_target_pairs={{0,2},{4,6},{2,0},{6,4},{1,3},{5,7},{3,1},{7,5},{8,10},{12,14},{10... | collective-permute-start | bytes 196616 | tf_op jit(solution)/shard_map/ppermute | solution.py:94
  24.0 7.5 %collective-permute-start.3 = (f32[128,128]{1,0:T(8,128)S(1)}, f32[128,128]{1,0:T(8,128)S(1)}, u32[]{:S(2)}, u32[]{:S(2)}) collective-permute-start(f32[128,128]{1,0:T(8,128)S(1)} %get-tuple-element.15), channel_id=1, source_target_pairs={{2,4},{4,2},{3,5},{5,3},{10,12},{12,10},{11,13},{13,11},{18,20},{2... | collective-permute-start | bytes 196616 | tf_op jit(solution)/shard_map/ppermute | solution.py:94
  44.7 1.0 %copy-start.3 = (bf16[128,4352]{1,0:T(8,128)(2,1)}, bf16[128,4352]{1,0:T(8,128)(2,1)S(1)}, u32[]{:S(2)}) copy-start(bf16[128,4352]{1,0:T(8,128)(2,1)S(1)} %get-tuple-element.9) | copy-start | bytes 3342340
  45.7 15.8 %copy-start.4 = (bf16[128,4352]{1,0:T(8,128)(2,1)S(1)}, bf16[128,4352]{1,0:T(8,128)(2,1)}, u32[]{:S(2)}) copy-start(bf16[128,4352]{1,0:T(8,128)(2,1)} %copy-done.3) | copy-start | bytes 3342340
  45.8 15.8 %copy-start.6 = (s32[6,128]{1,0:T(8,128)S(1)}, s32[6,128]{1,0:T(8,128)}, u32[]{:S(2)}) copy-start(s32[6,128]{1,0:T(8,128)} %param.12) | copy-start | bytes 9220
  45.8 15.7 %collective-permute-start.9 = (bf16[128,128]{1,0:T(8,128)(2,1)S(1)}, bf16[128,128]{1,0:T(8,128)(2,1)S(1)}, u32[]{:S(2)}, u32[]{:S(2)}) collective-permute-start(bf16[128,128]{1,0:T(8,128)(2,1)S(1)} %get-tuple-element.18), channel_id=1, source_target_pairs={{0,1},{1,0},{2,3},{3,2},{4,5},{5,4},{6,7},{7,6},{8,9},{9,8},{10,11... | collective-permute-start | bytes 98312 | tf_op jit(solution)/shard_map/ppermute | solution.py:94
  45.9 15.5 %collective-permute-start.7 = (bf16[128,128]{1,0:T(8,128)(2,1)S(1)}, bf16[128,128]{1,0:T(8,128)(2,1)S(1)}, u32[]{:S(2)}, u32[]{:S(2)}) collective-permute-start(bf16[128,128]{1,0:T(8,128)(2,1)S(1)} %get-tuple-element.19), channel_id=1, source_target_pairs={{2,4},{4,2},{3,5},{5,3},{10,12},{12,10},{11,13},{13,11},{18,20},{2... | collective-permute-start | bytes 98312 | tf_op jit(solution)/shard_map/ppermute | solution.py:94
  46.7 14.7 %collective-permute-start.8 = (bf16[128,128]{1,0:T(8,128)(2,1)S(1)}, bf16[128,128]{1,0:T(8,128)(2,1)S(1)}, u32[]{:S(2)}, u32[]{:S(2)}) collective-permute-start(bf16[128,128]{1,0:T(8,128)(2,1)S(1)} %get-tuple-element.20), channel_id=1, source_target_pairs={{0,2},{4,6},{2,0},{6,4},{1,3},{5,7},{3,1},{7,5},{8,10},{12,14},{10... | collective-permute-start | bytes 98312 | tf_op jit(solution)/shard_map/ppermute | solution.py:94
  52.5 8.8 %collective-permute-start.5 = (bf16[128,128]{1,0:T(8,128)(2,1)S(1)}, bf16[128,128]{1,0:T(8,128)(2,1)S(1)}, u32[]{:S(2)}, u32[]{:S(2)}) collective-permute-start(bf16[128,128]{1,0:T(8,128)(2,1)S(1)} %get-tuple-element.21), channel_id=1, source_target_pairs={{8,16},{16,8},{9,17},{17,9},{10,18},{18,10},{11,19},{19,11},{12,20... | collective-permute-start | bytes 98312 | tf_op jit(solution)/shard_map/ppermute | solution.py:94
  53.4 7.9 %collective-permute-start.6 = (bf16[128,128]{1,0:T(8,128)(2,1)S(1)}, bf16[128,128]{1,0:T(8,128)(2,1)S(1)}, u32[]{:S(2)}, u32[]{:S(2)}) collective-permute-start(bf16[128,128]{1,0:T(8,128)(2,1)S(1)} %get-tuple-element.22), channel_id=1, source_target_pairs={{0,8},{16,24},{8,0},{24,16},{1,9},{17,25},{9,1},{25,17},{2,10},{18... | collective-permute-start | bytes 98312 | tf_op jit(solution)/shard_map/ppermute | solution.py:94

commit v14 on v13

--- a/solution.py
+++ b/solution.py
@@ -155,8 +155,6 @@
         vectors, residual, NT, precision=lax.Precision.HIGHEST, preferred_element_type=jnp.float32
     )
     total_dev = coarse_inverse.shape[1] // kmax_here
-    spread = jnp.broadcast_to(coeffs_t[None], (total_dev,) + coeffs_t.shape)
-    held = lax.all_to_all(spread, AXES, 0, 0, tiled=True)
 
     outgoing = jnp.take(residual, send_rows, axis=1)
     incoming = []
@@ -164,6 +162,9 @@
         low, high, _ = halo_out(outgoing[:, 2 * axis_pos], outgoing[:, 2 * axis_pos + 1], axis)
         incoming += [low, high]
     slots = jnp.concatenate(incoming, axis=1)
+    slots, coeffs_t = lax.optimization_barrier((slots, coeffs_t))
+    spread = jnp.broadcast_to(coeffs_t[None], (total_dev,) + coeffs_t.shape)
+    held = lax.all_to_all(spread, AXES, 0, 0, tiled=True)
     after = coeffs_t
 
     own, zslots = local_solve(parent, residual, slots, diag_inverse, coupling, after)

time: 66.5 us -> 63.1 us (0.949)
  waiting for transfers between devices: 6.8 us -> 3.76 us
  matrix products: 11.2 us -> 12.3 us
  starting transfers between devices: 24.3 us -> 23.4 us
    ppermute x10, waiting for transfers between devices: 6.8 us -> 0.03 us  [swap(): return (lax.ppermute(value, axis, pairs), None)]
    all_to_all x1, waiting for transfers between devices: 0.01 us -> 3.73 us  [per_device(): held = lax.all_to_all(spread, AXES, 0, 0, tiled=True)]
    ppermute x10, starting transfers between devices: 17.5 us -> 14.2 us  [swap(): return (lax.ppermute(value, axis, pairs), None)]
    all_to_all x1, starting transfers between devices: 6.76 us -> 9.14 us  [per_device(): held = lax.all_to_all(spread, AXES, 0, 0, tiled=True)]
    dot_general x1, matrix products: 1.95 us -> 3.06 us  [per_device(): lax.dot_general(solved_t, vectors, (((0,), (0,)), ((), ())), precision=la...]
  transfers between devices with their start and end apart: 11 -> 11, of which waited for: 1 -> 1; matrix products, arithmetic and copies ran while one was open for 12% -> 12% of each run, Pallas kernels for 20% -> 21%
where the time goes in v14:
time: 63.1 us; the launch traced here: 62.7 us
  starting transfers between devices  23.4 us (37%)
  Pallas kernels  13.2 us (21%)
  matrix products  12.3 us (19%)
  local copies, waits for them, and re-layouts  6.4 us (10%)
  waiting for transfers between devices  3.76 us (6%)
  other arithmetic  2.69 us (4%)
  between operations  1 us (2%)
    ppermute x10, starting transfers between devices, swap(): return (lax.ppermute(value, axis, pairs), None)  14.2 us
    pallas_call x1, Pallas kernels, local_solve(): pl.pallas_call(solve_kernel, out_shape=(jax.ShapeDtypeStruct((nrhs_here,...  13.2 us
    all_to_all x1, starting transfers between devices, per_device(): held = lax.all_to_all(spread, AXES, 0, 0, tiled=True)  9.14 us
    dot_general x1, matrix products, per_device(): faces = jnp.dot(returned, onehot, preferred_element_type=jnp.float32)  4.61 us
    all_to_all x1, waiting for transfers between devices, per_device(): held = lax.all_to_all(spread, AXES, 0, 0, tiled=True)  3.73 us
    dot_general x1, matrix products, per_device(): lax.dot_general(solved_t, vectors, (((0,), (0,)), ((), ())), precision=la...  3.06 us
    unnamed x15, local copies, waits for them, and re-layouts  3.02 us
    gather x2, local copies, waits for them, and re-layouts, per_device(): outgoing = jnp.take(residual, send_rows, axis=1)  2.49 us
  transfers between devices with their start and end apart: 11, of which 1 were waited for; matrix products, arithmetic and copies ran while one was open for 12% of the time, Pallas kernels for 21%

profile of v14, /device:TPU:0, one launch (start us, length us, event | category | flops | bytes accessed | tf_op | source)
XLA Modules:
  0.0 62.7 jit_solution(881722843261095008)
XLA Ops:
  0.0 0.7 %compare_and_fusion = pred[6,128]{1,0:T(8,128)(4,1)S(1)} fusion(s32[6,128]{1,0:T(8,128)} %param.12), kind=kLoop, calls=%fused_computation.38 | loop fusion | flops 4608 | bytes 3840 | tf_op jit(solution)/shard_map/jit(_take)/and | solution.py:159
  0.7 0.7 %fusion.11 = s32[768]{0:T(1024)S(1)} fusion(s32[6,128]{1,0:T(8,128)} %param.12), kind=kLoop, calls=%fused_computation.39 | loop fusion | flops 2304 | bytes 6144 | tf_op jit(solution)/shard_map/jit(_take)/broadcast_in_dim | solution.py:159
  1.4 2.0 %copy.10 = f32[128,4352]{0,1:T(8,128)S(1)} copy(f32[128,4352]{1,0:T(8,128)} %res_ref.1) | data formatting | bytes 4456448 | tf_op args[0]
  3.5 1.6 %gather_fusion = f32[768,128]{1,0:T(8,128)S(1)} fusion(f32[128,4352]{0,1:T(8,128)S(1)} %copy.10, s32[1024]{0:T(1024)S(1)} %pad_clamp_fusion), kind=kCustom, calls=%fused_computation | custom fusion | bytes 789504 | tf_op jit(solution)/shard_map/jit(_take)/gather | solution.py:159
  5.0 0.9 %copy.11 = f32[6,128,128]{1,2,0:T(8,128)} copy(f32[6,128,128]{2,1,0:T(8,128)S(1)} %bitcast.24) | data formatting | bytes 786432 | tf_op jit(solution)/shard_map/jit(_take)/gather | solution.py:159
  6.0 1.0 %select_bitcast_fusion = f32[128,6,128]{2,0,1:T(8,128)S(1)} fusion(f32[6,128,128]{1,2,0:T(8,128)} %copy.11, pred[6,128]{1,0:T(8,128)(4,1)S(1)} %compare_and_fusion), kind=kLoop, calls=%fused_computation.10 | loop fusion | flops 98304 | bytes 787200 | tf_op jit(solution)/shard_map/jit(_take)/select_n | solution.py:159
  7.0 0.5 collective-permute-start.4
  7.5 2.6 %collective-permute-start.2 = (f32[128,128]{1,0:T(8,128)S(1)}, f32[128,128]{1,0:T(8,128)S(1)}, u32[]{:S(2)}, u32[]{:S(2)}) collective-permute-start(f32[128,128]{1,0:T(8,128)S(1)} %get-tuple-element.18), channel_id=1, source_target_pairs={{0,2},{4,6},{2,0},{6,4},{1,3},{5,7},{3,1},{7,5},{8,10},{12,14},{10... | collective-permute-start | bytes 196616 | tf_op jit(solution)/shard_map/ppermute | solution.py:94
  10.1 0.7 %collective-permute-start.3 = (f32[128,128]{1,0:T(8,128)S(1)}, f32[128,128]{1,0:T(8,128)S(1)}, u32[]{:S(2)}, u32[]{:S(2)}) collective-permute-start(f32[128,128]{1,0:T(8,128)S(1)} %get-tuple-element.19), channel_id=1, source_target_pairs={{2,4},{4,2},{3,5},{5,3},{10,12},{12,10},{11,13},{13,11},{18,20},{2... | collective-permute-start | bytes 196616 | tf_op jit(solution)/shard_map/ppermute | solution.py:94
  10.8 1.6 %collective-permute-start = (f32[128,128]{1,0:T(8,128)S(1)}, f32[128,128]{1,0:T(8,128)S(1)}, u32[]{:S(2)}, u32[]{:S(2)}) collective-permute-start(f32[128,128]{1,0:T(8,128)S(1)} %get-tuple-element.20), channel_id=1, source_target_pairs={{0,8},{16,24},{8,0},{24,16},{1,9},{17,25},{9,1},{25,17},{2,10},{18... | collective-permute-start | bytes 196616 | tf_op jit(solution)/shard_map/ppermute | solution.py:94
  12.4 0.7 %collective-permute-start.1 = (f32[128,128]{1,0:T(8,128)S(1)}, f32[128,128]{1,0:T(8,128)S(1)}, u32[]{:S(2)}, u32[]{:S(2)}) collective-permute-start(f32[128,128]{1,0:T(8,128)S(1)} %get-tuple-element.21), channel_id=1, source_target_pairs={{8,16},{16,8},{9,17},{17,9},{10,18},{18,10},{11,19},{19,11},{12,20... | collective-permute-start | bytes 196616 | tf_op jit(solution)/shard_map/ppermute | solution.py:94
  13.8 2.3 %fusion.6.after_ref = f32[40,128]{1,0:T(8,128)S(1)} fusion(f32[128,4352]{1,0:T(8,128)S(1)} %copy-done.1, f32[40,4352]{1,0:T(8,128)S(1)} %copy-done.5, f32[40]{0:T(128)S(1)} %compare_convert_fusion), kind=kOutput, calls=%fused_computation.8 | convolution fusion | flops 267560960 | bytes 2945184 | tf_op jit(solution)/shard_map/dot_general | solution.py:154
  16.3 0.9 %broadcast_in_dim.30 = f32[32,40,128]{2,1,0:T(8,128)} broadcast(f32[40,128]{1,0:T(8,128)S(1)} %fusion.6.after_ref), dimensions={1,2} | broadcast | bytes 675840 | tf_op jit(solution)/shard_map/broadcast_in_dim | solution.py:166
  17.2 9.1 %all-to-all-start = ((f32[32,40,128]{2,1,0:T(8,128)}), f32[32,40,128]{2,1,0:T(8,128)}, u32[]{:S(2)}, u32[]{:S(2)}) async-start(f32[32,40,128]{2,1,0:T(8,128)} %broadcast_in_dim.30), calls=%async_computation | async-start | bytes 1310720 | tf_op jit(solution)/shard_map/all_to_all | solution.py:167
  26.3 13.2 %shard_map.82 = (bf16[128,4352]{1,0:T(8,128)(2,1)S(1)}, bf16[128,768]{1,0:T(8,128)(2,1)S(1)}) custom-call(s32[20]{0:T(128)S(1)} %copy-done.2, f32[128,4352]{1,0:T(8,128)S(1)} %copy-done.1, f32[128,768]{1,0:T(8,128)S(1)} %select_dynamic-update-slice_fusion.slot_ref, bf16[20,256,256]{2,1,0:T(8,128)(2,1)} %inv_ref.1, bf16[19,256,256]{2,1,0:T(8,128)(2,1)} %cpl_ref.1, ...), custom_call_target="tpu_custom_call" | custom-call | tf_op jit(solution)/shard_map/pallas_call | solution.py:61
  39.5 1.0 %copy-done.3 = bf16[128,4352]{1,0:T(8,128)(2,1)} copy-done((bf16[128,4352]{1,0:T(8,128)(2,1)}, bf16[128,4352]{1,0:T(8,128)(2,1)S(1)}, u32[]{:S(2)}) %copy-start.3) | copy-done | bytes 1114136
  40.5 3.7 %all-to-all-done = f32[32,40,128]{2,1,0:T(8,128)} async-done(((f32[32,40,128]{2,1,0:T(8,128)}), f32[32,40,128]{2,1,0:T(8,128)}, u32[]{:S(2)}, u32[]{:S(2)}) %all-to-all-start) | async-done | bytes 655392 | tf_op jit(solution)/shard_map/all_to_all | solution.py:167
  44.4 0.8 %collective-permute-start.7 = (bf16[128,128]{1,0:T(8,128)(2,1)S(1)}, bf16[128,128]{1,0:T(8,128)(2,1)S(1)}, u32[]{:S(2)}, u32[]{:S(2)}) collective-permute-start(bf16[128,128]{1,0:T(8,128)(2,1)S(1)} %get-tuple-element.23), channel_id=1, source_target_pairs={{2,4},{4,2},{3,5},{5,3},{10,12},{12,10},{11,13},{13,11},{18,20},{2... | collective-permute-start | bytes 98312 | tf_op jit(solution)/shard_map/ppermute | solution.py:94
  45.2 4.1 %collective-permute-start.8 = (bf16[128,128]{1,0:T(8,128)(2,1)S(1)}, bf16[128,128]{1,0:T(8,128)(2,1)S(1)}, u32[]{:S(2)}, u32[]{:S(2)}) collective-permute-start(bf16[128,128]{1,0:T(8,128)(2,1)S(1)} %get-tuple-element.24), channel_id=1, source_target_pairs={{0,2},{4,6},{2,0},{6,4},{1,3},{5,7},{3,1},{7,5},{8,10},{12,14},{10... | collective-permute-start | bytes 98312 | tf_op jit(solution)/shard_map/ppermute | solution.py:94
  49.3 0.8 %collective-permute-start.5 = (bf16[128,128]{1,0:T(8,128)(2,1)S(1)}, bf16[128,128]{1,0:T(8,128)(2,1)S(1)}, u32[]{:S(2)}, u32[]{:S(2)}) collective-permute-start(bf16[128,128]{1,0:T(8,128)(2,1)S(1)} %get-tuple-element.25), channel_id=1, source_target_pairs={{8,16},{16,8},{9,17},{17,9},{10,18},{18,10},{11,19},{19,11},{12,20... | collective-permute-start | bytes 98312 | tf_op jit(solution)/shard_map/ppermute | solution.py:94
  50.2 2.3 %collective-permute-start.6 = (bf16[128,128]{1,0:T(8,128)(2,1)S(1)}, bf16[128,128]{1,0:T(8,128)(2,1)S(1)}, u32[]{:S(2)}, u32[]{:S(2)}) collective-permute-start(bf16[128,128]{1,0:T(8,128)(2,1)S(1)} %get-tuple-element.26), channel_id=1, source_target_pairs={{0,8},{16,24},{8,0},{24,16},{1,9},{17,25},{9,1},{25,17},{2,10},{18... | collective-permute-start | bytes 98312 | tf_op jit(solution)/shard_map/ppermute | solution.py:94
  52.5 2.3 %fusion.12 = f32[128,40]{1,0:T(8,128)S(1)} fusion(f32[1280,128]{1,0:T(8,128)} %bitcast.10, f32[40,1280]{1,0:T(8,128)S(1)} %copy-done), kind=kOutput, calls=%fused_computation.41 | convolution fusion | flops 78643200 | bytes 880640 | tf_op jit(solution)/shard_map/dot_general | solution.py:183
  54.8 3.1 %fusion.4 = f32[128,4352]{1,0:T(8,128)S(1)} fusion(f32[128,40]{1,0:T(8,128)S(1)} %fusion.12, f32[40,4352]{1,0:T(8,128)} %param.14, f32[40]{0:T(128)S(1)} %compare_convert_fusion), kind=kOutput, calls=%fused_computation.6 | convolution fusion | flops 267560960 | bytes 2945184 | tf_op jit(solution)/shard_map/dot_general | solution.py:190
  58.1 4.6 %fusion.3 = f32[128,4352]{1,0:T(8,128)} fusion(f32[128,4352]{1,0:T(8,128)S(1)} %fusion.4, bf16[128,768]{1,0:T(8,128)(2,1)S(1)} %select_dynamic-update-slice_fusion.6, s32[768]{0:T(1024)S(1)} %bitcast.25, bf16[128,4352]{1,0:T(8,128)(2,1)S(1)} %copy-done.4), kind=kOutput, calls=%fused_computation.5 | convolution fusion | flops 860651520 | bytes 5770240 | tf_op jit(solution)/shard_map/dot_general | solution.py:189
  (40 shorter events, 0.4 us)
Async XLA Ops:
  0.0 52.5 %copy-start = (f32[40,1280]{1,0:T(8,128)S(1)}, f32[40,1280]{1,0:T(8,128)}, u32[]{:S(2)}) copy-start(f32[40,1280]{1,0:T(8,128)} %param.15) | copy-start | bytes 614404
  3.4 10.3 %copy-start.5 = (f32[40,4352]{1,0:T(8,128)S(1)}, f32[40,4352]{1,0:T(8,128)}, u32[]{:S(2)}) copy-start(f32[40,4352]{1,0:T(8,128)} %param.14) | copy-start | bytes 2088964
  5.0 8.7 %copy-start.1 = (f32[128,4352]{1,0:T(8,128)S(1)}, f32[128,4352]{1,0:T(8,128)}, u32[]{:S(2)}) copy-start(f32[128,4352]{1,0:T(8,128)} %res_ref.1) | copy-start | bytes 6684676
  7.0 9.2 %collective-permute-start.4 = (f32[128,128]{1,0:T(8,128)S(1)}, f32[128,128]{1,0:T(8,128)S(1)}, u32[]{:S(2)}, u32[]{:S(2)}) collective-permute-start(f32[128,128]{1,0:T(8,128)S(1)} %get-tuple-element.17), channel_id=1, source_target_pairs={{0,1},{1,0},{2,3},{3,2},{4,5},{5,4},{6,7},{7,6},{8,9},{9,8},{10,11... | collective-permute-start | bytes 196616 | tf_op jit(solution)/shard_map/ppermute | solution.py:94
  7.5 8.6 %collective-permute-start.2 = (f32[128,128]{1,0:T(8,128)S(1)}, f32[128,128]{1,0:T(8,128)S(1)}, u32[]{:S(2)}, u32[]{:S(2)}) collective-permute-start(f32[128,128]{1,0:T(8,128)S(1)} %get-tuple-element.18), channel_id=1, source_target_pairs={{0,2},{4,6},{2,0},{6,4},{1,3},{5,7},{3,1},{7,5},{8,10},{12,14},{10... | collective-permute-start | bytes 196616 | tf_op jit(solution)/shard_map/ppermute | solution.py:94
  10.1 6.1 %collective-permute-start.3 = (f32[128,128]{1,0:T(8,128)S(1)}, f32[128,128]{1,0:T(8,128)S(1)}, u32[]{:S(2)}, u32[]{:S(2)}) collective-permute-start(f32[128,128]{1,0:T(8,128)S(1)} %get-tuple-element.19), channel_id=1, source_target_pairs={{2,4},{4,2},{3,5},{5,3},{10,12},{12,10},{11,13},{13,11},{18,20},{2... | collective-permute-start | bytes 196616 | tf_op jit(solution)/shard_map/ppermute | solution.py:94
  10.8 5.3 %collective-permute-start = (f32[128,128]{1,0:T(8,128)S(1)}, f32[128,128]{1,0:T(8,128)S(1)}, u32[]{:S(2)}, u32[]{:S(2)}) collective-permute-start(f32[128,128]{1,0:T(8,128)S(1)} %get-tuple-element.20), channel_id=1, source_target_pairs={{0,8},{16,24},{8,0},{24,16},{1,9},{17,25},{9,1},{25,17},{2,10},{18... | collective-permute-start | bytes 196616 | tf_op jit(solution)/shard_map/ppermute | solution.py:94
  12.4 3.7 %collective-permute-start.1 = (f32[128,128]{1,0:T(8,128)S(1)}, f32[128,128]{1,0:T(8,128)S(1)}, u32[]{:S(2)}, u32[]{:S(2)}) collective-permute-start(f32[128,128]{1,0:T(8,128)S(1)} %get-tuple-element.21), channel_id=1, source_target_pairs={{8,16},{16,8},{9,17},{17,9},{10,18},{18,10},{11,19},{19,11},{12,20... | collective-permute-start | bytes 196616 | tf_op jit(solution)/shard_map/ppermute | solution.py:94
  16.1 10.2 %copy-start.2 = (s32[20]{0:T(128)S(1)}, s32[20]{0:T(128)}, u32[]{:S(2)}) copy-start(s32[20]{0:T(128)} %parent_ref.1) | copy-start | bytes 244
  17.2 27.1 %all-to-all-start = ((f32[32,40,128]{2,1,0:T(8,128)}), f32[32,40,128]{2,1,0:T(8,128)}, u32[]{:S(2)}, u32[]{:S(2)}) async-start(f32[32,40,128]{2,1,0:T(8,128)} %broadcast_in_dim.30), calls=%async_computation | async-start | bytes 1310720 | tf_op jit(solution)/shard_map/all_to_all | solution.py:167
  39.5 1.0 %copy-start.3 = (bf16[128,4352]{1,0:T(8,128)(2,1)}, bf16[128,4352]{1,0:T(8,128)(2,1)S(1)}, u32[]{:S(2)}) copy-start(bf16[128,4352]{1,0:T(8,128)(2,1)S(1)} %get-tuple-element.13) | copy-start | bytes 3342340
  44.2 13.8 %copy-start.4 = (bf16[128,4352]{1,0:T(8,128)(2,1)S(1)}, bf16[128,4352]{1,0:T(8,128)(2,1)}, u32[]{:S(2)}) copy-start(bf16[128,4352]{1,0:T(8,128)(2,1)} %copy-done.3) | copy-start | bytes 3342340
  44.3 13.8 %copy-start.6 = (s32[6,128]{1,0:T(8,128)S(1)}, s32[6,128]{1,0:T(8,128)}, u32[]{:S(2)}) copy-start(s32[6,128]{1,0:T(8,128)} %param.12) | copy-start | bytes 9220
  44.3 13.7 %collective-permute-start.9 = (bf16[128,128]{1,0:T(8,128)(2,1)S(1)}, bf16[128,128]{1,0:T(8,128)(2,1)S(1)}, u32[]{:S(2)}, u32[]{:S(2)}) collective-permute-start(bf16[128,128]{1,0:T(8,128)(2,1)S(1)} %get-tuple-element.22), channel_id=1, source_target_pairs={{0,1},{1,0},{2,3},{3,2},{4,5},{5,4},{6,7},{7,6},{8,9},{9,8},{10,11... | collective-permute-start | bytes 98312 | tf_op jit(solution)/shard_map/ppermute | solution.py:94
  44.4 13.5 %collective-permute-start.7 = (bf16[128,128]{1,0:T(8,128)(2,1)S(1)}, bf16[128,128]{1,0:T(8,128)(2,1)S(1)}, u32[]{:S(2)}, u32[]{:S(2)}) collective-permute-start(bf16[128,128]{1,0:T(8,128)(2,1)S(1)} %get-tuple-element.23), channel_id=1, source_target_pairs={{2,4},{4,2},{3,5},{5,3},{10,12},{12,10},{11,13},{13,11},{18,20},{2... | collective-permute-start | bytes 98312 | tf_op jit(solution)/shard_map/ppermute | solution.py:94
  45.2 12.7 %collective-permute-start.8 = (bf16[128,128]{1,0:T(8,128)(2,1)S(1)}, bf16[128,128]{1,0:T(8,128)(2,1)S(1)}, u32[]{:S(2)}, u32[]{:S(2)}) collective-permute-start(bf16[128,128]{1,0:T(8,128)(2,1)S(1)} %get-tuple-element.24), channel_id=1, source_target_pairs={{0,2},{4,6},{2,0},{6,4},{1,3},{5,7},{3,1},{7,5},{8,10},{12,14},{10... | collective-permute-start | bytes 98312 | tf_op jit(solution)/shard_map/ppermute | solution.py:94
  49.3 8.5 %collective-permute-start.5 = (bf16[128,128]{1,0:T(8,128)(2,1)S(1)}, bf16[128,128]{1,0:T(8,128)(2,1)S(1)}, u32[]{:S(2)}, u32[]{:S(2)}) collective-permute-start(bf16[128,128]{1,0:T(8,128)(2,1)S(1)} %get-tuple-element.25), channel_id=1, source_target_pairs={{8,16},{16,8},{9,17},{17,9},{10,18},{18,10},{11,19},{19,11},{12,20... | collective-permute-start | bytes 98312 | tf_op jit(solution)/shard_map/ppermute | solution.py:94
  50.2 7.7 %collective-permute-start.6 = (bf16[128,128]{1,0:T(8,128)(2,1)S(1)}, bf16[128,128]{1,0:T(8,128)(2,1)S(1)}, u32[]{:S(2)}, u32[]{:S(2)}) collective-permute-start(bf16[128,128]{1,0:T(8,128)(2,1)S(1)} %get-tuple-element.26), channel_id=1, source_target_pairs={{0,8},{16,24},{8,0},{24,16},{1,9},{17,25},{9,1},{25,17},{2,10},{18... | collective-permute-start | bytes 98312 | tf_op jit(solution)/shard_map/ppermute | solution.py:94

commit v15 on v12

--- a/solution.py
+++ b/solution.py
@@ -78,11 +78,6 @@
             pltpu.VMEM((blocks_n, nrhs_here, block_w), jnp.float32),
         ],
         compiler_params=pltpu.CompilerParams(vmem_limit_bytes=48 * 1024 * 1024),
-        cost_estimate=pl.CostEstimate(
-            flops=4 * (2 * blocks_n - 1) * nrhs_here * block_w * block_w,
-            transcendentals=0,
-            bytes_accessed=2 * (diag_inverse.size + coupling.size) + 6 * residual.size,
-        ),
     )(parent, residual, slots, diag_inverse, coupling, after)
 
 
@@ -198,42 +193,30 @@
     coeffs_t = lax.dot_general(
         vectors, residual, NT, precision=lax.Precision.HIGHEST, preferred_element_type=jnp.float32
     )
-    held = coeffs_t.reshape((1,) * len(AXES) + coeffs_t.shape)
+    total_dev = coarse_inverse.shape[1] // kmax_here
 
     outgoing = jnp.take(residual, send_rows, axis=1)
-    last = len(AXES) - 1
-    late = lax.axis_size(AXES[last]) == 2
     incoming = []
     for axis_pos, axis in enumerate(AXES):
-        ride = axis_pos < last and doubling(axis)
-        low, high, got = halo_out(
-            outgoing[:, 2 * axis_pos],
-            outgoing[:, 2 * axis_pos + 1],
-            axis,
-            rows_of(held) if ride else None,
-        )
+        low, high, _ = halo_out(outgoing[:, 2 * axis_pos], outgoing[:, 2 * axis_pos + 1], axis)
         incoming += [low, high]
-        if ride:
-            held = gather_axis(merge(held, got.reshape(held.shape), axis, axis_pos, 1), axis, axis_pos, 2)
-        elif axis_pos < last or not late:
-            held = gather_axis(held, axis, axis_pos)
+    slots = jnp.concatenate(incoming, axis=1)
+    slots, coeffs_t = lax.optimization_barrier((slots, coeffs_t))
+    spread = jnp.broadcast_to(coeffs_t[None], (total_dev,) + coeffs_t.shape)
+    held = lax.all_to_all(spread, AXES, 0, 0, tiled=True)
     after = coeffs_t
-    slots = jnp.concatenate(incoming, axis=1)
 
     own, zslots = local_solve(parent, residual, slots, diag_inverse, coupling, after)
+    zslots, held = lax.optimization_barrier((zslots, held))
 
     returned = []
     for axis_pos, axis in enumerate(AXES):
-        ride = axis_pos == last and late
-        low, high, got = halo_back(
+        low, high, _ = halo_back(
             zslots[:, (2 * axis_pos) * face_w : (2 * axis_pos + 1) * face_w],
             zslots[:, (2 * axis_pos + 1) * face_w : (2 * axis_pos + 2) * face_w],
             axis,
-            rows_of(held) if ride else None,
         )
         returned += [low, high]
-        if ride:
-            held = merge(held, got.reshape(held.shape), axis, last, 1)
     returned = jnp.concatenate(returned, axis=1)
 
     solved_t = jnp.dot(

time: 67.8 us -> 61.5 us (0.907)
  waiting for transfers between devices: 6.67 us -> 1.9 us
  other arithmetic: 7.48 us -> 3.62 us
  matrix products: 3.56 us -> 4.64 us
  local copies, waits for them, and re-layouts: 8.29 us -> 9 us
    ppermute x5 -> x0, starting transfers between devices: 11.9 us -> none  [the longest x3 6.5 us: swap(): got = lax.ppermute(packed, axis, pairs)]
    all_to_all x0 -> x1, starting transfers between devices: none -> 9.13 us  [per_device(): held = lax.all_to_all(spread, AXES, 0, 0, tiled=True)]
    ppermute x5 -> x0, waiting for transfers between devices: 4.78 us -> none  [the longest x3 3.79 us: swap(): got = lax.ppermute(packed, axis, pairs)]
    unnamed x10, other arithmetic: 3.57 us -> 0.16 us
    ppermute x7 -> x10, starting transfers between devices: 11.2 us -> 14.4 us  [swap(): return (lax.ppermute(value, axis, pairs), None)]
    unnamed x15 -> x23, local copies, waits for them, and re-layouts: 3.21 us -> 5.62 us
    all_to_all x0 -> x1, waiting for transfers between devices: none -> 1.87 us  [per_device(): held = lax.all_to_all(spread, AXES, 0, 0, tiled=True)]
    ppermute x7 -> x10, waiting for transfers between devices: 1.89 us -> 0.03 us  [swap(): return (lax.ppermute(value, axis, pairs), None)]
  transfers between devices with their start and end apart: 12 -> 11, of which waited for: 4 -> 1; matrix products, arithmetic and copies ran while one was open for 7% -> 8% of each run, Pallas kernels for 0% -> 22%
where the time goes in v15:
time: 61.5 us; the launch traced here: 61 us
  starting transfers between devices  23.5 us (38%)
  Pallas kernels  17.3 us (28%)
  local copies, waits for them, and re-layouts  9 us (15%)
  matrix products  4.64 us (8%)
  other arithmetic  3.62 us (6%)
  waiting for transfers between devices  1.9 us (3%)
  between operations  1.02 us (2%)
    ppermute x10, starting transfers between devices, swap(): return (lax.ppermute(value, axis, pairs), None)  14.4 us
    pallas_call x1, Pallas kernels, local_solve(): pl.pallas_call(solve_kernel, out_shape=(jax.ShapeDtypeStruct((nrhs_here,...  13.1 us
    all_to_all x1, starting transfers between devices, per_device(): held = lax.all_to_all(spread, AXES, 0, 0, tiled=True)  9.13 us
    unnamed x23, local copies, waits for them, and re-layouts  5.62 us
    pallas_call x1, Pallas kernels, finish(): pl.pallas_call(finish_kernel, out_shape=jax.ShapeDtypeStruct(own.shape, j...  4.17 us
    gather x2, local copies, waits for them, and re-layouts, per_device(): outgoing = jnp.take(residual, send_rows, axis=1)  2.49 us
    dot_general x1, matrix products, per_device(): lax.dot_general(vectors, residual, NT, precision=lax.Precision.HIGHEST, p...  2.35 us
    dot_general x1, matrix products, per_device(): jnp.dot(coarse_inverse, rows_of(held), precision=lax.Precision.HIGHEST, p...  2.3 us
  transfers between devices with their start and end apart: 11, of which 1 were waited for; matrix products, arithmetic and copies ran while one was open for 8% of the time, Pallas kernels for 22%

profile of v15, /device:TPU:0, one launch (start us, length us, event | category | flops | bytes accessed | tf_op | source)
XLA Modules:
  0.0 61.0 jit_solution(316632742572550823)
XLA Ops:
  0.0 0.7 %compare_and_fusion = pred[6,128]{1,0:T(8,128)(4,1)S(1)} fusion(s32[6,128]{1,0:T(8,128)} %param.12), kind=kLoop, calls=%fused_computation.30 | loop fusion | flops 4608 | bytes 3840 | tf_op jit(solution)/shard_map/jit(_take)/and | solution.py:198
  0.7 0.7 %fusion.4 = s32[768]{0:T(1024)S(1)} fusion(s32[6,128]{1,0:T(8,128)} %param.12), kind=kLoop, calls=%fused_computation.31 | loop fusion | flops 2304 | bytes 6144 | tf_op jit(solution)/shard_map/jit(_take)/broadcast_in_dim | solution.py:198
  1.4 2.0 %copy.11 = f32[128,4352]{0,1:T(8,128)S(1)} copy(f32[128,4352]{1,0:T(8,128)} %res_ref.1) | data formatting | bytes 4456448 | tf_op args[0]
  3.5 1.6 %gather_fusion = f32[768,128]{1,0:T(8,128)S(1)} fusion(f32[128,4352]{0,1:T(8,128)S(1)} %copy.11, s32[1024]{0:T(1024)S(1)} %pad_clamp_fusion), kind=kCustom, calls=%fused_computation | custom fusion | bytes 789504 | tf_op jit(solution)/shard_map/jit(_take)/gather | solution.py:198
  5.0 0.9 %copy.12 = f32[6,128,128]{1,2,0:T(8,128)} copy(f32[6,128,128]{2,1,0:T(8,128)S(1)} %bitcast.28) | data formatting | bytes 786432 | tf_op jit(solution)/shard_map/jit(_take)/gather | solution.py:198
  6.0 1.0 %select_bitcast_fusion = f32[128,6,128]{2,0,1:T(8,128)S(1)} fusion(f32[6,128,128]{1,2,0:T(8,128)} %copy.12, pred[6,128]{1,0:T(8,128)(4,1)S(1)} %compare_and_fusion), kind=kLoop, calls=%fused_computation.3 | loop fusion | flops 98304 | bytes 787200 | tf_op jit(solution)/shard_map/jit(_take)/select_n | solution.py:198
  7.5 2.6 %collective-permute-start.2 = (f32[128,128]{1,0:T(8,128)S(1)}, f32[128,128]{1,0:T(8,128)S(1)}, u32[]{:S(2)}, u32[]{:S(2)}) collective-permute-start(f32[128,128]{1,0:T(8,128)S(1)} %get-tuple-element.18), channel_id=1, source_target_pairs={{0,2},{4,6},{2,0},{6,4},{1,3},{5,7},{3,1},{7,5},{8,10},{12,14},{10... | collective-permute-start | bytes 196616 | tf_op jit(solution)/shard_map/ppermute | solution.py:133
  10.1 0.7 %collective-permute-start.3 = (f32[128,128]{1,0:T(8,128)S(1)}, f32[128,128]{1,0:T(8,128)S(1)}, u32[]{:S(2)}, u32[]{:S(2)}) collective-permute-start(f32[128,128]{1,0:T(8,128)S(1)} %get-tuple-element.19), channel_id=1, source_target_pairs={{2,4},{4,2},{3,5},{5,3},{10,12},{12,10},{11,13},{13,11},{18,20},{2... | collective-permute-start | bytes 196616 | tf_op jit(solution)/shard_map/ppermute | solution.py:133
  10.8 1.6 %collective-permute-start = (f32[128,128]{1,0:T(8,128)S(1)}, f32[128,128]{1,0:T(8,128)S(1)}, u32[]{:S(2)}, u32[]{:S(2)}) collective-permute-start(f32[128,128]{1,0:T(8,128)S(1)} %get-tuple-element.20), channel_id=1, source_target_pairs={{0,8},{16,24},{8,0},{24,16},{1,9},{17,25},{9,1},{25,17},{2,10},{18... | collective-permute-start | bytes 196616 | tf_op jit(solution)/shard_map/ppermute | solution.py:133
  12.4 0.7 %collective-permute-start.1 = (f32[128,128]{1,0:T(8,128)S(1)}, f32[128,128]{1,0:T(8,128)S(1)}, u32[]{:S(2)}, u32[]{:S(2)}) collective-permute-start(f32[128,128]{1,0:T(8,128)S(1)} %get-tuple-element.21), channel_id=1, source_target_pairs={{8,16},{16,8},{9,17},{17,9},{10,18},{18,10},{11,19},{19,11},{12,20... | collective-permute-start | bytes 196616 | tf_op jit(solution)/shard_map/ppermute | solution.py:133
  13.8 2.3 %fusion.after_ref = f32[40,128]{1,0:T(8,128)S(1)} fusion(f32[128,4352]{1,0:T(8,128)S(1)} %copy-done.1, f32[40,4352]{1,0:T(8,128)S(1)} %copy-done.2, f32[40]{0:T(128)S(1)} %compare_convert_fusion), kind=kOutput, calls=%fused_computation.1 | convolution fusion | flops 267560960 | bytes 2945184 | tf_op jit(solution)/shard_map/dot_general | solution.py:193
  16.3 0.7 %copy-done.5 = f32[128,768]{1,0:T(8,128)} copy-done((f32[128,768]{1,0:T(8,128)}, f32[128,768]{1,0:T(8,128)S(1)}, u32[]{:S(2)}) %copy-start.5) | copy-done | bytes 393240
  17.0 0.9 %broadcast_in_dim.29 = f32[32,40,128]{2,1,0:T(8,128)} broadcast(f32[40,128]{1,0:T(8,128)S(1)} %fusion.after_ref), dimensions={1,2} | broadcast | bytes 675840 | tf_op jit(solution)/shard_map/broadcast_in_dim | solution.py:205
  17.9 9.1 %all-to-all-start = ((f32[32,40,128]{2,1,0:T(8,128)}), f32[32,40,128]{2,1,0:T(8,128)}, u32[]{:S(2)}, u32[]{:S(2)}) async-start(f32[32,40,128]{2,1,0:T(8,128)} %broadcast_in_dim.29), calls=%async_computation | async-start | bytes 1310720 | tf_op jit(solution)/shard_map/all_to_all | solution.py:206
  27.3 1.0 %copy-done.6 = f32[128,768]{1,0:T(8,128)S(1)} copy-done((f32[128,768]{1,0:T(8,128)S(1)}, f32[128,768]{1,0:T(8,128)}, u32[]{:S(2)}) %copy-start.6) | copy-done | bytes 393240
  28.3 13.1 %shard_map.82 = (bf16[128,4352]{1,0:T(8,128)(2,1)S(1)}, bf16[128,768]{1,0:T(8,128)(2,1)S(1)}) custom-call(s32[20]{0:T(128)S(1)} %copy-done.8, f32[128,4352]{1,0:T(8,128)S(1)} %copy-done.1, f32[128,768]{1,0:T(8,128)S(1)} %copy-done.6, bf16[20,256,256]{2,1,0:T(8,128)(2,1)} %inv_ref.1, bf16[19,256,256]{2,1,0:T(8,128)(2,1)} %cpl_ref.1, f32[40,128]{1,0:T(8,128)S(1)} %fusion.after_ref), custom_call_target="tpu_custom_call" | custom-call | tf_op jit(solution)/shard_map/pallas_call | solution.py:61
  41.4 1.0 %copy-done.3 = bf16[128,4352]{1,0:T(8,128)(2,1)} copy-done((bf16[128,4352]{1,0:T(8,128)(2,1)}, bf16[128,4352]{1,0:T(8,128)(2,1)S(1)}, u32[]{:S(2)}) %copy-start.3) | copy-done | bytes 1114136
  42.4 0.7 %copy-done.7 = bf16[128,768]{1,0:T(8,128)(2,1)} copy-done((bf16[128,768]{1,0:T(8,128)(2,1)}, bf16[128,768]{1,0:T(8,128)(2,1)S(1)}, u32[]{:S(2)}) %copy-start.7) | copy-done | bytes 196632
  43.1 1.9 %all-to-all-done = f32[32,40,128]{2,1,0:T(8,128)} async-done(((f32[32,40,128]{2,1,0:T(8,128)}), f32[32,40,128]{2,1,0:T(8,128)}, u32[]{:S(2)}, u32[]{:S(2)}) %all-to-all-start) | async-done | bytes 655392 | tf_op jit(solution)/shard_map/all_to_all | solution.py:206
  45.0 0.9 %slice_select_fusion.1 = (bf16[128,128]{1,0:T(8,128)(2,1)S(1)}, bf16[128,128]{1,0:T(8,128)(2,1)S(1)}, bf16[128,128]{1,0:T(8,128)(2,1)S(1)}, bf16[128,128]{1,0:T(8,128)(2,1)S(1)}, bf16[128,128]{1,0:T(8,128)(2,1)S(1)}) fusion(bf16[128,768]{1,0:T(8,128)(2,1)} %copy-done.7, pred[]{:T(512)S(6)} %eq.21, pred[]{:T(512)S(6)} %eq.20, pred[]{:T(512)S(6)} %eq.19), kind=kLoop, calls=%fused_computation.19 | loop fusion | flops 81920 | bytes 360451 | tf_op jit(solution)/shard_map/jit(_where)/select_n | solution.py:151
  46.7 4.1 %collective-permute-start.8 = (bf16[128,128]{1,0:T(8,128)(2,1)S(1)}, bf16[128,128]{1,0:T(8,128)(2,1)S(1)}, u32[]{:S(2)}, u32[]{:S(2)}) collective-permute-start(bf16[128,128]{1,0:T(8,128)(2,1)S(1)} %get-tuple-element.24), channel_id=1, source_target_pairs={{0,2},{4,6},{2,0},{6,4},{1,3},{5,7},{3,1},{7,5},{8,10},{12,14},{10... | collective-permute-start | bytes 98312 | tf_op jit(solution)/shard_map/ppermute | solution.py:133
  51.5 2.8 %collective-permute-start.6 = (bf16[128,128]{1,0:T(8,128)(2,1)S(1)}, bf16[128,128]{1,0:T(8,128)(2,1)S(1)}, u32[]{:S(2)}, u32[]{:S(2)}) collective-permute-start(bf16[128,128]{1,0:T(8,128)(2,1)S(1)} %get-tuple-element.26), channel_id=1, source_target_pairs={{0,8},{16,24},{8,0},{24,16},{1,9},{17,25},{9,1},{25,17},{2,10},{18... | collective-permute-start | bytes 98312 | tf_op jit(solution)/shard_map/ppermute | solution.py:133
  54.3 2.3 %fusion.5.solved_ref = f32[128,40]{1,0:T(8,128)S(1)} fusion(f32[1280,128]{1,0:T(8,128)} %bitcast.9, f32[40,1280]{1,0:T(8,128)S(1)} %copy-done), kind=kOutput, calls=%fused_computation.34 | convolution fusion | flops 78643200 | bytes 880640 | tf_op jit(solution)/shard_map/dot_general | solution.py:222
  56.9 4.2 %shard_map.83 = f32[128,4352]{1,0:T(8,128)} custom-call(s32[1]{0:T(128)} %copy.30.count_ref, s32[768,1]{1,0:T(8,128)S(1)} %bitcast.27, bf16[128,4352]{1,0:T(8,128)(2,1)S(1)} %copy-done.4, bf16[128,768]{1,0:T(8,128)(2,1)S(1)} %select_dynamic-update-slice_fusion.6.back_ref, f32[128,40]{1,0:T(8,128)S(1)} %fusion.5.solved_ref, f32[40,4352]{1,0:T(8,128)S(1)} %copy-done.2), custom_call_target="tpu_custom_call" | custom-call | tf_op jit(solution)/shard_map/pallas_call | solution.py:114
  (47 shorter events, 2.4 us)
Async XLA Ops:
  0.0 54.3 %copy-start = (f32[40,1280]{1,0:T(8,128)S(1)}, f32[40,1280]{1,0:T(8,128)}, u32[]{:S(2)}) copy-start(f32[40,1280]{1,0:T(8,128)} %param.15) | copy-start | bytes 614404
  3.4 10.3 %copy-start.2 = (f32[40,4352]{1,0:T(8,128)S(1)}, f32[40,4352]{1,0:T(8,128)}, u32[]{:S(2)}) copy-start(f32[40,4352]{1,0:T(8,128)} %vec_ref.1) | copy-start | bytes 2088964
  5.0 8.7 %copy-start.1 = (f32[128,4352]{1,0:T(8,128)S(1)}, f32[128,4352]{1,0:T(8,128)}, u32[]{:S(2)}) copy-start(f32[128,4352]{1,0:T(8,128)} %res_ref.1) | copy-start | bytes 6684676
  7.0 9.2 %collective-permute-start.4 = (f32[128,128]{1,0:T(8,128)S(1)}, f32[128,128]{1,0:T(8,128)S(1)}, u32[]{:S(2)}, u32[]{:S(2)}) collective-permute-start(f32[128,128]{1,0:T(8,128)S(1)} %get-tuple-element.17), channel_id=1, source_target_pairs={{0,1},{1,0},{2,3},{3,2},{4,5},{5,4},{6,7},{7,6},{8,9},{9,8},{10,11... | collective-permute-start | bytes 196616 | tf_op jit(solution)/shard_map/ppermute | solution.py:133
  7.5 8.6 %collective-permute-start.2 = (f32[128,128]{1,0:T(8,128)S(1)}, f32[128,128]{1,0:T(8,128)S(1)}, u32[]{:S(2)}, u32[]{:S(2)}) collective-permute-start(f32[128,128]{1,0:T(8,128)S(1)} %get-tuple-element.18), channel_id=1, source_target_pairs={{0,2},{4,6},{2,0},{6,4},{1,3},{5,7},{3,1},{7,5},{8,10},{12,14},{10... | collective-permute-start | bytes 196616 | tf_op jit(solution)/shard_map/ppermute | solution.py:133
  10.1 6.1 %collective-permute-start.3 = (f32[128,128]{1,0:T(8,128)S(1)}, f32[128,128]{1,0:T(8,128)S(1)}, u32[]{:S(2)}, u32[]{:S(2)}) collective-permute-start(f32[128,128]{1,0:T(8,128)S(1)} %get-tuple-element.19), channel_id=1, source_target_pairs={{2,4},{4,2},{3,5},{5,3},{10,12},{12,10},{11,13},{13,11},{18,20},{2... | collective-permute-start | bytes 196616 | tf_op jit(solution)/shard_map/ppermute | solution.py:133
  10.8 5.4 %collective-permute-start = (f32[128,128]{1,0:T(8,128)S(1)}, f32[128,128]{1,0:T(8,128)S(1)}, u32[]{:S(2)}, u32[]{:S(2)}) collective-permute-start(f32[128,128]{1,0:T(8,128)S(1)} %get-tuple-element.20), channel_id=1, source_target_pairs={{0,8},{16,24},{8,0},{24,16},{1,9},{17,25},{9,1},{25,17},{2,10},{18... | collective-permute-start | bytes 196616 | tf_op jit(solution)/shard_map/ppermute | solution.py:133
  12.4 3.7 %collective-permute-start.1 = (f32[128,128]{1,0:T(8,128)S(1)}, f32[128,128]{1,0:T(8,128)S(1)}, u32[]{:S(2)}, u32[]{:S(2)}) collective-permute-start(f32[128,128]{1,0:T(8,128)S(1)} %get-tuple-element.21), channel_id=1, source_target_pairs={{8,16},{16,8},{9,17},{17,9},{10,18},{18,10},{11,19},{19,11},{12,20... | collective-permute-start | bytes 196616 | tf_op jit(solution)/shard_map/ppermute | solution.py:133
  16.1 11.0 %copy-start.9 = (s32[6,128]{1,0:T(8,128)S(1)}, s32[6,128]{1,0:T(8,128)}, u32[]{:S(2)}) copy-start(s32[6,128]{1,0:T(8,128)} %param.12) | copy-start | bytes 9220
  16.1 11.2 %copy-start.8 = (s32[20]{0:T(128)S(1)}, s32[20]{0:T(128)}, u32[]{:S(2)}) copy-start(s32[20]{0:T(128)} %parent_ref.1) | copy-start | bytes 244
  16.3 0.7 %copy-start.5 = (f32[128,768]{1,0:T(8,128)}, f32[128,768]{1,0:T(8,128)S(1)}, u32[]{:S(2)}) copy-start(f32[128,768]{1,0:T(8,128)S(1)} %select_dynamic-update-slice_fusion.slot_ref) | copy-start | bytes 1179652
  17.9 27.0 %all-to-all-start = ((f32[32,40,128]{2,1,0:T(8,128)}), f32[32,40,128]{2,1,0:T(8,128)}, u32[]{:S(2)}, u32[]{:S(2)}) async-start(f32[32,40,128]{2,1,0:T(8,128)} %broadcast_in_dim.29), calls=%async_computation | async-start | bytes 1310720 | tf_op jit(solution)/shard_map/all_to_all | solution.py:206
  27.3 1.0 %copy-start.6 = (f32[128,768]{1,0:T(8,128)S(1)}, f32[128,768]{1,0:T(8,128)}, u32[]{:S(2)}) copy-start(f32[128,768]{1,0:T(8,128)} %copy-done.5) | copy-start | bytes 1179652
  41.4 1.0 %copy-start.3 = (bf16[128,4352]{1,0:T(8,128)(2,1)}, bf16[128,4352]{1,0:T(8,128)(2,1)S(1)}, u32[]{:S(2)}) copy-start(bf16[128,4352]{1,0:T(8,128)(2,1)S(1)} %get-tuple-element.13.own_ref) | copy-start | bytes 3342340
  42.4 0.7 %copy-start.7 = (bf16[128,768]{1,0:T(8,128)(2,1)}, bf16[128,768]{1,0:T(8,128)(2,1)S(1)}, u32[]{:S(2)}) copy-start(bf16[128,768]{1,0:T(8,128)(2,1)S(1)} %get-tuple-element.15) | copy-start | bytes 589828
  45.0 11.9 %copy-start.4 = (bf16[128,4352]{1,0:T(8,128)(2,1)S(1)}, bf16[128,4352]{1,0:T(8,128)(2,1)}, u32[]{:S(2)}) copy-start(bf16[128,4352]{1,0:T(8,128)(2,1)} %copy-done.3) | copy-start | bytes 3342340
  45.9 10.9 %collective-permute-start.9 = (bf16[128,128]{1,0:T(8,128)(2,1)S(1)}, bf16[128,128]{1,0:T(8,128)(2,1)S(1)}, u32[]{:S(2)}, u32[]{:S(2)}) collective-permute-start(bf16[128,128]{1,0:T(8,128)(2,1)S(1)} %get-tuple-element.22), channel_id=1, source_target_pairs={{0,1},{1,0},{2,3},{3,2},{4,5},{5,4},{6,7},{7,6},{8,9},{9,8},{10,11... | collective-permute-start | bytes 98312 | tf_op jit(solution)/shard_map/ppermute | solution.py:133
  46.1 10.6 %collective-permute-start.7 = (bf16[128,128]{1,0:T(8,128)(2,1)S(1)}, bf16[128,128]{1,0:T(8,128)(2,1)S(1)}, u32[]{:S(2)}, u32[]{:S(2)}) collective-permute-start(bf16[128,128]{1,0:T(8,128)(2,1)S(1)} %get-tuple-element.23), channel_id=1, source_target_pairs={{2,4},{4,2},{3,5},{5,3},{10,12},{12,10},{11,13},{13,11},{18,20},{2... | collective-permute-start | bytes 98312 | tf_op jit(solution)/shard_map/ppermute | solution.py:133
  46.7 10.0 %collective-permute-start.8 = (bf16[128,128]{1,0:T(8,128)(2,1)S(1)}, bf16[128,128]{1,0:T(8,128)(2,1)S(1)}, u32[]{:S(2)}, u32[]{:S(2)}) collective-permute-start(bf16[128,128]{1,0:T(8,128)(2,1)S(1)} %get-tuple-element.24), channel_id=1, source_target_pairs={{0,2},{4,6},{2,0},{6,4},{1,3},{5,7},{3,1},{7,5},{8,10},{12,14},{10... | collective-permute-start | bytes 98312 | tf_op jit(solution)/shard_map/ppermute | solution.py:133
  50.9 5.8 %collective-permute-start.5 = (bf16[128,128]{1,0:T(8,128)(2,1)S(1)}, bf16[128,128]{1,0:T(8,128)(2,1)S(1)}, u32[]{:S(2)}, u32[]{:S(2)}) collective-permute-start(bf16[128,128]{1,0:T(8,128)(2,1)S(1)} %get-tuple-element.25), channel_id=1, source_target_pairs={{8,16},{16,8},{9,17},{17,9},{10,18},{18,10},{11,19},{19,11},{12,20... | collective-permute-start | bytes 98312 | tf_op jit(solution)/shard_map/ppermute | solution.py:133
  51.5 5.1 %collective-permute-start.6 = (bf16[128,128]{1,0:T(8,128)(2,1)S(1)}, bf16[128,128]{1,0:T(8,128)(2,1)S(1)}, u32[]{:S(2)}, u32[]{:S(2)}) collective-permute-start(bf16[128,128]{1,0:T(8,128)(2,1)S(1)} %get-tuple-element.26), channel_id=1, source_target_pairs={{0,8},{16,24},{8,0},{24,16},{1,9},{17,25},{9,1},{25,17},{2,10},{18... | collective-permute-start | bytes 98312 | tf_op jit(solution)/shard_map/ppermute | solution.py:133

commit v16 on v15

--- a/solution.py
+++ b/solution.py
@@ -202,8 +202,15 @@
         incoming += [low, high]
     slots = jnp.concatenate(incoming, axis=1)
     slots, coeffs_t = lax.optimization_barrier((slots, coeffs_t))
-    spread = jnp.broadcast_to(coeffs_t[None], (total_dev,) + coeffs_t.shape)
-    held = lax.all_to_all(spread, AXES, 0, 0, tiled=True)
+    last = len(AXES) - 1
+    late = lax.axis_size(AXES[last]) == 2
+    spread_axes = AXES[:last] if late else AXES
+    spread_n = 1
+    for axis in spread_axes:
+        spread_n *= lax.axis_size(axis)
+    spread = jnp.broadcast_to(coeffs_t[None], (spread_n,) + coeffs_t.shape)
+    held = lax.all_to_all(spread, spread_axes, 0, 0, tiled=True)
+    held = held.reshape(tuple(lax.axis_size(a) for a in spread_axes) + (1,) * (len(AXES) - len(spread_axes)) + coeffs_t.shape)
     after = coeffs_t
 
     own, zslots = local_solve(parent, residual, slots, diag_inverse, coupling, after)
@@ -211,12 +218,16 @@
 
     returned = []
     for axis_pos, axis in enumerate(AXES):
-        low, high, _ = halo_back(
+        ride = axis_pos == last and late
+        low, high, got = halo_back(
             zslots[:, (2 * axis_pos) * face_w : (2 * axis_pos + 1) * face_w],
             zslots[:, (2 * axis_pos + 1) * face_w : (2 * axis_pos + 2) * face_w],
             axis,
+            rows_of(held) if ride else None,
         )
         returned += [low, high]
+        if ride:
+            held = merge(held, got.reshape(held.shape), axis, last, 1)
     returned = jnp.concatenate(returned, axis=1)
 
     solved_t = jnp.dot(

time: 61.5 us -> 65 us (1.057)
  starting transfers between devices: 23.5 us -> 26.4 us
  other arithmetic: 3.62 us -> 5.77 us
  matrix products: 4.64 us -> 3.56 us
    all_to_all x1, waiting for transfers between devices: 1.87 us -> 0.01 us  [per_device(): held = lax.all_to_all(spread, spread_axes, 0, 0, tiled=True)]
    ppermute x10 -> x9, starting transfers between devices: 14.4 us -> 16.2 us  [swap(): return (lax.ppermute(value, axis, pairs), None)]
    dot_general x1, matrix products: 2.3 us -> 1.21 us  [per_device(): jnp.dot(coarse_inverse, rows_of(held), precision=lax.Precision.HIGHEST, p...]
    concatenate x0 -> x1, other arithmetic: none -> 1 us  [swap(): packed = jnp.concatenate([value.astype(extra.dtype), extra], axis=0)]
    convert_element_type x0 -> x1, other arithmetic: none -> 0.95 us  [swap(): packed = jnp.concatenate([value.astype(extra.dtype), extra], axis=0)]
    all_to_all x1, starting transfers between devices: 9.13 us -> 10.1 us  [per_device(): held = lax.all_to_all(spread, spread_axes, 0, 0, tiled=True)]
    ppermute x10 -> x9, waiting for transfers between devices: 0.03 us -> 0.82 us  [swap(): return (lax.ppermute(value, axis, pairs), None)]
    ppermute x0 -> x1, waiting for transfers between devices: none -> 0.77 us  [swap(): got = lax.ppermute(packed, axis, pairs)]
  transfers between devices with their start and end apart: 11 -> 11, of which waited for: 1 -> 2; matrix products, arithmetic and copies ran while one was open for 8% -> 6% of each run, Pallas kernels for 22% -> 20%
where the time goes in v16:
time: 65 us; the launch traced here: 64.5 us
  starting transfers between devices  26.4 us (41%)
  Pallas kernels  17.3 us (27%)
  local copies, waits for them, and re-layouts  8.88 us (14%)
  other arithmetic  5.77 us (9%)
  matrix products  3.56 us (5%)
  waiting for transfers between devices  1.6 us (2%)
  between operations  1.02 us (2%)
    ppermute x9, starting transfers between devices, swap(): return (lax.ppermute(value, axis, pairs), None)  16.2 us
    pallas_call x1, Pallas kernels, local_solve(): pl.pallas_call(solve_kernel, out_shape=(jax.ShapeDtypeStruct((nrhs_here,...  13.1 us
    all_to_all x1, starting transfers between devices, per_device(): held = lax.all_to_all(spread, spread_axes, 0, 0, tiled=True)  10.1 us
    unnamed x23, local copies, waits for them, and re-layouts  5.62 us
    pallas_call x1, Pallas kernels, finish(): pl.pallas_call(finish_kernel, out_shape=jax.ShapeDtypeStruct(own.shape, j...  4.17 us
    gather x2, local copies, waits for them, and re-layouts, per_device(): outgoing = jnp.take(residual, send_rows, axis=1)  2.49 us
    dot_general x1, matrix products, per_device(): lax.dot_general(vectors, residual, NT, precision=lax.Precision.HIGHEST, p...  2.35 us
  transfers between devices with their start and end apart: 11, of which 2 were waited for; matrix products, arithmetic and copies ran while one was open for 6% of the time, Pallas kernels for 20%

profile of v16, /device:TPU:0, one launch (start us, length us, event | category | flops | bytes accessed | tf_op | source)
XLA Modules:
  0.0 64.5 jit_solution(12382857287246481191)
XLA Ops:
  0.0 0.7 %compare_and_fusion = pred[6,128]{1,0:T(8,128)(4,1)S(1)} fusion(s32[6,128]{1,0:T(8,128)} %param.12), kind=kLoop, calls=%fused_computation.33 | loop fusion | flops 4608 | bytes 3840 | tf_op jit(solution)/shard_map/jit(_take)/and | solution.py:198
  0.7 0.7 %fusion.4 = s32[768]{0:T(1024)S(1)} fusion(s32[6,128]{1,0:T(8,128)} %param.12), kind=kLoop, calls=%fused_computation.34 | loop fusion | flops 2304 | bytes 6144 | tf_op jit(solution)/shard_map/jit(_take)/broadcast_in_dim | solution.py:198
  1.4 2.0 %copy.11 = f32[128,4352]{0,1:T(8,128)S(1)} copy(f32[128,4352]{1,0:T(8,128)} %res_ref.1) | data formatting | bytes 4456448 | tf_op args[0]
  3.5 1.6 %gather_fusion = f32[768,128]{1,0:T(8,128)S(1)} fusion(f32[128,4352]{0,1:T(8,128)S(1)} %copy.11, s32[1024]{0:T(1024)S(1)} %pad_clamp_fusion), kind=kCustom, calls=%fused_computation | custom fusion | bytes 789504 | tf_op jit(solution)/shard_map/jit(_take)/gather | solution.py:198
  5.0 0.9 %copy.12 = f32[6,128,128]{1,2,0:T(8,128)} copy(f32[6,128,128]{2,1,0:T(8,128)S(1)} %bitcast.35) | data formatting | bytes 786432 | tf_op jit(solution)/shard_map/jit(_take)/gather | solution.py:198
  6.0 1.0 %select_bitcast_fusion = f32[128,6,128]{2,0,1:T(8,128)S(1)} fusion(f32[6,128,128]{1,2,0:T(8,128)} %copy.12, pred[6,128]{1,0:T(8,128)(4,1)S(1)} %compare_and_fusion), kind=kLoop, calls=%fused_computation.5 | loop fusion | flops 98304 | bytes 787200 | tf_op jit(solution)/shard_map/jit(_take)/select_n | solution.py:198
  7.5 2.6 %collective-permute-start.2 = (f32[128,128]{1,0:T(8,128)S(1)}, f32[128,128]{1,0:T(8,128)S(1)}, u32[]{:S(2)}, u32[]{:S(2)}) collective-permute-start(f32[128,128]{1,0:T(8,128)S(1)} %get-tuple-element.18), channel_id=1, source_target_pairs={{0,2},{4,6},{2,0},{6,4},{1,3},{5,7},{3,1},{7,5},{8,10},{12,14},{10... | collective-permute-start | bytes 196616 | tf_op jit(solution)/shard_map/ppermute | solution.py:133
  10.8 1.6 %collective-permute-start = (f32[128,128]{1,0:T(8,128)S(1)}, f32[128,128]{1,0:T(8,128)S(1)}, u32[]{:S(2)}, u32[]{:S(2)}) collective-permute-start(f32[128,128]{1,0:T(8,128)S(1)} %get-tuple-element.20), channel_id=1, source_target_pairs={{0,8},{16,24},{8,0},{24,16},{1,9},{17,25},{9,1},{25,17},{2,10},{18... | collective-permute-start | bytes 196616 | tf_op jit(solution)/shard_map/ppermute | solution.py:133
  13.8 2.3 %fusion.after_ref = f32[40,128]{1,0:T(8,128)S(1)} fusion(f32[128,4352]{1,0:T(8,128)S(1)} %copy-done.1, f32[40,4352]{1,0:T(8,128)S(1)} %copy-done.2, f32[40]{0:T(128)S(1)} %compare_convert_fusion), kind=kOutput, calls=%fused_computation.1 | convolution fusion | flops 267560960 | bytes 2945184 | tf_op jit(solution)/shard_map/dot_general | solution.py:193
  16.3 0.7 %copy-done.5 = f32[128,768]{1,0:T(8,128)} copy-done((f32[128,768]{1,0:T(8,128)}, f32[128,768]{1,0:T(8,128)S(1)}, u32[]{:S(2)}) %copy-start.5) | copy-done | bytes 393240
  17.0 0.7 %broadcast_in_dim.29 = f32[16,40,128]{2,1,0:T(8,128)} broadcast(f32[40,128]{1,0:T(8,128)S(1)} %fusion.after_ref), dimensions={1,2} | broadcast | bytes 348160 | tf_op jit(solution)/shard_map/broadcast_in_dim | solution.py:211
  17.8 10.1 %all-to-all-start = ((f32[16,40,128]{2,1,0:T(8,128)}), f32[16,40,128]{2,1,0:T(8,128)}, u32[]{:S(2)}, u32[]{:S(2)}) async-start(f32[16,40,128]{2,1,0:T(8,128)} %broadcast_in_dim.29), calls=%async_computation | async-start | bytes 655360 | tf_op jit(solution)/shard_map/all_to_all | solution.py:212
  28.1 1.0 %copy-done.6 = f32[128,768]{1,0:T(8,128)S(1)} copy-done((f32[128,768]{1,0:T(8,128)S(1)}, f32[128,768]{1,0:T(8,128)}, u32[]{:S(2)}) %copy-start.6) | copy-done | bytes 393240
  29.1 13.1 %shard_map.82 = (bf16[128,4352]{1,0:T(8,128)(2,1)S(1)}, bf16[128,768]{1,0:T(8,128)(2,1)S(1)}) custom-call(s32[20]{0:T(128)S(1)} %copy-done.8, f32[128,4352]{1,0:T(8,128)S(1)} %copy-done.1, f32[128,768]{1,0:T(8,128)S(1)} %copy-done.6, bf16[20,256,256]{2,1,0:T(8,128)(2,1)} %inv_ref.1, bf16[19,256,256]{2,1,0:T(8,128)(2,1)} %cpl_ref.1, f32[40,128]{1,0:T(8,128)S(1)} %fusion.after_ref), custom_call_target="tpu_custom_call" | custom-call | tf_op jit(solution)/shard_map/pallas_call | solution.py:61
  42.2 1.0 %copy-done.3 = bf16[128,4352]{1,0:T(8,128)(2,1)} copy-done((bf16[128,4352]{1,0:T(8,128)(2,1)}, bf16[128,4352]{1,0:T(8,128)(2,1)S(1)}, u32[]{:S(2)}) %copy-start.3) | copy-done | bytes 1114136
  43.9 1.0 %select_convert_fusion = (f32[128,128]{1,0:T(8,128)S(1)}, bf16[128,128]{1,0:T(8,128)(2,1)S(1)}, bf16[128,128]{1,0:T(8,128)(2,1)S(1)}, bf16[128,128]{1,0:T(8,128)(2,1)S(1)}, bf16[128,128]{1,0:T(8,128)(2,1)S(1)}) fusion(bf16[128,768]{1,0:T(8,128)(2,1)} %copy-done.7, pred[]{:T(512)S(6)} %eq.23, pred[]{:T(512)S(6)} %eq.22, pred[]{:T(512)S(6)} %eq.21), kind=kLoop, calls=%fused_computation.22 | loop fusion | flops 98304 | bytes 393219 | tf_op jit(solution)/shard_map/convert_element_type | solution.py:135
  45.6 4.6 %collective-permute-start.8 = (bf16[128,128]{1,0:T(8,128)(2,1)S(1)}, bf16[128,128]{1,0:T(8,128)(2,1)S(1)}, u32[]{:S(2)}, u32[]{:S(2)}) collective-permute-start(bf16[128,128]{1,0:T(8,128)(2,1)S(1)} %get-tuple-element.24), channel_id=1, source_target_pairs={{0,2},{4,6},{2,0},{6,4},{1,3},{5,7},{3,1},{7,5},{8,10},{12,14},{10... | collective-permute-start | bytes 98312 | tf_op jit(solution)/shard_map/ppermute | solution.py:133
  50.9 4.2 %collective-permute-start.6 = (bf16[128,128]{1,0:T(8,128)(2,1)S(1)}, bf16[128,128]{1,0:T(8,128)(2,1)S(1)}, u32[]{:S(2)}, u32[]{:S(2)}) collective-permute-start(bf16[128,128]{1,0:T(8,128)(2,1)S(1)} %get-tuple-element.26), channel_id=1, source_target_pairs={{0,8},{16,24},{8,0},{24,16},{1,9},{17,25},{9,1},{25,17},{2,10},{18... | collective-permute-start | bytes 98312 | tf_op jit(solution)/shard_map/ppermute | solution.py:133
  55.1 1.0 %pad_maximum_fusion = f32[768,128]{1,0:T(8,128)S(1)} fusion(f32[640,128]{1,0:T(8,128)} %bitcast.10, f32[128,128]{1,0:T(8,128)S(1)} %get-tuple-element.22), kind=kLoop, calls=%fused_computation.4 | loop fusion | flops 98304 | bytes 786432 | tf_op jit(solution)/shard_map/concatenate | solution.py:135
  56.2 0.8 %collective-permute-done.6 = bf16[128,128]{1,0:T(8,128)(2,1)S(1)} collective-permute-done((bf16[128,128]{1,0:T(8,128)(2,1)S(1)}, bf16[128,128]{1,0:T(8,128)(2,1)S(1)}, u32[]{:S(2)}, u32[]{:S(2)}) %collective-permute-start.6) | collective-permute-done | bytes 32800 | tf_op jit(solution)/shard_map/ppermute | solution.py:133
  57.1 0.8 %collective-permute-done.9 = f32[768,128]{1,0:T(8,128)S(1)} collective-permute-done((f32[768,128]{1,0:T(8,128)S(1)}, f32[768,128]{1,0:T(8,128)S(1)}, u32[]{:S(2)}, u32[]{:S(2)}) %collective-permute-start.9) | collective-permute-done | bytes 393248 | tf_op jit(solution)/shard_map/ppermute | solution.py:136
  57.9 1.2 %maximum_select_fusion = f32[4,4,2,40,128]{4,3,2,1,0:T(8,128)S(1)} fusion(f32[4,4,1,40,128]{4,3,2,1,0:T(8,128)S(1)} %bitcast.36, f32[4,4,1,40,128]{4,3,2,1,0:T(8,128)} %bitcast.9, pred[]{:T(512)S(6)} %eq.23), kind=kLoop, calls=%fused_computation.3 | loop fusion | flops 491520 | bytes 1310721 | tf_op jit(solution)/shard_map/jit(_where)/select_n | solution.py:163
  59.1 1.2 %fusion.5.solved_ref = f32[128,40]{1,0:T(8,128)S(1)} fusion(f32[1280,128]{1,0:T(8,128)S(1)} %bitcast.34, f32[40,1280]{1,0:T(8,128)S(1)} %copy-done), kind=kOutput, calls=%fused_computation.37 | convolution fusion | flops 78643200 | bytes 880640 | tf_op jit(solution)/shard_map/dot_general | solution.py:233
  60.4 4.2 %shard_map.83 = f32[128,4352]{1,0:T(8,128)} custom-call(s32[1]{0:T(128)} %copy.32.count_ref, s32[768,1]{1,0:T(8,128)S(1)} %bitcast.33, bf16[128,4352]{1,0:T(8,128)(2,1)S(1)} %copy-done.4, bf16[128,768]{1,0:T(8,128)(2,1)S(1)} %select_dynamic-update-slice_fusion.6.back_ref, f32[128,40]{1,0:T(8,128)S(1)} %fusion.5.solved_ref, f32[40,4352]{1,0:T(8,128)S(1)} %copy-done.2), custom_call_target="tpu_custom_call" | custom-call | tf_op jit(solution)/shard_map/pallas_call | solution.py:114
  (50 shorter events, 4.4 us)
Async XLA Ops:
  0.0 59.1 %copy-start = (f32[40,1280]{1,0:T(8,128)S(1)}, f32[40,1280]{1,0:T(8,128)}, u32[]{:S(2)}) copy-start(f32[40,1280]{1,0:T(8,128)} %param.15) | copy-start | bytes 614404
  3.4 10.3 %copy-start.2 = (f32[40,4352]{1,0:T(8,128)S(1)}, f32[40,4352]{1,0:T(8,128)}, u32[]{:S(2)}) copy-start(f32[40,4352]{1,0:T(8,128)} %vec_ref.1) | copy-start | bytes 2088964
  5.0 8.7 %copy-start.1 = (f32[128,4352]{1,0:T(8,128)S(1)}, f32[128,4352]{1,0:T(8,128)}, u32[]{:S(2)}) copy-start(f32[128,4352]{1,0:T(8,128)} %res_ref.1) | copy-start | bytes 6684676
  7.0 9.2 %collective-permute-start.4 = (f32[128,128]{1,0:T(8,128)S(1)}, f32[128,128]{1,0:T(8,128)S(1)}, u32[]{:S(2)}, u32[]{:S(2)}) collective-permute-start(f32[128,128]{1,0:T(8,128)S(1)} %get-tuple-element.17), channel_id=1, source_target_pairs={{0,1},{1,0},{2,3},{3,2},{4,5},{5,4},{6,7},{7,6},{8,9},{9,8},{10,11... | collective-permute-start | bytes 196616 | tf_op jit(solution)/shard_map/ppermute | solution.py:133
  7.5 8.6 %collective-permute-start.2 = (f32[128,128]{1,0:T(8,128)S(1)}, f32[128,128]{1,0:T(8,128)S(1)}, u32[]{:S(2)}, u32[]{:S(2)}) collective-permute-start(f32[128,128]{1,0:T(8,128)S(1)} %get-tuple-element.18), channel_id=1, source_target_pairs={{0,2},{4,6},{2,0},{6,4},{1,3},{5,7},{3,1},{7,5},{8,10},{12,14},{10... | collective-permute-start | bytes 196616 | tf_op jit(solution)/shard_map/ppermute | solution.py:133
  10.1 6.1 %collective-permute-start.3 = (f32[128,128]{1,0:T(8,128)S(1)}, f32[128,128]{1,0:T(8,128)S(1)}, u32[]{:S(2)}, u32[]{:S(2)}) collective-permute-start(f32[128,128]{1,0:T(8,128)S(1)} %get-tuple-element.19), channel_id=1, source_target_pairs={{2,4},{4,2},{3,5},{5,3},{10,12},{12,10},{11,13},{13,11},{18,20},{2... | collective-permute-start | bytes 196616 | tf_op jit(solution)/shard_map/ppermute | solution.py:133
  10.8 5.4 %collective-permute-start = (f32[128,128]{1,0:T(8,128)S(1)}, f32[128,128]{1,0:T(8,128)S(1)}, u32[]{:S(2)}, u32[]{:S(2)}) collective-permute-start(f32[128,128]{1,0:T(8,128)S(1)} %get-tuple-element.20), channel_id=1, source_target_pairs={{0,8},{16,24},{8,0},{24,16},{1,9},{17,25},{9,1},{25,17},{2,10},{18... | collective-permute-start | bytes 196616 | tf_op jit(solution)/shard_map/ppermute | solution.py:133
  12.4 3.7 %collective-permute-start.1 = (f32[128,128]{1,0:T(8,128)S(1)}, f32[128,128]{1,0:T(8,128)S(1)}, u32[]{:S(2)}, u32[]{:S(2)}) collective-permute-start(f32[128,128]{1,0:T(8,128)S(1)} %get-tuple-element.21), channel_id=1, source_target_pairs={{8,16},{16,8},{9,17},{17,9},{10,18},{18,10},{11,19},{19,11},{12,20... | collective-permute-start | bytes 196616 | tf_op jit(solution)/shard_map/ppermute | solution.py:133
  13.8 14.1 %copy-start.9 = (s32[6,128]{1,0:T(8,128)S(1)}, s32[6,128]{1,0:T(8,128)}, u32[]{:S(2)}) copy-start(s32[6,128]{1,0:T(8,128)} %param.12) | copy-start | bytes 9220
  13.8 14.3 %copy-start.8 = (s32[20]{0:T(128)S(1)}, s32[20]{0:T(128)}, u32[]{:S(2)}) copy-start(s32[20]{0:T(128)} %parent_ref.1) | copy-start | bytes 244
  16.3 0.7 %copy-start.5 = (f32[128,768]{1,0:T(8,128)}, f32[128,768]{1,0:T(8,128)S(1)}, u32[]{:S(2)}) copy-start(f32[128,768]{1,0:T(8,128)S(1)} %select_dynamic-update-slice_fusion.slot_ref) | copy-start | bytes 1179652
  17.8 26.1 %all-to-all-start = ((f32[16,40,128]{2,1,0:T(8,128)}), f32[16,40,128]{2,1,0:T(8,128)}, u32[]{:S(2)}, u32[]{:S(2)}) async-start(f32[16,40,128]{2,1,0:T(8,128)} %broadcast_in_dim.29), calls=%async_computation | async-start | bytes 655360 | tf_op jit(solution)/shard_map/all_to_all | solution.py:212
  28.1 1.0 %copy-start.6 = (f32[128,768]{1,0:T(8,128)S(1)}, f32[128,768]{1,0:T(8,128)}, u32[]{:S(2)}) copy-start(f32[128,768]{1,0:T(8,128)} %copy-done.5) | copy-start | bytes 1179652
  42.2 1.0 %copy-start.3 = (bf16[128,4352]{1,0:T(8,128)(2,1)}, bf16[128,4352]{1,0:T(8,128)(2,1)S(1)}, u32[]{:S(2)}) copy-start(bf16[128,4352]{1,0:T(8,128)(2,1)S(1)} %get-tuple-element.13.own_ref) | copy-start | bytes 3342340
  43.2 0.7 %copy-start.7 = (bf16[128,768]{1,0:T(8,128)(2,1)}, bf16[128,768]{1,0:T(8,128)(2,1)S(1)}, u32[]{:S(2)}) copy-start(bf16[128,768]{1,0:T(8,128)(2,1)S(1)} %get-tuple-element.15) | copy-start | bytes 589828
  43.9 16.4 %copy-start.4 = (bf16[128,4352]{1,0:T(8,128)(2,1)S(1)}, bf16[128,4352]{1,0:T(8,128)(2,1)}, u32[]{:S(2)}) copy-start(bf16[128,4352]{1,0:T(8,128)(2,1)} %copy-done.3) | copy-start | bytes 3342340
  44.9 12.2 %collective-permute-start.7 = (bf16[128,128]{1,0:T(8,128)(2,1)S(1)}, bf16[128,128]{1,0:T(8,128)(2,1)S(1)}, u32[]{:S(2)}, u32[]{:S(2)}) collective-permute-start(bf16[128,128]{1,0:T(8,128)(2,1)S(1)} %get-tuple-element.23), channel_id=1, source_target_pairs={{2,4},{4,2},{3,5},{5,3},{10,12},{12,10},{11,13},{13,11},{18,20},{2... | collective-permute-start | bytes 98312 | tf_op jit(solution)/shard_map/ppermute | solution.py:133
  45.6 11.5 %collective-permute-start.8 = (bf16[128,128]{1,0:T(8,128)(2,1)S(1)}, bf16[128,128]{1,0:T(8,128)(2,1)S(1)}, u32[]{:S(2)}, u32[]{:S(2)}) collective-permute-start(bf16[128,128]{1,0:T(8,128)(2,1)S(1)} %get-tuple-element.24), channel_id=1, source_target_pairs={{0,2},{4,6},{2,0},{6,4},{1,3},{5,7},{3,1},{7,5},{8,10},{12,14},{10... | collective-permute-start | bytes 98312 | tf_op jit(solution)/shard_map/ppermute | solution.py:133
  50.2 6.0 %collective-permute-start.5 = (bf16[128,128]{1,0:T(8,128)(2,1)S(1)}, bf16[128,128]{1,0:T(8,128)(2,1)S(1)}, u32[]{:S(2)}, u32[]{:S(2)}) collective-permute-start(bf16[128,128]{1,0:T(8,128)(2,1)S(1)} %get-tuple-element.25), channel_id=1, source_target_pairs={{8,16},{16,8},{9,17},{17,9},{10,18},{18,10},{11,19},{19,11},{12,20... | collective-permute-start | bytes 98312 | tf_op jit(solution)/shard_map/ppermute | solution.py:133
  50.9 6.1 %collective-permute-start.6 = (bf16[128,128]{1,0:T(8,128)(2,1)S(1)}, bf16[128,128]{1,0:T(8,128)(2,1)S(1)}, u32[]{:S(2)}, u32[]{:S(2)}) collective-permute-start(bf16[128,128]{1,0:T(8,128)(2,1)S(1)} %get-tuple-element.26), channel_id=1, source_target_pairs={{0,8},{16,24},{8,0},{24,16},{1,9},{17,25},{9,1},{25,17},{2,10},{18... | collective-permute-start | bytes 98312 | tf_op jit(solution)/shard_map/ppermute | solution.py:133
  56.1 1.8 %collective-permute-start.9 = (f32[768,128]{1,0:T(8,128)S(1)}, f32[768,128]{1,0:T(8,128)S(1)}, u32[]{:S(2)}, u32[]{:S(2)}) collective-permute-start(f32[768,128]{1,0:T(8,128)S(1)} %pad_maximum_fusion), channel_id=1, source_target_pairs={{0,1},{1,0},{2,3},{3,2},{4,5},{5,4},{6,7},{7,6},{8,9},{9,8},{10,11... | collective-permute-start | bytes 1179656 | tf_op jit(solution)/shard_map/ppermute | solution.py:136

commit v17 on v15

--- a/solution.py
+++ b/solution.py
@@ -77,7 +77,7 @@
             pltpu.VMEM((blocks_n, nrhs_here, block_w), jnp.bfloat16),
             pltpu.VMEM((blocks_n, nrhs_here, block_w), jnp.float32),
         ],
-        compiler_params=pltpu.CompilerParams(vmem_limit_bytes=48 * 1024 * 1024),
+        compiler_params=pltpu.CompilerParams(vmem_limit_bytes=12 * 1024 * 1024),
     )(parent, residual, slots, diag_inverse, coupling, after)
 
 
@@ -116,7 +116,7 @@
         out_shape=jax.ShapeDtypeStruct(own.shape, jnp.float32),
         in_specs=[pl.BlockSpec(memory_space=pltpu.SMEM)] + [pl.BlockSpec(memory_space=vmem)] * 5,
         out_specs=pl.BlockSpec(memory_space=vmem),
-        compiler_params=pltpu.CompilerParams(vmem_limit_bytes=48 * 1024 * 1024),
+        compiler_params=pltpu.CompilerParams(vmem_limit_bytes=8 * 1024 * 1024),
     )(counts, send_rows.reshape(-1, 1), own, returned, solved, deflation)
 
 

time: 61.5 us -> 63.1 us (1.026)
  local copies, waits for them, and re-layouts: 9 us -> 12.4 us
  Pallas kernels: 17.3 us -> 15.4 us
  starting transfers between devices: 23.5 us -> 25 us
  waiting for transfers between devices: 1.9 us -> 0.44 us
    unnamed x23 -> x27, local copies, waits for them, and re-layouts: 5.62 us -> 9.04 us
    pallas_call x1, Pallas kernels: 13.1 us -> 11.2 us  [local_solve(): pl.pallas_call(solve_kernel, out_shape=(jax.ShapeDtypeStruct((nrhs_here,...]
    ppermute x10, starting transfers between devices: 14.4 us -> 15.9 us  [swap(): return (lax.ppermute(value, axis, pairs), None)]
    all_to_all x1, waiting for transfers between devices: 1.87 us -> 0.41 us  [per_device(): held = lax.all_to_all(spread, AXES, 0, 0, tiled=True)]
  transfers between devices with their start and end apart: 11 -> 11, of which waited for: 1 -> 1; matrix products, arithmetic and copies ran while one was open for 8% -> 8% of each run, Pallas kernels for 22% -> 18%
where the time goes in v17:
time: 63.1 us; the launch traced here: 62.5 us
  starting transfers between devices  25 us (40%)
  Pallas kernels  15.4 us (24%)
  local copies, waits for them, and re-layouts  12.4 us (20%)
  matrix products  4.64 us (7%)
  other arithmetic  3.62 us (6%)
  between operations  1.02 us (2%)
    ppermute x10, starting transfers between devices, swap(): return (lax.ppermute(value, axis, pairs), None)  15.9 us
    pallas_call x1, Pallas kernels, local_solve(): pl.pallas_call(solve_kernel, out_shape=(jax.ShapeDtypeStruct((nrhs_here,...  11.2 us
    all_to_all x1, starting transfers between devices, per_device(): held = lax.all_to_all(spread, AXES, 0, 0, tiled=True)  9.13 us
    unnamed x27, local copies, waits for them, and re-layouts  9.04 us
    pallas_call x1, Pallas kernels, finish(): pl.pallas_call(finish_kernel, out_shape=jax.ShapeDtypeStruct(own.shape, j...  4.19 us
    gather x2, local copies, waits for them, and re-layouts, per_device(): outgoing = jnp.take(residual, send_rows, axis=1)  2.49 us
    dot_general x1, matrix products, per_device(): lax.dot_general(vectors, residual, NT, precision=lax.Precision.HIGHEST, p...  2.35 us
    dot_general x1, matrix products, per_device(): jnp.dot(coarse_inverse, rows_of(held), precision=lax.Precision.HIGHEST, p...  2.29 us
  transfers between devices with their start and end apart: 11, of which 1 were waited for; matrix products, arithmetic and copies ran while one was open for 8% of the time, Pallas kernels for 18%

profile of v17, /device:TPU:0, one launch (start us, length us, event | category | flops | bytes accessed | tf_op | source)
XLA Modules:
  0.0 62.5 jit_solution(13348074102907174239)
XLA Ops:
  0.0 0.7 %compare_and_fusion = pred[6,128]{1,0:T(8,128)(4,1)S(1)} fusion(s32[6,128]{1,0:T(8,128)} %param.12), kind=kLoop, calls=%fused_computation.30 | loop fusion | flops 4608 | bytes 3840 | tf_op jit(solution)/shard_map/jit(_take)/and | solution.py:198
  0.7 0.7 %fusion.4 = s32[768]{0:T(1024)S(1)} fusion(s32[6,128]{1,0:T(8,128)} %param.12), kind=kLoop, calls=%fused_computation.31 | loop fusion | flops 2304 | bytes 6144 | tf_op jit(solution)/shard_map/jit(_take)/broadcast_in_dim | solution.py:198
  1.4 2.0 %copy.11 = f32[128,4352]{0,1:T(8,128)S(1)} copy(f32[128,4352]{1,0:T(8,128)} %res_ref.1) | data formatting | bytes 4456448 | tf_op args[0]
  3.5 1.6 %gather_fusion = f32[768,128]{1,0:T(8,128)S(1)} fusion(f32[128,4352]{0,1:T(8,128)S(1)} %copy.11, s32[1024]{0:T(1024)S(1)} %pad_clamp_fusion), kind=kCustom, calls=%fused_computation | custom fusion | bytes 789504 | tf_op jit(solution)/shard_map/jit(_take)/gather | solution.py:198
  5.0 0.9 %copy.12 = f32[6,128,128]{1,2,0:T(8,128)} copy(f32[6,128,128]{2,1,0:T(8,128)S(1)} %bitcast.28) | data formatting | bytes 786432 | tf_op jit(solution)/shard_map/jit(_take)/gather | solution.py:198
  6.0 1.0 %select_bitcast_fusion = f32[128,6,128]{2,0,1:T(8,128)S(1)} fusion(f32[6,128,128]{1,2,0:T(8,128)} %copy.12, pred[6,128]{1,0:T(8,128)(4,1)S(1)} %compare_and_fusion), kind=kLoop, calls=%fused_computation.3 | loop fusion | flops 98304 | bytes 787200 | tf_op jit(solution)/shard_map/jit(_take)/select_n | solution.py:198
  7.5 2.6 %collective-permute-start.2 = (f32[128,128]{1,0:T(8,128)S(1)}, f32[128,128]{1,0:T(8,128)S(1)}, u32[]{:S(2)}, u32[]{:S(2)}) collective-permute-start(f32[128,128]{1,0:T(8,128)S(1)} %get-tuple-element.18), channel_id=1, source_target_pairs={{0,2},{4,6},{2,0},{6,4},{1,3},{5,7},{3,1},{7,5},{8,10},{12,14},{10... | collective-permute-start | bytes 196616 | tf_op jit(solution)/shard_map/ppermute | solution.py:133
  10.1 0.7 %collective-permute-start.3 = (f32[128,128]{1,0:T(8,128)S(1)}, f32[128,128]{1,0:T(8,128)S(1)}, u32[]{:S(2)}, u32[]{:S(2)}) collective-permute-start(f32[128,128]{1,0:T(8,128)S(1)} %get-tuple-element.19), channel_id=1, source_target_pairs={{2,4},{4,2},{3,5},{5,3},{10,12},{12,10},{11,13},{13,11},{18,20},{2... | collective-permute-start | bytes 196616 | tf_op jit(solution)/shard_map/ppermute | solution.py:133
  10.8 1.6 %collective-permute-start = (f32[128,128]{1,0:T(8,128)S(1)}, f32[128,128]{1,0:T(8,128)S(1)}, u32[]{:S(2)}, u32[]{:S(2)}) collective-permute-start(f32[128,128]{1,0:T(8,128)S(1)} %get-tuple-element.20), channel_id=1, source_target_pairs={{0,8},{16,24},{8,0},{24,16},{1,9},{17,25},{9,1},{25,17},{2,10},{18... | collective-permute-start | bytes 196616 | tf_op jit(solution)/shard_map/ppermute | solution.py:133
  13.8 2.3 %fusion.after_ref = f32[40,128]{1,0:T(8,128)S(1)} fusion(f32[128,4352]{1,0:T(8,128)S(1)} %copy-done.1, f32[40,4352]{1,0:T(8,128)S(1)} %copy-done.2, f32[40]{0:T(128)S(1)} %compare_convert_fusion), kind=kOutput, calls=%fused_computation.1 | convolution fusion | flops 267560960 | bytes 2945184 | tf_op jit(solution)/shard_map/dot_general | solution.py:193
  16.3 0.7 %copy-done.7 = f32[128,768]{1,0:T(8,128)} copy-done((f32[128,768]{1,0:T(8,128)}, f32[128,768]{1,0:T(8,128)S(1)}, u32[]{:S(2)}) %copy-start.7) | copy-done | bytes 393240
  17.0 0.9 %broadcast_in_dim.29 = f32[32,40,128]{2,1,0:T(8,128)} broadcast(f32[40,128]{1,0:T(8,128)S(1)} %fusion.after_ref), dimensions={1,2} | broadcast | bytes 675840 | tf_op jit(solution)/shard_map/broadcast_in_dim | solution.py:205
  18.0 9.1 %all-to-all-start = ((f32[32,40,128]{2,1,0:T(8,128)}), f32[32,40,128]{2,1,0:T(8,128)}, u32[]{:S(2)}, u32[]{:S(2)}) async-start(f32[32,40,128]{2,1,0:T(8,128)} %broadcast_in_dim.29), calls=%async_computation | async-start | bytes 1310720 | tf_op jit(solution)/shard_map/all_to_all | solution.py:206
  27.3 1.7 %copy-done.3 = bf16[20,256,256]{2,1,0:T(8,128)(2,1)S(1)} copy-done((bf16[20,256,256]{2,1,0:T(8,128)(2,1)S(1)}, bf16[20,256,256]{2,1,0:T(8,128)(2,1)}, u32[]{:S(2)}) %copy-start.3) | copy-done | bytes 2621464
  29.1 1.7 %copy-done.4 = bf16[19,256,256]{2,1,0:T(8,128)(2,1)S(1)} copy-done((bf16[19,256,256]{2,1,0:T(8,128)(2,1)S(1)}, bf16[19,256,256]{2,1,0:T(8,128)(2,1)}, u32[]{:S(2)}) %copy-start.4) | copy-done | bytes 2490392
  30.8 1.0 %copy-done.8 = f32[128,768]{1,0:T(8,128)S(1)} copy-done((f32[128,768]{1,0:T(8,128)S(1)}, f32[128,768]{1,0:T(8,128)}, u32[]{:S(2)}) %copy-start.8) | copy-done | bytes 393240
  31.8 11.2 %shard_map.82 = (bf16[128,4352]{1,0:T(8,128)(2,1)S(1)}, bf16[128,768]{1,0:T(8,128)(2,1)S(1)}) custom-call(s32[20]{0:T(128)S(1)} %copy-done.10, f32[128,4352]{1,0:T(8,128)S(1)} %copy-done.1, f32[128,768]{1,0:T(8,128)S(1)} %copy-done.8, bf16[20,256,256]{2,1,0:T(8,128)(2,1)S(1)} %copy-done.3, bf16[19,256,256]{2,1,0:T(8,128)(2,1)S(1)} %copy-done.4, ...), custom_call_target="tpu_custom_call" | custom-call | tf_op jit(solution)/shard_map/pallas_call | solution.py:61
  42.9 1.0 %copy-done.5 = bf16[128,4352]{1,0:T(8,128)(2,1)} copy-done((bf16[128,4352]{1,0:T(8,128)(2,1)}, bf16[128,4352]{1,0:T(8,128)(2,1)S(1)}, u32[]{:S(2)}) %copy-start.5) | copy-done | bytes 1114136
  43.9 0.7 %copy-done.9 = bf16[128,768]{1,0:T(8,128)(2,1)} copy-done((bf16[128,768]{1,0:T(8,128)(2,1)}, bf16[128,768]{1,0:T(8,128)(2,1)S(1)}, u32[]{:S(2)}) %copy-start.9) | copy-done | bytes 196632
  45.0 0.9 %slice_select_fusion.1 = (bf16[128,128]{1,0:T(8,128)(2,1)S(1)}, bf16[128,128]{1,0:T(8,128)(2,1)S(1)}, bf16[128,128]{1,0:T(8,128)(2,1)S(1)}, bf16[128,128]{1,0:T(8,128)(2,1)S(1)}, bf16[128,128]{1,0:T(8,128)(2,1)S(1)}) fusion(bf16[128,768]{1,0:T(8,128)(2,1)} %copy-done.9, pred[]{:T(512)S(6)} %eq.21, pred[]{:T(512)S(6)} %eq.20, pred[]{:T(512)S(6)} %eq.19), kind=kLoop, calls=%fused_computation.19 | loop fusion | flops 81920 | bytes 360451 | tf_op jit(solution)/shard_map/jit(_where)/select_n | solution.py:151
  46.8 4.1 %collective-permute-start.8 = (bf16[128,128]{1,0:T(8,128)(2,1)S(1)}, bf16[128,128]{1,0:T(8,128)(2,1)S(1)}, u32[]{:S(2)}, u32[]{:S(2)}) collective-permute-start(bf16[128,128]{1,0:T(8,128)(2,1)S(1)} %get-tuple-element.24), channel_id=1, source_target_pairs={{0,2},{4,6},{2,0},{6,4},{1,3},{5,7},{3,1},{7,5},{8,10},{12,14},{10... | collective-permute-start | bytes 98312 | tf_op jit(solution)/shard_map/ppermute | solution.py:133
  51.6 4.3 %collective-permute-start.6 = (bf16[128,128]{1,0:T(8,128)(2,1)S(1)}, bf16[128,128]{1,0:T(8,128)(2,1)S(1)}, u32[]{:S(2)}, u32[]{:S(2)}) collective-permute-start(bf16[128,128]{1,0:T(8,128)(2,1)S(1)} %get-tuple-element.26), channel_id=1, source_target_pairs={{0,8},{16,24},{8,0},{24,16},{1,9},{17,25},{9,1},{25,17},{2,10},{18... | collective-permute-start | bytes 98312 | tf_op jit(solution)/shard_map/ppermute | solution.py:133
  55.8 2.3 %fusion.5.solved_ref = f32[128,40]{1,0:T(8,128)S(1)} fusion(f32[1280,128]{1,0:T(8,128)} %bitcast.9, f32[40,1280]{1,0:T(8,128)S(1)} %copy-done), kind=kOutput, calls=%fused_computation.34 | convolution fusion | flops 78643200 | bytes 880640 | tf_op jit(solution)/shard_map/dot_general | solution.py:222
  58.3 4.2 %shard_map.83 = f32[128,4352]{1,0:T(8,128)} custom-call(s32[1]{0:T(128)} %copy.30.count_ref, s32[768,1]{1,0:T(8,128)S(1)} %bitcast.27, bf16[128,4352]{1,0:T(8,128)(2,1)S(1)} %copy-done.6, bf16[128,768]{1,0:T(8,128)(2,1)S(1)} %select_dynamic-update-slice_fusion.6.back_ref, f32[128,40]{1,0:T(8,128)S(1)} %fusion.5.solved_ref, f32[40,4352]{1,0:T(8,128)S(1)} %copy-done.2), custom_call_target="tpu_custom_call" | custom-call | tf_op jit(solution)/shard_map/pallas_call | solution.py:114
  (51 shorter events, 3.5 us)
Async XLA Ops:
  0.0 55.8 %copy-start = (f32[40,1280]{1,0:T(8,128)S(1)}, f32[40,1280]{1,0:T(8,128)}, u32[]{:S(2)}) copy-start(f32[40,1280]{1,0:T(8,128)} %param.15) | copy-start | bytes 614404
  3.4 10.3 %copy-start.2 = (f32[40,4352]{1,0:T(8,128)S(1)}, f32[40,4352]{1,0:T(8,128)}, u32[]{:S(2)}) copy-start(f32[40,4352]{1,0:T(8,128)} %vec_ref.1) | copy-start | bytes 2088964
  5.0 8.7 %copy-start.1 = (f32[128,4352]{1,0:T(8,128)S(1)}, f32[128,4352]{1,0:T(8,128)}, u32[]{:S(2)}) copy-start(f32[128,4352]{1,0:T(8,128)} %res_ref.1) | copy-start | bytes 6684676
  7.0 9.2 %collective-permute-start.4 = (f32[128,128]{1,0:T(8,128)S(1)}, f32[128,128]{1,0:T(8,128)S(1)}, u32[]{:S(2)}, u32[]{:S(2)}) collective-permute-start(f32[128,128]{1,0:T(8,128)S(1)} %get-tuple-element.17), channel_id=1, source_target_pairs={{0,1},{1,0},{2,3},{3,2},{4,5},{5,4},{6,7},{7,6},{8,9},{9,8},{10,11... | collective-permute-start | bytes 196616 | tf_op jit(solution)/shard_map/ppermute | solution.py:133
  7.5 8.6 %collective-permute-start.2 = (f32[128,128]{1,0:T(8,128)S(1)}, f32[128,128]{1,0:T(8,128)S(1)}, u32[]{:S(2)}, u32[]{:S(2)}) collective-permute-start(f32[128,128]{1,0:T(8,128)S(1)} %get-tuple-element.18), channel_id=1, source_target_pairs={{0,2},{4,6},{2,0},{6,4},{1,3},{5,7},{3,1},{7,5},{8,10},{12,14},{10... | collective-permute-start | bytes 196616 | tf_op jit(solution)/shard_map/ppermute | solution.py:133
  10.1 6.1 %collective-permute-start.3 = (f32[128,128]{1,0:T(8,128)S(1)}, f32[128,128]{1,0:T(8,128)S(1)}, u32[]{:S(2)}, u32[]{:S(2)}) collective-permute-start(f32[128,128]{1,0:T(8,128)S(1)} %get-tuple-element.19), channel_id=1, source_target_pairs={{2,4},{4,2},{3,5},{5,3},{10,12},{12,10},{11,13},{13,11},{18,20},{2... | collective-permute-start | bytes 196616 | tf_op jit(solution)/shard_map/ppermute | solution.py:133
  10.8 5.4 %collective-permute-start = (f32[128,128]{1,0:T(8,128)S(1)}, f32[128,128]{1,0:T(8,128)S(1)}, u32[]{:S(2)}, u32[]{:S(2)}) collective-permute-start(f32[128,128]{1,0:T(8,128)S(1)} %get-tuple-element.20), channel_id=1, source_target_pairs={{0,8},{16,24},{8,0},{24,16},{1,9},{17,25},{9,1},{25,17},{2,10},{18... | collective-permute-start | bytes 196616 | tf_op jit(solution)/shard_map/ppermute | solution.py:133
  12.4 3.7 %collective-permute-start.1 = (f32[128,128]{1,0:T(8,128)S(1)}, f32[128,128]{1,0:T(8,128)S(1)}, u32[]{:S(2)}, u32[]{:S(2)}) collective-permute-start(f32[128,128]{1,0:T(8,128)S(1)} %get-tuple-element.21), channel_id=1, source_target_pairs={{8,16},{16,8},{9,17},{17,9},{10,18},{18,10},{11,19},{19,11},{12,20... | collective-permute-start | bytes 196616 | tf_op jit(solution)/shard_map/ppermute | solution.py:133
  16.1 11.0 %copy-start.11 = (s32[6,128]{1,0:T(8,128)S(1)}, s32[6,128]{1,0:T(8,128)}, u32[]{:S(2)}) copy-start(s32[6,128]{1,0:T(8,128)} %param.12) | copy-start | bytes 9220
  16.1 11.2 %copy-start.10 = (s32[20]{0:T(128)S(1)}, s32[20]{0:T(128)}, u32[]{:S(2)}) copy-start(s32[20]{0:T(128)} %parent_ref.1) | copy-start | bytes 244
  16.3 0.7 %copy-start.7 = (f32[128,768]{1,0:T(8,128)}, f32[128,768]{1,0:T(8,128)S(1)}, u32[]{:S(2)}) copy-start(f32[128,768]{1,0:T(8,128)S(1)} %select_dynamic-update-slice_fusion.slot_ref) | copy-start | bytes 1179652
  18.0 27.0 %all-to-all-start = ((f32[32,40,128]{2,1,0:T(8,128)}), f32[32,40,128]{2,1,0:T(8,128)}, u32[]{:S(2)}, u32[]{:S(2)}) async-start(f32[32,40,128]{2,1,0:T(8,128)} %broadcast_in_dim.29), calls=%async_computation | async-start | bytes 1310720 | tf_op jit(solution)/shard_map/all_to_all | solution.py:206
  27.3 1.7 %copy-start.3 = (bf16[20,256,256]{2,1,0:T(8,128)(2,1)S(1)}, bf16[20,256,256]{2,1,0:T(8,128)(2,1)}, u32[]{:S(2)}) copy-start(bf16[20,256,256]{2,1,0:T(8,128)(2,1)} %inv_ref.1) | copy-start | bytes 7864324
  29.1 1.7 %copy-start.4 = (bf16[19,256,256]{2,1,0:T(8,128)(2,1)S(1)}, bf16[19,256,256]{2,1,0:T(8,128)(2,1)}, u32[]{:S(2)}) copy-start(bf16[19,256,256]{2,1,0:T(8,128)(2,1)} %cpl_ref.1) | copy-start | bytes 7471108
  30.8 1.0 %copy-start.8 = (f32[128,768]{1,0:T(8,128)S(1)}, f32[128,768]{1,0:T(8,128)}, u32[]{:S(2)}) copy-start(f32[128,768]{1,0:T(8,128)} %copy-done.7) | copy-start | bytes 1179652
  42.9 1.0 %copy-start.5 = (bf16[128,4352]{1,0:T(8,128)(2,1)}, bf16[128,4352]{1,0:T(8,128)(2,1)S(1)}, u32[]{:S(2)}) copy-start(bf16[128,4352]{1,0:T(8,128)(2,1)S(1)} %get-tuple-element.13.own_ref) | copy-start | bytes 3342340
  43.9 0.7 %copy-start.9 = (bf16[128,768]{1,0:T(8,128)(2,1)}, bf16[128,768]{1,0:T(8,128)(2,1)S(1)}, u32[]{:S(2)}) copy-start(bf16[128,768]{1,0:T(8,128)(2,1)S(1)} %get-tuple-element.15) | copy-start | bytes 589828
  45.0 13.3 %copy-start.6 = (bf16[128,4352]{1,0:T(8,128)(2,1)S(1)}, bf16[128,4352]{1,0:T(8,128)(2,1)}, u32[]{:S(2)}) copy-start(bf16[128,4352]{1,0:T(8,128)(2,1)} %copy-done.5) | copy-start | bytes 3342340
  46.0 12.3 %collective-permute-start.9 = (bf16[128,128]{1,0:T(8,128)(2,1)S(1)}, bf16[128,128]{1,0:T(8,128)(2,1)S(1)}, u32[]{:S(2)}, u32[]{:S(2)}) collective-permute-start(bf16[128,128]{1,0:T(8,128)(2,1)S(1)} %get-tuple-element.22), channel_id=1, source_target_pairs={{0,1},{1,0},{2,3},{3,2},{4,5},{5,4},{6,7},{7,6},{8,9},{9,8},{10,11... | collective-permute-start | bytes 98312 | tf_op jit(solution)/shard_map/ppermute | solution.py:133
  46.1 12.1 %collective-permute-start.7 = (bf16[128,128]{1,0:T(8,128)(2,1)S(1)}, bf16[128,128]{1,0:T(8,128)(2,1)S(1)}, u32[]{:S(2)}, u32[]{:S(2)}) collective-permute-start(bf16[128,128]{1,0:T(8,128)(2,1)S(1)} %get-tuple-element.23), channel_id=1, source_target_pairs={{2,4},{4,2},{3,5},{5,3},{10,12},{12,10},{11,13},{13,11},{18,20},{2... | collective-permute-start | bytes 98312 | tf_op jit(solution)/shard_map/ppermute | solution.py:133
  46.8 11.5 %collective-permute-start.8 = (bf16[128,128]{1,0:T(8,128)(2,1)S(1)}, bf16[128,128]{1,0:T(8,128)(2,1)S(1)}, u32[]{:S(2)}, u32[]{:S(2)}) collective-permute-start(bf16[128,128]{1,0:T(8,128)(2,1)S(1)} %get-tuple-element.24), channel_id=1, source_target_pairs={{0,2},{4,6},{2,0},{6,4},{1,3},{5,7},{3,1},{7,5},{8,10},{12,14},{10... | collective-permute-start | bytes 98312 | tf_op jit(solution)/shard_map/ppermute | solution.py:133
  50.9 7.2 %collective-permute-start.5 = (bf16[128,128]{1,0:T(8,128)(2,1)S(1)}, bf16[128,128]{1,0:T(8,128)(2,1)S(1)}, u32[]{:S(2)}, u32[]{:S(2)}) collective-permute-start(bf16[128,128]{1,0:T(8,128)(2,1)S(1)} %get-tuple-element.25), channel_id=1, source_target_pairs={{8,16},{16,8},{9,17},{17,9},{10,18},{18,10},{11,19},{19,11},{12,20... | collective-permute-start | bytes 98312 | tf_op jit(solution)/shard_map/ppermute | solution.py:133
  51.6 6.6 %collective-permute-start.6 = (bf16[128,128]{1,0:T(8,128)(2,1)S(1)}, bf16[128,128]{1,0:T(8,128)(2,1)S(1)}, u32[]{:S(2)}, u32[]{:S(2)}) collective-permute-start(bf16[128,128]{1,0:T(8,128)(2,1)S(1)} %get-tuple-element.26), channel_id=1, source_target_pairs={{0,8},{16,24},{8,0},{24,16},{1,9},{17,25},{9,1},{25,17},{2,10},{18... | collective-permute-start | bytes 98312 | tf_op jit(solution)/shard_map/ppermute | solution.py:133

commit v18 on v15

--- a/solution.py
+++ b/solution.py
@@ -103,8 +103,8 @@
         onehot = (rows == here).astype(jnp.bfloat16)
         total = own_ref[:, cols].astype(jnp.float32)
         total += jnp.dot(back, onehot, preferred_element_type=jnp.float32)
-        v1, v2, v3 = split3(jnp.where(keep, vec_ref[:, cols], 0.0))
-        for left, right in ((s1, v1), (s1, v2), (s2, v1), (s1, v3), (s3, v1), (s2, v2)):
+        v1, v2, _ = split3(jnp.where(keep, vec_ref[:, cols], 0.0))
+        for left, right in ((s1, v1), (s1, v2), (s2, v1)):
             total += jnp.dot(left, right, preferred_element_type=jnp.float32)
         out_ref[:, cols] = total
 
@@ -191,7 +191,7 @@
     mask = (lax.iota(jnp.int32, kmax_here) < counts[0]).astype(jnp.float32)
     vectors = deflation * mask[:, None]
     coeffs_t = lax.dot_general(
-        vectors, residual, NT, precision=lax.Precision.HIGHEST, preferred_element_type=jnp.float32
+        vectors, residual, NT, precision=lax.Precision.HIGH, preferred_element_type=jnp.float32
     )
     total_dev = coarse_inverse.shape[1] // kmax_here
 
@@ -220,7 +220,7 @@
     returned = jnp.concatenate(returned, axis=1)
 
     solved_t = jnp.dot(
-        coarse_inverse, rows_of(held), precision=lax.Precision.HIGHEST, preferred_element_type=jnp.float32
+        coarse_inverse, rows_of(held), precision=lax.Precision.HIGH, preferred_element_type=jnp.float32
     )
     return finish(send_rows, counts, own, returned, solved_t.T, deflation)
 

time: 61.5 us -> 60.2 us (0.979)
  matrix products: 4.64 us -> 3.05 us
  starting transfers between devices: 23.5 us -> 24.6 us
  Pallas kernels: 17.3 us -> 16.5 us
    dot_general x2, matrix products: 4.64 us -> 3.05 us  [the longest x1 1.79 us: per_device(): jnp.dot(coarse_inverse, rows_of(held), precision=lax.Precision.HIGH, pref...]
    all_to_all x1, starting transfers between devices: 9.13 us -> 10.2 us  [per_device(): held = lax.all_to_all(spread, AXES, 0, 0, tiled=True)]
    pallas_call x1, Pallas kernels: 4.17 us -> 3.34 us  [finish(): pl.pallas_call(finish_kernel, out_shape=jax.ShapeDtypeStruct(own.shape, j...]
  transfers between devices with their start and end apart: 11 -> 11, of which waited for: 1 -> 2; matrix products, arithmetic and copies ran while one was open for 8% -> 6% of each run, Pallas kernels for 22% -> 22%
where the time goes in v18:
time: 60.2 us; the launch traced here: 59.8 us
  starting transfers between devices  24.6 us (41%)
  Pallas kernels  16.5 us (27%)
  local copies, waits for them, and re-layouts  9.01 us (15%)
  other arithmetic  3.62 us (6%)
  matrix products  3.05 us (5%)
  waiting for transfers between devices  2 us (3%)
  between operations  1.01 us (2%)
    ppermute x10, starting transfers between devices, swap(): return (lax.ppermute(value, axis, pairs), None)  14.4 us
    pallas_call x1, Pallas kernels, local_solve(): pl.pallas_call(solve_kernel, out_shape=(jax.ShapeDtypeStruct((nrhs_here,...  13.1 us
    all_to_all x1, starting transfers between devices, per_device(): held = lax.all_to_all(spread, AXES, 0, 0, tiled=True)  10.2 us
    unnamed x23, local copies, waits for them, and re-layouts  5.62 us
    pallas_call x1, Pallas kernels, finish(): pl.pallas_call(finish_kernel, out_shape=jax.ShapeDtypeStruct(own.shape, j...  3.34 us
    gather x2, local copies, waits for them, and re-layouts, per_device(): outgoing = jnp.take(residual, send_rows, axis=1)  2.49 us
    all_to_all x1, waiting for transfers between devices, per_device(): held = lax.all_to_all(spread, AXES, 0, 0, tiled=True)  1.86 us
    dot_general x1, matrix products, per_device(): jnp.dot(coarse_inverse, rows_of(held), precision=lax.Precision.HIGH, pref...  1.79 us
  transfers between devices with their start and end apart: 11, of which 2 were waited for; matrix products, arithmetic and copies ran while one was open for 6% of the time, Pallas kernels for 22%

profile of v18, /device:TPU:0, one launch (start us, length us, event | category | flops | bytes accessed | tf_op | source)
XLA Modules:
  0.0 59.8 jit_solution(7253686572929466401)
XLA Ops:
  0.0 0.7 %compare_and_fusion = pred[6,128]{1,0:T(8,128)(4,1)S(1)} fusion(s32[6,128]{1,0:T(8,128)} %param.12), kind=kLoop, calls=%fused_computation.30 | loop fusion | flops 4608 | bytes 3840 | tf_op jit(solution)/shard_map/jit(_take)/and | solution.py:198
  0.7 0.7 %fusion.4 = s32[768]{0:T(1024)S(1)} fusion(s32[6,128]{1,0:T(8,128)} %param.12), kind=kLoop, calls=%fused_computation.31 | loop fusion | flops 2304 | bytes 6144 | tf_op jit(solution)/shard_map/jit(_take)/broadcast_in_dim | solution.py:198
  1.4 2.0 %copy.11 = f32[128,4352]{0,1:T(8,128)S(1)} copy(f32[128,4352]{1,0:T(8,128)} %res_ref.1) | data formatting | bytes 4456448 | tf_op args[0]
  3.5 1.6 %gather_fusion = f32[768,128]{1,0:T(8,128)S(1)} fusion(f32[128,4352]{0,1:T(8,128)S(1)} %copy.11, s32[1024]{0:T(1024)S(1)} %pad_clamp_fusion), kind=kCustom, calls=%fused_computation | custom fusion | bytes 789504 | tf_op jit(solution)/shard_map/jit(_take)/gather | solution.py:198
  5.0 0.9 %copy.12 = f32[6,128,128]{1,2,0:T(8,128)} copy(f32[6,128,128]{2,1,0:T(8,128)S(1)} %bitcast.28) | data formatting | bytes 786432 | tf_op jit(solution)/shard_map/jit(_take)/gather | solution.py:198
  6.0 1.0 %select_bitcast_fusion = f32[128,6,128]{2,0,1:T(8,128)S(1)} fusion(f32[6,128,128]{1,2,0:T(8,128)} %copy.12, pred[6,128]{1,0:T(8,128)(4,1)S(1)} %compare_and_fusion), kind=kLoop, calls=%fused_computation.3 | loop fusion | flops 98304 | bytes 787200 | tf_op jit(solution)/shard_map/jit(_take)/select_n | solution.py:198
  7.5 2.6 %collective-permute-start.2 = (f32[128,128]{1,0:T(8,128)S(1)}, f32[128,128]{1,0:T(8,128)S(1)}, u32[]{:S(2)}, u32[]{:S(2)}) collective-permute-start(f32[128,128]{1,0:T(8,128)S(1)} %get-tuple-element.18), channel_id=1, source_target_pairs={{0,2},{4,6},{2,0},{6,4},{1,3},{5,7},{3,1},{7,5},{8,10},{12,14},{10... | collective-permute-start | bytes 196616 | tf_op jit(solution)/shard_map/ppermute | solution.py:133
  10.1 0.7 %collective-permute-start.3 = (f32[128,128]{1,0:T(8,128)S(1)}, f32[128,128]{1,0:T(8,128)S(1)}, u32[]{:S(2)}, u32[]{:S(2)}) collective-permute-start(f32[128,128]{1,0:T(8,128)S(1)} %get-tuple-element.19), channel_id=1, source_target_pairs={{2,4},{4,2},{3,5},{5,3},{10,12},{12,10},{11,13},{13,11},{18,20},{2... | collective-permute-start | bytes 196616 | tf_op jit(solution)/shard_map/ppermute | solution.py:133
  10.8 1.6 %collective-permute-start = (f32[128,128]{1,0:T(8,128)S(1)}, f32[128,128]{1,0:T(8,128)S(1)}, u32[]{:S(2)}, u32[]{:S(2)}) collective-permute-start(f32[128,128]{1,0:T(8,128)S(1)} %get-tuple-element.20), channel_id=1, source_target_pairs={{0,8},{16,24},{8,0},{24,16},{1,9},{17,25},{9,1},{25,17},{2,10},{18... | collective-permute-start | bytes 196616 | tf_op jit(solution)/shard_map/ppermute | solution.py:133
  12.4 0.7 %collective-permute-start.1 = (f32[128,128]{1,0:T(8,128)S(1)}, f32[128,128]{1,0:T(8,128)S(1)}, u32[]{:S(2)}, u32[]{:S(2)}) collective-permute-start(f32[128,128]{1,0:T(8,128)S(1)} %get-tuple-element.21), channel_id=1, source_target_pairs={{8,16},{16,8},{9,17},{17,9},{10,18},{18,10},{11,19},{19,11},{12,20... | collective-permute-start | bytes 196616 | tf_op jit(solution)/shard_map/ppermute | solution.py:133
  13.8 1.3 %fusion.after_ref = f32[40,128]{1,0:T(8,128)S(1)} fusion(f32[128,4352]{1,0:T(8,128)S(1)} %copy-done.1, f32[40,4352]{1,0:T(8,128)S(1)} %copy-done.2, f32[40]{0:T(128)S(1)} %compare_convert_fusion), kind=kOutput, calls=%fused_computation.1 | convolution fusion | flops 133867520 | bytes 2945184 | tf_op jit(solution)/shard_map/dot_general | solution.py:193
  15.3 0.7 %copy-done.5 = f32[128,768]{1,0:T(8,128)} copy-done((f32[128,768]{1,0:T(8,128)}, f32[128,768]{1,0:T(8,128)S(1)}, u32[]{:S(2)}) %copy-start.5) | copy-done | bytes 393240
  16.0 0.9 %broadcast_in_dim.29 = f32[32,40,128]{2,1,0:T(8,128)} broadcast(f32[40,128]{1,0:T(8,128)S(1)} %fusion.after_ref), dimensions={1,2} | broadcast | bytes 675840 | tf_op jit(solution)/shard_map/broadcast_in_dim | solution.py:205
  16.9 10.2 %all-to-all-start = ((f32[32,40,128]{2,1,0:T(8,128)}), f32[32,40,128]{2,1,0:T(8,128)}, u32[]{:S(2)}, u32[]{:S(2)}) async-start(f32[32,40,128]{2,1,0:T(8,128)} %broadcast_in_dim.29), calls=%async_computation | async-start | bytes 1310720 | tf_op jit(solution)/shard_map/all_to_all | solution.py:206
  27.3 1.0 %copy-done.6 = f32[128,768]{1,0:T(8,128)S(1)} copy-done((f32[128,768]{1,0:T(8,128)S(1)}, f32[128,768]{1,0:T(8,128)}, u32[]{:S(2)}) %copy-start.6) | copy-done | bytes 393240
  28.3 13.1 %shard_map.82 = (bf16[128,4352]{1,0:T(8,128)(2,1)S(1)}, bf16[128,768]{1,0:T(8,128)(2,1)S(1)}) custom-call(s32[20]{0:T(128)S(1)} %copy-done.8, f32[128,4352]{1,0:T(8,128)S(1)} %copy-done.1, f32[128,768]{1,0:T(8,128)S(1)} %copy-done.6, bf16[20,256,256]{2,1,0:T(8,128)(2,1)} %inv_ref.1, bf16[19,256,256]{2,1,0:T(8,128)(2,1)} %cpl_ref.1, f32[40,128]{1,0:T(8,128)S(1)} %fusion.after_ref), custom_call_target="tpu_custom_call" | custom-call | tf_op jit(solution)/shard_map/pallas_call | solution.py:61
  41.5 1.0 %copy-done.3 = bf16[128,4352]{1,0:T(8,128)(2,1)} copy-done((bf16[128,4352]{1,0:T(8,128)(2,1)}, bf16[128,4352]{1,0:T(8,128)(2,1)S(1)}, u32[]{:S(2)}) %copy-start.3) | copy-done | bytes 1114136
  42.4 0.7 %copy-done.7 = bf16[128,768]{1,0:T(8,128)(2,1)} copy-done((bf16[128,768]{1,0:T(8,128)(2,1)}, bf16[128,768]{1,0:T(8,128)(2,1)S(1)}, u32[]{:S(2)}) %copy-start.7) | copy-done | bytes 196632
  43.1 1.9 %all-to-all-done = f32[32,40,128]{2,1,0:T(8,128)} async-done(((f32[32,40,128]{2,1,0:T(8,128)}), f32[32,40,128]{2,1,0:T(8,128)}, u32[]{:S(2)}, u32[]{:S(2)}) %all-to-all-start) | async-done | bytes 655392 | tf_op jit(solution)/shard_map/all_to_all | solution.py:206
  45.0 0.9 %slice_select_fusion.1 = (bf16[128,128]{1,0:T(8,128)(2,1)S(1)}, bf16[128,128]{1,0:T(8,128)(2,1)S(1)}, bf16[128,128]{1,0:T(8,128)(2,1)S(1)}, bf16[128,128]{1,0:T(8,128)(2,1)S(1)}, bf16[128,128]{1,0:T(8,128)(2,1)S(1)}) fusion(bf16[128,768]{1,0:T(8,128)(2,1)} %copy-done.7, pred[]{:T(512)S(6)} %eq.21, pred[]{:T(512)S(6)} %eq.20, pred[]{:T(512)S(6)} %eq.19), kind=kLoop, calls=%fused_computation.19 | loop fusion | flops 81920 | bytes 360451 | tf_op jit(solution)/shard_map/jit(_where)/select_n | solution.py:151
  46.7 4.1 %collective-permute-start.8 = (bf16[128,128]{1,0:T(8,128)(2,1)S(1)}, bf16[128,128]{1,0:T(8,128)(2,1)S(1)}, u32[]{:S(2)}, u32[]{:S(2)}) collective-permute-start(bf16[128,128]{1,0:T(8,128)(2,1)S(1)} %get-tuple-element.24), channel_id=1, source_target_pairs={{0,2},{4,6},{2,0},{6,4},{1,3},{5,7},{3,1},{7,5},{8,10},{12,14},{10... | collective-permute-start | bytes 98312 | tf_op jit(solution)/shard_map/ppermute | solution.py:133
  51.5 2.8 %collective-permute-start.6 = (bf16[128,128]{1,0:T(8,128)(2,1)S(1)}, bf16[128,128]{1,0:T(8,128)(2,1)S(1)}, u32[]{:S(2)}, u32[]{:S(2)}) collective-permute-start(bf16[128,128]{1,0:T(8,128)(2,1)S(1)} %get-tuple-element.26), channel_id=1, source_target_pairs={{0,8},{16,24},{8,0},{24,16},{1,9},{17,25},{9,1},{25,17},{2,10},{18... | collective-permute-start | bytes 98312 | tf_op jit(solution)/shard_map/ppermute | solution.py:133
  54.4 1.8 %fusion.5.solved_ref = f32[128,40]{1,0:T(8,128)S(1)} fusion(f32[1280,128]{1,0:T(8,128)} %bitcast.9, f32[40,1280]{1,0:T(8,128)S(1)} %copy-done), kind=kOutput, calls=%fused_computation.34 | convolution fusion | flops 39321600 | bytes 880640 | tf_op jit(solution)/shard_map/dot_general | solution.py:222
  56.4 3.3 %shard_map.83 = f32[128,4352]{1,0:T(8,128)} custom-call(s32[1]{0:T(128)} %copy.30.count_ref, s32[768,1]{1,0:T(8,128)S(1)} %bitcast.27, bf16[128,4352]{1,0:T(8,128)(2,1)S(1)} %copy-done.4, bf16[128,768]{1,0:T(8,128)(2,1)S(1)} %select_dynamic-update-slice_fusion.6.back_ref, f32[128,40]{1,0:T(8,128)S(1)} %fusion.5.solved_ref, f32[40,4352]{1,0:T(8,128)S(1)} %copy-done.2), custom_call_target="tpu_custom_call" | custom-call | tf_op jit(solution)/shard_map/pallas_call | solution.py:114
  (47 shorter events, 2.6 us)
Async XLA Ops:
  0.0 54.4 %copy-start = (f32[40,1280]{1,0:T(8,128)S(1)}, f32[40,1280]{1,0:T(8,128)}, u32[]{:S(2)}) copy-start(f32[40,1280]{1,0:T(8,128)} %param.15) | copy-start | bytes 614404
  3.4 10.3 %copy-start.2 = (f32[40,4352]{1,0:T(8,128)S(1)}, f32[40,4352]{1,0:T(8,128)}, u32[]{:S(2)}) copy-start(f32[40,4352]{1,0:T(8,128)} %vec_ref.1) | copy-start | bytes 2088964
  5.0 8.7 %copy-start.1 = (f32[128,4352]{1,0:T(8,128)S(1)}, f32[128,4352]{1,0:T(8,128)}, u32[]{:S(2)}) copy-start(f32[128,4352]{1,0:T(8,128)} %res_ref.1) | copy-start | bytes 6684676
  7.0 8.2 %collective-permute-start.4 = (f32[128,128]{1,0:T(8,128)S(1)}, f32[128,128]{1,0:T(8,128)S(1)}, u32[]{:S(2)}, u32[]{:S(2)}) collective-permute-start(f32[128,128]{1,0:T(8,128)S(1)} %get-tuple-element.17), channel_id=1, source_target_pairs={{0,1},{1,0},{2,3},{3,2},{4,5},{5,4},{6,7},{7,6},{8,9},{9,8},{10,11... | collective-permute-start | bytes 196616 | tf_op jit(solution)/shard_map/ppermute | solution.py:133
  7.5 7.6 %collective-permute-start.2 = (f32[128,128]{1,0:T(8,128)S(1)}, f32[128,128]{1,0:T(8,128)S(1)}, u32[]{:S(2)}, u32[]{:S(2)}) collective-permute-start(f32[128,128]{1,0:T(8,128)S(1)} %get-tuple-element.18), channel_id=1, source_target_pairs={{0,2},{4,6},{2,0},{6,4},{1,3},{5,7},{3,1},{7,5},{8,10},{12,14},{10... | collective-permute-start | bytes 196616 | tf_op jit(solution)/shard_map/ppermute | solution.py:133
  10.1 5.0 %collective-permute-start.3 = (f32[128,128]{1,0:T(8,128)S(1)}, f32[128,128]{1,0:T(8,128)S(1)}, u32[]{:S(2)}, u32[]{:S(2)}) collective-permute-start(f32[128,128]{1,0:T(8,128)S(1)} %get-tuple-element.19), channel_id=1, source_target_pairs={{2,4},{4,2},{3,5},{5,3},{10,12},{12,10},{11,13},{13,11},{18,20},{2... | collective-permute-start | bytes 196616 | tf_op jit(solution)/shard_map/ppermute | solution.py:133
  10.8 4.3 %collective-permute-start = (f32[128,128]{1,0:T(8,128)S(1)}, f32[128,128]{1,0:T(8,128)S(1)}, u32[]{:S(2)}, u32[]{:S(2)}) collective-permute-start(f32[128,128]{1,0:T(8,128)S(1)} %get-tuple-element.20), channel_id=1, source_target_pairs={{0,8},{16,24},{8,0},{24,16},{1,9},{17,25},{9,1},{25,17},{2,10},{18... | collective-permute-start | bytes 196616 | tf_op jit(solution)/shard_map/ppermute | solution.py:133
  12.4 2.7 %collective-permute-start.1 = (f32[128,128]{1,0:T(8,128)S(1)}, f32[128,128]{1,0:T(8,128)S(1)}, u32[]{:S(2)}, u32[]{:S(2)}) collective-permute-start(f32[128,128]{1,0:T(8,128)S(1)} %get-tuple-element.21), channel_id=1, source_target_pairs={{8,16},{16,8},{9,17},{17,9},{10,18},{18,10},{11,19},{19,11},{12,20... | collective-permute-start | bytes 196616 | tf_op jit(solution)/shard_map/ppermute | solution.py:133
  15.0 12.0 %copy-start.9 = (s32[6,128]{1,0:T(8,128)S(1)}, s32[6,128]{1,0:T(8,128)}, u32[]{:S(2)}) copy-start(s32[6,128]{1,0:T(8,128)} %param.12) | copy-start | bytes 9220
  15.1 12.2 %copy-start.8 = (s32[20]{0:T(128)S(1)}, s32[20]{0:T(128)}, u32[]{:S(2)}) copy-start(s32[20]{0:T(128)} %parent_ref.1) | copy-start | bytes 244
  15.2 0.7 %copy-start.5 = (f32[128,768]{1,0:T(8,128)}, f32[128,768]{1,0:T(8,128)S(1)}, u32[]{:S(2)}) copy-start(f32[128,768]{1,0:T(8,128)S(1)} %select_dynamic-update-slice_fusion.slot_ref) | copy-start | bytes 1179652
  16.9 28.1 %all-to-all-start = ((f32[32,40,128]{2,1,0:T(8,128)}), f32[32,40,128]{2,1,0:T(8,128)}, u32[]{:S(2)}, u32[]{:S(2)}) async-start(f32[32,40,128]{2,1,0:T(8,128)} %broadcast_in_dim.29), calls=%async_computation | async-start | bytes 1310720 | tf_op jit(solution)/shard_map/all_to_all | solution.py:206
  27.3 1.0 %copy-start.6 = (f32[128,768]{1,0:T(8,128)S(1)}, f32[128,768]{1,0:T(8,128)}, u32[]{:S(2)}) copy-start(f32[128,768]{1,0:T(8,128)} %copy-done.5) | copy-start | bytes 1179652
  41.4 1.0 %copy-start.3 = (bf16[128,4352]{1,0:T(8,128)(2,1)}, bf16[128,4352]{1,0:T(8,128)(2,1)S(1)}, u32[]{:S(2)}) copy-start(bf16[128,4352]{1,0:T(8,128)(2,1)S(1)} %get-tuple-element.13.own_ref) | copy-start | bytes 3342340
  42.4 0.7 %copy-start.7 = (bf16[128,768]{1,0:T(8,128)(2,1)}, bf16[128,768]{1,0:T(8,128)(2,1)S(1)}, u32[]{:S(2)}) copy-start(bf16[128,768]{1,0:T(8,128)(2,1)S(1)} %get-tuple-element.15) | copy-start | bytes 589828
  45.0 11.5 %copy-start.4 = (bf16[128,4352]{1,0:T(8,128)(2,1)S(1)}, bf16[128,4352]{1,0:T(8,128)(2,1)}, u32[]{:S(2)}) copy-start(bf16[128,4352]{1,0:T(8,128)(2,1)} %copy-done.3) | copy-start | bytes 3342340
  45.9 10.4 %collective-permute-start.9 = (bf16[128,128]{1,0:T(8,128)(2,1)S(1)}, bf16[128,128]{1,0:T(8,128)(2,1)S(1)}, u32[]{:S(2)}, u32[]{:S(2)}) collective-permute-start(bf16[128,128]{1,0:T(8,128)(2,1)S(1)} %get-tuple-element.22), channel_id=1, source_target_pairs={{0,1},{1,0},{2,3},{3,2},{4,5},{5,4},{6,7},{7,6},{8,9},{9,8},{10,11... | collective-permute-start | bytes 98312 | tf_op jit(solution)/shard_map/ppermute | solution.py:133
  46.1 10.2 %collective-permute-start.7 = (bf16[128,128]{1,0:T(8,128)(2,1)S(1)}, bf16[128,128]{1,0:T(8,128)(2,1)S(1)}, u32[]{:S(2)}, u32[]{:S(2)}) collective-permute-start(bf16[128,128]{1,0:T(8,128)(2,1)S(1)} %get-tuple-element.23), channel_id=1, source_target_pairs={{2,4},{4,2},{3,5},{5,3},{10,12},{12,10},{11,13},{13,11},{18,20},{2... | collective-permute-start | bytes 98312 | tf_op jit(solution)/shard_map/ppermute | solution.py:133
  46.7 9.6 %collective-permute-start.8 = (bf16[128,128]{1,0:T(8,128)(2,1)S(1)}, bf16[128,128]{1,0:T(8,128)(2,1)S(1)}, u32[]{:S(2)}, u32[]{:S(2)}) collective-permute-start(bf16[128,128]{1,0:T(8,128)(2,1)S(1)} %get-tuple-element.24), channel_id=1, source_target_pairs={{0,2},{4,6},{2,0},{6,4},{1,3},{5,7},{3,1},{7,5},{8,10},{12,14},{10... | collective-permute-start | bytes 98312 | tf_op jit(solution)/shard_map/ppermute | solution.py:133
  50.9 5.3 %collective-permute-start.5 = (bf16[128,128]{1,0:T(8,128)(2,1)S(1)}, bf16[128,128]{1,0:T(8,128)(2,1)S(1)}, u32[]{:S(2)}, u32[]{:S(2)}) collective-permute-start(bf16[128,128]{1,0:T(8,128)(2,1)S(1)} %get-tuple-element.25), channel_id=1, source_target_pairs={{8,16},{16,8},{9,17},{17,9},{10,18},{18,10},{11,19},{19,11},{12,20... | collective-permute-start | bytes 98312 | tf_op jit(solution)/shard_map/ppermute | solution.py:133
  51.5 4.7 %collective-permute-start.6 = (bf16[128,128]{1,0:T(8,128)(2,1)S(1)}, bf16[128,128]{1,0:T(8,128)(2,1)S(1)}, u32[]{:S(2)}, u32[]{:S(2)}) collective-permute-start(bf16[128,128]{1,0:T(8,128)(2,1)S(1)} %get-tuple-element.26), channel_id=1, source_target_pairs={{0,8},{16,24},{8,0},{24,16},{1,9},{17,25},{9,1},{25,17},{2,10},{18... | collective-permute-start | bytes 98312 | tf_op jit(solution)/shard_map/ppermute | solution.py:133

commit v19 on v18

--- a/solution.py
+++ b/solution.py
@@ -93,13 +93,14 @@
     owned_n = own_ref.shape[1]
     kmax_here = vec_ref.shape[0]
     keep = lax.broadcasted_iota(jnp.int32, (kmax_here, 1), 0) < count_ref[0]
-    chunk = 256
+    chunk = 512
     rows = rows_ref[...]
     back = back_ref[...]
-    s1, s2, s3 = split3(solved_ref[...])
+    s1, s2, _ = split3(solved_ref[...])
     for start in range(0, owned_n, chunk):
-        cols = pl.ds(start, chunk)
-        here = lax.broadcasted_iota(jnp.int32, (rows.shape[0], chunk), 1) + start
+        width = min(chunk, owned_n - start)
+        cols = pl.ds(start, width)
+        here = lax.broadcasted_iota(jnp.int32, (rows.shape[0], width), 1) + start
         onehot = (rows == here).astype(jnp.bfloat16)
         total = own_ref[:, cols].astype(jnp.float32)
         total += jnp.dot(back, onehot, preferred_element_type=jnp.float32)

time: 60.2 us -> 60.2 us (level)
  no operation moved by 1% of the time
where the time goes in v19:
time: 60.2 us; the launch traced here: 59.8 us
  starting transfers between devices  24.6 us (41%)
  Pallas kernels  16.5 us (27%)
  local copies, waits for them, and re-layouts  9.01 us (15%)
  other arithmetic  3.62 us (6%)
  matrix products  3.05 us (5%)
  waiting for transfers between devices  2.01 us (3%)
  between operations  1.01 us (2%)
    ppermute x10, starting transfers between devices, swap(): return (lax.ppermute(value, axis, pairs), None)  14.4 us
    pallas_call x1, Pallas kernels, local_solve(): pl.pallas_call(solve_kernel, out_shape=(jax.ShapeDtypeStruct((nrhs_here,...  13.1 us
    all_to_all x1, starting transfers between devices, per_device(): held = lax.all_to_all(spread, AXES, 0, 0, tiled=True)  10.2 us
    unnamed x23, local copies, waits for them, and re-layouts  5.62 us
    pallas_call x1, Pallas kernels, finish(): pl.pallas_call(finish_kernel, out_shape=jax.ShapeDtypeStruct(own.shape, j...  3.33 us
    gather x2, local copies, waits for them, and re-layouts, per_device(): outgoing = jnp.take(residual, send_rows, axis=1)  2.49 us
    all_to_all x1, waiting for transfers between devices, per_device(): held = lax.all_to_all(spread, AXES, 0, 0, tiled=True)  1.87 us
    dot_general x1, matrix products, per_device(): jnp.dot(coarse_inverse, rows_of(held), precision=lax.Precision.HIGH, pref...  1.79 us
  transfers between devices with their start and end apart: 11, of which 2 were waited for; matrix products, arithmetic and copies ran while one was open for 6% of the time, Pallas kernels for 22%

profile of v19, /device:TPU:0, one launch (start us, length us, event | category | flops | bytes accessed | tf_op | source)
XLA Modules:
  0.0 59.8 jit_solution(5828773804772314693)
XLA Ops:
  0.0 0.7 %compare_and_fusion = pred[6,128]{1,0:T(8,128)(4,1)S(1)} fusion(s32[6,128]{1,0:T(8,128)} %param.12), kind=kLoop, calls=%fused_computation.30 | loop fusion | flops 4608 | bytes 3840 | tf_op jit(solution)/shard_map/jit(_take)/and | solution.py:199
  0.7 0.7 %fusion.4 = s32[768]{0:T(1024)S(1)} fusion(s32[6,128]{1,0:T(8,128)} %param.12), kind=kLoop, calls=%fused_computation.31 | loop fusion | flops 2304 | bytes 6144 | tf_op jit(solution)/shard_map/jit(_take)/broadcast_in_dim | solution.py:199
  1.4 2.0 %copy.11 = f32[128,4352]{0,1:T(8,128)S(1)} copy(f32[128,4352]{1,0:T(8,128)} %res_ref.1) | data formatting | bytes 4456448 | tf_op args[0]
  3.5 1.6 %gather_fusion = f32[768,128]{1,0:T(8,128)S(1)} fusion(f32[128,4352]{0,1:T(8,128)S(1)} %copy.11, s32[1024]{0:T(1024)S(1)} %pad_clamp_fusion), kind=kCustom, calls=%fused_computation | custom fusion | bytes 789504 | tf_op jit(solution)/shard_map/jit(_take)/gather | solution.py:199
  5.0 0.9 %copy.12 = f32[6,128,128]{1,2,0:T(8,128)} copy(f32[6,128,128]{2,1,0:T(8,128)S(1)} %bitcast.28) | data formatting | bytes 786432 | tf_op jit(solution)/shard_map/jit(_take)/gather | solution.py:199
  6.0 1.0 %select_bitcast_fusion = f32[128,6,128]{2,0,1:T(8,128)S(1)} fusion(f32[6,128,128]{1,2,0:T(8,128)} %copy.12, pred[6,128]{1,0:T(8,128)(4,1)S(1)} %compare_and_fusion), kind=kLoop, calls=%fused_computation.3 | loop fusion | flops 98304 | bytes 787200 | tf_op jit(solution)/shard_map/jit(_take)/select_n | solution.py:199
  7.5 2.6 %collective-permute-start.2 = (f32[128,128]{1,0:T(8,128)S(1)}, f32[128,128]{1,0:T(8,128)S(1)}, u32[]{:S(2)}, u32[]{:S(2)}) collective-permute-start(f32[128,128]{1,0:T(8,128)S(1)} %get-tuple-element.18), channel_id=1, source_target_pairs={{0,2},{4,6},{2,0},{6,4},{1,3},{5,7},{3,1},{7,5},{8,10},{12,14},{10... | collective-permute-start | bytes 196616 | tf_op jit(solution)/shard_map/ppermute | solution.py:134
  10.1 0.7 %collective-permute-start.3 = (f32[128,128]{1,0:T(8,128)S(1)}, f32[128,128]{1,0:T(8,128)S(1)}, u32[]{:S(2)}, u32[]{:S(2)}) collective-permute-start(f32[128,128]{1,0:T(8,128)S(1)} %get-tuple-element.19), channel_id=1, source_target_pairs={{2,4},{4,2},{3,5},{5,3},{10,12},{12,10},{11,13},{13,11},{18,20},{2... | collective-permute-start | bytes 196616 | tf_op jit(solution)/shard_map/ppermute | solution.py:134
  10.8 1.6 %collective-permute-start = (f32[128,128]{1,0:T(8,128)S(1)}, f32[128,128]{1,0:T(8,128)S(1)}, u32[]{:S(2)}, u32[]{:S(2)}) collective-permute-start(f32[128,128]{1,0:T(8,128)S(1)} %get-tuple-element.20), channel_id=1, source_target_pairs={{0,8},{16,24},{8,0},{24,16},{1,9},{17,25},{9,1},{25,17},{2,10},{18... | collective-permute-start | bytes 196616 | tf_op jit(solution)/shard_map/ppermute | solution.py:134
  12.4 0.7 %collective-permute-start.1 = (f32[128,128]{1,0:T(8,128)S(1)}, f32[128,128]{1,0:T(8,128)S(1)}, u32[]{:S(2)}, u32[]{:S(2)}) collective-permute-start(f32[128,128]{1,0:T(8,128)S(1)} %get-tuple-element.21), channel_id=1, source_target_pairs={{8,16},{16,8},{9,17},{17,9},{10,18},{18,10},{11,19},{19,11},{12,20... | collective-permute-start | bytes 196616 | tf_op jit(solution)/shard_map/ppermute | solution.py:134
  13.8 1.3 %fusion.after_ref = f32[40,128]{1,0:T(8,128)S(1)} fusion(f32[128,4352]{1,0:T(8,128)S(1)} %copy-done.1, f32[40,4352]{1,0:T(8,128)S(1)} %copy-done.2, f32[40]{0:T(128)S(1)} %compare_convert_fusion), kind=kOutput, calls=%fused_computation.1 | convolution fusion | flops 133867520 | bytes 2945184 | tf_op jit(solution)/shard_map/dot_general | solution.py:194
  15.3 0.7 %copy-done.5 = f32[128,768]{1,0:T(8,128)} copy-done((f32[128,768]{1,0:T(8,128)}, f32[128,768]{1,0:T(8,128)S(1)}, u32[]{:S(2)}) %copy-start.5) | copy-done | bytes 393240
  16.0 0.9 %broadcast_in_dim.29 = f32[32,40,128]{2,1,0:T(8,128)} broadcast(f32[40,128]{1,0:T(8,128)S(1)} %fusion.after_ref), dimensions={1,2} | broadcast | bytes 675840 | tf_op jit(solution)/shard_map/broadcast_in_dim | solution.py:206
  16.9 10.2 %all-to-all-start = ((f32[32,40,128]{2,1,0:T(8,128)}), f32[32,40,128]{2,1,0:T(8,128)}, u32[]{:S(2)}, u32[]{:S(2)}) async-start(f32[32,40,128]{2,1,0:T(8,128)} %broadcast_in_dim.29), calls=%async_computation | async-start | bytes 1310720 | tf_op jit(solution)/shard_map/all_to_all | solution.py:207
  27.3 1.0 %copy-done.6 = f32[128,768]{1,0:T(8,128)S(1)} copy-done((f32[128,768]{1,0:T(8,128)S(1)}, f32[128,768]{1,0:T(8,128)}, u32[]{:S(2)}) %copy-start.6) | copy-done | bytes 393240
  28.3 13.1 %shard_map.82 = (bf16[128,4352]{1,0:T(8,128)(2,1)S(1)}, bf16[128,768]{1,0:T(8,128)(2,1)S(1)}) custom-call(s32[20]{0:T(128)S(1)} %copy-done.8, f32[128,4352]{1,0:T(8,128)S(1)} %copy-done.1, f32[128,768]{1,0:T(8,128)S(1)} %copy-done.6, bf16[20,256,256]{2,1,0:T(8,128)(2,1)} %inv_ref.1, bf16[19,256,256]{2,1,0:T(8,128)(2,1)} %cpl_ref.1, f32[40,128]{1,0:T(8,128)S(1)} %fusion.after_ref), custom_call_target="tpu_custom_call" | custom-call | tf_op jit(solution)/shard_map/pallas_call | solution.py:61
  41.4 1.0 %copy-done.3 = bf16[128,4352]{1,0:T(8,128)(2,1)} copy-done((bf16[128,4352]{1,0:T(8,128)(2,1)}, bf16[128,4352]{1,0:T(8,128)(2,1)S(1)}, u32[]{:S(2)}) %copy-start.3) | copy-done | bytes 1114136
  42.4 0.7 %copy-done.7 = bf16[128,768]{1,0:T(8,128)(2,1)} copy-done((bf16[128,768]{1,0:T(8,128)(2,1)}, bf16[128,768]{1,0:T(8,128)(2,1)S(1)}, u32[]{:S(2)}) %copy-start.7) | copy-done | bytes 196632
  43.1 1.9 %all-to-all-done = f32[32,40,128]{2,1,0:T(8,128)} async-done(((f32[32,40,128]{2,1,0:T(8,128)}), f32[32,40,128]{2,1,0:T(8,128)}, u32[]{:S(2)}, u32[]{:S(2)}) %all-to-all-start) | async-done | bytes 655392 | tf_op jit(solution)/shard_map/all_to_all | solution.py:207
  45.0 0.9 %slice_select_fusion.1 = (bf16[128,128]{1,0:T(8,128)(2,1)S(1)}, bf16[128,128]{1,0:T(8,128)(2,1)S(1)}, bf16[128,128]{1,0:T(8,128)(2,1)S(1)}, bf16[128,128]{1,0:T(8,128)(2,1)S(1)}, bf16[128,128]{1,0:T(8,128)(2,1)S(1)}) fusion(bf16[128,768]{1,0:T(8,128)(2,1)} %copy-done.7, pred[]{:T(512)S(6)} %eq.21, pred[]{:T(512)S(6)} %eq.20, pred[]{:T(512)S(6)} %eq.19), kind=kLoop, calls=%fused_computation.19 | loop fusion | flops 81920 | bytes 360451 | tf_op jit(solution)/shard_map/jit(_where)/select_n | solution.py:152
  46.7 4.1 %collective-permute-start.8 = (bf16[128,128]{1,0:T(8,128)(2,1)S(1)}, bf16[128,128]{1,0:T(8,128)(2,1)S(1)}, u32[]{:S(2)}, u32[]{:S(2)}) collective-permute-start(bf16[128,128]{1,0:T(8,128)(2,1)S(1)} %get-tuple-element.24), channel_id=1, source_target_pairs={{0,2},{4,6},{2,0},{6,4},{1,3},{5,7},{3,1},{7,5},{8,10},{12,14},{10... | collective-permute-start | bytes 98312 | tf_op jit(solution)/shard_map/ppermute | solution.py:134
  51.5 2.8 %collective-permute-start.6 = (bf16[128,128]{1,0:T(8,128)(2,1)S(1)}, bf16[128,128]{1,0:T(8,128)(2,1)S(1)}, u32[]{:S(2)}, u32[]{:S(2)}) collective-permute-start(bf16[128,128]{1,0:T(8,128)(2,1)S(1)} %get-tuple-element.26), channel_id=1, source_target_pairs={{0,8},{16,24},{8,0},{24,16},{1,9},{17,25},{9,1},{25,17},{2,10},{18... | collective-permute-start | bytes 98312 | tf_op jit(solution)/shard_map/ppermute | solution.py:134
  54.3 1.8 %fusion.5.solved_ref = f32[128,40]{1,0:T(8,128)S(1)} fusion(f32[1280,128]{1,0:T(8,128)} %bitcast.9, f32[40,1280]{1,0:T(8,128)S(1)} %copy-done), kind=kOutput, calls=%fused_computation.34 | convolution fusion | flops 39321600 | bytes 880640 | tf_op jit(solution)/shard_map/dot_general | solution.py:223
  56.4 3.3 %shard_map.83 = f32[128,4352]{1,0:T(8,128)} custom-call(s32[1]{0:T(128)} %copy.30.count_ref, s32[768,1]{1,0:T(8,128)S(1)} %bitcast.27, bf16[128,4352]{1,0:T(8,128)(2,1)S(1)} %copy-done.4, bf16[128,768]{1,0:T(8,128)(2,1)S(1)} %select_dynamic-update-slice_fusion.6.back_ref, f32[128,40]{1,0:T(8,128)S(1)} %fusion.5.solved_ref, f32[40,4352]{1,0:T(8,128)S(1)} %copy-done.2), custom_call_target="tpu_custom_call" | custom-call | tf_op jit(solution)/shard_map/pallas_call | solution.py:115
  (47 shorter events, 2.6 us)
Async XLA Ops:
  0.0 54.3 %copy-start = (f32[40,1280]{1,0:T(8,128)S(1)}, f32[40,1280]{1,0:T(8,128)}, u32[]{:S(2)}) copy-start(f32[40,1280]{1,0:T(8,128)} %param.15) | copy-start | bytes 614404
  3.4 10.3 %copy-start.2 = (f32[40,4352]{1,0:T(8,128)S(1)}, f32[40,4352]{1,0:T(8,128)}, u32[]{:S(2)}) copy-start(f32[40,4352]{1,0:T(8,128)} %vec_ref.1) | copy-start | bytes 2088964
  5.0 8.7 %copy-start.1 = (f32[128,4352]{1,0:T(8,128)S(1)}, f32[128,4352]{1,0:T(8,128)}, u32[]{:S(2)}) copy-start(f32[128,4352]{1,0:T(8,128)} %res_ref.1) | copy-start | bytes 6684676
  7.0 8.2 %collective-permute-start.4 = (f32[128,128]{1,0:T(8,128)S(1)}, f32[128,128]{1,0:T(8,128)S(1)}, u32[]{:S(2)}, u32[]{:S(2)}) collective-permute-start(f32[128,128]{1,0:T(8,128)S(1)} %get-tuple-element.17), channel_id=1, source_target_pairs={{0,1},{1,0},{2,3},{3,2},{4,5},{5,4},{6,7},{7,6},{8,9},{9,8},{10,11... | collective-permute-start | bytes 196616 | tf_op jit(solution)/shard_map/ppermute | solution.py:134
  7.5 7.6 %collective-permute-start.2 = (f32[128,128]{1,0:T(8,128)S(1)}, f32[128,128]{1,0:T(8,128)S(1)}, u32[]{:S(2)}, u32[]{:S(2)}) collective-permute-start(f32[128,128]{1,0:T(8,128)S(1)} %get-tuple-element.18), channel_id=1, source_target_pairs={{0,2},{4,6},{2,0},{6,4},{1,3},{5,7},{3,1},{7,5},{8,10},{12,14},{10... | collective-permute-start | bytes 196616 | tf_op jit(solution)/shard_map/ppermute | solution.py:134
  10.1 5.0 %collective-permute-start.3 = (f32[128,128]{1,0:T(8,128)S(1)}, f32[128,128]{1,0:T(8,128)S(1)}, u32[]{:S(2)}, u32[]{:S(2)}) collective-permute-start(f32[128,128]{1,0:T(8,128)S(1)} %get-tuple-element.19), channel_id=1, source_target_pairs={{2,4},{4,2},{3,5},{5,3},{10,12},{12,10},{11,13},{13,11},{18,20},{2... | collective-permute-start | bytes 196616 | tf_op jit(solution)/shard_map/ppermute | solution.py:134
  10.8 4.3 %collective-permute-start = (f32[128,128]{1,0:T(8,128)S(1)}, f32[128,128]{1,0:T(8,128)S(1)}, u32[]{:S(2)}, u32[]{:S(2)}) collective-permute-start(f32[128,128]{1,0:T(8,128)S(1)} %get-tuple-element.20), channel_id=1, source_target_pairs={{0,8},{16,24},{8,0},{24,16},{1,9},{17,25},{9,1},{25,17},{2,10},{18... | collective-permute-start | bytes 196616 | tf_op jit(solution)/shard_map/ppermute | solution.py:134
  12.4 2.7 %collective-permute-start.1 = (f32[128,128]{1,0:T(8,128)S(1)}, f32[128,128]{1,0:T(8,128)S(1)}, u32[]{:S(2)}, u32[]{:S(2)}) collective-permute-start(f32[128,128]{1,0:T(8,128)S(1)} %get-tuple-element.21), channel_id=1, source_target_pairs={{8,16},{16,8},{9,17},{17,9},{10,18},{18,10},{11,19},{19,11},{12,20... | collective-permute-start | bytes 196616 | tf_op jit(solution)/shard_map/ppermute | solution.py:134
  15.0 12.0 %copy-start.9 = (s32[6,128]{1,0:T(8,128)S(1)}, s32[6,128]{1,0:T(8,128)}, u32[]{:S(2)}) copy-start(s32[6,128]{1,0:T(8,128)} %param.12) | copy-start | bytes 9220
  15.1 12.2 %copy-start.8 = (s32[20]{0:T(128)S(1)}, s32[20]{0:T(128)}, u32[]{:S(2)}) copy-start(s32[20]{0:T(128)} %parent_ref.1) | copy-start | bytes 244
  15.2 0.7 %copy-start.5 = (f32[128,768]{1,0:T(8,128)}, f32[128,768]{1,0:T(8,128)S(1)}, u32[]{:S(2)}) copy-start(f32[128,768]{1,0:T(8,128)S(1)} %select_dynamic-update-slice_fusion.slot_ref) | copy-start | bytes 1179652
  16.9 28.1 %all-to-all-start = ((f32[32,40,128]{2,1,0:T(8,128)}), f32[32,40,128]{2,1,0:T(8,128)}, u32[]{:S(2)}, u32[]{:S(2)}) async-start(f32[32,40,128]{2,1,0:T(8,128)} %broadcast_in_dim.29), calls=%async_computation | async-start | bytes 1310720 | tf_op jit(solution)/shard_map/all_to_all | solution.py:207
  27.3 1.0 %copy-start.6 = (f32[128,768]{1,0:T(8,128)S(1)}, f32[128,768]{1,0:T(8,128)}, u32[]{:S(2)}) copy-start(f32[128,768]{1,0:T(8,128)} %copy-done.5) | copy-start | bytes 1179652
  41.4 1.0 %copy-start.3 = (bf16[128,4352]{1,0:T(8,128)(2,1)}, bf16[128,4352]{1,0:T(8,128)(2,1)S(1)}, u32[]{:S(2)}) copy-start(bf16[128,4352]{1,0:T(8,128)(2,1)S(1)} %get-tuple-element.13.own_ref) | copy-start | bytes 3342340
  42.4 0.7 %copy-start.7 = (bf16[128,768]{1,0:T(8,128)(2,1)}, bf16[128,768]{1,0:T(8,128)(2,1)S(1)}, u32[]{:S(2)}) copy-start(bf16[128,768]{1,0:T(8,128)(2,1)S(1)} %get-tuple-element.15) | copy-start | bytes 589828
  45.0 11.4 %copy-start.4 = (bf16[128,4352]{1,0:T(8,128)(2,1)S(1)}, bf16[128,4352]{1,0:T(8,128)(2,1)}, u32[]{:S(2)}) copy-start(bf16[128,4352]{1,0:T(8,128)(2,1)} %copy-done.3) | copy-start | bytes 3342340
  45.9 10.4 %collective-permute-start.9 = (bf16[128,128]{1,0:T(8,128)(2,1)S(1)}, bf16[128,128]{1,0:T(8,128)(2,1)S(1)}, u32[]{:S(2)}, u32[]{:S(2)}) collective-permute-start(bf16[128,128]{1,0:T(8,128)(2,1)S(1)} %get-tuple-element.22), channel_id=1, source_target_pairs={{0,1},{1,0},{2,3},{3,2},{4,5},{5,4},{6,7},{7,6},{8,9},{9,8},{10,11... | collective-permute-start | bytes 98312 | tf_op jit(solution)/shard_map/ppermute | solution.py:134
  46.1 10.2 %collective-permute-start.7 = (bf16[128,128]{1,0:T(8,128)(2,1)S(1)}, bf16[128,128]{1,0:T(8,128)(2,1)S(1)}, u32[]{:S(2)}, u32[]{:S(2)}) collective-permute-start(bf16[128,128]{1,0:T(8,128)(2,1)S(1)} %get-tuple-element.23), channel_id=1, source_target_pairs={{2,4},{4,2},{3,5},{5,3},{10,12},{12,10},{11,13},{13,11},{18,20},{2... | collective-permute-start | bytes 98312 | tf_op jit(solution)/shard_map/ppermute | solution.py:134
  46.7 9.6 %collective-permute-start.8 = (bf16[128,128]{1,0:T(8,128)(2,1)S(1)}, bf16[128,128]{1,0:T(8,128)(2,1)S(1)}, u32[]{:S(2)}, u32[]{:S(2)}) collective-permute-start(bf16[128,128]{1,0:T(8,128)(2,1)S(1)} %get-tuple-element.24), channel_id=1, source_target_pairs={{0,2},{4,6},{2,0},{6,4},{1,3},{5,7},{3,1},{7,5},{8,10},{12,14},{10... | collective-permute-start | bytes 98312 | tf_op jit(solution)/shard_map/ppermute | solution.py:134
  50.9 5.3 %collective-permute-start.5 = (bf16[128,128]{1,0:T(8,128)(2,1)S(1)}, bf16[128,128]{1,0:T(8,128)(2,1)S(1)}, u32[]{:S(2)}, u32[]{:S(2)}) collective-permute-start(bf16[128,128]{1,0:T(8,128)(2,1)S(1)} %get-tuple-element.25), channel_id=1, source_target_pairs={{8,16},{16,8},{9,17},{17,9},{10,18},{18,10},{11,19},{19,11},{12,20... | collective-permute-start | bytes 98312 | tf_op jit(solution)/shard_map/ppermute | solution.py:134
  51.5 4.7 %collective-permute-start.6 = (bf16[128,128]{1,0:T(8,128)(2,1)S(1)}, bf16[128,128]{1,0:T(8,128)(2,1)S(1)}, u32[]{:S(2)}, u32[]{:S(2)}) collective-permute-start(bf16[128,128]{1,0:T(8,128)(2,1)S(1)} %get-tuple-element.26), channel_id=1, source_target_pairs={{0,8},{16,24},{8,0},{24,16},{1,9},{17,25},{9,1},{25,17},{2,10},{18... | collective-permute-start | bytes 98312 | tf_op jit(solution)/shard_map/ppermute | solution.py:134

commit v20 on v19

--- a/solution.py
+++ b/solution.py
@@ -27,6 +27,7 @@
         return jnp.clip(parent_ref[b], 0, blocks_n - 1)
 
     for b in range(blocks_n):
+        carry_ref[b] = jnp.zeros(carry_ref.shape[1:], carry_ref.dtype)
         ref, cols = columns(b)
         x = ref[:, cols]
         if b == 0:
@@ -40,7 +41,6 @@
             lower, inv_ref[b], NT, preferred_element_type=jnp.float32
         ).astype(jnp.bfloat16)
 
-    carry_ref[...] = jnp.zeros(carry_ref.shape, carry_ref.dtype)
     for b in reversed(range(blocks_n)):
         upper = (y_ref[b].astype(jnp.float32) - carry_ref[b]).astype(jnp.bfloat16)
         result = jnp.dot(upper, inv_ref[b], preferred_element_type=jnp.float32).astype(jnp.bfloat16)

time: 60.2 us -> 60.2 us (level)
  no operation moved by 1% of the time
where the time goes in v20:
time: 60.2 us; the launch traced here: 59.8 us
  starting transfers between devices  24.6 us (41%)
  Pallas kernels  16.5 us (27%)
  local copies, waits for them, and re-layouts  9 us (15%)
  other arithmetic  3.62 us (6%)
  matrix products  3.06 us (5%)
  waiting for transfers between devices  1.99 us (3%)
  between operations  1.01 us (2%)
    ppermute x10, starting transfers between devices, swap(): return (lax.ppermute(value, axis, pairs), None)  14.4 us
    pallas_call x1, Pallas kernels, local_solve(): pl.pallas_call(solve_kernel, out_shape=(jax.ShapeDtypeStruct((nrhs_here,...  13.1 us
    all_to_all x1, starting transfers between devices, per_device(): held = lax.all_to_all(spread, AXES, 0, 0, tiled=True)  10.2 us
    unnamed x23, local copies, waits for them, and re-layouts  5.62 us
    pallas_call x1, Pallas kernels, finish(): pl.pallas_call(finish_kernel, out_shape=jax.ShapeDtypeStruct(own.shape, j...  3.33 us
    gather x2, local copies, waits for them, and re-layouts, per_device(): outgoing = jnp.take(residual, send_rows, axis=1)  2.49 us
    all_to_all x1, waiting for transfers between devices, per_device(): held = lax.all_to_all(spread, AXES, 0, 0, tiled=True)  1.86 us
    dot_general x1, matrix products, per_device(): jnp.dot(coarse_inverse, rows_of(held), precision=lax.Precision.HIGH, pref...  1.79 us
  transfers between devices with their start and end apart: 11, of which 2 were waited for; matrix products, arithmetic and copies ran while one was open for 6% of the time, Pallas kernels for 22%

profile of v20, /device:TPU:0, one launch (start us, length us, event | category | flops | bytes accessed | tf_op | source)
XLA Modules:
  0.0 59.8 jit_solution(5828773804772314693)
XLA Ops:
  0.0 0.7 %compare_and_fusion = pred[6,128]{1,0:T(8,128)(4,1)S(1)} fusion(s32[6,128]{1,0:T(8,128)} %param.12), kind=kLoop, calls=%fused_computation.30 | loop fusion | flops 4608 | bytes 3840 | tf_op jit(solution)/shard_map/jit(_take)/and | solution.py:199
  0.7 0.7 %fusion.4 = s32[768]{0:T(1024)S(1)} fusion(s32[6,128]{1,0:T(8,128)} %param.12), kind=kLoop, calls=%fused_computation.31 | loop fusion | flops 2304 | bytes 6144 | tf_op jit(solution)/shard_map/jit(_take)/broadcast_in_dim | solution.py:199
  1.4 2.0 %copy.11 = f32[128,4352]{0,1:T(8,128)S(1)} copy(f32[128,4352]{1,0:T(8,128)} %res_ref.1) | data formatting | bytes 4456448 | tf_op args[0]
  3.5 1.6 %gather_fusion = f32[768,128]{1,0:T(8,128)S(1)} fusion(f32[128,4352]{0,1:T(8,128)S(1)} %copy.11, s32[1024]{0:T(1024)S(1)} %pad_clamp_fusion), kind=kCustom, calls=%fused_computation | custom fusion | bytes 789504 | tf_op jit(solution)/shard_map/jit(_take)/gather | solution.py:199
  5.0 0.9 %copy.12 = f32[6,128,128]{1,2,0:T(8,128)} copy(f32[6,128,128]{2,1,0:T(8,128)S(1)} %bitcast.28) | data formatting | bytes 786432 | tf_op jit(solution)/shard_map/jit(_take)/gather | solution.py:199
  6.0 1.0 %select_bitcast_fusion = f32[128,6,128]{2,0,1:T(8,128)S(1)} fusion(f32[6,128,128]{1,2,0:T(8,128)} %copy.12, pred[6,128]{1,0:T(8,128)(4,1)S(1)} %compare_and_fusion), kind=kLoop, calls=%fused_computation.3 | loop fusion | flops 98304 | bytes 787200 | tf_op jit(solution)/shard_map/jit(_take)/select_n | solution.py:199
  7.5 2.6 %collective-permute-start.2 = (f32[128,128]{1,0:T(8,128)S(1)}, f32[128,128]{1,0:T(8,128)S(1)}, u32[]{:S(2)}, u32[]{:S(2)}) collective-permute-start(f32[128,128]{1,0:T(8,128)S(1)} %get-tuple-element.18), channel_id=1, source_target_pairs={{0,2},{4,6},{2,0},{6,4},{1,3},{5,7},{3,1},{7,5},{8,10},{12,14},{10... | collective-permute-start | bytes 196616 | tf_op jit(solution)/shard_map/ppermute | solution.py:134
  10.1 0.7 %collective-permute-start.3 = (f32[128,128]{1,0:T(8,128)S(1)}, f32[128,128]{1,0:T(8,128)S(1)}, u32[]{:S(2)}, u32[]{:S(2)}) collective-permute-start(f32[128,128]{1,0:T(8,128)S(1)} %get-tuple-element.19), channel_id=1, source_target_pairs={{2,4},{4,2},{3,5},{5,3},{10,12},{12,10},{11,13},{13,11},{18,20},{2... | collective-permute-start | bytes 196616 | tf_op jit(solution)/shard_map/ppermute | solution.py:134
  10.8 1.6 %collective-permute-start = (f32[128,128]{1,0:T(8,128)S(1)}, f32[128,128]{1,0:T(8,128)S(1)}, u32[]{:S(2)}, u32[]{:S(2)}) collective-permute-start(f32[128,128]{1,0:T(8,128)S(1)} %get-tuple-element.20), channel_id=1, source_target_pairs={{0,8},{16,24},{8,0},{24,16},{1,9},{17,25},{9,1},{25,17},{2,10},{18... | collective-permute-start | bytes 196616 | tf_op jit(solution)/shard_map/ppermute | solution.py:134
  12.4 0.7 %collective-permute-start.1 = (f32[128,128]{1,0:T(8,128)S(1)}, f32[128,128]{1,0:T(8,128)S(1)}, u32[]{:S(2)}, u32[]{:S(2)}) collective-permute-start(f32[128,128]{1,0:T(8,128)S(1)} %get-tuple-element.21), channel_id=1, source_target_pairs={{8,16},{16,8},{9,17},{17,9},{10,18},{18,10},{11,19},{19,11},{12,20... | collective-permute-start | bytes 196616 | tf_op jit(solution)/shard_map/ppermute | solution.py:134
  13.8 1.3 %fusion.after_ref = f32[40,128]{1,0:T(8,128)S(1)} fusion(f32[128,4352]{1,0:T(8,128)S(1)} %copy-done.1, f32[40,4352]{1,0:T(8,128)S(1)} %copy-done.2, f32[40]{0:T(128)S(1)} %compare_convert_fusion), kind=kOutput, calls=%fused_computation.1 | convolution fusion | flops 133867520 | bytes 2945184 | tf_op jit(solution)/shard_map/dot_general | solution.py:194
  15.3 0.7 %copy-done.5 = f32[128,768]{1,0:T(8,128)} copy-done((f32[128,768]{1,0:T(8,128)}, f32[128,768]{1,0:T(8,128)S(1)}, u32[]{:S(2)}) %copy-start.5) | copy-done | bytes 393240
  16.0 0.9 %broadcast_in_dim.29 = f32[32,40,128]{2,1,0:T(8,128)} broadcast(f32[40,128]{1,0:T(8,128)S(1)} %fusion.after_ref), dimensions={1,2} | broadcast | bytes 675840 | tf_op jit(solution)/shard_map/broadcast_in_dim | solution.py:206
  16.9 10.2 %all-to-all-start = ((f32[32,40,128]{2,1,0:T(8,128)}), f32[32,40,128]{2,1,0:T(8,128)}, u32[]{:S(2)}, u32[]{:S(2)}) async-start(f32[32,40,128]{2,1,0:T(8,128)} %broadcast_in_dim.29), calls=%async_computation | async-start | bytes 1310720 | tf_op jit(solution)/shard_map/all_to_all | solution.py:207
  27.3 1.0 %copy-done.6 = f32[128,768]{1,0:T(8,128)S(1)} copy-done((f32[128,768]{1,0:T(8,128)S(1)}, f32[128,768]{1,0:T(8,128)}, u32[]{:S(2)}) %copy-start.6) | copy-done | bytes 393240
  28.3 13.1 %shard_map.82 = (bf16[128,4352]{1,0:T(8,128)(2,1)S(1)}, bf16[128,768]{1,0:T(8,128)(2,1)S(1)}) custom-call(s32[20]{0:T(128)S(1)} %copy-done.8, f32[128,4352]{1,0:T(8,128)S(1)} %copy-done.1, f32[128,768]{1,0:T(8,128)S(1)} %copy-done.6, bf16[20,256,256]{2,1,0:T(8,128)(2,1)} %inv_ref.1, bf16[19,256,256]{2,1,0:T(8,128)(2,1)} %cpl_ref.1, f32[40,128]{1,0:T(8,128)S(1)} %fusion.after_ref), custom_call_target="tpu_custom_call" | custom-call | tf_op jit(solution)/shard_map/pallas_call | solution.py:61
  41.5 1.0 %copy-done.3 = bf16[128,4352]{1,0:T(8,128)(2,1)} copy-done((bf16[128,4352]{1,0:T(8,128)(2,1)}, bf16[128,4352]{1,0:T(8,128)(2,1)S(1)}, u32[]{:S(2)}) %copy-start.3) | copy-done | bytes 1114136
  42.4 0.7 %copy-done.7 = bf16[128,768]{1,0:T(8,128)(2,1)} copy-done((bf16[128,768]{1,0:T(8,128)(2,1)}, bf16[128,768]{1,0:T(8,128)(2,1)S(1)}, u32[]{:S(2)}) %copy-start.7) | copy-done | bytes 196632
  43.1 1.9 %all-to-all-done = f32[32,40,128]{2,1,0:T(8,128)} async-done(((f32[32,40,128]{2,1,0:T(8,128)}), f32[32,40,128]{2,1,0:T(8,128)}, u32[]{:S(2)}, u32[]{:S(2)}) %all-to-all-start) | async-done | bytes 655392 | tf_op jit(solution)/shard_map/all_to_all | solution.py:207
  45.0 0.9 %slice_select_fusion.1 = (bf16[128,128]{1,0:T(8,128)(2,1)S(1)}, bf16[128,128]{1,0:T(8,128)(2,1)S(1)}, bf16[128,128]{1,0:T(8,128)(2,1)S(1)}, bf16[128,128]{1,0:T(8,128)(2,1)S(1)}, bf16[128,128]{1,0:T(8,128)(2,1)S(1)}) fusion(bf16[128,768]{1,0:T(8,128)(2,1)} %copy-done.7, pred[]{:T(512)S(6)} %eq.21, pred[]{:T(512)S(6)} %eq.20, pred[]{:T(512)S(6)} %eq.19), kind=kLoop, calls=%fused_computation.19 | loop fusion | flops 81920 | bytes 360451 | tf_op jit(solution)/shard_map/jit(_where)/select_n | solution.py:152
  46.7 4.1 %collective-permute-start.8 = (bf16[128,128]{1,0:T(8,128)(2,1)S(1)}, bf16[128,128]{1,0:T(8,128)(2,1)S(1)}, u32[]{:S(2)}, u32[]{:S(2)}) collective-permute-start(bf16[128,128]{1,0:T(8,128)(2,1)S(1)} %get-tuple-element.24), channel_id=1, source_target_pairs={{0,2},{4,6},{2,0},{6,4},{1,3},{5,7},{3,1},{7,5},{8,10},{12,14},{10... | collective-permute-start | bytes 98312 | tf_op jit(solution)/shard_map/ppermute | solution.py:134
  51.5 2.8 %collective-permute-start.6 = (bf16[128,128]{1,0:T(8,128)(2,1)S(1)}, bf16[128,128]{1,0:T(8,128)(2,1)S(1)}, u32[]{:S(2)}, u32[]{:S(2)}) collective-permute-start(bf16[128,128]{1,0:T(8,128)(2,1)S(1)} %get-tuple-element.26), channel_id=1, source_target_pairs={{0,8},{16,24},{8,0},{24,16},{1,9},{17,25},{9,1},{25,17},{2,10},{18... | collective-permute-start | bytes 98312 | tf_op jit(solution)/shard_map/ppermute | solution.py:134
  54.4 1.8 %fusion.5.solved_ref = f32[128,40]{1,0:T(8,128)S(1)} fusion(f32[1280,128]{1,0:T(8,128)} %bitcast.9, f32[40,1280]{1,0:T(8,128)S(1)} %copy-done), kind=kOutput, calls=%fused_computation.34 | convolution fusion | flops 39321600 | bytes 880640 | tf_op jit(solution)/shard_map/dot_general | solution.py:223
  56.4 3.3 %shard_map.83 = f32[128,4352]{1,0:T(8,128)} custom-call(s32[1]{0:T(128)} %copy.30.count_ref, s32[768,1]{1,0:T(8,128)S(1)} %bitcast.27, bf16[128,4352]{1,0:T(8,128)(2,1)S(1)} %copy-done.4, bf16[128,768]{1,0:T(8,128)(2,1)S(1)} %select_dynamic-update-slice_fusion.6.back_ref, f32[128,40]{1,0:T(8,128)S(1)} %fusion.5.solved_ref, f32[40,4352]{1,0:T(8,128)S(1)} %copy-done.2), custom_call_target="tpu_custom_call" | custom-call | tf_op jit(solution)/shard_map/pallas_call | solution.py:115
  (47 shorter events, 2.6 us)
Async XLA Ops:
  0.0 54.4 %copy-start = (f32[40,1280]{1,0:T(8,128)S(1)}, f32[40,1280]{1,0:T(8,128)}, u32[]{:S(2)}) copy-start(f32[40,1280]{1,0:T(8,128)} %param.15) | copy-start | bytes 614404
  3.4 10.3 %copy-start.2 = (f32[40,4352]{1,0:T(8,128)S(1)}, f32[40,4352]{1,0:T(8,128)}, u32[]{:S(2)}) copy-start(f32[40,4352]{1,0:T(8,128)} %vec_ref.1) | copy-start | bytes 2088964
  5.0 8.7 %copy-start.1 = (f32[128,4352]{1,0:T(8,128)S(1)}, f32[128,4352]{1,0:T(8,128)}, u32[]{:S(2)}) copy-start(f32[128,4352]{1,0:T(8,128)} %res_ref.1) | copy-start | bytes 6684676
  7.0 8.2 %collective-permute-start.4 = (f32[128,128]{1,0:T(8,128)S(1)}, f32[128,128]{1,0:T(8,128)S(1)}, u32[]{:S(2)}, u32[]{:S(2)}) collective-permute-start(f32[128,128]{1,0:T(8,128)S(1)} %get-tuple-element.17), channel_id=1, source_target_pairs={{0,1},{1,0},{2,3},{3,2},{4,5},{5,4},{6,7},{7,6},{8,9},{9,8},{10,11... | collective-permute-start | bytes 196616 | tf_op jit(solution)/shard_map/ppermute | solution.py:134
  7.5 7.6 %collective-permute-start.2 = (f32[128,128]{1,0:T(8,128)S(1)}, f32[128,128]{1,0:T(8,128)S(1)}, u32[]{:S(2)}, u32[]{:S(2)}) collective-permute-start(f32[128,128]{1,0:T(8,128)S(1)} %get-tuple-element.18), channel_id=1, source_target_pairs={{0,2},{4,6},{2,0},{6,4},{1,3},{5,7},{3,1},{7,5},{8,10},{12,14},{10... | collective-permute-start | bytes 196616 | tf_op jit(solution)/shard_map/ppermute | solution.py:134
  10.1 5.0 %collective-permute-start.3 = (f32[128,128]{1,0:T(8,128)S(1)}, f32[128,128]{1,0:T(8,128)S(1)}, u32[]{:S(2)}, u32[]{:S(2)}) collective-permute-start(f32[128,128]{1,0:T(8,128)S(1)} %get-tuple-element.19), channel_id=1, source_target_pairs={{2,4},{4,2},{3,5},{5,3},{10,12},{12,10},{11,13},{13,11},{18,20},{2... | collective-permute-start | bytes 196616 | tf_op jit(solution)/shard_map/ppermute | solution.py:134
  10.8 4.3 %collective-permute-start = (f32[128,128]{1,0:T(8,128)S(1)}, f32[128,128]{1,0:T(8,128)S(1)}, u32[]{:S(2)}, u32[]{:S(2)}) collective-permute-start(f32[128,128]{1,0:T(8,128)S(1)} %get-tuple-element.20), channel_id=1, source_target_pairs={{0,8},{16,24},{8,0},{24,16},{1,9},{17,25},{9,1},{25,17},{2,10},{18... | collective-permute-start | bytes 196616 | tf_op jit(solution)/shard_map/ppermute | solution.py:134
  12.4 2.7 %collective-permute-start.1 = (f32[128,128]{1,0:T(8,128)S(1)}, f32[128,128]{1,0:T(8,128)S(1)}, u32[]{:S(2)}, u32[]{:S(2)}) collective-permute-start(f32[128,128]{1,0:T(8,128)S(1)} %get-tuple-element.21), channel_id=1, source_target_pairs={{8,16},{16,8},{9,17},{17,9},{10,18},{18,10},{11,19},{19,11},{12,20... | collective-permute-start | bytes 196616 | tf_op jit(solution)/shard_map/ppermute | solution.py:134
  15.1 12.0 %copy-start.9 = (s32[6,128]{1,0:T(8,128)S(1)}, s32[6,128]{1,0:T(8,128)}, u32[]{:S(2)}) copy-start(s32[6,128]{1,0:T(8,128)} %param.12) | copy-start | bytes 9220
  15.1 12.2 %copy-start.8 = (s32[20]{0:T(128)S(1)}, s32[20]{0:T(128)}, u32[]{:S(2)}) copy-start(s32[20]{0:T(128)} %parent_ref.1) | copy-start | bytes 244
  15.2 0.7 %copy-start.5 = (f32[128,768]{1,0:T(8,128)}, f32[128,768]{1,0:T(8,128)S(1)}, u32[]{:S(2)}) copy-start(f32[128,768]{1,0:T(8,128)S(1)} %select_dynamic-update-slice_fusion.slot_ref) | copy-start | bytes 1179652
  16.9 28.1 %all-to-all-start = ((f32[32,40,128]{2,1,0:T(8,128)}), f32[32,40,128]{2,1,0:T(8,128)}, u32[]{:S(2)}, u32[]{:S(2)}) async-start(f32[32,40,128]{2,1,0:T(8,128)} %broadcast_in_dim.29), calls=%async_computation | async-start | bytes 1310720 | tf_op jit(solution)/shard_map/all_to_all | solution.py:207
  27.3 1.0 %copy-start.6 = (f32[128,768]{1,0:T(8,128)S(1)}, f32[128,768]{1,0:T(8,128)}, u32[]{:S(2)}) copy-start(f32[128,768]{1,0:T(8,128)} %copy-done.5) | copy-start | bytes 1179652
  41.4 1.0 %copy-start.3 = (bf16[128,4352]{1,0:T(8,128)(2,1)}, bf16[128,4352]{1,0:T(8,128)(2,1)S(1)}, u32[]{:S(2)}) copy-start(bf16[128,4352]{1,0:T(8,128)(2,1)S(1)} %get-tuple-element.13.own_ref) | copy-start | bytes 3342340
  42.4 0.7 %copy-start.7 = (bf16[128,768]{1,0:T(8,128)(2,1)}, bf16[128,768]{1,0:T(8,128)(2,1)S(1)}, u32[]{:S(2)}) copy-start(bf16[128,768]{1,0:T(8,128)(2,1)S(1)} %get-tuple-element.15) | copy-start | bytes 589828
  45.0 11.5 %copy-start.4 = (bf16[128,4352]{1,0:T(8,128)(2,1)S(1)}, bf16[128,4352]{1,0:T(8,128)(2,1)}, u32[]{:S(2)}) copy-start(bf16[128,4352]{1,0:T(8,128)(2,1)} %copy-done.3) | copy-start | bytes 3342340
  45.9 10.4 %collective-permute-start.9 = (bf16[128,128]{1,0:T(8,128)(2,1)S(1)}, bf16[128,128]{1,0:T(8,128)(2,1)S(1)}, u32[]{:S(2)}, u32[]{:S(2)}) collective-permute-start(bf16[128,128]{1,0:T(8,128)(2,1)S(1)} %get-tuple-element.22), channel_id=1, source_target_pairs={{0,1},{1,0},{2,3},{3,2},{4,5},{5,4},{6,7},{7,6},{8,9},{9,8},{10,11... | collective-permute-start | bytes 98312 | tf_op jit(solution)/shard_map/ppermute | solution.py:134
  46.1 10.2 %collective-permute-start.7 = (bf16[128,128]{1,0:T(8,128)(2,1)S(1)}, bf16[128,128]{1,0:T(8,128)(2,1)S(1)}, u32[]{:S(2)}, u32[]{:S(2)}) collective-permute-start(bf16[128,128]{1,0:T(8,128)(2,1)S(1)} %get-tuple-element.23), channel_id=1, source_target_pairs={{2,4},{4,2},{3,5},{5,3},{10,12},{12,10},{11,13},{13,11},{18,20},{2... | collective-permute-start | bytes 98312 | tf_op jit(solution)/shard_map/ppermute | solution.py:134
  46.7 9.6 %collective-permute-start.8 = (bf16[128,128]{1,0:T(8,128)(2,1)S(1)}, bf16[128,128]{1,0:T(8,128)(2,1)S(1)}, u32[]{:S(2)}, u32[]{:S(2)}) collective-permute-start(bf16[128,128]{1,0:T(8,128)(2,1)S(1)} %get-tuple-element.24), channel_id=1, source_target_pairs={{0,2},{4,6},{2,0},{6,4},{1,3},{5,7},{3,1},{7,5},{8,10},{12,14},{10... | collective-permute-start | bytes 98312 | tf_op jit(solution)/shard_map/ppermute | solution.py:134
  50.9 5.3 %collective-permute-start.5 = (bf16[128,128]{1,0:T(8,128)(2,1)S(1)}, bf16[128,128]{1,0:T(8,128)(2,1)S(1)}, u32[]{:S(2)}, u32[]{:S(2)}) collective-permute-start(bf16[128,128]{1,0:T(8,128)(2,1)S(1)} %get-tuple-element.25), channel_id=1, source_target_pairs={{8,16},{16,8},{9,17},{17,9},{10,18},{18,10},{11,19},{19,11},{12,20... | collective-permute-start | bytes 98312 | tf_op jit(solution)/shard_map/ppermute | solution.py:134
  51.5 4.7 %collective-permute-start.6 = (bf16[128,128]{1,0:T(8,128)(2,1)S(1)}, bf16[128,128]{1,0:T(8,128)(2,1)S(1)}, u32[]{:S(2)}, u32[]{:S(2)}) collective-permute-start(bf16[128,128]{1,0:T(8,128)(2,1)S(1)} %get-tuple-element.26), channel_id=1, source_target_pairs={{0,8},{16,24},{8,0},{24,16},{1,9},{17,25},{9,1},{25,17},{2,10},{18... | collective-permute-start | bytes 98312 | tf_op jit(solution)/shard_map/ppermute | solution.py:134

commit v21 on v19

--- a/solution.py
+++ b/solution.py
@@ -28,7 +28,10 @@
 
     for b in range(blocks_n):
         ref, cols = columns(b)
-        x = ref[:, cols]
+        if b < owned_blocks:
+            x = ref[:, cols]
+        else:
+            x = ref[cols, :].T
         if b == 0:
             lower = x.astype(jnp.bfloat16)
         else:
@@ -62,7 +65,7 @@
         solve_kernel,
         out_shape=(
             jax.ShapeDtypeStruct((nrhs_here, owned_n), jnp.bfloat16),
-            jax.ShapeDtypeStruct(slots.shape, jnp.bfloat16),
+            jax.ShapeDtypeStruct(slots.shape[::-1], jnp.bfloat16),
         ),
         in_specs=[
             pl.BlockSpec(memory_space=pltpu.SMEM),
@@ -196,12 +199,12 @@
     )
     total_dev = coarse_inverse.shape[1] // kmax_here
 
-    outgoing = jnp.take(residual, send_rows, axis=1)
+    outgoing = jnp.take(residual.T, send_rows, axis=0)
     incoming = []
     for axis_pos, axis in enumerate(AXES):
-        low, high, _ = halo_out(outgoing[:, 2 * axis_pos], outgoing[:, 2 * axis_pos + 1], axis)
+        low, high, _ = halo_out(outgoing[2 * axis_pos], outgoing[2 * axis_pos + 1], axis)
         incoming += [low, high]
-    slots = jnp.concatenate(incoming, axis=1)
+    slots = jnp.concatenate(incoming, axis=0)
     slots, coeffs_t = lax.optimization_barrier((slots, coeffs_t))
     spread = jnp.broadcast_to(coeffs_t[None], (total_dev,) + coeffs_t.shape)
     held = lax.all_to_all(spread, AXES, 0, 0, tiled=True)

time: 60.2 us -> 61.2 us (1.017)
  local copies, waits for them, and re-layouts: 9.01 us -> 10.8 us
  other arithmetic: 3.62 us -> 2.76 us
    unnamed x23, local copies, waits for them, and re-layouts: 5.62 us -> 6.61 us
    select_n x1, other arithmetic: 1.02 us -> 0.17 us  [per_device(): outgoing = jnp.take(residual.T, send_rows, axis=0)]
    gather x2 -> x1, local copies, waits for them, and re-layouts: 2.49 us -> 3.34 us  [per_device(): outgoing = jnp.take(residual.T, send_rows, axis=0)]
where the time goes in v21:
time: 61.2 us; the launch traced here: 60.7 us
  starting transfers between devices  24.6 us (40%)
  Pallas kernels  16.5 us (27%)
  local copies, waits for them, and re-layouts  10.8 us (18%)
  matrix products  3.06 us (5%)
  other arithmetic  2.76 us (5%)
  waiting for transfers between devices  1.99 us (3%)
  between operations  0.99 us (2%)
    ppermute x10, starting transfers between devices, swap(): return (lax.ppermute(value, axis, pairs), None)  14.4 us
    pallas_call x1, Pallas kernels, local_solve(): pl.pallas_call(solve_kernel, out_shape=(jax.ShapeDtypeStruct((nrhs_here,...  13.1 us
    all_to_all x1, starting transfers between devices, per_device(): held = lax.all_to_all(spread, AXES, 0, 0, tiled=True)  10.2 us
    unnamed x23, local copies, waits for them, and re-layouts  6.61 us
    gather x1, local copies, waits for them, and re-layouts, per_device(): outgoing = jnp.take(residual.T, send_rows, axis=0)  3.34 us
    pallas_call x1, Pallas kernels, finish(): pl.pallas_call(finish_kernel, out_shape=jax.ShapeDtypeStruct(own.shape, j...  3.33 us
    all_to_all x1, waiting for transfers between devices, per_device(): held = lax.all_to_all(spread, AXES, 0, 0, tiled=True)  1.85 us
    dot_general x1, matrix products, per_device(): jnp.dot(coarse_inverse, rows_of(held), precision=lax.Precision.HIGH, pref...  1.79 us
  transfers between devices with their start and end apart: 11, of which 2 were waited for; matrix products, arithmetic and copies ran while one was open for 6% of the time, Pallas kernels for 22%

profile of v21, /device:TPU:0, one launch (start us, length us, event | category | flops | bytes accessed | tf_op | source)
XLA Modules:
  0.0 60.7 jit_solution(14084726513836123563)
XLA Ops:
  0.0 0.7 %compare_and_fusion = pred[6,128]{1,0:T(8,128)(4,1)S(1)} fusion(s32[6,128]{1,0:T(8,128)} %param.12), kind=kLoop, calls=%fused_computation.30 | loop fusion | flops 4608 | bytes 3840 | tf_op jit(solution)/shard_map/jit(_take)/and | solution.py:202
  0.7 0.7 %fusion.4 = s32[768]{0:T(1024)S(1)} fusion(s32[6,128]{1,0:T(8,128)} %param.12), kind=kLoop, calls=%fused_computation.31 | loop fusion | flops 2304 | bytes 6144 | tf_op jit(solution)/shard_map/jit(_take)/broadcast_in_dim | solution.py:202
  1.4 3.0 %copy.11 = f32[128,4352]{0,1:T(8,128)} copy(f32[128,4352]{1,0:T(8,128)} %res_ref.1) | data formatting | bytes 4456448 | tf_op args[0]
  4.4 3.3 %gather_fusion = f32[768,128]{1,0:T(8,128)S(1)} fusion(f32[4352,128]{1,0:T(8,128)} %bitcast.27, s32[1024]{0:T(1024)S(1)} %pad_clamp_fusion), kind=kCustom, calls=%fused_computation | custom fusion | bytes 789504 | tf_op jit(solution)/shard_map/jit(_take)/gather | solution.py:202
  8.5 2.6 %collective-permute-start.2 = (f32[128,128]{1,0:T(8,128)S(1)}, f32[128,128]{1,0:T(8,128)S(1)}, u32[]{:S(2)}, u32[]{:S(2)}) collective-permute-start(f32[128,128]{1,0:T(8,128)S(1)} %get-tuple-element.18), channel_id=1, source_target_pairs={{0,2},{4,6},{2,0},{6,4},{1,3},{5,7},{3,1},{7,5},{8,10},{12,14},{10... | collective-permute-start | bytes 196616 | tf_op jit(solution)/shard_map/ppermute | solution.py:137
  11.1 0.7 %collective-permute-start.3 = (f32[128,128]{1,0:T(8,128)S(1)}, f32[128,128]{1,0:T(8,128)S(1)}, u32[]{:S(2)}, u32[]{:S(2)}) collective-permute-start(f32[128,128]{1,0:T(8,128)S(1)} %get-tuple-element.19), channel_id=1, source_target_pairs={{2,4},{4,2},{3,5},{5,3},{10,12},{12,10},{11,13},{13,11},{18,20},{2... | collective-permute-start | bytes 196616 | tf_op jit(solution)/shard_map/ppermute | solution.py:137
  11.7 1.6 %collective-permute-start = (f32[128,128]{1,0:T(8,128)S(1)}, f32[128,128]{1,0:T(8,128)S(1)}, u32[]{:S(2)}, u32[]{:S(2)}) collective-permute-start(f32[128,128]{1,0:T(8,128)S(1)} %get-tuple-element.20), channel_id=1, source_target_pairs={{0,8},{16,24},{8,0},{24,16},{1,9},{17,25},{9,1},{25,17},{2,10},{18... | collective-permute-start | bytes 196616 | tf_op jit(solution)/shard_map/ppermute | solution.py:137
  13.4 0.7 %collective-permute-start.1 = (f32[128,128]{1,0:T(8,128)S(1)}, f32[128,128]{1,0:T(8,128)S(1)}, u32[]{:S(2)}, u32[]{:S(2)}) collective-permute-start(f32[128,128]{1,0:T(8,128)S(1)} %get-tuple-element.21), channel_id=1, source_target_pairs={{8,16},{16,8},{9,17},{17,9},{10,18},{18,10},{11,19},{19,11},{12,20... | collective-permute-start | bytes 196616 | tf_op jit(solution)/shard_map/ppermute | solution.py:137
  14.7 1.3 %fusion.after_ref = f32[40,128]{1,0:T(8,128)S(1)} fusion(f32[128,4352]{1,0:T(8,128)S(1)} %copy-done.1, f32[40,4352]{1,0:T(8,128)S(1)} %copy-done.2, f32[40]{0:T(128)S(1)} %compare_convert_fusion), kind=kOutput, calls=%fused_computation.1 | convolution fusion | flops 133867520 | bytes 2945184 | tf_op jit(solution)/shard_map/dot_general | solution.py:197
  16.2 0.7 %copy-done.5 = f32[768,128]{1,0:T(8,128)} copy-done((f32[768,128]{1,0:T(8,128)}, f32[768,128]{1,0:T(8,128)S(1)}, u32[]{:S(2)}) %copy-start.5) | copy-done | bytes 393240
  17.0 0.9 %broadcast_in_dim.29 = f32[32,40,128]{2,1,0:T(8,128)} broadcast(f32[40,128]{1,0:T(8,128)S(1)} %fusion.after_ref), dimensions={1,2} | broadcast | bytes 675840 | tf_op jit(solution)/shard_map/broadcast_in_dim | solution.py:209
  17.8 10.2 %all-to-all-start = ((f32[32,40,128]{2,1,0:T(8,128)}), f32[32,40,128]{2,1,0:T(8,128)}, u32[]{:S(2)}, u32[]{:S(2)}) async-start(f32[32,40,128]{2,1,0:T(8,128)} %broadcast_in_dim.29), calls=%async_computation | async-start | bytes 1310720 | tf_op jit(solution)/shard_map/all_to_all | solution.py:210
  28.3 1.0 %copy-done.6 = f32[768,128]{1,0:T(8,128)S(1)} copy-done((f32[768,128]{1,0:T(8,128)S(1)}, f32[768,128]{1,0:T(8,128)}, u32[]{:S(2)}) %copy-start.6) | copy-done | bytes 393240
  29.3 13.1 %shard_map.82 = (bf16[128,4352]{1,0:T(8,128)(2,1)S(1)}, bf16[128,768]{1,0:T(8,128)(2,1)S(1)}) custom-call(s32[20]{0:T(128)S(1)} %copy-done.8, f32[128,4352]{1,0:T(8,128)S(1)} %copy-done.1, f32[768,128]{1,0:T(8,128)S(1)} %copy-done.6, bf16[20,256,256]{2,1,0:T(8,128)(2,1)} %inv_ref.1, bf16[19,256,256]{2,1,0:T(8,128)(2,1)} %cpl_ref.1, f32[40,128]{1,0:T(8,128)S(1)} %fusion.after_ref), custom_call_target="tpu_custom_call" | custom-call | tf_op jit(solution)/shard_map/pallas_call | solution.py:64
  42.4 1.0 %copy-done.3 = bf16[128,4352]{1,0:T(8,128)(2,1)} copy-done((bf16[128,4352]{1,0:T(8,128)(2,1)}, bf16[128,4352]{1,0:T(8,128)(2,1)S(1)}, u32[]{:S(2)}) %copy-start.3) | copy-done | bytes 1114136
  43.4 0.7 %copy-done.7 = bf16[128,768]{1,0:T(8,128)(2,1)} copy-done((bf16[128,768]{1,0:T(8,128)(2,1)}, bf16[128,768]{1,0:T(8,128)(2,1)S(1)}, u32[]{:S(2)}) %copy-start.7) | copy-done | bytes 196632
  44.1 1.9 %all-to-all-done = f32[32,40,128]{2,1,0:T(8,128)} async-done(((f32[32,40,128]{2,1,0:T(8,128)}), f32[32,40,128]{2,1,0:T(8,128)}, u32[]{:S(2)}, u32[]{:S(2)}) %all-to-all-start) | async-done | bytes 655392 | tf_op jit(solution)/shard_map/all_to_all | solution.py:210
  45.9 0.9 %slice_select_fusion.1 = (bf16[128,128]{1,0:T(8,128)(2,1)S(1)}, bf16[128,128]{1,0:T(8,128)(2,1)S(1)}, bf16[128,128]{1,0:T(8,128)(2,1)S(1)}, bf16[128,128]{1,0:T(8,128)(2,1)S(1)}, bf16[128,128]{1,0:T(8,128)(2,1)S(1)}) fusion(bf16[128,768]{1,0:T(8,128)(2,1)} %copy-done.7, pred[]{:T(512)S(6)} %eq.21, pred[]{:T(512)S(6)} %eq.20, pred[]{:T(512)S(6)} %eq.19), kind=kLoop, calls=%fused_computation.19 | loop fusion | flops 81920 | bytes 360451 | tf_op jit(solution)/shard_map/jit(_where)/select_n | solution.py:155
  47.0 0.7 %collective-permute-start.7 = (bf16[128,128]{1,0:T(8,128)(2,1)S(1)}, bf16[128,128]{1,0:T(8,128)(2,1)S(1)}, u32[]{:S(2)}, u32[]{:S(2)}) collective-permute-start(bf16[128,128]{1,0:T(8,128)(2,1)S(1)} %get-tuple-element.23), channel_id=1, source_target_pairs={{2,4},{4,2},{3,5},{5,3},{10,12},{12,10},{11,13},{13,11},{18,20},{2... | collective-permute-start | bytes 98312 | tf_op jit(solution)/shard_map/ppermute | solution.py:137
  47.7 4.1 %collective-permute-start.8 = (bf16[128,128]{1,0:T(8,128)(2,1)S(1)}, bf16[128,128]{1,0:T(8,128)(2,1)S(1)}, u32[]{:S(2)}, u32[]{:S(2)}) collective-permute-start(bf16[128,128]{1,0:T(8,128)(2,1)S(1)} %get-tuple-element.24), channel_id=1, source_target_pairs={{0,2},{4,6},{2,0},{6,4},{1,3},{5,7},{3,1},{7,5},{8,10},{12,14},{10... | collective-permute-start | bytes 98312 | tf_op jit(solution)/shard_map/ppermute | solution.py:137
  51.8 0.7 %collective-permute-start.5 = (bf16[128,128]{1,0:T(8,128)(2,1)S(1)}, bf16[128,128]{1,0:T(8,128)(2,1)S(1)}, u32[]{:S(2)}, u32[]{:S(2)}) collective-permute-start(bf16[128,128]{1,0:T(8,128)(2,1)S(1)} %get-tuple-element.25), channel_id=1, source_target_pairs={{8,16},{16,8},{9,17},{17,9},{10,18},{18,10},{11,19},{19,11},{12,20... | collective-permute-start | bytes 98312 | tf_op jit(solution)/shard_map/ppermute | solution.py:137
  52.5 2.8 %collective-permute-start.6 = (bf16[128,128]{1,0:T(8,128)(2,1)S(1)}, bf16[128,128]{1,0:T(8,128)(2,1)S(1)}, u32[]{:S(2)}, u32[]{:S(2)}) collective-permute-start(bf16[128,128]{1,0:T(8,128)(2,1)S(1)} %get-tuple-element.26), channel_id=1, source_target_pairs={{0,8},{16,24},{8,0},{24,16},{1,9},{17,25},{9,1},{25,17},{2,10},{18... | collective-permute-start | bytes 98312 | tf_op jit(solution)/shard_map/ppermute | solution.py:137
  55.3 1.8 %fusion.5.solved_ref = f32[128,40]{1,0:T(8,128)S(1)} fusion(f32[1280,128]{1,0:T(8,128)} %bitcast.9, f32[40,1280]{1,0:T(8,128)S(1)} %copy-done), kind=kOutput, calls=%fused_computation.34 | convolution fusion | flops 39321600 | bytes 880640 | tf_op jit(solution)/shard_map/dot_general | solution.py:226
  57.4 3.3 %shard_map.83 = f32[128,4352]{1,0:T(8,128)} custom-call(s32[1]{0:T(128)} %copy.29.count_ref, s32[768,1]{1,0:T(8,128)S(1)} %bitcast.26, bf16[128,4352]{1,0:T(8,128)(2,1)S(1)} %copy-done.4, bf16[128,768]{1,0:T(8,128)(2,1)S(1)} %select_dynamic-update-slice_fusion.6.back_ref, f32[128,40]{1,0:T(8,128)S(1)} %fusion.5.solved_ref, f32[40,4352]{1,0:T(8,128)S(1)} %copy-done.2), custom_call_target="tpu_custom_call" | custom-call | tf_op jit(solution)/shard_map/pallas_call | solution.py:118
  (46 shorter events, 1.4 us)
Async XLA Ops:
  0.0 55.3 %copy-start = (f32[40,1280]{1,0:T(8,128)S(1)}, f32[40,1280]{1,0:T(8,128)}, u32[]{:S(2)}) copy-start(f32[40,1280]{1,0:T(8,128)} %param.15) | copy-start | bytes 614404
  4.4 10.3 %copy-start.1 = (f32[128,4352]{1,0:T(8,128)S(1)}, f32[128,4352]{1,0:T(8,128)}, u32[]{:S(2)}) copy-start(f32[128,4352]{1,0:T(8,128)} %res_ref.1) | copy-start | bytes 6684676
  4.4 10.3 %copy-start.2 = (f32[40,4352]{1,0:T(8,128)S(1)}, f32[40,4352]{1,0:T(8,128)}, u32[]{:S(2)}) copy-start(f32[40,4352]{1,0:T(8,128)} %vec_ref.1) | copy-start | bytes 2088964
  8.0 8.2 %collective-permute-start.4 = (f32[128,128]{1,0:T(8,128)S(1)}, f32[128,128]{1,0:T(8,128)S(1)}, u32[]{:S(2)}, u32[]{:S(2)}) collective-permute-start(f32[128,128]{1,0:T(8,128)S(1)} %get-tuple-element.17), channel_id=1, source_target_pairs={{0,1},{1,0},{2,3},{3,2},{4,5},{5,4},{6,7},{7,6},{8,9},{9,8},{10,11... | collective-permute-start | bytes 196616 | tf_op jit(solution)/shard_map/ppermute | solution.py:137
  8.5 7.6 %collective-permute-start.2 = (f32[128,128]{1,0:T(8,128)S(1)}, f32[128,128]{1,0:T(8,128)S(1)}, u32[]{:S(2)}, u32[]{:S(2)}) collective-permute-start(f32[128,128]{1,0:T(8,128)S(1)} %get-tuple-element.18), channel_id=1, source_target_pairs={{0,2},{4,6},{2,0},{6,4},{1,3},{5,7},{3,1},{7,5},{8,10},{12,14},{10... | collective-permute-start | bytes 196616 | tf_op jit(solution)/shard_map/ppermute | solution.py:137
  11.1 5.0 %collective-permute-start.3 = (f32[128,128]{1,0:T(8,128)S(1)}, f32[128,128]{1,0:T(8,128)S(1)}, u32[]{:S(2)}, u32[]{:S(2)}) collective-permute-start(f32[128,128]{1,0:T(8,128)S(1)} %get-tuple-element.19), channel_id=1, source_target_pairs={{2,4},{4,2},{3,5},{5,3},{10,12},{12,10},{11,13},{13,11},{18,20},{2... | collective-permute-start | bytes 196616 | tf_op jit(solution)/shard_map/ppermute | solution.py:137
  11.7 4.3 %collective-permute-start = (f32[128,128]{1,0:T(8,128)S(1)}, f32[128,128]{1,0:T(8,128)S(1)}, u32[]{:S(2)}, u32[]{:S(2)}) collective-permute-start(f32[128,128]{1,0:T(8,128)S(1)} %get-tuple-element.20), channel_id=1, source_target_pairs={{0,8},{16,24},{8,0},{24,16},{1,9},{17,25},{9,1},{25,17},{2,10},{18... | collective-permute-start | bytes 196616 | tf_op jit(solution)/shard_map/ppermute | solution.py:137
  13.4 2.7 %collective-permute-start.1 = (f32[128,128]{1,0:T(8,128)S(1)}, f32[128,128]{1,0:T(8,128)S(1)}, u32[]{:S(2)}, u32[]{:S(2)}) collective-permute-start(f32[128,128]{1,0:T(8,128)S(1)} %get-tuple-element.21), channel_id=1, source_target_pairs={{8,16},{16,8},{9,17},{17,9},{10,18},{18,10},{11,19},{19,11},{12,20... | collective-permute-start | bytes 196616 | tf_op jit(solution)/shard_map/ppermute | solution.py:137
  16.0 12.0 %copy-start.9 = (s32[6,128]{1,0:T(8,128)S(1)}, s32[6,128]{1,0:T(8,128)}, u32[]{:S(2)}) copy-start(s32[6,128]{1,0:T(8,128)} %param.12) | copy-start | bytes 9220
  16.0 12.2 %copy-start.8 = (s32[20]{0:T(128)S(1)}, s32[20]{0:T(128)}, u32[]{:S(2)}) copy-start(s32[20]{0:T(128)} %parent_ref.1) | copy-start | bytes 244
  16.2 0.7 %copy-start.5 = (f32[768,128]{1,0:T(8,128)}, f32[768,128]{1,0:T(8,128)S(1)}, u32[]{:S(2)}) copy-start(f32[768,128]{1,0:T(8,128)S(1)} %select_dynamic-update-slice_fusion.slot_ref) | copy-start | bytes 1179652
  17.8 28.1 %all-to-all-start = ((f32[32,40,128]{2,1,0:T(8,128)}), f32[32,40,128]{2,1,0:T(8,128)}, u32[]{:S(2)}, u32[]{:S(2)}) async-start(f32[32,40,128]{2,1,0:T(8,128)} %broadcast_in_dim.29), calls=%async_computation | async-start | bytes 1310720 | tf_op jit(solution)/shard_map/all_to_all | solution.py:210
  28.3 1.0 %copy-start.6 = (f32[768,128]{1,0:T(8,128)S(1)}, f32[768,128]{1,0:T(8,128)}, u32[]{:S(2)}) copy-start(f32[768,128]{1,0:T(8,128)} %copy-done.5) | copy-start | bytes 1179652
  42.4 1.0 %copy-start.3 = (bf16[128,4352]{1,0:T(8,128)(2,1)}, bf16[128,4352]{1,0:T(8,128)(2,1)S(1)}, u32[]{:S(2)}) copy-start(bf16[128,4352]{1,0:T(8,128)(2,1)S(1)} %get-tuple-element.13.own_ref) | copy-start | bytes 3342340
  43.4 0.7 %copy-start.7 = (bf16[128,768]{1,0:T(8,128)(2,1)}, bf16[128,768]{1,0:T(8,128)(2,1)S(1)}, u32[]{:S(2)}) copy-start(bf16[128,768]{1,0:T(8,128)(2,1)S(1)} %get-tuple-element.15) | copy-start | bytes 589828
  45.9 11.5 %copy-start.4 = (bf16[128,4352]{1,0:T(8,128)(2,1)S(1)}, bf16[128,4352]{1,0:T(8,128)(2,1)}, u32[]{:S(2)}) copy-start(bf16[128,4352]{1,0:T(8,128)(2,1)} %copy-done.3) | copy-start | bytes 3342340
  46.9 10.4 %collective-permute-start.9 = (bf16[128,128]{1,0:T(8,128)(2,1)S(1)}, bf16[128,128]{1,0:T(8,128)(2,1)S(1)}, u32[]{:S(2)}, u32[]{:S(2)}) collective-permute-start(bf16[128,128]{1,0:T(8,128)(2,1)S(1)} %get-tuple-element.22), channel_id=1, source_target_pairs={{0,1},{1,0},{2,3},{3,2},{4,5},{5,4},{6,7},{7,6},{8,9},{9,8},{10,11... | collective-permute-start | bytes 98312 | tf_op jit(solution)/shard_map/ppermute | solution.py:137
  47.0 10.2 %collective-permute-start.7 = (bf16[128,128]{1,0:T(8,128)(2,1)S(1)}, bf16[128,128]{1,0:T(8,128)(2,1)S(1)}, u32[]{:S(2)}, u32[]{:S(2)}) collective-permute-start(bf16[128,128]{1,0:T(8,128)(2,1)S(1)} %get-tuple-element.23), channel_id=1, source_target_pairs={{2,4},{4,2},{3,5},{5,3},{10,12},{12,10},{11,13},{13,11},{18,20},{2... | collective-permute-start | bytes 98312 | tf_op jit(solution)/shard_map/ppermute | solution.py:137
  47.7 9.6 %collective-permute-start.8 = (bf16[128,128]{1,0:T(8,128)(2,1)S(1)}, bf16[128,128]{1,0:T(8,128)(2,1)S(1)}, u32[]{:S(2)}, u32[]{:S(2)}) collective-permute-start(bf16[128,128]{1,0:T(8,128)(2,1)S(1)} %get-tuple-element.24), channel_id=1, source_target_pairs={{0,2},{4,6},{2,0},{6,4},{1,3},{5,7},{3,1},{7,5},{8,10},{12,14},{10... | collective-permute-start | bytes 98312 | tf_op jit(solution)/shard_map/ppermute | solution.py:137
  51.8 5.3 %collective-permute-start.5 = (bf16[128,128]{1,0:T(8,128)(2,1)S(1)}, bf16[128,128]{1,0:T(8,128)(2,1)S(1)}, u32[]{:S(2)}, u32[]{:S(2)}) collective-permute-start(bf16[128,128]{1,0:T(8,128)(2,1)S(1)} %get-tuple-element.25), channel_id=1, source_target_pairs={{8,16},{16,8},{9,17},{17,9},{10,18},{18,10},{11,19},{19,11},{12,20... | collective-permute-start | bytes 98312 | tf_op jit(solution)/shard_map/ppermute | solution.py:137
  52.5 4.7 %collective-permute-start.6 = (bf16[128,128]{1,0:T(8,128)(2,1)S(1)}, bf16[128,128]{1,0:T(8,128)(2,1)S(1)}, u32[]{:S(2)}, u32[]{:S(2)}) collective-permute-start(bf16[128,128]{1,0:T(8,128)(2,1)S(1)} %get-tuple-element.26), channel_id=1, source_target_pairs={{0,8},{16,24},{8,0},{24,16},{1,9},{17,25},{9,1},{25,17},{2,10},{18... | collective-permute-start | bytes 98312 | tf_op jit(solution)/shard_map/ppermute | solution.py:137

commit v22 on v19

--- a/solution.py
+++ b/solution.py
@@ -138,11 +138,11 @@
     return got[:rows].astype(value.dtype), got[rows:]
 
 
-def halo_out(down, up, axis, extra=None):
+def halo_out(one, two, axis, extra=None):
     even = lax.axis_index(axis) % 2 == 0
     first, second = matchings(lax.axis_size(axis))
-    r1, got = swap(jnp.where(even, up, down), axis, first, extra)
-    r2, _ = swap(jnp.where(even, down, up), axis, second)
+    r1, got = swap(one, axis, first, extra)
+    r2, _ = swap(two, axis, second)
     return jnp.where(even, r1, r2), jnp.where(even, r2, r1), got
 
 
@@ -196,7 +196,12 @@
     )
     total_dev = coarse_inverse.shape[1] // kmax_here
 
-    outgoing = jnp.take(residual, send_rows, axis=1)
+    order = []
+    for axis_pos, axis in enumerate(AXES):
+        even = lax.axis_index(axis) % 2 == 0
+        down, up = send_rows[2 * axis_pos], send_rows[2 * axis_pos + 1]
+        order += [jnp.where(even, up, down), jnp.where(even, down, up)]
+    outgoing = jnp.take(residual, jnp.stack(order), axis=1)
     incoming = []
     for axis_pos, axis in enumerate(AXES):
         low, high, _ = halo_out(outgoing[:, 2 * axis_pos], outgoing[:, 2 * axis_pos + 1], axis)

time: 60.2 us -> 62.6 us (1.040)
  other arithmetic: 3.62 us -> 6.82 us
  starting transfers between devices: 24.6 us -> 23.4 us
    all_to_all x1, starting transfers between devices: 10.2 us -> 3.37 us  [per_device(): held = lax.all_to_all(spread, AXES, 0, 0, tiled=True)]
    ppermute x10, starting transfers between devices: 14.4 us -> 20 us  [swap(): return (lax.ppermute(value, axis, pairs), None)]
    unnamed x10 -> x15, other arithmetic: 0.15 us -> 4.01 us
    another operation x0 -> x1, other arithmetic: none -> 0.77 us  [per_device(): outgoing = jnp.take(residual, jnp.stack(order), axis=1)]
    and x1, other arithmetic: 0.73 us -> 0.01 us  [per_device(): outgoing = jnp.take(residual, jnp.stack(order), axis=1)]
    broadcast_in_dim x1 -> x0, other arithmetic: 0.69 us -> none  [per_device(): outgoing = jnp.take(residual, send_rows, axis=1)]
  transfers between devices with their start and end apart: 11 -> 11, of which waited for: 2 -> 3; matrix products, arithmetic and copies ran while one was open for 6% -> 5% of each run, Pallas kernels for 22% -> 21%
where the time goes in v22:
time: 62.6 us; the launch traced here: 62 us
  starting transfers between devices  23.4 us (37%)
  Pallas kernels  16.5 us (26%)
  local copies, waits for them, and re-layouts  9.06 us (14%)
  other arithmetic  6.82 us (11%)
  matrix products  3.05 us (5%)
  waiting for transfers between devices  2.19 us (3%)
  between operations  1.04 us (2%)
    ppermute x10, starting transfers between devices, swap(): return (lax.ppermute(value, axis, pairs), None)  20 us
    pallas_call x1, Pallas kernels, local_solve(): pl.pallas_call(solve_kernel, out_shape=(jax.ShapeDtypeStruct((nrhs_here,...  13.2 us
    unnamed x23, local copies, waits for them, and re-layouts  5.62 us
    unnamed x15, other arithmetic  4.01 us
    all_to_all x1, starting transfers between devices, per_device(): held = lax.all_to_all(spread, AXES, 0, 0, tiled=True)  3.37 us
    pallas_call x1, Pallas kernels, finish(): pl.pallas_call(finish_kernel, out_shape=jax.ShapeDtypeStruct(own.shape, j...  3.33 us
    gather x2, local copies, waits for them, and re-layouts, per_device(): outgoing = jnp.take(residual, jnp.stack(order), axis=1)  2.49 us
    all_to_all x1, waiting for transfers between devices, per_device(): held = lax.all_to_all(spread, AXES, 0, 0, tiled=True)  1.85 us
  transfers between devices with their start and end apart: 11, of which 3 were waited for; matrix products, arithmetic and copies ran while one was open for 5% of the time, Pallas kernels for 21%

profile of v22, /device:TPU:0, one launch (start us, length us, event | category | flops | bytes accessed | tf_op | source)
XLA Modules:
  0.0 62.0 jit_solution(12305115891209693402)
XLA Ops:
  0.0 0.8 %constant_dynamic-update-slice_fusion.5 = (s32[6,128,1]{1,2,0:T(1,128)S(1)}, s32[1,128]{1,0:T(1,128)S(1)}) fusion(s32[6,128]{1,0:T(8,128)} %param.12, pred[]{:T(512)S(6)} %eq.25), kind=kLoop, calls=%fused_computation.21 | loop fusion | flops 127 | bytes 2049
  0.8 0.8 %constant_dynamic-update-slice_fusion.4 = (s32[6,128,1]{1,2,0:T(1,128)S(1)}, s32[1,128]{1,0:T(1,128)S(1)}) fusion(s32[6,128,1]{1,2,0:T(1,128)S(1)} %get-tuple-element.27, s32[6,128]{1,0:T(8,128)} %param.12, pred[]{:T(512)S(6)} %eq.25), kind=kLoop, calls=%fused_computation.20 | loop fusion | flops 128 | bytes 2049
  1.5 0.8 %constant_dynamic-update-slice_fusion.3 = (s32[6,128,1]{1,2,0:T(1,128)S(1)}, s32[1,128]{1,0:T(1,128)S(1)}) fusion(s32[6,128,1]{1,2,0:T(1,128)S(1)} %get-tuple-element.25, s32[6,128]{1,0:T(8,128)} %param.12, pred[]{:T(512)S(6)} %eq.26), kind=kLoop, calls=%fused_computation.19 | loop fusion | flops 128 | bytes 2049
  2.3 0.8 %constant_dynamic-update-slice_fusion.2 = (s32[6,128,1]{1,2,0:T(1,128)S(1)}, s32[1,128]{1,0:T(1,128)S(1)}) fusion(s32[6,128,1]{1,2,0:T(1,128)S(1)} %get-tuple-element.23, s32[6,128]{1,0:T(8,128)} %param.12, pred[]{:T(512)S(6)} %eq.26), kind=kLoop, calls=%fused_computation.18 | loop fusion | flops 128 | bytes 2049
  3.1 0.8 %constant_dynamic-update-slice_fusion.1 = (s32[6,128,1]{1,2,0:T(1,128)S(1)}, s32[1,128]{1,0:T(1,128)S(1)}) fusion(s32[6,128,1]{1,2,0:T(1,128)S(1)} %get-tuple-element.21, s32[6,128]{1,0:T(8,128)} %param.12, pred[]{:T(512)S(6)} %eq.27), kind=kLoop, calls=%fused_computation.17 | loop fusion | flops 128 | bytes 2049
  3.9 0.8 %constant_dynamic-update-slice_fusion = (s32[6,128,1]{1,2,0:T(1,128)S(1)}, s32[1,128]{1,0:T(1,128)S(1)}) fusion(s32[6,128,1]{1,2,0:T(1,128)S(1)} %get-tuple-element.19, s32[6,128]{1,0:T(8,128)} %param.12, pred[]{:T(512)S(6)} %eq.27), kind=kLoop, calls=%fused_computation.16 | loop fusion | flops 128 | bytes 2049 | tf_op jit(solution)/shard_map/stack | solution.py:204
  4.7 2.0 %copy.11 = f32[128,4352]{0,1:T(8,128)S(1)} copy(f32[128,4352]{1,0:T(8,128)} %res_ref.1) | data formatting | bytes 4456448 | tf_op args[0]
  6.7 1.6 %gather_fusion = f32[768,128]{1,0:T(8,128)S(1)} fusion(f32[128,4352]{0,1:T(8,128)S(1)} %copy.11, s32[1024]{0:T(1024)S(1)} %pad_clamp_fusion), kind=kCustom, calls=%fused_computation | custom fusion | bytes 789504 | tf_op jit(solution)/shard_map/jit(_take)/gather | solution.py:204
  8.3 0.9 %copy.12 = f32[6,128,128]{1,2,0:T(8,128)} copy(f32[6,128,128]{2,1,0:T(8,128)S(1)} %bitcast.39) | data formatting | bytes 786432 | tf_op jit(solution)/shard_map/jit(_take)/gather | solution.py:204
  9.2 1.0 %select_bitcast_fusion = f32[128,6,128]{2,0,1:T(8,128)S(1)} fusion(f32[6,128,128]{1,2,0:T(8,128)} %copy.12, pred[6,128]{1,0:T(8,128)(4,1)S(1)} %compare_and_fusion), kind=kLoop, calls=%fused_computation.3 | loop fusion | flops 98304 | bytes 787200 | tf_op jit(solution)/shard_map/jit(_take)/select_n | solution.py:204
  11.5 5.3 %collective-permute-start.2 = (f32[128,128]{1,0:T(8,128)S(1)}, f32[128,128]{1,0:T(8,128)S(1)}, u32[]{:S(2)}, u32[]{:S(2)}) collective-permute-start(f32[128,128]{1,0:T(8,128)S(1)} %get-tuple-element.31), channel_id=1, source_target_pairs={{0,2},{4,6},{2,0},{6,4},{1,3},{5,7},{3,1},{7,5},{8,10},{12,14},{10... | collective-permute-start | bytes 196616 | tf_op jit(solution)/shard_map/ppermute | solution.py:134
  17.4 4.5 %collective-permute-start = (f32[128,128]{1,0:T(8,128)S(1)}, f32[128,128]{1,0:T(8,128)S(1)}, u32[]{:S(2)}, u32[]{:S(2)}) collective-permute-start(f32[128,128]{1,0:T(8,128)S(1)} %get-tuple-element.33), channel_id=1, source_target_pairs={{0,8},{16,24},{8,0},{24,16},{1,9},{17,25},{9,1},{25,17},{2,10},{18... | collective-permute-start | bytes 196616 | tf_op jit(solution)/shard_map/ppermute | solution.py:134
  22.6 1.3 %fusion.after_ref = f32[40,128]{1,0:T(8,128)S(1)} fusion(f32[128,4352]{1,0:T(8,128)S(1)} %copy-done.1, f32[40,4352]{1,0:T(8,128)S(1)} %copy-done.2, f32[40]{0:T(128)S(1)} %compare_convert_fusion), kind=kOutput, calls=%fused_computation.1 | convolution fusion | flops 133867520 | bytes 2945184 | tf_op jit(solution)/shard_map/dot_general | solution.py:194
  25.0 0.9 %broadcast_in_dim.26 = f32[32,40,128]{2,1,0:T(8,128)} broadcast(f32[40,128]{1,0:T(8,128)S(1)} %fusion.after_ref), dimensions={1,2} | broadcast | bytes 675840 | tf_op jit(solution)/shard_map/broadcast_in_dim | solution.py:211
  25.9 3.4 %all-to-all-start = ((f32[32,40,128]{2,1,0:T(8,128)}), f32[32,40,128]{2,1,0:T(8,128)}, u32[]{:S(2)}, u32[]{:S(2)}) async-start(f32[32,40,128]{2,1,0:T(8,128)} %broadcast_in_dim.26), calls=%async_computation | async-start | bytes 1310720 | tf_op jit(solution)/shard_map/all_to_all | solution.py:212
  29.6 1.0 %copy-done.6 = f32[128,768]{1,0:T(8,128)S(1)} copy-done((f32[128,768]{1,0:T(8,128)S(1)}, f32[128,768]{1,0:T(8,128)}, u32[]{:S(2)}) %copy-start.6) | copy-done | bytes 393240
  30.5 13.2 %shard_map.82 = (bf16[128,4352]{1,0:T(8,128)(2,1)S(1)}, bf16[128,768]{1,0:T(8,128)(2,1)S(1)}) custom-call(s32[20]{0:T(128)S(1)} %copy-done.8, f32[128,4352]{1,0:T(8,128)S(1)} %copy-done.1, f32[128,768]{1,0:T(8,128)S(1)} %copy-done.6, bf16[20,256,256]{2,1,0:T(8,128)(2,1)} %inv_ref.1, bf16[19,256,256]{2,1,0:T(8,128)(2,1)} %cpl_ref.1, f32[40,128]{1,0:T(8,128)S(1)} %fusion.after_ref), custom_call_target="tpu_custom_call" | custom-call | tf_op jit(solution)/shard_map/pallas_call | solution.py:61
  43.7 1.0 %copy-done.3 = bf16[128,4352]{1,0:T(8,128)(2,1)} copy-done((bf16[128,4352]{1,0:T(8,128)(2,1)}, bf16[128,4352]{1,0:T(8,128)(2,1)S(1)}, u32[]{:S(2)}) %copy-start.3) | copy-done | bytes 1114136
  45.4 1.8 %all-to-all-done = f32[32,40,128]{2,1,0:T(8,128)} async-done(((f32[32,40,128]{2,1,0:T(8,128)}), f32[32,40,128]{2,1,0:T(8,128)}, u32[]{:S(2)}, u32[]{:S(2)}) %all-to-all-start) | async-done | bytes 655392 | tf_op jit(solution)/shard_map/all_to_all | solution.py:212
  47.2 0.9 %slice_select_fusion = (bf16[128,128]{1,0:T(8,128)(2,1)S(1)}, bf16[128,128]{1,0:T(8,128)(2,1)S(1)}, bf16[128,128]{1,0:T(8,128)(2,1)S(1)}, bf16[128,128]{1,0:T(8,128)(2,1)S(1)}, bf16[128,128]{1,0:T(8,128)(2,1)S(1)}) fusion(bf16[128,768]{1,0:T(8,128)(2,1)} %copy-done.7, pred[]{:T(512)S(6)} %eq.27, pred[]{:T(512)S(6)} %eq.26, pred[]{:T(512)S(6)} %eq.25), kind=kLoop, calls=%fused_computation.28 | loop fusion | flops 81920 | bytes 360451 | tf_op jit(solution)/shard_map/jit(_where)/select_n | solution.py:152
  49.0 4.1 %collective-permute-start.8 = (bf16[128,128]{1,0:T(8,128)(2,1)S(1)}, bf16[128,128]{1,0:T(8,128)(2,1)S(1)}, u32[]{:S(2)}, u32[]{:S(2)}) collective-permute-start(bf16[128,128]{1,0:T(8,128)(2,1)S(1)} %get-tuple-element.36), channel_id=1, source_target_pairs={{0,2},{4,6},{2,0},{6,4},{1,3},{5,7},{3,1},{7,5},{8,10},{12,14},{10... | collective-permute-start | bytes 98312 | tf_op jit(solution)/shard_map/ppermute | solution.py:134
  53.8 2.8 %collective-permute-start.6 = (bf16[128,128]{1,0:T(8,128)(2,1)S(1)}, bf16[128,128]{1,0:T(8,128)(2,1)S(1)}, u32[]{:S(2)}, u32[]{:S(2)}) collective-permute-start(bf16[128,128]{1,0:T(8,128)(2,1)S(1)} %get-tuple-element.38), channel_id=1, source_target_pairs={{0,8},{16,24},{8,0},{24,16},{1,9},{17,25},{9,1},{25,17},{2,10},{18... | collective-permute-start | bytes 98312 | tf_op jit(solution)/shard_map/ppermute | solution.py:134
  56.6 1.8 %fusion.4.solved_ref = f32[128,40]{1,0:T(8,128)S(1)} fusion(f32[1280,128]{1,0:T(8,128)} %bitcast.14, f32[40,1280]{1,0:T(8,128)S(1)} %copy-done), kind=kOutput, calls=%fused_computation.46 | convolution fusion | flops 39321600 | bytes 880640 | tf_op jit(solution)/shard_map/dot_general | solution.py:228
  58.7 3.3 %shard_map.83 = f32[128,4352]{1,0:T(8,128)} custom-call(s32[1]{0:T(128)} %copy.35.count_ref, s32[768,1]{1,0:T(8,128)S(1)} %bitcast.38, bf16[128,4352]{1,0:T(8,128)(2,1)S(1)} %copy-done.4, bf16[128,768]{1,0:T(8,128)(2,1)S(1)} %constant_dynamic-update-slice_fusion.6.back_ref, f32[128,40]{1,0:T(8,128)S(1)} %fusion.4.solved_ref, f32[40,4352]{1,0:T(8,128)S(1)} %copy-done.2), custom_call_target="tpu_custom_call" | custom-call | tf_op jit(solution)/shard_map/pallas_call | solution.py:115
  (54 shorter events, 5.5 us)
Async XLA Ops:
  0.0 56.6 %copy-start = (f32[40,1280]{1,0:T(8,128)S(1)}, f32[40,1280]{1,0:T(8,128)}, u32[]{:S(2)}) copy-start(f32[40,1280]{1,0:T(8,128)} %param.15) | copy-start | bytes 614404
  6.7 15.9 %copy-start.2 = (f32[40,4352]{1,0:T(8,128)S(1)}, f32[40,4352]{1,0:T(8,128)}, u32[]{:S(2)}) copy-start(f32[40,4352]{1,0:T(8,128)} %vec_ref.1) | copy-start | bytes 2088964
  8.3 14.3 %copy-start.1 = (f32[128,4352]{1,0:T(8,128)S(1)}, f32[128,4352]{1,0:T(8,128)}, u32[]{:S(2)}) copy-start(f32[128,4352]{1,0:T(8,128)} %res_ref.1) | copy-start | bytes 6684676
  10.3 13.9 %collective-permute-start.4 = (f32[128,128]{1,0:T(8,128)S(1)}, f32[128,128]{1,0:T(8,128)S(1)}, u32[]{:S(2)}, u32[]{:S(2)}) collective-permute-start(f32[128,128]{1,0:T(8,128)S(1)} %get-tuple-element.29), channel_id=1, source_target_pairs={{0,1},{1,0},{2,3},{3,2},{4,5},{5,4},{6,7},{7,6},{8,9},{9,8},{10,11... | collective-permute-start | bytes 196616 | tf_op jit(solution)/shard_map/ppermute | solution.py:134
  10.8 13.4 %collective-permute-start.3 = (f32[128,128]{1,0:T(8,128)S(1)}, f32[128,128]{1,0:T(8,128)S(1)}, u32[]{:S(2)}, u32[]{:S(2)}) collective-permute-start(f32[128,128]{1,0:T(8,128)S(1)} %get-tuple-element.30), channel_id=1, source_target_pairs={{2,4},{4,2},{3,5},{5,3},{10,12},{12,10},{11,13},{13,11},{18,20},{2... | collective-permute-start | bytes 196616 | tf_op jit(solution)/shard_map/ppermute | solution.py:134
  11.5 12.7 %collective-permute-start.2 = (f32[128,128]{1,0:T(8,128)S(1)}, f32[128,128]{1,0:T(8,128)S(1)}, u32[]{:S(2)}, u32[]{:S(2)}) collective-permute-start(f32[128,128]{1,0:T(8,128)S(1)} %get-tuple-element.31), channel_id=1, source_target_pairs={{0,2},{4,6},{2,0},{6,4},{1,3},{5,7},{3,1},{7,5},{8,10},{12,14},{10... | collective-permute-start | bytes 196616 | tf_op jit(solution)/shard_map/ppermute | solution.py:134
  16.8 7.1 %collective-permute-start.1 = (f32[128,128]{1,0:T(8,128)S(1)}, f32[128,128]{1,0:T(8,128)S(1)}, u32[]{:S(2)}, u32[]{:S(2)}) collective-permute-start(f32[128,128]{1,0:T(8,128)S(1)} %get-tuple-element.32), channel_id=1, source_target_pairs={{8,16},{16,8},{9,17},{17,9},{10,18},{18,10},{11,19},{19,11},{12,20... | collective-permute-start | bytes 196616 | tf_op jit(solution)/shard_map/ppermute | solution.py:134
  17.4 6.7 %collective-permute-start = (f32[128,128]{1,0:T(8,128)S(1)}, f32[128,128]{1,0:T(8,128)S(1)}, u32[]{:S(2)}, u32[]{:S(2)}) collective-permute-start(f32[128,128]{1,0:T(8,128)S(1)} %get-tuple-element.33), channel_id=1, source_target_pairs={{0,8},{16,24},{8,0},{24,16},{1,9},{17,25},{9,1},{25,17},{2,10},{18... | collective-permute-start | bytes 196616 | tf_op jit(solution)/shard_map/ppermute | solution.py:134
  23.9 5.4 %copy-start.9 = (s32[6,128]{1,0:T(8,128)S(1)}, s32[6,128]{1,0:T(8,128)}, u32[]{:S(2)}) copy-start(s32[6,128]{1,0:T(8,128)} %param.12) | copy-start | bytes 9220
  23.9 5.6 %copy-start.8 = (s32[20]{0:T(128)S(1)}, s32[20]{0:T(128)}, u32[]{:S(2)}) copy-start(s32[20]{0:T(128)} %parent_ref.1) | copy-start | bytes 244
  24.3 0.7 %copy-start.5 = (f32[128,768]{1,0:T(8,128)}, f32[128,768]{1,0:T(8,128)S(1)}, u32[]{:S(2)}) copy-start(f32[128,768]{1,0:T(8,128)S(1)} %select_dynamic-update-slice_fusion.slot_ref) | copy-start | bytes 1179652
  25.9 21.3 %all-to-all-start = ((f32[32,40,128]{2,1,0:T(8,128)}), f32[32,40,128]{2,1,0:T(8,128)}, u32[]{:S(2)}, u32[]{:S(2)}) async-start(f32[32,40,128]{2,1,0:T(8,128)} %broadcast_in_dim.26), calls=%async_computation | async-start | bytes 1310720 | tf_op jit(solution)/shard_map/all_to_all | solution.py:212
  29.5 1.0 %copy-start.6 = (f32[128,768]{1,0:T(8,128)S(1)}, f32[128,768]{1,0:T(8,128)}, u32[]{:S(2)}) copy-start(f32[128,768]{1,0:T(8,128)} %copy-done.5) | copy-start | bytes 1179652
  43.7 1.0 %copy-start.3 = (bf16[128,4352]{1,0:T(8,128)(2,1)}, bf16[128,4352]{1,0:T(8,128)(2,1)S(1)}, u32[]{:S(2)}) copy-start(bf16[128,4352]{1,0:T(8,128)(2,1)S(1)} %get-tuple-element.13.own_ref) | copy-start | bytes 3342340
  44.7 0.7 %copy-start.7 = (bf16[128,768]{1,0:T(8,128)(2,1)}, bf16[128,768]{1,0:T(8,128)(2,1)S(1)}, u32[]{:S(2)}) copy-start(bf16[128,768]{1,0:T(8,128)(2,1)S(1)} %get-tuple-element.15) | copy-start | bytes 589828
  47.2 11.5 %copy-start.4 = (bf16[128,4352]{1,0:T(8,128)(2,1)S(1)}, bf16[128,4352]{1,0:T(8,128)(2,1)}, u32[]{:S(2)}) copy-start(bf16[128,4352]{1,0:T(8,128)(2,1)} %copy-done.3) | copy-start | bytes 3342340
  48.2 10.5 %collective-permute-start.9 = (bf16[128,128]{1,0:T(8,128)(2,1)S(1)}, bf16[128,128]{1,0:T(8,128)(2,1)S(1)}, u32[]{:S(2)}, u32[]{:S(2)}) collective-permute-start(bf16[128,128]{1,0:T(8,128)(2,1)S(1)} %get-tuple-element.34), channel_id=1, source_target_pairs={{0,1},{1,0},{2,3},{3,2},{4,5},{5,4},{6,7},{7,6},{8,9},{9,8},{10,11... | collective-permute-start | bytes 98312 | tf_op jit(solution)/shard_map/ppermute | solution.py:134
  48.3 10.2 %collective-permute-start.7 = (bf16[128,128]{1,0:T(8,128)(2,1)S(1)}, bf16[128,128]{1,0:T(8,128)(2,1)S(1)}, u32[]{:S(2)}, u32[]{:S(2)}) collective-permute-start(bf16[128,128]{1,0:T(8,128)(2,1)S(1)} %get-tuple-element.35), channel_id=1, source_target_pairs={{2,4},{4,2},{3,5},{5,3},{10,12},{12,10},{11,13},{13,11},{18,20},{2... | collective-permute-start | bytes 98312 | tf_op jit(solution)/shard_map/ppermute | solution.py:134
  49.0 9.6 %collective-permute-start.8 = (bf16[128,128]{1,0:T(8,128)(2,1)S(1)}, bf16[128,128]{1,0:T(8,128)(2,1)S(1)}, u32[]{:S(2)}, u32[]{:S(2)}) collective-permute-start(bf16[128,128]{1,0:T(8,128)(2,1)S(1)} %get-tuple-element.36), channel_id=1, source_target_pairs={{0,2},{4,6},{2,0},{6,4},{1,3},{5,7},{3,1},{7,5},{8,10},{12,14},{10... | collective-permute-start | bytes 98312 | tf_op jit(solution)/shard_map/ppermute | solution.py:134
  53.1 5.3 %collective-permute-start.5 = (bf16[128,128]{1,0:T(8,128)(2,1)S(1)}, bf16[128,128]{1,0:T(8,128)(2,1)S(1)}, u32[]{:S(2)}, u32[]{:S(2)}) collective-permute-start(bf16[128,128]{1,0:T(8,128)(2,1)S(1)} %get-tuple-element.37), channel_id=1, source_target_pairs={{8,16},{16,8},{9,17},{17,9},{10,18},{18,10},{11,19},{19,11},{12,20... | collective-permute-start | bytes 98312 | tf_op jit(solution)/shard_map/ppermute | solution.py:134
  53.8 4.7 %collective-permute-start.6 = (bf16[128,128]{1,0:T(8,128)(2,1)S(1)}, bf16[128,128]{1,0:T(8,128)(2,1)S(1)}, u32[]{:S(2)}, u32[]{:S(2)}) collective-permute-start(bf16[128,128]{1,0:T(8,128)(2,1)S(1)} %get-tuple-element.38), channel_id=1, source_target_pairs={{0,8},{16,24},{8,0},{24,16},{1,9},{17,25},{9,1},{25,17},{2,10},{18... | collective-permute-start | bytes 98312 | tf_op jit(solution)/shard_map/ppermute | solution.py:134

commit v23 on v22

--- a/solution.py
+++ b/solution.py
@@ -196,12 +196,16 @@
     )
     total_dev = coarse_inverse.shape[1] // kmax_here
 
-    order = []
-    for axis_pos, axis in enumerate(AXES):
-        even = lax.axis_index(axis) % 2 == 0
-        down, up = send_rows[2 * axis_pos], send_rows[2 * axis_pos + 1]
-        order += [jnp.where(even, up, down), jnp.where(even, down, up)]
-    outgoing = jnp.take(residual, jnp.stack(order), axis=1)
+    sizes = [lax.axis_size(axis) for axis in AXES]
+    strides = [1] * len(AXES)
+    for axis_pos in reversed(range(len(AXES) - 1)):
+        strides[axis_pos] = strides[axis_pos + 1] * sizes[axis_pos + 1]
+    face_stride = jnp.array([strides[f // 2] for f in range(slots_n)], jnp.int32)
+    face_size = jnp.array([sizes[f // 2] for f in range(slots_n)], jnp.int32)
+    even = (lax.axis_index(AXES) // face_stride) % face_size % 2 == 0
+    flip = jnp.array([f ^ 1 for f in range(slots_n)], jnp.int32)
+    order = jnp.where(even[:, None], send_rows[flip], send_rows)
+    outgoing = jnp.take(residual, order, axis=1)
     incoming = []
     for axis_pos, axis in enumerate(AXES):
         low, high, _ = halo_out(outgoing[:, 2 * axis_pos], outgoing[:, 2 * axis_pos + 1], axis)

time: 62.6 us -> 63 us (level)
  local copies, waits for them, and re-layouts: 9.06 us -> 11 us
  other arithmetic: 6.82 us -> 5.32 us
    unnamed x15 -> x10, other arithmetic: 4.01 us -> 0.15 us
    gather x2 -> x3, local copies, waits for them, and re-layouts: 2.49 us -> 3.73 us  [the longest x2 2.49 us: per_device(): outgoing = jnp.take(residual, order, axis=1)]
    eq x0 -> x1, other arithmetic: none -> 0.93 us  [per_device(): even = lax.axis_index(AXES) // face_stride % face_size % 2 == 0]
    another operation x1 -> x0, other arithmetic: 0.77 us -> none  [per_device(): outgoing = jnp.take(residual, jnp.stack(order), axis=1)]
    broadcast_in_dim x0 -> x1, other arithmetic: none -> 0.76 us  [per_device(): outgoing = jnp.take(residual, order, axis=1)]
    and x1, other arithmetic: 0.01 us -> 0.76 us  [per_device(): outgoing = jnp.take(residual, order, axis=1)]
    gather x1 -> x2, other arithmetic: 0.01 us -> 0.71 us  [the longest x1 0.7 us: per_device(): order = jnp.where(even[:, None], send_rows[flip], send_rows)]
    squeeze x1, local copies, waits for them, and re-layouts: 0.02 us -> 0.71 us  [per_device(): outgoing[:, 2 * axis_pos]]
where the time goes in v23:
time: 63 us; the launch traced here: 62.5 us
  starting transfers between devices  23.3 us (37%)
  Pallas kernels  16.5 us (26%)
  local copies, waits for them, and re-layouts  11 us (17%)
  other arithmetic  5.32 us (8%)
  matrix products  3.06 us (5%)
  waiting for transfers between devices  2.37 us (4%)
  between operations  1.06 us (2%)
    ppermute x10, starting transfers between devices, swap(): return (lax.ppermute(value, axis, pairs), None)  19.9 us
    pallas_call x1, Pallas kernels, local_solve(): pl.pallas_call(solve_kernel, out_shape=(jax.ShapeDtypeStruct((nrhs_here,...  13.1 us
    unnamed x23, local copies, waits for them, and re-layouts  5.62 us
    all_to_all x1, starting transfers between devices, per_device(): held = lax.all_to_all(spread, AXES, 0, 0, tiled=True)  3.37 us
    pallas_call x1, Pallas kernels, finish(): pl.pallas_call(finish_kernel, out_shape=jax.ShapeDtypeStruct(own.shape, j...  3.33 us
    gather x2, local copies, waits for them, and re-layouts, per_device(): outgoing = jnp.take(residual, order, axis=1)  2.49 us
    all_to_all x1, waiting for transfers between devices, per_device(): held = lax.all_to_all(spread, AXES, 0, 0, tiled=True)  1.86 us
    dot_general x1, matrix products, per_device(): jnp.dot(coarse_inverse, rows_of(held), precision=lax.Precision.HIGH, pref...  1.79 us
  transfers between devices with their start and end apart: 11, of which 3 were waited for; matrix products, arithmetic and copies ran while one was open for 5% of the time, Pallas kernels for 21%

profile of v23, /device:TPU:0, one launch (start us, length us, event | category | flops | bytes accessed | tf_op | source)
XLA Modules:
  0.0 62.5 jit_solution(5347028378291005191)
XLA Ops:
  0.7 1.2 %gather_fusion = s32[6,128]{1,0:T(8,128)S(1)} fusion(s32[6,128]{1,0:T(8,128)} %param.15, s32[1024]{0:T(1024)S(1)} %pad_clamp_fusion.1), kind=kCustom, calls=%fused_computation | custom fusion | bytes 6168 | tf_op jit(solution)/shard_map/gather | solution.py:207
  1.9 0.9 %fusion.3 = pred[6]{0:T(512)(128)(4,1)S(1)} fusion(s32[6]{0:T(128)} %constant.98, s32[6]{0:T(128)} %constant.87.clone, pred[]{:T(512)S(6)} %ne.57, s32[]{:T(128)S(6)} %add.43), kind=kLoop, calls=%fused_computation.39 | loop fusion | flops 144 | bytes 59 | tf_op jit(solution)/shard_map/eq | solution.py:205
  2.9 0.8 %compare_and_fusion = pred[6,128]{1,0:T(8,128)(4,1)S(1)} fusion(s32[6,128]{1,0:T(8,128)S(1)} %gather_fusion, s32[6,128]{1,0:T(8,128)} %param.15, pred[6]{0:T(512)(128)(4,1)S(1)} %fusion.3), kind=kLoop, calls=%fused_computation.31 | loop fusion | flops 5376 | bytes 6918 | tf_op jit(solution)/shard_map/jit(_take)/and | solution.py:208
  3.6 0.8 %fusion.5 = s32[768]{0:T(1024)S(1)} fusion(s32[6,128]{1,0:T(8,128)S(1)} %gather_fusion, s32[6,128]{1,0:T(8,128)} %param.15, pred[6]{0:T(512)(128)(4,1)S(1)} %fusion.3), kind=kLoop, calls=%fused_computation.41 | loop fusion | flops 3072 | bytes 9222 | tf_op jit(solution)/shard_map/jit(_take)/broadcast_in_dim | solution.py:208
  4.4 2.0 %copy.14 = f32[128,4352]{0,1:T(8,128)S(1)} copy(f32[128,4352]{1,0:T(8,128)} %res_ref.1) | data formatting | bytes 4456448 | tf_op args[0]
  6.4 1.6 %gather_fusion.1 = f32[768,128]{1,0:T(8,128)S(1)} fusion(f32[128,4352]{0,1:T(8,128)S(1)} %copy.14, s32[1024]{0:T(1024)S(1)} %pad_clamp_fusion), kind=kCustom, calls=%fused_computation.1 | custom fusion | bytes 789504 | tf_op jit(solution)/shard_map/jit(_take)/gather | solution.py:208
  8.0 0.9 %copy.15 = f32[6,128,128]{1,2,0:T(8,128)} copy(f32[6,128,128]{2,1,0:T(8,128)S(1)} %bitcast.28) | data formatting | bytes 786432 | tf_op jit(solution)/shard_map/jit(_take)/gather | solution.py:208
  8.9 1.0 %select_bitcast_fusion = f32[128,6,128]{2,0,1:T(8,128)S(1)} fusion(f32[6,128,128]{1,2,0:T(8,128)} %copy.15, pred[6,128]{1,0:T(8,128)(4,1)S(1)} %compare_and_fusion), kind=kLoop, calls=%fused_computation.4 | loop fusion | flops 98304 | bytes 787200 | tf_op jit(solution)/shard_map/jit(_take)/select_n | solution.py:208
  10.0 0.7 %slice_bitcast_fusion = (f32[128,128]{1,0:T(8,128)S(1)}, f32[128,128]{1,0:T(8,128)}, f32[128,128]{1,0:T(8,128)}, f32[128,128]{1,0:T(8,128)}, f32[128,128]{1,0:T(8,128)}) fusion(f32[128,6,128]{2,0,1:T(8,128)S(1)} %select_bitcast_fusion), kind=kLoop, calls=%fused_computation.6 | loop fusion | bytes 655360 | tf_op jit(solution)/shard_map/squeeze | solution.py:211
  11.8 5.3 %collective-permute-start.2 = (f32[128,128]{1,0:T(8,128)}, f32[128,128]{1,0:T(8,128)S(1)}, u32[]{:S(2)}, u32[]{:S(2)}) collective-permute-start(f32[128,128]{1,0:T(8,128)} %get-tuple-element.19), channel_id=1, source_target_pairs={{0,2},{4,6},{2,0},{6,4},{1,3},{5,7},{3,1},{7,5},{8,10},{12,14},{10... | collective-permute-start | bytes 196616 | tf_op jit(solution)/shard_map/ppermute | solution.py:134
  17.7 4.5 %collective-permute-start = (f32[128,128]{1,0:T(8,128)}, f32[128,128]{1,0:T(8,128)S(1)}, u32[]{:S(2)}, u32[]{:S(2)}) collective-permute-start(f32[128,128]{1,0:T(8,128)} %get-tuple-element.21), channel_id=1, source_target_pairs={{0,8},{16,24},{8,0},{24,16},{1,9},{17,25},{9,1},{25,17},{2,10},{18... | collective-permute-start | bytes 196616 | tf_op jit(solution)/shard_map/ppermute | solution.py:134
  22.9 1.3 %fusion.after_ref = f32[40,128]{1,0:T(8,128)S(1)} fusion(f32[128,4352]{1,0:T(8,128)S(1)} %copy-done.1, f32[40,4352]{1,0:T(8,128)S(1)} %copy-done.2, f32[40]{0:T(128)S(1)} %compare_convert_fusion), kind=kOutput, calls=%fused_computation.2 | convolution fusion | flops 133867520 | bytes 2945184 | tf_op jit(solution)/shard_map/dot_general | solution.py:194
  24.8 0.7 %copy-done.5 = f32[128,768]{1,0:T(8,128)} copy-done((f32[128,768]{1,0:T(8,128)}, f32[128,768]{1,0:T(8,128)S(1)}, u32[]{:S(2)}) %copy-start.5) | copy-done | bytes 393240
  25.5 0.9 %broadcast_in_dim.43 = f32[32,40,128]{2,1,0:T(8,128)} broadcast(f32[40,128]{1,0:T(8,128)S(1)} %fusion.after_ref), dimensions={1,2} | broadcast | bytes 675840 | tf_op jit(solution)/shard_map/broadcast_in_dim | solution.py:215
  26.4 3.4 %all-to-all-start = ((f32[32,40,128]{2,1,0:T(8,128)}), f32[32,40,128]{2,1,0:T(8,128)}, u32[]{:S(2)}, u32[]{:S(2)}) async-start(f32[32,40,128]{2,1,0:T(8,128)} %broadcast_in_dim.43), calls=%async_computation | async-start | bytes 1310720 | tf_op jit(solution)/shard_map/all_to_all | solution.py:216
  30.0 1.0 %copy-done.6 = f32[128,768]{1,0:T(8,128)S(1)} copy-done((f32[128,768]{1,0:T(8,128)S(1)}, f32[128,768]{1,0:T(8,128)}, u32[]{:S(2)}) %copy-start.6) | copy-done | bytes 393240
  31.0 13.1 %shard_map.109 = (bf16[128,4352]{1,0:T(8,128)(2,1)S(1)}, bf16[128,768]{1,0:T(8,128)(2,1)S(1)}) custom-call(s32[20]{0:T(128)S(1)} %copy-done.8, f32[128,4352]{1,0:T(8,128)S(1)} %copy-done.1, f32[128,768]{1,0:T(8,128)S(1)} %copy-done.6, bf16[20,256,256]{2,1,0:T(8,128)(2,1)} %inv_ref.1, bf16[19,256,256]{2,1,0:T(8,128)(2,1)} %cpl_ref.1, f32[40,128]{1,0:T(8,128)S(1)} %fusion.after_ref), custom_call_target="tpu_custom_call" | custom-call | tf_op jit(solution)/shard_map/pallas_call | solution.py:61
  44.2 1.0 %copy-done.3 = bf16[128,4352]{1,0:T(8,128)(2,1)} copy-done((bf16[128,4352]{1,0:T(8,128)(2,1)}, bf16[128,4352]{1,0:T(8,128)(2,1)S(1)}, u32[]{:S(2)}) %copy-start.3) | copy-done | bytes 1114136
  45.9 1.9 %all-to-all-done = f32[32,40,128]{2,1,0:T(8,128)} async-done(((f32[32,40,128]{2,1,0:T(8,128)}), f32[32,40,128]{2,1,0:T(8,128)}, u32[]{:S(2)}, u32[]{:S(2)}) %all-to-all-start) | async-done | bytes 655392 | tf_op jit(solution)/shard_map/all_to_all | solution.py:216
  47.7 0.9 %slice_select_fusion = (bf16[128,128]{1,0:T(8,128)(2,1)S(1)}, bf16[128,128]{1,0:T(8,128)(2,1)S(1)}, bf16[128,128]{1,0:T(8,128)(2,1)S(1)}, bf16[128,128]{1,0:T(8,128)(2,1)S(1)}, bf16[128,128]{1,0:T(8,128)(2,1)S(1)}) fusion(bf16[128,768]{1,0:T(8,128)(2,1)} %copy-done.7, pred[]{:T(512)S(6)} %eq.32, pred[]{:T(512)S(6)} %eq.31, pred[]{:T(512)S(6)} %eq.28), kind=kLoop, calls=%fused_computation.19 | loop fusion | flops 81920 | bytes 360451 | tf_op jit(solution)/shard_map/jit(_where)/select_n | solution.py:152
  49.5 4.1 %collective-permute-start.8 = (bf16[128,128]{1,0:T(8,128)(2,1)S(1)}, bf16[128,128]{1,0:T(8,128)(2,1)S(1)}, u32[]{:S(2)}, u32[]{:S(2)}) collective-permute-start(bf16[128,128]{1,0:T(8,128)(2,1)S(1)} %get-tuple-element.24), channel_id=1, source_target_pairs={{0,2},{4,6},{2,0},{6,4},{1,3},{5,7},{3,1},{7,5},{8,10},{12,14},{10... | collective-permute-start | bytes 98312 | tf_op jit(solution)/shard_map/ppermute | solution.py:134
  54.3 2.8 %collective-permute-start.6 = (bf16[128,128]{1,0:T(8,128)(2,1)S(1)}, bf16[128,128]{1,0:T(8,128)(2,1)S(1)}, u32[]{:S(2)}, u32[]{:S(2)}) collective-permute-start(bf16[128,128]{1,0:T(8,128)(2,1)S(1)} %get-tuple-element.26), channel_id=1, source_target_pairs={{0,8},{16,24},{8,0},{24,16},{1,9},{17,25},{9,1},{25,17},{2,10},{18... | collective-permute-start | bytes 98312 | tf_op jit(solution)/shard_map/ppermute | solution.py:134
  57.1 1.8 %fusion.6.solved_ref = f32[128,40]{1,0:T(8,128)S(1)} fusion(f32[1280,128]{1,0:T(8,128)} %bitcast.9, f32[40,1280]{1,0:T(8,128)S(1)} %copy-done), kind=kOutput, calls=%fused_computation.42 | convolution fusion | flops 39321600 | bytes 880640 | tf_op jit(solution)/shard_map/dot_general | solution.py:232
  59.2 3.3 %shard_map.110 = f32[128,4352]{1,0:T(8,128)} custom-call(s32[1]{0:T(128)} %copy.33.count_ref, s32[768,1]{1,0:T(8,128)S(1)} %bitcast.27, bf16[128,4352]{1,0:T(8,128)(2,1)S(1)} %copy-done.4, bf16[128,768]{1,0:T(8,128)(2,1)S(1)} %select_dynamic-update-slice_fusion.6.back_ref, f32[128,40]{1,0:T(8,128)S(1)} %fusion.6.solved_ref, f32[40,4352]{1,0:T(8,128)S(1)} %copy-done.2), custom_call_target="tpu_custom_call" | custom-call | tf_op jit(solution)/shard_map/pallas_call | solution.py:115
  (50 shorter events, 5.5 us)
Async XLA Ops:
  0.0 57.1 %copy-start = (f32[40,1280]{1,0:T(8,128)S(1)}, f32[40,1280]{1,0:T(8,128)}, u32[]{:S(2)}) copy-start(f32[40,1280]{1,0:T(8,128)} %param.18) | copy-start | bytes 614404
  6.4 16.4 %copy-start.2 = (f32[40,4352]{1,0:T(8,128)S(1)}, f32[40,4352]{1,0:T(8,128)}, u32[]{:S(2)}) copy-start(f32[40,4352]{1,0:T(8,128)} %vec_ref.1) | copy-start | bytes 2088964
  8.0 14.9 %copy-start.1 = (f32[128,4352]{1,0:T(8,128)S(1)}, f32[128,4352]{1,0:T(8,128)}, u32[]{:S(2)}) copy-start(f32[128,4352]{1,0:T(8,128)} %res_ref.1) | copy-start | bytes 6684676
  10.7 14.1 %collective-permute-start.4 = (f32[128,128]{1,0:T(8,128)S(1)}, f32[128,128]{1,0:T(8,128)S(1)}, u32[]{:S(2)}, u32[]{:S(2)}) collective-permute-start(f32[128,128]{1,0:T(8,128)S(1)} %get-tuple-element.17), channel_id=1, source_target_pairs={{0,1},{1,0},{2,3},{3,2},{4,5},{5,4},{6,7},{7,6},{8,9},{9,8},{10,11... | collective-permute-start | bytes 196616 | tf_op jit(solution)/shard_map/ppermute | solution.py:134
  11.1 13.6 %collective-permute-start.3 = (f32[128,128]{1,0:T(8,128)}, f32[128,128]{1,0:T(8,128)S(1)}, u32[]{:S(2)}, u32[]{:S(2)}) collective-permute-start(f32[128,128]{1,0:T(8,128)} %get-tuple-element.18), channel_id=1, source_target_pairs={{2,4},{4,2},{3,5},{5,3},{10,12},{12,10},{11,13},{13,11},{18,20},{2... | collective-permute-start | bytes 196616 | tf_op jit(solution)/shard_map/ppermute | solution.py:134
  11.8 12.9 %collective-permute-start.2 = (f32[128,128]{1,0:T(8,128)}, f32[128,128]{1,0:T(8,128)S(1)}, u32[]{:S(2)}, u32[]{:S(2)}) collective-permute-start(f32[128,128]{1,0:T(8,128)} %get-tuple-element.19), channel_id=1, source_target_pairs={{0,2},{4,6},{2,0},{6,4},{1,3},{5,7},{3,1},{7,5},{8,10},{12,14},{10... | collective-permute-start | bytes 196616 | tf_op jit(solution)/shard_map/ppermute | solution.py:134
  17.1 7.2 %collective-permute-start.1 = (f32[128,128]{1,0:T(8,128)}, f32[128,128]{1,0:T(8,128)S(1)}, u32[]{:S(2)}, u32[]{:S(2)}) collective-permute-start(f32[128,128]{1,0:T(8,128)} %get-tuple-element.20), channel_id=1, source_target_pairs={{8,16},{16,8},{9,17},{17,9},{10,18},{18,10},{11,19},{19,11},{12,20... | collective-permute-start | bytes 196616 | tf_op jit(solution)/shard_map/ppermute | solution.py:134
  17.7 6.9 %collective-permute-start = (f32[128,128]{1,0:T(8,128)}, f32[128,128]{1,0:T(8,128)S(1)}, u32[]{:S(2)}, u32[]{:S(2)}) collective-permute-start(f32[128,128]{1,0:T(8,128)} %get-tuple-element.21), channel_id=1, source_target_pairs={{0,8},{16,24},{8,0},{24,16},{1,9},{17,25},{9,1},{25,17},{2,10},{18... | collective-permute-start | bytes 196616 | tf_op jit(solution)/shard_map/ppermute | solution.py:134
  24.2 5.6 %copy-start.9 = (s32[6,128]{1,0:T(8,128)S(1)}, s32[6,128]{1,0:T(8,128)}, u32[]{:S(2)}) copy-start(s32[6,128]{1,0:T(8,128)} %param.15) | copy-start | bytes 9220
  24.2 5.8 %copy-start.8 = (s32[20]{0:T(128)S(1)}, s32[20]{0:T(128)}, u32[]{:S(2)}) copy-start(s32[20]{0:T(128)} %parent_ref.1) | copy-start | bytes 244
  24.8 0.7 %copy-start.5 = (f32[128,768]{1,0:T(8,128)}, f32[128,768]{1,0:T(8,128)S(1)}, u32[]{:S(2)}) copy-start(f32[128,768]{1,0:T(8,128)S(1)} %select_dynamic-update-slice_fusion.slot_ref) | copy-start | bytes 1179652
  26.4 21.3 %all-to-all-start = ((f32[32,40,128]{2,1,0:T(8,128)}), f32[32,40,128]{2,1,0:T(8,128)}, u32[]{:S(2)}, u32[]{:S(2)}) async-start(f32[32,40,128]{2,1,0:T(8,128)} %broadcast_in_dim.43), calls=%async_computation | async-start | bytes 1310720 | tf_op jit(solution)/shard_map/all_to_all | solution.py:216
  30.0 1.0 %copy-start.6 = (f32[128,768]{1,0:T(8,128)S(1)}, f32[128,768]{1,0:T(8,128)}, u32[]{:S(2)}) copy-start(f32[128,768]{1,0:T(8,128)} %copy-done.5) | copy-start | bytes 1179652
  44.2 1.0 %copy-start.3 = (bf16[128,4352]{1,0:T(8,128)(2,1)}, bf16[128,4352]{1,0:T(8,128)(2,1)S(1)}, u32[]{:S(2)}) copy-start(bf16[128,4352]{1,0:T(8,128)(2,1)S(1)} %get-tuple-element.13.own_ref) | copy-start | bytes 3342340
  45.2 0.7 %copy-start.7 = (bf16[128,768]{1,0:T(8,128)(2,1)}, bf16[128,768]{1,0:T(8,128)(2,1)S(1)}, u32[]{:S(2)}) copy-start(bf16[128,768]{1,0:T(8,128)(2,1)S(1)} %get-tuple-element.15) | copy-start | bytes 589828
  47.7 11.5 %copy-start.4 = (bf16[128,4352]{1,0:T(8,128)(2,1)S(1)}, bf16[128,4352]{1,0:T(8,128)(2,1)}, u32[]{:S(2)}) copy-start(bf16[128,4352]{1,0:T(8,128)(2,1)} %copy-done.3) | copy-start | bytes 3342340
  48.7 10.4 %collective-permute-start.9 = (bf16[128,128]{1,0:T(8,128)(2,1)S(1)}, bf16[128,128]{1,0:T(8,128)(2,1)S(1)}, u32[]{:S(2)}, u32[]{:S(2)}) collective-permute-start(bf16[128,128]{1,0:T(8,128)(2,1)S(1)} %get-tuple-element.22), channel_id=1, source_target_pairs={{0,1},{1,0},{2,3},{3,2},{4,5},{5,4},{6,7},{7,6},{8,9},{9,8},{10,11... | collective-permute-start | bytes 98312 | tf_op jit(solution)/shard_map/ppermute | solution.py:134
  48.8 10.2 %collective-permute-start.7 = (bf16[128,128]{1,0:T(8,128)(2,1)S(1)}, bf16[128,128]{1,0:T(8,128)(2,1)S(1)}, u32[]{:S(2)}, u32[]{:S(2)}) collective-permute-start(bf16[128,128]{1,0:T(8,128)(2,1)S(1)} %get-tuple-element.23), channel_id=1, source_target_pairs={{2,4},{4,2},{3,5},{5,3},{10,12},{12,10},{11,13},{13,11},{18,20},{2... | collective-permute-start | bytes 98312 | tf_op jit(solution)/shard_map/ppermute | solution.py:134
  49.5 9.6 %collective-permute-start.8 = (bf16[128,128]{1,0:T(8,128)(2,1)S(1)}, bf16[128,128]{1,0:T(8,128)(2,1)S(1)}, u32[]{:S(2)}, u32[]{:S(2)}) collective-permute-start(bf16[128,128]{1,0:T(8,128)(2,1)S(1)} %get-tuple-element.24), channel_id=1, source_target_pairs={{0,2},{4,6},{2,0},{6,4},{1,3},{5,7},{3,1},{7,5},{8,10},{12,14},{10... | collective-permute-start | bytes 98312 | tf_op jit(solution)/shard_map/ppermute | solution.py:134
  53.6 5.3 %collective-permute-start.5 = (bf16[128,128]{1,0:T(8,128)(2,1)S(1)}, bf16[128,128]{1,0:T(8,128)(2,1)S(1)}, u32[]{:S(2)}, u32[]{:S(2)}) collective-permute-start(bf16[128,128]{1,0:T(8,128)(2,1)S(1)} %get-tuple-element.25), channel_id=1, source_target_pairs={{8,16},{16,8},{9,17},{17,9},{10,18},{18,10},{11,19},{19,11},{12,20... | collective-permute-start | bytes 98312 | tf_op jit(solution)/shard_map/ppermute | solution.py:134
  54.3 4.7 %collective-permute-start.6 = (bf16[128,128]{1,0:T(8,128)(2,1)S(1)}, bf16[128,128]{1,0:T(8,128)(2,1)S(1)}, u32[]{:S(2)}, u32[]{:S(2)}) collective-permute-start(bf16[128,128]{1,0:T(8,128)(2,1)S(1)} %get-tuple-element.26), channel_id=1, source_target_pairs={{0,8},{16,24},{8,0},{24,16},{1,9},{17,25},{9,1},{25,17},{2,10},{18... | collective-permute-start | bytes 98312 | tf_op jit(solution)/shard_map/ppermute | solution.py:134

commit v24 on v19

--- a/solution.py
+++ b/solution.py
@@ -89,14 +89,20 @@
     return first, second, third
 
 
-def finish_kernel(count_ref, rows_ref, own_ref, back_ref, solved_ref, vec_ref, out_ref):
+def finish_kernel(count_ref, rows_ref, own_ref, back_ref, held_ref, inverse_ref, vec_ref, out_ref):
     owned_n = own_ref.shape[1]
     kmax_here = vec_ref.shape[0]
     keep = lax.broadcasted_iota(jnp.int32, (kmax_here, 1), 0) < count_ref[0]
     chunk = 512
     rows = rows_ref[...]
     back = back_ref[...]
-    s1, s2, _ = split3(solved_ref[...])
+    h1, h2, _ = split3(held_ref[...])
+    c1, c2, _ = split3(inverse_ref[...])
+    solved = sum(
+        lax.dot_general(left, right, NT, preferred_element_type=jnp.float32)
+        for left, right in ((h1, c1), (h1, c2), (h2, c1))
+    )
+    s1, s2, _ = split3(solved)
     for start in range(0, owned_n, chunk):
         width = min(chunk, owned_n - start)
         cols = pl.ds(start, width)
@@ -110,15 +116,15 @@
         out_ref[:, cols] = total
 
 
-def finish(send_rows, counts, own, returned, solved, deflation):
+def finish(send_rows, counts, own, returned, held_t, coarse_inverse, deflation):
     vmem = pltpu.VMEM
     return pl.pallas_call(
         finish_kernel,
         out_shape=jax.ShapeDtypeStruct(own.shape, jnp.float32),
-        in_specs=[pl.BlockSpec(memory_space=pltpu.SMEM)] + [pl.BlockSpec(memory_space=vmem)] * 5,
+        in_specs=[pl.BlockSpec(memory_space=pltpu.SMEM)] + [pl.BlockSpec(memory_space=vmem)] * 6,
         out_specs=pl.BlockSpec(memory_space=vmem),
         compiler_params=pltpu.CompilerParams(vmem_limit_bytes=48 * 1024 * 1024),
-    )(counts, send_rows.reshape(-1, 1), own, returned, solved, deflation)
+    )(counts, send_rows.reshape(-1, 1), own, returned, held_t, coarse_inverse, deflation)
 
 
 def matchings(count):
@@ -220,10 +226,7 @@
         returned += [low, high]
     returned = jnp.concatenate(returned, axis=1)
 
-    solved_t = jnp.dot(
-        coarse_inverse, rows_of(held), precision=lax.Precision.HIGH, preferred_element_type=jnp.float32
-    )
-    return finish(send_rows, counts, own, returned, solved_t.T, deflation)
+    return finish(send_rows, counts, own, returned, rows_of(held).T, coarse_inverse, deflation)
 
 
 def solution(mesh):

time: 60.2 us -> 60.6 us (level)
  waiting for transfers between devices: 2.01 us -> 6.05 us
  matrix products: 3.05 us -> 1.3 us
  local copies, waits for them, and re-layouts: 9.01 us -> 7.91 us
  other arithmetic: 3.62 us -> 2.64 us
    unnamed x23 -> x17, local copies, waits for them, and re-layouts: 5.62 us -> 3.21 us
    ppermute x10, waiting for transfers between devices: 0.14 us -> 2.33 us  [swap(): return (lax.ppermute(value, axis, pairs), None)]
    all_to_all x1, waiting for transfers between devices: 1.87 us -> 3.71 us  [per_device(): held = lax.all_to_all(spread, AXES, 0, 0, tiled=True)]
    dot_general x1 -> x0, matrix products: 1.79 us -> none  [per_device(): jnp.dot(coarse_inverse, rows_of(held), precision=lax.Precision.HIGH, pref...]
    reshape x0 -> x1, local copies, waits for them, and re-layouts: none -> 1.32 us  [rows_of(): return held.reshape(-1, held.shape[-1])]
    select_n x1, other arithmetic: 0.95 us -> 0.02 us  [halo_back(): r1, got = swap(jnp.where(even, lo, hi), axis, first, extra)]
    pallas_call x1, Pallas kernels: 3.33 us -> 3.96 us  [finish(): pl.pallas_call(finish_kernel, out_shape=jax.ShapeDtypeStruct(own.shape, j...]
  transfers between devices with their start and end apart: 11 -> 11, of which waited for: 2 -> 2; matrix products, arithmetic and copies ran while one was open for 6% -> 5% of each run, Pallas kernels for 22% -> 22%
where the time goes in v24:
time: 60.6 us; the launch traced here: 60.2 us
  starting transfers between devices  24.2 us (40%)
  Pallas kernels  17.1 us (28%)
  local copies, waits for them, and re-layouts  7.91 us (13%)
  waiting for transfers between devices  6.05 us (10%)
  other arithmetic  2.64 us (4%)
  matrix products  1.3 us (2%)
  between operations  0.99 us (2%)
    ppermute x10, starting transfers between devices, swap(): return (lax.ppermute(value, axis, pairs), None)  14 us
    pallas_call x1, Pallas kernels, local_solve(): pl.pallas_call(solve_kernel, out_shape=(jax.ShapeDtypeStruct((nrhs_here,...  13.2 us
    all_to_all x1, starting transfers between devices, per_device(): held = lax.all_to_all(spread, AXES, 0, 0, tiled=True)  10.2 us
    pallas_call x1, Pallas kernels, finish(): pl.pallas_call(finish_kernel, out_shape=jax.ShapeDtypeStruct(own.shape, j...  3.96 us
    all_to_all x1, waiting for transfers between devices, per_device(): held = lax.all_to_all(spread, AXES, 0, 0, tiled=True)  3.71 us
    unnamed x17, local copies, waits for them, and re-layouts  3.21 us
    gather x2, local copies, waits for them, and re-layouts, per_device(): outgoing = jnp.take(residual, send_rows, axis=1)  2.49 us
    ppermute x10, waiting for transfers between devices, swap(): return (lax.ppermute(value, axis, pairs), None)  2.33 us
  transfers between devices with their start and end apart: 11, of which 2 were waited for; matrix products, arithmetic and copies ran while one was open for 5% of the time, Pallas kernels for 22%

profile of v24, /device:TPU:0, one launch (start us, length us, event | category | flops | bytes accessed | tf_op | source)
XLA Modules:
  0.0 60.2 jit_solution(3587225470713824298)
XLA Ops:
  0.0 0.7 %compare_and_fusion = pred[6,128]{1,0:T(8,128)(4,1)S(1)} fusion(s32[6,128]{1,0:T(8,128)} %param.12), kind=kLoop, calls=%fused_computation.30 | loop fusion | flops 4608 | bytes 3840 | tf_op jit(solution)/shard_map/jit(_take)/and | solution.py:205
  0.7 0.7 %fusion.4 = s32[768]{0:T(1024)S(1)} fusion(s32[6,128]{1,0:T(8,128)} %param.12), kind=kLoop, calls=%fused_computation.31 | loop fusion | flops 2304 | bytes 6144 | tf_op jit(solution)/shard_map/jit(_take)/broadcast_in_dim | solution.py:205
  1.4 2.0 %copy.11 = f32[128,4352]{0,1:T(8,128)S(1)} copy(f32[128,4352]{1,0:T(8,128)} %res_ref.1) | data formatting | bytes 4456448 | tf_op args[0]
  3.4 1.6 %gather_fusion = f32[768,128]{1,0:T(8,128)S(1)} fusion(f32[128,4352]{0,1:T(8,128)S(1)} %copy.11, s32[1024]{0:T(1024)S(1)} %pad_clamp_fusion), kind=kCustom, calls=%fused_computation | custom fusion | bytes 789504 | tf_op jit(solution)/shard_map/jit(_take)/gather | solution.py:205
  5.0 0.9 %copy.12 = f32[6,128,128]{1,2,0:T(8,128)} copy(f32[6,128,128]{2,1,0:T(8,128)S(1)} %bitcast.28) | data formatting | bytes 786432 | tf_op jit(solution)/shard_map/jit(_take)/gather | solution.py:205
  5.9 1.0 %select_bitcast_fusion = f32[128,6,128]{2,0,1:T(8,128)S(1)} fusion(f32[6,128,128]{1,2,0:T(8,128)} %copy.12, pred[6,128]{1,0:T(8,128)(4,1)S(1)} %compare_and_fusion), kind=kLoop, calls=%fused_computation.3 | loop fusion | flops 98304 | bytes 787200 | tf_op jit(solution)/shard_map/jit(_take)/select_n | solution.py:205
  7.0 0.5 collective-permute-start.4
  7.5 2.6 %collective-permute-start.2 = (f32[128,128]{1,0:T(8,128)S(1)}, f32[128,128]{1,0:T(8,128)S(1)}, u32[]{:S(2)}, u32[]{:S(2)}) collective-permute-start(f32[128,128]{1,0:T(8,128)S(1)} %get-tuple-element.18), channel_id=1, source_target_pairs={{0,2},{4,6},{2,0},{6,4},{1,3},{5,7},{3,1},{7,5},{8,10},{12,14},{10... | collective-permute-start | bytes 196616 | tf_op jit(solution)/shard_map/ppermute | solution.py:140
  10.1 0.7 %collective-permute-start.3 = (f32[128,128]{1,0:T(8,128)S(1)}, f32[128,128]{1,0:T(8,128)S(1)}, u32[]{:S(2)}, u32[]{:S(2)}) collective-permute-start(f32[128,128]{1,0:T(8,128)S(1)} %get-tuple-element.19), channel_id=1, source_target_pairs={{2,4},{4,2},{3,5},{5,3},{10,12},{12,10},{11,13},{13,11},{18,20},{2... | collective-permute-start | bytes 196616 | tf_op jit(solution)/shard_map/ppermute | solution.py:140
  10.7 1.6 %collective-permute-start = (f32[128,128]{1,0:T(8,128)S(1)}, f32[128,128]{1,0:T(8,128)S(1)}, u32[]{:S(2)}, u32[]{:S(2)}) collective-permute-start(f32[128,128]{1,0:T(8,128)S(1)} %get-tuple-element.20), channel_id=1, source_target_pairs={{0,8},{16,24},{8,0},{24,16},{1,9},{17,25},{9,1},{25,17},{2,10},{18... | collective-permute-start | bytes 196616 | tf_op jit(solution)/shard_map/ppermute | solution.py:140
  12.4 0.7 %collective-permute-start.1 = (f32[128,128]{1,0:T(8,128)S(1)}, f32[128,128]{1,0:T(8,128)S(1)}, u32[]{:S(2)}, u32[]{:S(2)}) collective-permute-start(f32[128,128]{1,0:T(8,128)S(1)} %get-tuple-element.21), channel_id=1, source_target_pairs={{8,16},{16,8},{9,17},{17,9},{10,18},{18,10},{11,19},{19,11},{12,20... | collective-permute-start | bytes 196616 | tf_op jit(solution)/shard_map/ppermute | solution.py:140
  13.7 1.3 %fusion.after_ref = f32[40,128]{1,0:T(8,128)S(1)} fusion(f32[128,4352]{1,0:T(8,128)S(1)} %copy-done, f32[40,4352]{1,0:T(8,128)S(1)} %copy-done.1, f32[40]{0:T(128)S(1)} %compare_convert_fusion), kind=kOutput, calls=%fused_computation.1 | convolution fusion | flops 133867520 | bytes 2945184 | tf_op jit(solution)/shard_map/dot_general | solution.py:200
  15.2 0.9 %broadcast_in_dim.29 = f32[32,40,128]{2,1,0:T(8,128)} broadcast(f32[40,128]{1,0:T(8,128)S(1)} %fusion.after_ref), dimensions={1,2} | broadcast | bytes 675840 | tf_op jit(solution)/shard_map/broadcast_in_dim | solution.py:212
  16.1 10.2 %all-to-all-start = ((f32[32,40,128]{2,1,0:T(8,128)}), f32[32,40,128]{2,1,0:T(8,128)}, u32[]{:S(2)}, u32[]{:S(2)}) async-start(f32[32,40,128]{2,1,0:T(8,128)} %broadcast_in_dim.29), calls=%async_computation | async-start | bytes 1310720 | tf_op jit(solution)/shard_map/all_to_all | solution.py:213
  26.3 13.2 %shard_map.82 = (bf16[128,4352]{1,0:T(8,128)(2,1)S(1)}, bf16[128,768]{1,0:T(8,128)(2,1)S(1)}) custom-call(s32[20]{0:T(128)S(1)} %copy-done.5, f32[128,4352]{1,0:T(8,128)S(1)} %copy-done, f32[128,768]{1,0:T(8,128)S(1)} %select_dynamic-update-slice_fusion.slot_ref, bf16[20,256,256]{2,1,0:T(8,128)(2,1)} %inv_ref.1, bf16[19,256,256]{2,1,0:T(8,128)(2,1)} %cpl_ref.1, ...), custom_call_target="tpu_custom_call" | custom-call | tf_op jit(solution)/shard_map/pallas_call | solution.py:61
  39.5 1.0 %copy-done.2 = bf16[128,4352]{1,0:T(8,128)(2,1)} copy-done((bf16[128,4352]{1,0:T(8,128)(2,1)}, bf16[128,4352]{1,0:T(8,128)(2,1)S(1)}, u32[]{:S(2)}) %copy-start.2) | copy-done | bytes 1114136
  40.5 3.7 %all-to-all-done = f32[32,40,128]{2,1,0:T(8,128)} async-done(((f32[32,40,128]{2,1,0:T(8,128)}), f32[32,40,128]{2,1,0:T(8,128)}, u32[]{:S(2)}, u32[]{:S(2)}) %all-to-all-start) | async-done | bytes 655392 | tf_op jit(solution)/shard_map/all_to_all | solution.py:213
  44.2 0.8 %collective-permute-start.5 = (bf16[128,128]{1,0:T(8,128)(2,1)S(1)}, bf16[128,128]{1,0:T(8,128)(2,1)S(1)}, u32[]{:S(2)}, u32[]{:S(2)}) collective-permute-start(bf16[128,128]{1,0:T(8,128)(2,1)S(1)} %get-tuple-element.25), channel_id=1, source_target_pairs={{8,16},{16,8},{9,17},{17,9},{10,18},{18,10},{11,19},{19,11},{12,20... | collective-permute-start | bytes 98312 | tf_op jit(solution)/shard_map/ppermute | solution.py:140
  45.0 2.8 %collective-permute-start.6 = (bf16[128,128]{1,0:T(8,128)(2,1)S(1)}, bf16[128,128]{1,0:T(8,128)(2,1)S(1)}, u32[]{:S(2)}, u32[]{:S(2)}) collective-permute-start(bf16[128,128]{1,0:T(8,128)(2,1)S(1)} %get-tuple-element.26), channel_id=1, source_target_pairs={{0,8},{16,24},{8,0},{24,16},{1,9},{17,25},{9,1},{25,17},{2,10},{18... | collective-permute-start | bytes 98312 | tf_op jit(solution)/shard_map/ppermute | solution.py:140
  48.0 1.3 %copy.13 = f32[1280,128]{0,1:T(8,128)S(1)} copy(f32[1280,128]{1,0:T(8,128)} %bitcast.9) | data formatting | bytes 1310720 | tf_op jit(solution)/shard_map/reshape | solution.py:189
  49.7 0.7 %collective-permute-start.7 = (bf16[128,128]{1,0:T(8,128)(2,1)S(1)}, bf16[128,128]{1,0:T(8,128)(2,1)S(1)}, u32[]{:S(2)}, u32[]{:S(2)}) collective-permute-start(bf16[128,128]{1,0:T(8,128)(2,1)S(1)} %get-tuple-element.23), channel_id=1, source_target_pairs={{2,4},{4,2},{3,5},{5,3},{10,12},{12,10},{11,13},{13,11},{18,20},{2... | collective-permute-start | bytes 98312 | tf_op jit(solution)/shard_map/ppermute | solution.py:140
  50.3 3.5 %collective-permute-start.8 = (bf16[128,128]{1,0:T(8,128)(2,1)S(1)}, bf16[128,128]{1,0:T(8,128)(2,1)S(1)}, u32[]{:S(2)}, u32[]{:S(2)}) collective-permute-start(bf16[128,128]{1,0:T(8,128)(2,1)S(1)} %get-tuple-element.24), channel_id=1, source_target_pairs={{0,2},{4,6},{2,0},{6,4},{1,3},{5,7},{3,1},{7,5},{8,10},{12,14},{10... | collective-permute-start | bytes 98312 | tf_op jit(solution)/shard_map/ppermute | solution.py:140
  53.8 2.3 %collective-permute-done.8 = bf16[128,128]{1,0:T(8,128)(2,1)S(1)} collective-permute-done((bf16[128,128]{1,0:T(8,128)(2,1)S(1)}, bf16[128,128]{1,0:T(8,128)(2,1)S(1)}, u32[]{:S(2)}, u32[]{:S(2)}) %collective-permute-start.8) | collective-permute-done | bytes 32800 | tf_op jit(solution)/shard_map/ppermute | solution.py:140
  56.3 4.0 %shard_map.83 = f32[128,4352]{1,0:T(8,128)} custom-call(s32[1]{0:T(128)} %copy.29.count_ref, s32[768,1]{1,0:T(8,128)S(1)} %bitcast.27, bf16[128,4352]{1,0:T(8,128)(2,1)S(1)} %copy-done.3, bf16[128,768]{1,0:T(8,128)(2,1)S(1)} %select_dynamic-update-slice_fusion.6.back_ref, f32[128,1280]{1,0:T(8,128)S(1)} %bitcast.26, f32[40,1280]{1,0:T(8,128)S(1)} %copy-done.4, ...), custom_call_target="tpu_custom_call" | custom-call | tf_op jit(solution)/shard_map/pallas_call | solution.py:121
  (41 shorter events, 0.8 us)
Async XLA Ops:
  3.4 10.3 %copy-start.1 = (f32[40,4352]{1,0:T(8,128)S(1)}, f32[40,4352]{1,0:T(8,128)}, u32[]{:S(2)}) copy-start(f32[40,4352]{1,0:T(8,128)} %vec_ref.1) | copy-start | bytes 2088964
  5.0 8.7 %copy-start = (f32[128,4352]{1,0:T(8,128)S(1)}, f32[128,4352]{1,0:T(8,128)}, u32[]{:S(2)}) copy-start(f32[128,4352]{1,0:T(8,128)} %res_ref.1) | copy-start | bytes 6684676
  7.0 8.2 %collective-permute-start.4 = (f32[128,128]{1,0:T(8,128)S(1)}, f32[128,128]{1,0:T(8,128)S(1)}, u32[]{:S(2)}, u32[]{:S(2)}) collective-permute-start(f32[128,128]{1,0:T(8,128)S(1)} %get-tuple-element.17), channel_id=1, source_target_pairs={{0,1},{1,0},{2,3},{3,2},{4,5},{5,4},{6,7},{7,6},{8,9},{9,8},{10,11... | collective-permute-start | bytes 196616 | tf_op jit(solution)/shard_map/ppermute | solution.py:140
  7.5 7.6 %collective-permute-start.2 = (f32[128,128]{1,0:T(8,128)S(1)}, f32[128,128]{1,0:T(8,128)S(1)}, u32[]{:S(2)}, u32[]{:S(2)}) collective-permute-start(f32[128,128]{1,0:T(8,128)S(1)} %get-tuple-element.18), channel_id=1, source_target_pairs={{0,2},{4,6},{2,0},{6,4},{1,3},{5,7},{3,1},{7,5},{8,10},{12,14},{10... | collective-permute-start | bytes 196616 | tf_op jit(solution)/shard_map/ppermute | solution.py:140
  10.1 5.1 %collective-permute-start.3 = (f32[128,128]{1,0:T(8,128)S(1)}, f32[128,128]{1,0:T(8,128)S(1)}, u32[]{:S(2)}, u32[]{:S(2)}) collective-permute-start(f32[128,128]{1,0:T(8,128)S(1)} %get-tuple-element.19), channel_id=1, source_target_pairs={{2,4},{4,2},{3,5},{5,3},{10,12},{12,10},{11,13},{13,11},{18,20},{2... | collective-permute-start | bytes 196616 | tf_op jit(solution)/shard_map/ppermute | solution.py:140
  10.7 4.3 %collective-permute-start = (f32[128,128]{1,0:T(8,128)S(1)}, f32[128,128]{1,0:T(8,128)S(1)}, u32[]{:S(2)}, u32[]{:S(2)}) collective-permute-start(f32[128,128]{1,0:T(8,128)S(1)} %get-tuple-element.20), channel_id=1, source_target_pairs={{0,8},{16,24},{8,0},{24,16},{1,9},{17,25},{9,1},{25,17},{2,10},{18... | collective-permute-start | bytes 196616 | tf_op jit(solution)/shard_map/ppermute | solution.py:140
  12.4 2.7 %collective-permute-start.1 = (f32[128,128]{1,0:T(8,128)S(1)}, f32[128,128]{1,0:T(8,128)S(1)}, u32[]{:S(2)}, u32[]{:S(2)}) collective-permute-start(f32[128,128]{1,0:T(8,128)S(1)} %get-tuple-element.21), channel_id=1, source_target_pairs={{8,16},{16,8},{9,17},{17,9},{10,18},{18,10},{11,19},{19,11},{12,20... | collective-permute-start | bytes 196616 | tf_op jit(solution)/shard_map/ppermute | solution.py:140
  15.0 11.2 %copy-start.5 = (s32[20]{0:T(128)S(1)}, s32[20]{0:T(128)}, u32[]{:S(2)}) copy-start(s32[20]{0:T(128)} %parent_ref.1) | copy-start | bytes 244
  16.1 28.1 %all-to-all-start = ((f32[32,40,128]{2,1,0:T(8,128)}), f32[32,40,128]{2,1,0:T(8,128)}, u32[]{:S(2)}, u32[]{:S(2)}) async-start(f32[32,40,128]{2,1,0:T(8,128)} %broadcast_in_dim.29), calls=%async_computation | async-start | bytes 1310720 | tf_op jit(solution)/shard_map/all_to_all | solution.py:213
  26.3 21.5 %copy-start.6 = (s32[6,128]{1,0:T(8,128)S(1)}, s32[6,128]{1,0:T(8,128)}, u32[]{:S(2)}) copy-start(s32[6,128]{1,0:T(8,128)} %param.12) | copy-start | bytes 9220
  39.5 1.0 %copy-start.2 = (bf16[128,4352]{1,0:T(8,128)(2,1)}, bf16[128,4352]{1,0:T(8,128)(2,1)S(1)}, u32[]{:S(2)}) copy-start(bf16[128,4352]{1,0:T(8,128)(2,1)S(1)} %get-tuple-element.13.own_ref) | copy-start | bytes 3342340
  40.5 15.8 %copy-start.4 = (f32[40,1280]{1,0:T(8,128)S(1)}, f32[40,1280]{1,0:T(8,128)}, u32[]{:S(2)}) copy-start(f32[40,1280]{1,0:T(8,128)} %inverse_ref.1) | copy-start | bytes 614404
  44.2 12.1 %copy-start.3 = (bf16[128,4352]{1,0:T(8,128)(2,1)S(1)}, bf16[128,4352]{1,0:T(8,128)(2,1)}, u32[]{:S(2)}) copy-start(bf16[128,4352]{1,0:T(8,128)(2,1)} %copy-done.2) | copy-start | bytes 3342340
  44.2 9.6 %collective-permute-start.5 = (bf16[128,128]{1,0:T(8,128)(2,1)S(1)}, bf16[128,128]{1,0:T(8,128)(2,1)S(1)}, u32[]{:S(2)}, u32[]{:S(2)}) collective-permute-start(bf16[128,128]{1,0:T(8,128)(2,1)S(1)} %get-tuple-element.25), channel_id=1, source_target_pairs={{8,16},{16,8},{9,17},{17,9},{10,18},{18,10},{11,19},{19,11},{12,20... | collective-permute-start | bytes 98312 | tf_op jit(solution)/shard_map/ppermute | solution.py:140
  45.0 8.8 %collective-permute-start.6 = (bf16[128,128]{1,0:T(8,128)(2,1)S(1)}, bf16[128,128]{1,0:T(8,128)(2,1)S(1)}, u32[]{:S(2)}, u32[]{:S(2)}) collective-permute-start(bf16[128,128]{1,0:T(8,128)(2,1)S(1)} %get-tuple-element.26), channel_id=1, source_target_pairs={{0,8},{16,24},{8,0},{24,16},{1,9},{17,25},{9,1},{25,17},{2,10},{18... | collective-permute-start | bytes 98312 | tf_op jit(solution)/shard_map/ppermute | solution.py:140
  49.3 6.9 %collective-permute-start.9 = (bf16[128,128]{1,0:T(8,128)(2,1)S(1)}, bf16[128,128]{1,0:T(8,128)(2,1)S(1)}, u32[]{:S(2)}, u32[]{:S(2)}) collective-permute-start(bf16[128,128]{1,0:T(8,128)(2,1)S(1)} %get-tuple-element.22), channel_id=1, source_target_pairs={{0,1},{1,0},{2,3},{3,2},{4,5},{5,4},{6,7},{7,6},{8,9},{9,8},{10,11... | collective-permute-start | bytes 98312 | tf_op jit(solution)/shard_map/ppermute | solution.py:140
  49.7 4.2 %collective-permute-start.7 = (bf16[128,128]{1,0:T(8,128)(2,1)S(1)}, bf16[128,128]{1,0:T(8,128)(2,1)S(1)}, u32[]{:S(2)}, u32[]{:S(2)}) collective-permute-start(bf16[128,128]{1,0:T(8,128)(2,1)S(1)} %get-tuple-element.23), channel_id=1, source_target_pairs={{2,4},{4,2},{3,5},{5,3},{10,12},{12,10},{11,13},{13,11},{18,20},{2... | collective-permute-start | bytes 98312 | tf_op jit(solution)/shard_map/ppermute | solution.py:140
  50.3 5.8 %collective-permute-start.8 = (bf16[128,128]{1,0:T(8,128)(2,1)S(1)}, bf16[128,128]{1,0:T(8,128)(2,1)S(1)}, u32[]{:S(2)}, u32[]{:S(2)}) collective-permute-start(bf16[128,128]{1,0:T(8,128)(2,1)S(1)} %get-tuple-element.24), channel_id=1, source_target_pairs={{0,2},{4,6},{2,0},{6,4},{1,3},{5,7},{3,1},{7,5},{8,10},{12,14},{10... | collective-permute-start | bytes 98312 | tf_op jit(solution)/shard_map/ppermute | solution.py:140

commit v25 on v19

--- a/solution.py
+++ b/solution.py
@@ -93,7 +93,7 @@
     owned_n = own_ref.shape[1]
     kmax_here = vec_ref.shape[0]
     keep = lax.broadcasted_iota(jnp.int32, (kmax_here, 1), 0) < count_ref[0]
-    chunk = 512
+    chunk = 1024
     rows = rows_ref[...]
     back = back_ref[...]
     s1, s2, _ = split3(solved_ref[...])

time: 60.2 us -> 60.3 us (level)
  no operation moved by 1% of the time
where the time goes in v25:
time: 60.3 us; the launch traced here: 59.8 us
  starting transfers between devices  24.6 us (41%)
  Pallas kernels  16.5 us (27%)
  local copies, waits for them, and re-layouts  9.01 us (15%)
  other arithmetic  3.62 us (6%)
  matrix products  3.05 us (5%)
  waiting for transfers between devices  2 us (3%)
  between operations  1.01 us (2%)
    ppermute x10, starting transfers between devices, swap(): return (lax.ppermute(value, axis, pairs), None)  14.4 us
    pallas_call x1, Pallas kernels, local_solve(): pl.pallas_call(solve_kernel, out_shape=(jax.ShapeDtypeStruct((nrhs_here,...  13.1 us
    all_to_all x1, starting transfers between devices, per_device(): held = lax.all_to_all(spread, AXES, 0, 0, tiled=True)  10.2 us
    unnamed x23, local copies, waits for them, and re-layouts  5.62 us
    pallas_call x1, Pallas kernels, finish(): pl.pallas_call(finish_kernel, out_shape=jax.ShapeDtypeStruct(own.shape, j...  3.37 us
    gather x2, local copies, waits for them, and re-layouts, per_device(): outgoing = jnp.take(residual, send_rows, axis=1)  2.49 us
    all_to_all x1, waiting for transfers between devices, per_device(): held = lax.all_to_all(spread, AXES, 0, 0, tiled=True)  1.86 us
    dot_general x1, matrix products, per_device(): jnp.dot(coarse_inverse, rows_of(held), precision=lax.Precision.HIGH, pref...  1.79 us
  transfers between devices with their start and end apart: 11, of which 2 were waited for; matrix products, arithmetic and copies ran while one was open for 6% of the time, Pallas kernels for 22%

profile of v25, /device:TPU:0, one launch (start us, length us, event | category | flops | bytes accessed | tf_op | source)
XLA Modules:
  0.0 59.8 jit_solution(7487931043537460452)
XLA Ops:
  0.0 0.7 %compare_and_fusion = pred[6,128]{1,0:T(8,128)(4,1)S(1)} fusion(s32[6,128]{1,0:T(8,128)} %param.12), kind=kLoop, calls=%fused_computation.30 | loop fusion | flops 4608 | bytes 3840 | tf_op jit(solution)/shard_map/jit(_take)/and | solution.py:199
  0.7 0.7 %fusion.4 = s32[768]{0:T(1024)S(1)} fusion(s32[6,128]{1,0:T(8,128)} %param.12), kind=kLoop, calls=%fused_computation.31 | loop fusion | flops 2304 | bytes 6144 | tf_op jit(solution)/shard_map/jit(_take)/broadcast_in_dim | solution.py:199
  1.4 2.0 %copy.11 = f32[128,4352]{0,1:T(8,128)S(1)} copy(f32[128,4352]{1,0:T(8,128)} %res_ref.1) | data formatting | bytes 4456448 | tf_op args[0]
  3.5 1.6 %gather_fusion = f32[768,128]{1,0:T(8,128)S(1)} fusion(f32[128,4352]{0,1:T(8,128)S(1)} %copy.11, s32[1024]{0:T(1024)S(1)} %pad_clamp_fusion), kind=kCustom, calls=%fused_computation | custom fusion | bytes 789504 | tf_op jit(solution)/shard_map/jit(_take)/gather | solution.py:199
  5.0 0.9 %copy.12 = f32[6,128,128]{1,2,0:T(8,128)} copy(f32[6,128,128]{2,1,0:T(8,128)S(1)} %bitcast.28) | data formatting | bytes 786432 | tf_op jit(solution)/shard_map/jit(_take)/gather | solution.py:199
  6.0 1.0 %select_bitcast_fusion = f32[128,6,128]{2,0,1:T(8,128)S(1)} fusion(f32[6,128,128]{1,2,0:T(8,128)} %copy.12, pred[6,128]{1,0:T(8,128)(4,1)S(1)} %compare_and_fusion), kind=kLoop, calls=%fused_computation.3 | loop fusion | flops 98304 | bytes 787200 | tf_op jit(solution)/shard_map/jit(_take)/select_n | solution.py:199
  7.5 2.6 %collective-permute-start.2 = (f32[128,128]{1,0:T(8,128)S(1)}, f32[128,128]{1,0:T(8,128)S(1)}, u32[]{:S(2)}, u32[]{:S(2)}) collective-permute-start(f32[128,128]{1,0:T(8,128)S(1)} %get-tuple-element.18), channel_id=1, source_target_pairs={{0,2},{4,6},{2,0},{6,4},{1,3},{5,7},{3,1},{7,5},{8,10},{12,14},{10... | collective-permute-start | bytes 196616 | tf_op jit(solution)/shard_map/ppermute | solution.py:134
  10.1 0.7 %collective-permute-start.3 = (f32[128,128]{1,0:T(8,128)S(1)}, f32[128,128]{1,0:T(8,128)S(1)}, u32[]{:S(2)}, u32[]{:S(2)}) collective-permute-start(f32[128,128]{1,0:T(8,128)S(1)} %get-tuple-element.19), channel_id=1, source_target_pairs={{2,4},{4,2},{3,5},{5,3},{10,12},{12,10},{11,13},{13,11},{18,20},{2... | collective-permute-start | bytes 196616 | tf_op jit(solution)/shard_map/ppermute | solution.py:134
  10.8 1.6 %collective-permute-start = (f32[128,128]{1,0:T(8,128)S(1)}, f32[128,128]{1,0:T(8,128)S(1)}, u32[]{:S(2)}, u32[]{:S(2)}) collective-permute-start(f32[128,128]{1,0:T(8,128)S(1)} %get-tuple-element.20), channel_id=1, source_target_pairs={{0,8},{16,24},{8,0},{24,16},{1,9},{17,25},{9,1},{25,17},{2,10},{18... | collective-permute-start | bytes 196616 | tf_op jit(solution)/shard_map/ppermute | solution.py:134
  12.4 0.7 %collective-permute-start.1 = (f32[128,128]{1,0:T(8,128)S(1)}, f32[128,128]{1,0:T(8,128)S(1)}, u32[]{:S(2)}, u32[]{:S(2)}) collective-permute-start(f32[128,128]{1,0:T(8,128)S(1)} %get-tuple-element.21), channel_id=1, source_target_pairs={{8,16},{16,8},{9,17},{17,9},{10,18},{18,10},{11,19},{19,11},{12,20... | collective-permute-start | bytes 196616 | tf_op jit(solution)/shard_map/ppermute | solution.py:134
  13.8 1.3 %fusion.after_ref = f32[40,128]{1,0:T(8,128)S(1)} fusion(f32[128,4352]{1,0:T(8,128)S(1)} %copy-done.1, f32[40,4352]{1,0:T(8,128)S(1)} %copy-done.2, f32[40]{0:T(128)S(1)} %compare_convert_fusion), kind=kOutput, calls=%fused_computation.1 | convolution fusion | flops 133867520 | bytes 2945184 | tf_op jit(solution)/shard_map/dot_general | solution.py:194
  15.3 0.7 %copy-done.5 = f32[128,768]{1,0:T(8,128)} copy-done((f32[128,768]{1,0:T(8,128)}, f32[128,768]{1,0:T(8,128)S(1)}, u32[]{:S(2)}) %copy-start.5) | copy-done | bytes 393240
  16.0 0.9 %broadcast_in_dim.29 = f32[32,40,128]{2,1,0:T(8,128)} broadcast(f32[40,128]{1,0:T(8,128)S(1)} %fusion.after_ref), dimensions={1,2} | broadcast | bytes 675840 | tf_op jit(solution)/shard_map/broadcast_in_dim | solution.py:206
  16.9 10.2 %all-to-all-start = ((f32[32,40,128]{2,1,0:T(8,128)}), f32[32,40,128]{2,1,0:T(8,128)}, u32[]{:S(2)}, u32[]{:S(2)}) async-start(f32[32,40,128]{2,1,0:T(8,128)} %broadcast_in_dim.29), calls=%async_computation | async-start | bytes 1310720 | tf_op jit(solution)/shard_map/all_to_all | solution.py:207
  27.3 1.0 %copy-done.6 = f32[128,768]{1,0:T(8,128)S(1)} copy-done((f32[128,768]{1,0:T(8,128)S(1)}, f32[128,768]{1,0:T(8,128)}, u32[]{:S(2)}) %copy-start.6) | copy-done | bytes 393240
  28.3 13.1 %shard_map.82 = (bf16[128,4352]{1,0:T(8,128)(2,1)S(1)}, bf16[128,768]{1,0:T(8,128)(2,1)S(1)}) custom-call(s32[20]{0:T(128)S(1)} %copy-done.8, f32[128,4352]{1,0:T(8,128)S(1)} %copy-done.1, f32[128,768]{1,0:T(8,128)S(1)} %copy-done.6, bf16[20,256,256]{2,1,0:T(8,128)(2,1)} %inv_ref.1, bf16[19,256,256]{2,1,0:T(8,128)(2,1)} %cpl_ref.1, f32[40,128]{1,0:T(8,128)S(1)} %fusion.after_ref), custom_call_target="tpu_custom_call" | custom-call | tf_op jit(solution)/shard_map/pallas_call | solution.py:61
  41.5 1.0 %copy-done.3 = bf16[128,4352]{1,0:T(8,128)(2,1)} copy-done((bf16[128,4352]{1,0:T(8,128)(2,1)}, bf16[128,4352]{1,0:T(8,128)(2,1)S(1)}, u32[]{:S(2)}) %copy-start.3) | copy-done | bytes 1114136
  42.4 0.7 %copy-done.7 = bf16[128,768]{1,0:T(8,128)(2,1)} copy-done((bf16[128,768]{1,0:T(8,128)(2,1)}, bf16[128,768]{1,0:T(8,128)(2,1)S(1)}, u32[]{:S(2)}) %copy-start.7) | copy-done | bytes 196632
  43.1 1.9 %all-to-all-done = f32[32,40,128]{2,1,0:T(8,128)} async-done(((f32[32,40,128]{2,1,0:T(8,128)}), f32[32,40,128]{2,1,0:T(8,128)}, u32[]{:S(2)}, u32[]{:S(2)}) %all-to-all-start) | async-done | bytes 655392 | tf_op jit(solution)/shard_map/all_to_all | solution.py:207
  45.0 0.9 %slice_select_fusion.1 = (bf16[128,128]{1,0:T(8,128)(2,1)S(1)}, bf16[128,128]{1,0:T(8,128)(2,1)S(1)}, bf16[128,128]{1,0:T(8,128)(2,1)S(1)}, bf16[128,128]{1,0:T(8,128)(2,1)S(1)}, bf16[128,128]{1,0:T(8,128)(2,1)S(1)}) fusion(bf16[128,768]{1,0:T(8,128)(2,1)} %copy-done.7, pred[]{:T(512)S(6)} %eq.21, pred[]{:T(512)S(6)} %eq.20, pred[]{:T(512)S(6)} %eq.19), kind=kLoop, calls=%fused_computation.19 | loop fusion | flops 81920 | bytes 360451 | tf_op jit(solution)/shard_map/jit(_where)/select_n | solution.py:152
  46.7 4.1 %collective-permute-start.8 = (bf16[128,128]{1,0:T(8,128)(2,1)S(1)}, bf16[128,128]{1,0:T(8,128)(2,1)S(1)}, u32[]{:S(2)}, u32[]{:S(2)}) collective-permute-start(bf16[128,128]{1,0:T(8,128)(2,1)S(1)} %get-tuple-element.24), channel_id=1, source_target_pairs={{0,2},{4,6},{2,0},{6,4},{1,3},{5,7},{3,1},{7,5},{8,10},{12,14},{10... | collective-permute-start | bytes 98312 | tf_op jit(solution)/shard_map/ppermute | solution.py:134
  51.5 2.8 %collective-permute-start.6 = (bf16[128,128]{1,0:T(8,128)(2,1)S(1)}, bf16[128,128]{1,0:T(8,128)(2,1)S(1)}, u32[]{:S(2)}, u32[]{:S(2)}) collective-permute-start(bf16[128,128]{1,0:T(8,128)(2,1)S(1)} %get-tuple-element.26), channel_id=1, source_target_pairs={{0,8},{16,24},{8,0},{24,16},{1,9},{17,25},{9,1},{25,17},{2,10},{18... | collective-permute-start | bytes 98312 | tf_op jit(solution)/shard_map/ppermute | solution.py:134
  54.4 1.8 %fusion.5.solved_ref = f32[128,40]{1,0:T(8,128)S(1)} fusion(f32[1280,128]{1,0:T(8,128)} %bitcast.9, f32[40,1280]{1,0:T(8,128)S(1)} %copy-done), kind=kOutput, calls=%fused_computation.34 | convolution fusion | flops 39321600 | bytes 880640 | tf_op jit(solution)/shard_map/dot_general | solution.py:223
  56.4 3.4 %shard_map.83 = f32[128,4352]{1,0:T(8,128)} custom-call(s32[1]{0:T(128)} %copy.30.count_ref, s32[768,1]{1,0:T(8,128)S(1)} %bitcast.27, bf16[128,4352]{1,0:T(8,128)(2,1)S(1)} %copy-done.4, bf16[128,768]{1,0:T(8,128)(2,1)S(1)} %select_dynamic-update-slice_fusion.6.back_ref, f32[128,40]{1,0:T(8,128)S(1)} %fusion.5.solved_ref, f32[40,4352]{1,0:T(8,128)S(1)} %copy-done.2), custom_call_target="tpu_custom_call" | custom-call | tf_op jit(solution)/shard_map/pallas_call | solution.py:115
  (47 shorter events, 2.6 us)
Async XLA Ops:
  0.0 54.4 %copy-start = (f32[40,1280]{1,0:T(8,128)S(1)}, f32[40,1280]{1,0:T(8,128)}, u32[]{:S(2)}) copy-start(f32[40,1280]{1,0:T(8,128)} %param.15) | copy-start | bytes 614404
  3.4 10.3 %copy-start.2 = (f32[40,4352]{1,0:T(8,128)S(1)}, f32[40,4352]{1,0:T(8,128)}, u32[]{:S(2)}) copy-start(f32[40,4352]{1,0:T(8,128)} %vec_ref.1) | copy-start | bytes 2088964
  5.0 8.7 %copy-start.1 = (f32[128,4352]{1,0:T(8,128)S(1)}, f32[128,4352]{1,0:T(8,128)}, u32[]{:S(2)}) copy-start(f32[128,4352]{1,0:T(8,128)} %res_ref.1) | copy-start | bytes 6684676
  7.0 8.2 %collective-permute-start.4 = (f32[128,128]{1,0:T(8,128)S(1)}, f32[128,128]{1,0:T(8,128)S(1)}, u32[]{:S(2)}, u32[]{:S(2)}) collective-permute-start(f32[128,128]{1,0:T(8,128)S(1)} %get-tuple-element.17), channel_id=1, source_target_pairs={{0,1},{1,0},{2,3},{3,2},{4,5},{5,4},{6,7},{7,6},{8,9},{9,8},{10,11... | collective-permute-start | bytes 196616 | tf_op jit(solution)/shard_map/ppermute | solution.py:134
  7.5 7.6 %collective-permute-start.2 = (f32[128,128]{1,0:T(8,128)S(1)}, f32[128,128]{1,0:T(8,128)S(1)}, u32[]{:S(2)}, u32[]{:S(2)}) collective-permute-start(f32[128,128]{1,0:T(8,128)S(1)} %get-tuple-element.18), channel_id=1, source_target_pairs={{0,2},{4,6},{2,0},{6,4},{1,3},{5,7},{3,1},{7,5},{8,10},{12,14},{10... | collective-permute-start | bytes 196616 | tf_op jit(solution)/shard_map/ppermute | solution.py:134
  10.1 5.0 %collective-permute-start.3 = (f32[128,128]{1,0:T(8,128)S(1)}, f32[128,128]{1,0:T(8,128)S(1)}, u32[]{:S(2)}, u32[]{:S(2)}) collective-permute-start(f32[128,128]{1,0:T(8,128)S(1)} %get-tuple-element.19), channel_id=1, source_target_pairs={{2,4},{4,2},{3,5},{5,3},{10,12},{12,10},{11,13},{13,11},{18,20},{2... | collective-permute-start | bytes 196616 | tf_op jit(solution)/shard_map/ppermute | solution.py:134
  10.8 4.3 %collective-permute-start = (f32[128,128]{1,0:T(8,128)S(1)}, f32[128,128]{1,0:T(8,128)S(1)}, u32[]{:S(2)}, u32[]{:S(2)}) collective-permute-start(f32[128,128]{1,0:T(8,128)S(1)} %get-tuple-element.20), channel_id=1, source_target_pairs={{0,8},{16,24},{8,0},{24,16},{1,9},{17,25},{9,1},{25,17},{2,10},{18... | collective-permute-start | bytes 196616 | tf_op jit(solution)/shard_map/ppermute | solution.py:134
  12.4 2.7 %collective-permute-start.1 = (f32[128,128]{1,0:T(8,128)S(1)}, f32[128,128]{1,0:T(8,128)S(1)}, u32[]{:S(2)}, u32[]{:S(2)}) collective-permute-start(f32[128,128]{1,0:T(8,128)S(1)} %get-tuple-element.21), channel_id=1, source_target_pairs={{8,16},{16,8},{9,17},{17,9},{10,18},{18,10},{11,19},{19,11},{12,20... | collective-permute-start | bytes 196616 | tf_op jit(solution)/shard_map/ppermute | solution.py:134
  15.0 12.0 %copy-start.9 = (s32[6,128]{1,0:T(8,128)S(1)}, s32[6,128]{1,0:T(8,128)}, u32[]{:S(2)}) copy-start(s32[6,128]{1,0:T(8,128)} %param.12) | copy-start | bytes 9220
  15.1 12.2 %copy-start.8 = (s32[20]{0:T(128)S(1)}, s32[20]{0:T(128)}, u32[]{:S(2)}) copy-start(s32[20]{0:T(128)} %parent_ref.1) | copy-start | bytes 244
  15.2 0.7 %copy-start.5 = (f32[128,768]{1,0:T(8,128)}, f32[128,768]{1,0:T(8,128)S(1)}, u32[]{:S(2)}) copy-start(f32[128,768]{1,0:T(8,128)S(1)} %select_dynamic-update-slice_fusion.slot_ref) | copy-start | bytes 1179652
  16.9 28.1 %all-to-all-start = ((f32[32,40,128]{2,1,0:T(8,128)}), f32[32,40,128]{2,1,0:T(8,128)}, u32[]{:S(2)}, u32[]{:S(2)}) async-start(f32[32,40,128]{2,1,0:T(8,128)} %broadcast_in_dim.29), calls=%async_computation | async-start | bytes 1310720 | tf_op jit(solution)/shard_map/all_to_all | solution.py:207
  27.3 1.0 %copy-start.6 = (f32[128,768]{1,0:T(8,128)S(1)}, f32[128,768]{1,0:T(8,128)}, u32[]{:S(2)}) copy-start(f32[128,768]{1,0:T(8,128)} %copy-done.5) | copy-start | bytes 1179652
  41.4 1.0 %copy-start.3 = (bf16[128,4352]{1,0:T(8,128)(2,1)}, bf16[128,4352]{1,0:T(8,128)(2,1)S(1)}, u32[]{:S(2)}) copy-start(bf16[128,4352]{1,0:T(8,128)(2,1)S(1)} %get-tuple-element.13.own_ref) | copy-start | bytes 3342340
  42.4 0.7 %copy-start.7 = (bf16[128,768]{1,0:T(8,128)(2,1)}, bf16[128,768]{1,0:T(8,128)(2,1)S(1)}, u32[]{:S(2)}) copy-start(bf16[128,768]{1,0:T(8,128)(2,1)S(1)} %get-tuple-element.15) | copy-start | bytes 589828
  45.0 11.5 %copy-start.4 = (bf16[128,4352]{1,0:T(8,128)(2,1)S(1)}, bf16[128,4352]{1,0:T(8,128)(2,1)}, u32[]{:S(2)}) copy-start(bf16[128,4352]{1,0:T(8,128)(2,1)} %copy-done.3) | copy-start | bytes 3342340
  45.9 10.4 %collective-permute-start.9 = (bf16[128,128]{1,0:T(8,128)(2,1)S(1)}, bf16[128,128]{1,0:T(8,128)(2,1)S(1)}, u32[]{:S(2)}, u32[]{:S(2)}) collective-permute-start(bf16[128,128]{1,0:T(8,128)(2,1)S(1)} %get-tuple-element.22), channel_id=1, source_target_pairs={{0,1},{1,0},{2,3},{3,2},{4,5},{5,4},{6,7},{7,6},{8,9},{9,8},{10,11... | collective-permute-start | bytes 98312 | tf_op jit(solution)/shard_map/ppermute | solution.py:134
  46.1 10.2 %collective-permute-start.7 = (bf16[128,128]{1,0:T(8,128)(2,1)S(1)}, bf16[128,128]{1,0:T(8,128)(2,1)S(1)}, u32[]{:S(2)}, u32[]{:S(2)}) collective-permute-start(bf16[128,128]{1,0:T(8,128)(2,1)S(1)} %get-tuple-element.23), channel_id=1, source_target_pairs={{2,4},{4,2},{3,5},{5,3},{10,12},{12,10},{11,13},{13,11},{18,20},{2... | collective-permute-start | bytes 98312 | tf_op jit(solution)/shard_map/ppermute | solution.py:134
  46.7 9.6 %collective-permute-start.8 = (bf16[128,128]{1,0:T(8,128)(2,1)S(1)}, bf16[128,128]{1,0:T(8,128)(2,1)S(1)}, u32[]{:S(2)}, u32[]{:S(2)}) collective-permute-start(bf16[128,128]{1,0:T(8,128)(2,1)S(1)} %get-tuple-element.24), channel_id=1, source_target_pairs={{0,2},{4,6},{2,0},{6,4},{1,3},{5,7},{3,1},{7,5},{8,10},{12,14},{10... | collective-permute-start | bytes 98312 | tf_op jit(solution)/shard_map/ppermute | solution.py:134
  50.9 5.3 %collective-permute-start.5 = (bf16[128,128]{1,0:T(8,128)(2,1)S(1)}, bf16[128,128]{1,0:T(8,128)(2,1)S(1)}, u32[]{:S(2)}, u32[]{:S(2)}) collective-permute-start(bf16[128,128]{1,0:T(8,128)(2,1)S(1)} %get-tuple-element.25), channel_id=1, source_target_pairs={{8,16},{16,8},{9,17},{17,9},{10,18},{18,10},{11,19},{19,11},{12,20... | collective-permute-start | bytes 98312 | tf_op jit(solution)/shard_map/ppermute | solution.py:134
  51.5 4.7 %collective-permute-start.6 = (bf16[128,128]{1,0:T(8,128)(2,1)S(1)}, bf16[128,128]{1,0:T(8,128)(2,1)S(1)}, u32[]{:S(2)}, u32[]{:S(2)}) collective-permute-start(bf16[128,128]{1,0:T(8,128)(2,1)S(1)} %get-tuple-element.26), channel_id=1, source_target_pairs={{0,8},{16,24},{8,0},{24,16},{1,9},{17,25},{9,1},{25,17},{2,10},{18... | collective-permute-start | bytes 98312 | tf_op jit(solution)/shard_map/ppermute | solution.py:134
